TPU v7x, 32 devices: a whole 2x2x4 slice. The times are simulated.
32 devices in a mesh: lat: 4 (over y, x), lon: 8 (over z, core).
Axes of the slice: x: 2, y: 2, z: 4, core: 2. Of those that a mesh axis runs over, the one named last changes fastest.
Arguments:
- swath_input: bfloat16 [64, 64, 64, 256], P(('lat', 'lon')), may hold values from -6 to 6
- conv_weight: bfloat16 [3, 3, 256, 256], replicated, may hold values from -0.125 to 0.125
- conv_bias: float32 [256], replicated, may hold values from -3 to 3
- block_band: int32 [64, 1], P(('lat', 'lon')), may hold values from 0 to 3, as said below
- row_offset: int32 [64], P(('lat', 'lon')), may hold values from 0 to 8
- col_offset: int32 [64], P(('lat', 'lon')), may hold values from 0 to 8
- row_weights: bfloat16 [64, 16, 32], P(('lat', 'lon')), may hold values from -1 to 1
- col_weights: bfloat16 [64, 16, 32], P(('lat', 'lon')), may hold values from -1 to 1
- background: bfloat16 [96, 192, 256], P('lat', 'lon'), may hold values from -6 to 6
- depth_weight: float32 [2, 7, 7, 256], replicated, may hold values from -0.875 to 0.875
- norm_gain: float32 [2, 256], replicated, may hold values from 0.1 to 1.9
- up_weight: bfloat16 [2, 256, 1024], replicated, may hold values from -0.375 to 0.375
- down_weight: bfloat16 [2, 1024, 256], replicated, may hold values from -0.1875 to 0.1875
Outputs:
- weather_grid: bfloat16 [96, 192, 256], P('lat', 'lon')
Inputs may be any that keep to these rules, and one draw needn't show every extreme that they name: `block_band`: block b's band is the latitude band (b // 2) // 8 of the device that holds it, or one next to it; every device sends at least one block to a neighbouring band, at most 2 to each, and some device sends exactly 2 to one.
All inputs are finite; a program needn't handle non-finite values.
Results may differ from a plain program's by a relative error of at most 0.011.
Values may be sent and summed in bfloat16 or wider, within the bound.
No kernel may reach another device: no remote copies, remote signals or barrier semaphores. Data moves between devices by JAX's collectives and lax.ppermute only.
A program may use at most 64 MiB of HBM per device.

v0:
```python
import jax
import jax.numpy as jnp
from jax import lax
from jax.sharding import PartitionSpec as P

KS = 7
HALO = 3
LAYERS = 2
CAP = 2
RB = 16
RW = 16


def shifted(value, axis, steps):
    count = lax.axis_size(axis)
    leading, last = (max(0, -steps), min(count, count - steps))
    return lax.ppermute(value, axis, [(source, source + steps) for source in range(leading, last)])


def with_halo(value, sides, width, wrap):
    for axis, dim in sides:
        size, length = (lax.axis_size(axis), value.shape[dim])
        up = [(i, (i + 1) % size) for i in range(size if wrap else size - 1)]
        down = [(j, i) for i, j in up]
        last = lax.slice_in_dim(value, length - width, length, axis=dim)
        leading = lax.slice_in_dim(value, 0, width, axis=dim)
        before = lax.ppermute(last, axis, up)
        after = lax.ppermute(leading, axis, down)
        value = jnp.concatenate([before, value, after], axis=dim)
    return value


def resample_local(blocks, row_mix, col_mix):
    row_mixed = jnp.einsum("nri,nijc->nrjc", row_mix, blocks, preferred_element_type=jnp.float32)
    both_mixed = jnp.einsum(
        "nrjc,nuj->nruc", row_mixed, col_mix.astype(jnp.float32), precision=lax.Precision.HIGHEST
    )
    return both_mixed.astype(jnp.bfloat16)


def place_rows(onehot, values):
    flat_values = values.reshape(values.shape[0], -1)
    placed = jnp.dot(onehot.astype(values.dtype), flat_values, preferred_element_type=jnp.float32)
    return placed.astype(values.dtype).reshape((onehot.shape[0],) + values.shape[1:])


def place_ints(onehot, values):
    return jnp.sum(jnp.where(onehot, values[None, :], 0), axis=1)


def keep_local(keep, values):
    shaped = keep.reshape((keep.shape[0],) + (1,) * (values.ndim - 1))
    return jnp.where(shaped, values, jnp.zeros_like(values))


def layer_apply(padded, depth_kernel, gain, up_matrix, down_matrix):
    height = padded.shape[0] - (KS - 1)
    width = padded.shape[1] - (KS - 1)
    channels = padded.shape[2]
    widened = padded.astype(jnp.float32)
    kernel = depth_kernel.reshape(KS, KS, 1, channels)
    mixed = lax.conv_general_dilated(
        widened[None],
        kernel,
        (1, 1),
        ((0, 0), (0, 0)),
        dimension_numbers=("NHWC", "HWIO", "NHWC"),
        feature_group_count=channels,
        precision=lax.Precision.HIGHEST,
    )[0]
    centered = mixed - jnp.mean(mixed, axis=-1, keepdims=True)
    variance = jnp.mean(centered * centered, axis=-1, keepdims=True)
    normed = (centered * lax.rsqrt(variance + 1e-06) * gain).astype(jnp.bfloat16)
    flat_cells = normed.reshape(height * width, -1)
    hidden = jax.nn.gelu(jnp.dot(flat_cells, up_matrix, preferred_element_type=jnp.float32)).astype(
        jnp.bfloat16
    )
    output = jnp.dot(hidden, down_matrix, preferred_element_type=jnp.float32).reshape(
        height, width, -1
    )
    residual_part = widened[HALO : HALO + height, HALO : HALO + width]
    return (residual_part + output).astype(jnp.bfloat16)


def per_device(
    swath_input,
    conv_weight,
    conv_bias,
    block_band,
    row_offset,
    col_offset,
    row_weights,
    col_weights,
    background,
    depth_weight,
    norm_gain,
    up_weight,
    down_weight,
):
    blocks_here = swath_input.shape[0]
    tile_rows = background.shape[0]
    tile_cols = background.shape[1]
    convolved = lax.conv_general_dilated(
        swath_input,
        conv_weight,
        (2, 2),
        ((1, 1), (1, 1)),
        dimension_numbers=("NHWC", "HWIO", "NHWC"),
        preferred_element_type=jnp.float32,
    )
    features = jax.nn.gelu(convolved + conv_bias).astype(jnp.bfloat16)
    own_band = lax.axis_index("lat")
    offset_band = block_band[:, 0] - own_band
    staying = offset_band == 0
    positions = jnp.arange(blocks_here, dtype=jnp.int32)
    row_list = [row_offset]
    col_list = [col_offset]
    block_list = [keep_local(staying, features)]
    rowmix_list = [row_weights]
    colmix_list = [col_weights]
    for step in (1, -1):
        going = offset_band == step
        earlier = jnp.sum(going[None, :] & (positions[None, :] < positions[:, None]), axis=1)
        table = (jnp.arange(CAP, dtype=jnp.int32)[:, None] == earlier[None, :]) & going[None, :]
        got_blocks, got_rowmix, got_colmix, got_rows, got_cols = shifted(
            (
                place_rows(table, features),
                place_rows(table, row_weights),
                place_rows(table, col_weights),
                place_ints(table, row_offset),
                place_ints(table, col_offset),
            ),
            "lat",
            step,
        )
        block_list.append(got_blocks)
        rowmix_list.append(got_rowmix)
        colmix_list.append(got_colmix)
        row_list.append(got_rows)
        col_list.append(got_cols)
    arrived = resample_local(
        jnp.concatenate(block_list, axis=0),
        jnp.concatenate(rowmix_list, axis=0),
        jnp.concatenate(colmix_list, axis=0),
    )
    all_rows = jnp.concatenate(row_list, axis=0)
    all_cols = jnp.concatenate(col_list, axis=0)
    row_place = (
        jnp.arange(tile_rows, dtype=jnp.int32)[None, :, None]
        == all_rows[:, None, None] + jnp.arange(RB, dtype=jnp.int32)[None, None, :]
    ).astype(jnp.bfloat16)
    col_place = (
        jnp.arange(tile_cols, dtype=jnp.int32)[None, :, None]
        == all_cols[:, None, None] + jnp.arange(RW, dtype=jnp.int32)[None, None, :]
    ).astype(jnp.bfloat16)
    lifted = jnp.einsum(
        "shr,sruc->shuc", row_place, arrived, preferred_element_type=jnp.float32
    ).astype(jnp.bfloat16)
    summed = jnp.einsum("swu,shuc->hwc", col_place, lifted, preferred_element_type=jnp.float32)
    state = (background.astype(jnp.float32) + summed).astype(jnp.bfloat16)
    for layer_index in range(LAYERS):
        widened = with_halo(state, (("lon", 1),), HALO, True)
        widened = with_halo(widened, (("lat", 0),), HALO, False)
        state = layer_apply(
            widened,
            depth_weight[layer_index],
            norm_gain[layer_index],
            up_weight[layer_index],
            down_weight[layer_index],
        )
    return state


def solution(mesh):
    in_specs = (
        P(("lat", "lon"), None, None, None),
        P(),
        P(),
        P(("lat", "lon"), None),
        P(("lat", "lon")),
        P(("lat", "lon")),
        P(("lat", "lon"), None, None),
        P(("lat", "lon"), None, None),
        P("lat", "lon", None),
        P(),
        P(),
        P(),
        P(),
    )
    out_specs = P("lat", "lon", None)
    return jax.shard_map(
        per_device, mesh=mesh, in_specs=in_specs, out_specs=out_specs, check_vma=False
    )
```

profile of v0, /device:TPU:0, one launch (start us, length us, event | category | flops | bytes accessed | tf_op | source)
XLA Modules:
  0.0 162.6 jit_solution(6493290220384638495)
XLA Ops:
  0.0 4.7 %copy.82 = bf16[2,64,64,256]{3,1,2,0:T(8,128)(2,1)S(1)} copy(bf16[2,64,64,256]{3,2,1,0:T(8,128)(2,1)} %param.13) | data formatting | bytes 8388608 | tf_op args[0]
  4.7 0.7 pad
  5.5 3.3 %fusion.1 = bf16[64,2,8,12,256]{4,0,3,2,1:T(8,128)(2,1)S(1)} fusion(bf16[64,2,7,2,256]{4,0,3,2,1:T(8,128)(2,1)S(1)} %slice.79, bf16[64,2,8,10,256]{4,0,3,2,1:T(8,128)(2,1)S(1)} %bitcast.126), kind=kLoop, calls=%fused_computation.4 | loop fusion | flops 18874368 | bytes 12451840 | tf_op jit(solution)/shard_map/conv_general_dilated | solution.py:103
  9.1 7.1 %copy_select_fusion = (bf16[32,16,5,256]{3,1,2,0:T(8,128)(2,1)}, bf16[32,16,5,256]{3,1,2,0:T(8,128)(2,1)S(1)}) fusion(pred[32,16,5,256]{3,0,2,1:T(32,128)(4,1)S(1)} %bitcast.137, f32[256]{0:T(256)S(1)} %copy-done.11, bf16[3,3,256,256]{3,2,1,0:T(8,128)(2,1)S(1)} %copy-done, bf16[64,2,8,12,256]{4,0,3,2,1:T(8,128)(2,1)S(1)} %fusion.1, ...), kind=kOutput, calls=%fused_computation.28 | convolution fusion | flops 2996305920 | bytes 10749008 | tf_op jit(solution)/shard_map/conv_general_dilated | solution.py:103
  17.3 1.1 copy.49
  18.6 0.7 select_reduce_fusion.1
  19.3 1.2 convolution_convert_fusion.1
  21.3 5.8 %collective-permute-start.6 = (bf16[2,32,32,256]{3,1,2,0:T(8,128)(2,1)S(1)}, bf16[2,32,32,256]{3,1,2,0:T(8,128)(2,1)}, u32[]{:S(2)}, u32[]{:S(2)}) collective-permute-start(bf16[2,32,32,256]{3,1,2,0:T(8,128)(2,1)S(1)} %copy.34), channel_id=1, source_target_pairs={{0,8},{8,16},{16,24},{1,9},{9,17},{17,25},{2,10},{10,18},{18,26},{... | collective-permute-start | bytes 3145736 | tf_op jit(solution)/shard_map/ppermute | solution.py:17
  27.1 1.2 convolution_convert_fusion
  28.5 1.5 copy.35
  30.1 1.3 collective-permute-start.7
  32.3 5.1 %collective-permute-start.4 = (bf16[2,16,32]{2,1,0:T(8,128)(2,1)}, bf16[2,16,32]{2,1,0:T(8,128)(2,1)}, u32[]{:S(2)}, u32[]{:S(2)}) collective-permute-start(bf16[2,16,32]{2,1,0:T(8,128)(2,1)} %reshape.188), channel_id=1, source_target_pairs={{0,8},{8,16},{16,24},{1,9},{9,17},{17,25},{2,10},{10,18},{18,26},{... | collective-permute-start | bytes 6152 | tf_op jit(solution)/shard_map/ppermute | solution.py:17
  38.2 1.3 collective-permute-start.5
  39.5 5.1 %collective-permute-start = (s32[2]{0:T(128)}, s32[2]{0:T(128)}, u32[]{:S(2)}, u32[]{:S(2)}) collective-permute-start(s32[2]{0:T(128)} %get-tuple-element.8), channel_id=1, source_target_pairs={{0,8},{8,16},{16,24},{1,9},{9,17},{17,25},{2,10},{10,18},{18,26},{... | collective-permute-start | bytes 32 | tf_op jit(solution)/shard_map/ppermute | solution.py:17
  44.7 0.7 convolution_convert_fusion.6
  46.1 1.7 %copy.31 = bf16[32,16,5,256]{3,0,2,1:T(8,128)(2,1)S(1)} copy(bf16[32,16,5,256]{3,1,2,0:T(8,128)(2,1)} %get-tuple-element.24) | data formatting | bytes 2621440 | tf_op jit(solution)/shard_map/jit(_where)/select_n | solution.py:53
  47.8 1.3 reshape.185
  49.2 1.3 reshape.186
  50.6 1.3 collective-permute-start.1
  51.9 24.5 %collective-permute-done.1 = s32[2]{0:T(128)S(1)} collective-permute-done((s32[2]{0:T(128)}, s32[2]{0:T(128)S(1)}, u32[]{:S(2)}, u32[]{:S(2)}) %collective-permute-start.1) | collective-permute-done | bytes 40 | tf_op jit(solution)/shard_map/ppermute | solution.py:17
  76.4 5.3 %collective-permute-start.8 = (s32[2]{0:T(128)}, s32[2]{0:T(128)S(1)}, u32[]{:S(2)}, u32[]{:S(2)}) collective-permute-start(s32[2]{0:T(128)} %get-tuple-element.5), channel_id=1, source_target_pairs={{0,8},{8,16},{16,24},{1,9},{9,17},{17,25},{2,10},{10,18},{18,26},{... | collective-permute-start | bytes 32 | tf_op jit(solution)/shard_map/ppermute | solution.py:17
  81.8 0.7 pad_add_fusion
  83.1 1.3 collective-permute-start.9
  84.4 4.6 %collective-permute-done.9 = s32[2]{0:T(128)S(1)} collective-permute-done((s32[2]{0:T(128)}, s32[2]{0:T(128)S(1)}, u32[]{:S(2)}, u32[]{:S(2)}) %collective-permute-start.9) | collective-permute-done | bytes 40 | tf_op jit(solution)/shard_map/ppermute | solution.py:17
  89.0 4.8 %collective-permute-start.2 = (bf16[2,16,32]{2,1,0:T(8,128)(2,1)}, bf16[2,16,32]{2,1,0:T(8,128)(2,1)S(1)}, u32[]{:S(2)}, u32[]{:S(2)}) collective-permute-start(bf16[2,16,32]{2,1,0:T(8,128)(2,1)} %reshape.185), channel_id=1, source_target_pairs={{0,8},{8,16},{16,24},{1,9},{9,17},{17,25},{2,10},{10,18},{18,26},{... | collective-permute-start | bytes 6152 | tf_op jit(solution)/shard_map/ppermute | solution.py:17
  93.9 0.7 pad_add_fusion.1
  94.7 1.3 collective-permute-start.3
  96.1 2.1 %fusion.5 = f32[6,16,32,256]{3,1,2,0:T(8,128)S(1)} fusion(bf16[2,32,32,256]{3,1,2,0:T(8,128)(2,1)} %collective-permute-done.7, bf16[2,32,32,256]{3,1,2,0:T(8,128)(2,1)} %collective-permute-done.6, bf16[2,32,32,256]{3,1,2,0:T(8,128)(2,1)S(1)} %slice_bitcast_fusion.1, bf16[2,16,32]{2,1,0:T(8,128)(2,1)} %collective-permute-done.5, ...), kind=kOutput, calls=%fused_computation.12 | convolution fusion | flops 59787264 | bytes 6297600 | tf_op jit(solution)/shard_map/nri,nijc->nrjc/dot_general | solution.py:34
  98.2 2.3 %collective-permute-done.3 = bf16[2,16,32]{2,1,0:T(8,128)(2,1)S(1)} collective-permute-done((bf16[2,16,32]{2,1,0:T(8,128)(2,1)}, bf16[2,16,32]{2,1,0:T(8,128)(2,1)S(1)}, u32[]{:S(2)}, u32[]{:S(2)}) %collective-permute-start.3) | collective-permute-done | bytes 2080 | tf_op jit(solution)/shard_map/ppermute | solution.py:17
  100.5 3.0 %fusion.42 = bf16[6,16,16,256]{3,2,1,0:T(8,128)(2,1)S(1)} fusion(f32[6,16,32,256]{3,1,2,0:T(8,128)S(1)} %fusion.5, bf16[2,16,32]{2,1,0:T(8,128)(2,1)S(1)} %collective-permute-done.3, bf16[2,16,32]{2,1,0:T(8,128)(2,1)S(1)} %collective-permute-done.2, bf16[2,16,32]{2,1,0:T(8,128)(2,1)S(1)} %copy-done.2), kind=kOutput, calls=%fused_computation.47 | convolution fusion | flops 151406592 | bytes 3938304 | tf_op jit(solution)/shard_map/nrjc,nuj->nruc/dot_general | solution.py:35
  103.5 0.8 convolution_convert_fusion.2
  104.9 3.5 %collective-permute-start.11 = (bf16[24,3,256]{2,1,0:T(4,128)(2,1)S(1)}, bf16[24,3,256]{2,1,0:T(4,128)(2,1)S(1)}, u32[]{:S(2)}, u32[]{:S(2)}) collective-permute-start(bf16[24,3,256]{2,1,0:T(4,128)(2,1)S(1)} %get-tuple-element.18), channel_id=1, source_target_pairs={{1,0},{2,1},{3,2},{4,3},{5,4},{6,5},{7,6},{0,7},{9,8},{10,9},{11,1... | collective-permute-start | bytes 110600 | tf_op jit(solution)/shard_map/ppermute | solution.py:28
  108.4 1.8 %collective-permute-done.10 = bf16[24,3,256]{2,1,0:T(4,128)(2,1)S(1)} collective-permute-done((bf16[24,3,256]{2,1,0:T(4,128)(2,1)S(1)}, bf16[24,3,256]{2,1,0:T(4,128)(2,1)S(1)}, u32[]{:S(2)}, u32[]{:S(2)}) %collective-permute-start.10) | collective-permute-done | bytes 36896 | tf_op jit(solution)/shard_map/ppermute | solution.py:27
  110.3 4.8 %collective-permute-start.12 = (bf16[3,30,256]{2,1,0:T(8,128)(2,1)S(1)}, bf16[3,30,256]{2,1,0:T(8,128)(2,1)S(1)}, u32[]{:S(2)}, u32[]{:S(2)}) collective-permute-start(bf16[3,30,256]{2,1,0:T(8,128)(2,1)S(1)} %get-tuple-element.13), channel_id=1, source_target_pairs={{0,8},{8,16},{16,24},{1,9},{9,17},{17,25},{2,10},{10,18},{18,26},{... | collective-permute-start | bytes 138248 | tf_op jit(solution)/shard_map/ppermute | solution.py:27
  115.1 1.6 collective-permute-start.13
  116.8 4.3 %collective-permute-done.13 = bf16[3,30,256]{2,1,0:T(8,128)(2,1)S(1)} collective-permute-done((bf16[3,30,256]{2,1,0:T(8,128)(2,1)S(1)}, bf16[3,30,256]{2,1,0:T(8,128)(2,1)S(1)}, u32[]{:S(2)}, u32[]{:S(2)}) %collective-permute-start.13) | collective-permute-done | bytes 46112 | tf_op jit(solution)/shard_map/ppermute | solution.py:28
  121.3 9.3 %fusion.92 = (f32[24,24]{1,0:T(8,128)S(1)}, f32[1,24,24,256]{3,0,2,1:T(1,128)S(1)}) fusion(f32[2,7,7,256]{3,0,2,1:T(2,128)S(1)} %copy-done.10, bf16[1,30,30,256]{3,2,1,0:T(8,128)(2,1)S(1)} %maximum_bitcast_fusion), kind=kOutput, calls=%fused_computation.139 | convolution fusion | flops 86851008 | bytes 1133824 | tf_op jit(solution)/shard_map/conv_general_dilated | solution.py:62
  130.9 1.5 multiply_convert_fusion.1
  132.5 0.9 fusion.28
  134.3 3.5 %collective-permute-start.15 = (bf16[24,3,256]{2,1,0:T(4,128)(2,1)S(1)}, bf16[24,3,256]{2,1,0:T(4,128)(2,1)S(1)}, u32[]{:S(2)}, u32[]{:S(2)}) collective-permute-start(bf16[24,3,256]{2,1,0:T(4,128)(2,1)S(1)} %get-tuple-element.16), channel_id=1, source_target_pairs={{1,0},{2,1},{3,2},{4,3},{5,4},{6,5},{7,6},{0,7},{9,8},{10,9},{11,1... | collective-permute-start | bytes 110600 | tf_op jit(solution)/shard_map/ppermute | solution.py:28
  137.8 2.0 %collective-permute-done.14 = bf16[24,3,256]{2,1,0:T(4,128)(2,1)S(1)} collective-permute-done((bf16[24,3,256]{2,1,0:T(4,128)(2,1)S(1)}, bf16[24,3,256]{2,1,0:T(4,128)(2,1)S(1)}, u32[]{:S(2)}, u32[]{:S(2)}) %collective-permute-start.14) | collective-permute-done | bytes 36896 | tf_op jit(solution)/shard_map/ppermute | solution.py:27
  139.9 3.2 %collective-permute-start.16 = (bf16[3,30,256]{2,1,0:T(8,128)(2,1)S(1)}, bf16[3,30,256]{2,1,0:T(8,128)(2,1)S(1)}, u32[]{:S(2)}, u32[]{:S(2)}) collective-permute-start(bf16[3,30,256]{2,1,0:T(8,128)(2,1)S(1)} %get-tuple-element.11), channel_id=1, source_target_pairs={{0,8},{8,16},{16,24},{1,9},{9,17},{17,25},{2,10},{10,18},{18,26},{... | collective-permute-start | bytes 138248 | tf_op jit(solution)/shard_map/ppermute | solution.py:27
  143.1 1.3 collective-permute-start.17
  144.8 4.3 %collective-permute-done.17 = bf16[3,30,256]{2,1,0:T(8,128)(2,1)S(1)} collective-permute-done((bf16[3,30,256]{2,1,0:T(8,128)(2,1)S(1)}, bf16[3,30,256]{2,1,0:T(8,128)(2,1)S(1)}, u32[]{:S(2)}, u32[]{:S(2)}) %collective-permute-start.17) | collective-permute-done | bytes 46112 | tf_op jit(solution)/shard_map/ppermute | solution.py:28
  149.3 9.3 %fusion.93 = (f32[24,24]{1,0:T(8,128)S(1)}, f32[1,24,24,256]{3,0,2,1:T(1,128)S(1)}) fusion(f32[2,7,7,256]{3,0,2,1:T(2,128)S(1)} %copy-done.10, bf16[1,30,30,256]{3,2,1,0:T(8,128)(2,1)S(1)} %maximum_bitcast_fusion.1), kind=kOutput, calls=%fused_computation.140 | convolution fusion | flops 86851008 | bytes 1133824 | tf_op jit(solution)/shard_map/conv_general_dilated | solution.py:62
  158.9 1.5 multiply_convert_fusion
  160.4 0.9 fusion.36
  161.4 1.2 fusion.48
  (76 shorter events, 9.0 us)
Async XLA Ops:
  0.0 9.1 %copy-start = (bf16[3,3,256,256]{3,2,1,0:T(8,128)(2,1)S(1)}, bf16[3,3,256,256]{3,2,1,0:T(8,128)(2,1)}, u32[]{:S(2)}) copy-start(bf16[3,3,256,256]{3,2,1,0:T(8,128)(2,1)} %param.14) | copy-start | bytes 3538948
  5.5 3.3 %copy-start.7 = (s32[2,1]{0,1:T(1,128)S(1)}, s32[2,1]{0,1:T(1,128)}, u32[]{:S(2)}) copy-start(s32[2,1]{0,1:T(1,128)} %param.16) | copy-start | bytes 28
  5.5 3.6 %copy-start.11 = (f32[256]{0:T(256)S(1)}, f32[256]{0:T(256)}, u32[]{:S(2)}) copy-start(f32[256]{0:T(256)} %param.15) | copy-start | bytes 3076
  5.5 3.6 %copy-start.12 = (pred[16,5]{0,1:T(8,128)(4,1)S(1)}, pred[16,5]{0,1:T(8,128)(4,1)}, u32[]{:S(2)}) copy-start(pred[16,5]{0,1:T(8,128)(4,1)} %constant.50) | copy-start | bytes 244
  16.7 1.9 %copy-start.5 = (s32[2]{0:T(128)S(1)}, s32[2]{0:T(128)}, u32[]{:S(2)}) copy-start(s32[2]{0:T(128)} %param.17) | copy-start | bytes 28
  16.7 1.8 %copy-start.6 = (s32[2]{0:T(128)S(1)}, s32[2]{0:T(128)}, u32[]{:S(2)}) copy-start(s32[2]{0:T(128)} %param.18) | copy-start | bytes 28
  21.3 74.7 %collective-permute-start.6 = (bf16[2,32,32,256]{3,1,2,0:T(8,128)(2,1)S(1)}, bf16[2,32,32,256]{3,1,2,0:T(8,128)(2,1)}, u32[]{:S(2)}, u32[]{:S(2)}) collective-permute-start(bf16[2,32,32,256]{3,1,2,0:T(8,128)(2,1)S(1)} %copy.34), channel_id=1, source_target_pairs={{0,8},{8,16},{16,24},{1,9},{9,17},{17,25},{2,10},{10,18},{18,26},{... | collective-permute-start | bytes 3145736 | tf_op jit(solution)/shard_map/ppermute | solution.py:17
  28.4 3.0 %copy-start.3 = (bf16[2,16,32]{2,1,0:T(8,128)(2,1)S(1)}, bf16[2,16,32]{2,1,0:T(8,128)(2,1)}, u32[]{:S(2)}) copy-start(bf16[2,16,32]{2,1,0:T(8,128)(2,1)} %param.19) | copy-start | bytes 6148
  28.4 16.2 %copy-start.2 = (bf16[2,16,32]{2,1,0:T(8,128)(2,1)S(1)}, bf16[2,16,32]{2,1,0:T(8,128)(2,1)}, u32[]{:S(2)}) copy-start(bf16[2,16,32]{2,1,0:T(8,128)(2,1)} %param.20) | copy-start | bytes 6148
  30.1 66.0 %collective-permute-start.7 = (bf16[2,32,32,256]{3,1,2,0:T(8,128)(2,1)}, bf16[2,32,32,256]{3,1,2,0:T(8,128)(2,1)}, u32[]{:S(2)}, u32[]{:S(2)}) collective-permute-start(bf16[2,32,32,256]{3,1,2,0:T(8,128)(2,1)} %copy.35), channel_id=1, source_target_pairs={{8,0},{16,8},{24,16},{9,1},{17,9},{25,17},{10,2},{18,10},{26,18},{... | collective-permute-start | bytes 3145736 | tf_op jit(solution)/shard_map/ppermute | solution.py:17
  32.3 62.4 %collective-permute-start.4 = (bf16[2,16,32]{2,1,0:T(8,128)(2,1)}, bf16[2,16,32]{2,1,0:T(8,128)(2,1)}, u32[]{:S(2)}, u32[]{:S(2)}) collective-permute-start(bf16[2,16,32]{2,1,0:T(8,128)(2,1)} %reshape.188), channel_id=1, source_target_pairs={{0,8},{8,16},{16,24},{1,9},{9,17},{17,25},{2,10},{10,18},{18,26},{... | collective-permute-start | bytes 6152 | tf_op jit(solution)/shard_map/ppermute | solution.py:17
  38.2 57.8 %collective-permute-start.5 = (bf16[2,16,32]{2,1,0:T(8,128)(2,1)}, bf16[2,16,32]{2,1,0:T(8,128)(2,1)}, u32[]{:S(2)}, u32[]{:S(2)}) collective-permute-start(bf16[2,16,32]{2,1,0:T(8,128)(2,1)} %reshape.189), channel_id=1, source_target_pairs={{8,0},{16,8},{24,16},{9,1},{17,9},{25,17},{10,2},{18,10},{26,18},{... | collective-permute-start | bytes 6152 | tf_op jit(solution)/shard_map/ppermute | solution.py:17
  39.5 11.1 %collective-permute-start = (s32[2]{0:T(128)}, s32[2]{0:T(128)}, u32[]{:S(2)}, u32[]{:S(2)}) collective-permute-start(s32[2]{0:T(128)} %get-tuple-element.8), channel_id=1, source_target_pairs={{0,8},{8,16},{16,24},{1,9},{9,17},{17,25},{2,10},{10,18},{18,26},{... | collective-permute-start | bytes 32 | tf_op jit(solution)/shard_map/ppermute | solution.py:17
  50.6 25.8 %collective-permute-start.1 = (s32[2]{0:T(128)}, s32[2]{0:T(128)S(1)}, u32[]{:S(2)}, u32[]{:S(2)}) collective-permute-start(s32[2]{0:T(128)} %get-tuple-element.7), channel_id=1, source_target_pairs={{8,0},{16,8},{24,16},{9,1},{17,9},{25,17},{10,2},{18,10},{26,18},{... | collective-permute-start | bytes 32 | tf_op jit(solution)/shard_map/ppermute | solution.py:17
  76.4 6.7 %collective-permute-start.8 = (s32[2]{0:T(128)}, s32[2]{0:T(128)S(1)}, u32[]{:S(2)}, u32[]{:S(2)}) collective-permute-start(s32[2]{0:T(128)} %get-tuple-element.5), channel_id=1, source_target_pairs={{0,8},{8,16},{16,24},{1,9},{9,17},{17,25},{2,10},{10,18},{18,26},{... | collective-permute-start | bytes 32 | tf_op jit(solution)/shard_map/ppermute | solution.py:17
  83.1 5.9 %collective-permute-start.9 = (s32[2]{0:T(128)}, s32[2]{0:T(128)S(1)}, u32[]{:S(2)}, u32[]{:S(2)}) collective-permute-start(s32[2]{0:T(128)} %get-tuple-element.6), channel_id=1, source_target_pairs={{8,0},{16,8},{24,16},{9,1},{17,9},{25,17},{10,2},{18,10},{26,18},{... | collective-permute-start | bytes 32 | tf_op jit(solution)/shard_map/ppermute | solution.py:17
  89.0 9.2 %collective-permute-start.2 = (bf16[2,16,32]{2,1,0:T(8,128)(2,1)}, bf16[2,16,32]{2,1,0:T(8,128)(2,1)S(1)}, u32[]{:S(2)}, u32[]{:S(2)}) collective-permute-start(bf16[2,16,32]{2,1,0:T(8,128)(2,1)} %reshape.185), channel_id=1, source_target_pairs={{0,8},{8,16},{16,24},{1,9},{9,17},{17,25},{2,10},{10,18},{18,26},{... | collective-permute-start | bytes 6152 | tf_op jit(solution)/shard_map/ppermute | solution.py:17
  94.7 5.7 %collective-permute-start.3 = (bf16[2,16,32]{2,1,0:T(8,128)(2,1)}, bf16[2,16,32]{2,1,0:T(8,128)(2,1)S(1)}, u32[]{:S(2)}, u32[]{:S(2)}) collective-permute-start(bf16[2,16,32]{2,1,0:T(8,128)(2,1)} %reshape.186), channel_id=1, source_target_pairs={{8,0},{16,8},{24,16},{9,1},{17,9},{25,17},{10,2},{18,10},{26,18},{... | collective-permute-start | bytes 6152 | tf_op jit(solution)/shard_map/ppermute | solution.py:17
  98.2 6.1 %copy-start.1 = (bf16[24,24,256]{2,1,0:T(8,128)(2,1)S(1)}, bf16[24,24,256]{2,1,0:T(8,128)(2,1)}, u32[]{:S(2)}) copy-start(bf16[24,24,256]{2,1,0:T(8,128)(2,1)} %param.21) | copy-start | bytes 884740
  103.5 13.2 %copy-start.4 = (f32[2,256]{1,0:T(2,128)S(1)}, f32[2,256]{1,0:T(2,128)}, u32[]{:S(2)}) copy-start(f32[2,256]{1,0:T(2,128)} %param.23) | copy-start | bytes 6148
  103.5 17.8 %copy-start.10 = (f32[2,7,7,256]{3,0,2,1:T(2,128)S(1)}, f32[2,7,7,256]{3,0,2,1:T(2,128)}, u32[]{:S(2)}) copy-start(f32[2,7,7,256]{3,0,2,1:T(2,128)} %param.22) | copy-start | bytes 301060
  104.8 5.4 %collective-permute-start.10 = (bf16[24,3,256]{2,1,0:T(4,128)(2,1)S(1)}, bf16[24,3,256]{2,1,0:T(4,128)(2,1)S(1)}, u32[]{:S(2)}, u32[]{:S(2)}) collective-permute-start(bf16[24,3,256]{2,1,0:T(4,128)(2,1)S(1)} %get-tuple-element.17), channel_id=1, source_target_pairs={{0,1},{1,2},{2,3},{3,4},{4,5},{5,6},{6,7},{7,0},{8,9},{9,10},{10,1... | collective-permute-start | bytes 110600 | tf_op jit(solution)/shard_map/ppermute | solution.py:27
  104.9 5.3 %collective-permute-start.11 = (bf16[24,3,256]{2,1,0:T(4,128)(2,1)S(1)}, bf16[24,3,256]{2,1,0:T(4,128)(2,1)S(1)}, u32[]{:S(2)}, u32[]{:S(2)}) collective-permute-start(bf16[24,3,256]{2,1,0:T(4,128)(2,1)S(1)} %get-tuple-element.18), channel_id=1, source_target_pairs={{1,0},{2,1},{3,2},{4,3},{5,4},{6,5},{7,6},{0,7},{9,8},{10,9},{11,1... | collective-permute-start | bytes 110600 | tf_op jit(solution)/shard_map/ppermute | solution.py:28
  110.3 6.6 %collective-permute-start.12 = (bf16[3,30,256]{2,1,0:T(8,128)(2,1)S(1)}, bf16[3,30,256]{2,1,0:T(8,128)(2,1)S(1)}, u32[]{:S(2)}, u32[]{:S(2)}) collective-permute-start(bf16[3,30,256]{2,1,0:T(8,128)(2,1)S(1)} %get-tuple-element.13), channel_id=1, source_target_pairs={{0,8},{8,16},{16,24},{1,9},{9,17},{17,25},{2,10},{10,18},{18,26},{... | collective-permute-start | bytes 138248 | tf_op jit(solution)/shard_map/ppermute | solution.py:27
  115.1 6.0 %collective-permute-start.13 = (bf16[3,30,256]{2,1,0:T(8,128)(2,1)S(1)}, bf16[3,30,256]{2,1,0:T(8,128)(2,1)S(1)}, u32[]{:S(2)}, u32[]{:S(2)}) collective-permute-start(bf16[3,30,256]{2,1,0:T(8,128)(2,1)S(1)} %get-tuple-element.14), channel_id=1, source_target_pairs={{8,0},{16,8},{24,16},{9,1},{17,9},{25,17},{10,2},{18,10},{26,18},{... | collective-permute-start | bytes 138248 | tf_op jit(solution)/shard_map/ppermute | solution.py:28
  130.6 1.9 %copy-start.8 = (bf16[2,256,1024]{2,1,0:T(8,128)(2,1)S(1)}, bf16[2,256,1024]{2,1,0:T(8,128)(2,1)}, u32[]{:S(2)}) copy-start(bf16[2,256,1024]{2,1,0:T(8,128)(2,1)} %param.24) | copy-start | bytes 3145732
  132.4 1.2 copy-start.9
  134.2 5.6 %collective-permute-start.14 = (bf16[24,3,256]{2,1,0:T(4,128)(2,1)S(1)}, bf16[24,3,256]{2,1,0:T(4,128)(2,1)S(1)}, u32[]{:S(2)}, u32[]{:S(2)}) collective-permute-start(bf16[24,3,256]{2,1,0:T(4,128)(2,1)S(1)} %get-tuple-element.15), channel_id=1, source_target_pairs={{0,1},{1,2},{2,3},{3,4},{4,5},{5,6},{6,7},{7,0},{8,9},{9,10},{10,1... | collective-permute-start | bytes 110600 | tf_op jit(solution)/shard_map/ppermute | solution.py:27
  134.3 5.6 %collective-permute-start.15 = (bf16[24,3,256]{2,1,0:T(4,128)(2,1)S(1)}, bf16[24,3,256]{2,1,0:T(4,128)(2,1)S(1)}, u32[]{:S(2)}, u32[]{:S(2)}) collective-permute-start(bf16[24,3,256]{2,1,0:T(4,128)(2,1)S(1)} %get-tuple-element.16), channel_id=1, source_target_pairs={{1,0},{2,1},{3,2},{4,3},{5,4},{6,5},{7,6},{0,7},{9,8},{10,9},{11,1... | collective-permute-start | bytes 110600 | tf_op jit(solution)/shard_map/ppermute | solution.py:28
  139.9 4.9 %collective-permute-start.16 = (bf16[3,30,256]{2,1,0:T(8,128)(2,1)S(1)}, bf16[3,30,256]{2,1,0:T(8,128)(2,1)S(1)}, u32[]{:S(2)}, u32[]{:S(2)}) collective-permute-start(bf16[3,30,256]{2,1,0:T(8,128)(2,1)S(1)} %get-tuple-element.11), channel_id=1, source_target_pairs={{0,8},{8,16},{16,24},{1,9},{9,17},{17,25},{2,10},{10,18},{18,26},{... | collective-permute-start | bytes 138248 | tf_op jit(solution)/shard_map/ppermute | solution.py:27
  143.1 6.0 %collective-permute-start.17 = (bf16[3,30,256]{2,1,0:T(8,128)(2,1)S(1)}, bf16[3,30,256]{2,1,0:T(8,128)(2,1)S(1)}, u32[]{:S(2)}, u32[]{:S(2)}) collective-permute-start(bf16[3,30,256]{2,1,0:T(8,128)(2,1)S(1)} %get-tuple-element.12), channel_id=1, source_target_pairs={{8,0},{16,8},{24,16},{9,1},{17,9},{25,17},{10,2},{18,10},{26,18},{... | collective-permute-start | bytes 138248 | tf_op jit(solution)/shard_map/ppermute | solution.py:28
where the time goes:
time: 163 us
  starting transfers between devices  50.6 us (31%)
  waiting for transfers between devices  45 us (28%)
  matrix products  39.7 us (24%)
  local copies, waits for them, and re-layouts  16.9 us (10%)
  other arithmetic  9.81 us (6%)
    ppermute x10, starting transfers between devices, shifted(): lax.ppermute(value, axis, [(source, source + steps) for source in range(l...  32.6 us
    ppermute x10, waiting for transfers between devices, shifted(): lax.ppermute(value, axis, [(source, source + steps) for source in range(l...  32.1 us
    conv_general_dilated x2, matrix products, layer_apply(): lax.conv_general_dilated(widened[None], kernel, (1, 1), ((0, 0), (0, 0)),...  18.5 us
    ppermute x4, starting transfers between devices, with_halo(): after = lax.ppermute(leading, axis, down)  9.91 us
    ppermute x4, waiting for transfers between devices, with_halo(): after = lax.ppermute(leading, axis, down)  8.51 us
    ppermute x4, starting transfers between devices, with_halo(): before = lax.ppermute(last, axis, up)  8.12 us
    unnamed x33, local copies, waits for them, and re-layouts  7.19 us
    conv_general_dilated x1, matrix products, per_device(): lax.conv_general_dilated(swath_input, conv_weight, (2, 2), ((1, 1), (1, 1...  7.11 us
  transfers between devices with their start and end apart: 18, of which 10 were waited for; matrix products, arithmetic and copies ran while one was open for 9% of the time, Pallas kernels for 0%

commit v1 on v0

--- a/solution.py
+++ b/solution.py
@@ -53,21 +53,21 @@
     return jnp.where(shaped, values, jnp.zeros_like(values))
 
 
+def depthwise(widened, depth_kernel, height, width):
+    mixed = None
+    for e in range(KS):
+        column = widened[:, e : e + width]
+        for a in range(KS):
+            term = column[a : a + height] * depth_kernel[a, e]
+            mixed = term if mixed is None else mixed + term
+    return mixed
+
+
 def layer_apply(padded, depth_kernel, gain, up_matrix, down_matrix):
     height = padded.shape[0] - (KS - 1)
     width = padded.shape[1] - (KS - 1)
-    channels = padded.shape[2]
     widened = padded.astype(jnp.float32)
-    kernel = depth_kernel.reshape(KS, KS, 1, channels)
-    mixed = lax.conv_general_dilated(
-        widened[None],
-        kernel,
-        (1, 1),
-        ((0, 0), (0, 0)),
-        dimension_numbers=("NHWC", "HWIO", "NHWC"),
-        feature_group_count=channels,
-        precision=lax.Precision.HIGHEST,
-    )[0]
+    mixed = depthwise(widened, depth_kernel, height, width)
     centered = mixed - jnp.mean(mixed, axis=-1, keepdims=True)
     variance = jnp.mean(centered * centered, axis=-1, keepdims=True)
     normed = (centered * lax.rsqrt(variance + 1e-06) * gain).astype(jnp.bfloat16)
@@ -100,6 +100,8 @@
     blocks_here = swath_input.shape[0]
     tile_rows = background.shape[0]
     tile_cols = background.shape[1]
+    channels = background.shape[2]
+    bands = lax.axis_size("lat")
     convolved = lax.conv_general_dilated(
         swath_input,
         conv_weight,
@@ -109,40 +111,33 @@
         preferred_element_type=jnp.float32,
     )
     features = jax.nn.gelu(convolved + conv_bias).astype(jnp.bfloat16)
+    resampled = resample_local(features, row_weights, col_weights)
     own_band = lax.axis_index("lat")
     offset_band = block_band[:, 0] - own_band
     staying = offset_band == 0
     positions = jnp.arange(blocks_here, dtype=jnp.int32)
     row_list = [row_offset]
     col_list = [col_offset]
-    block_list = [keep_local(staying, features)]
-    rowmix_list = [row_weights]
-    colmix_list = [col_weights]
+    block_list = [keep_local(staying, resampled)]
     for step in (1, -1):
         going = offset_band == step
         earlier = jnp.sum(going[None, :] & (positions[None, :] < positions[:, None]), axis=1)
         table = (jnp.arange(CAP, dtype=jnp.int32)[:, None] == earlier[None, :]) & going[None, :]
-        got_blocks, got_rowmix, got_colmix, got_rows, got_cols = shifted(
-            (
-                place_rows(table, features),
-                place_rows(table, row_weights),
-                place_rows(table, col_weights),
-                place_ints(table, row_offset),
-                place_ints(table, col_offset),
-            ),
-            "lat",
-            step,
-        )
-        block_list.append(got_blocks)
-        rowmix_list.append(got_rowmix)
-        colmix_list.append(got_colmix)
-        row_list.append(got_rows)
-        col_list.append(got_cols)
-    arrived = resample_local(
-        jnp.concatenate(block_list, axis=0),
-        jnp.concatenate(rowmix_list, axis=0),
-        jnp.concatenate(colmix_list, axis=0),
-    )
+        sent_blocks = place_rows(table, resampled)
+        sent_rows = place_ints(table, row_offset)
+        sent_cols = place_ints(table, col_offset)
+        lane = jnp.arange(channels, dtype=jnp.int32)[None, :]
+        header = jnp.where(
+            lane == 0, sent_rows[:, None], jnp.where(lane == 1, sent_cols[:, None], 0)
+        ).astype(jnp.bfloat16)
+        header = jnp.broadcast_to(header[:, None, None, :], (CAP, 1, RW, channels))
+        payload = jnp.concatenate([sent_blocks, header], axis=1)
+        got = shifted(payload, "lat", step)
+        block_list.append(got[:, :RB])
+        got_header = got[:, RB, 0, :].astype(jnp.int32)
+        row_list.append(got_header[:, 0])
+        col_list.append(got_header[:, 1])
+    arrived = jnp.concatenate(block_list, axis=0)
     all_rows = jnp.concatenate(row_list, axis=0)
     all_cols = jnp.concatenate(col_list, axis=0)
     row_place = (
@@ -158,17 +153,24 @@
     ).astype(jnp.bfloat16)
     summed = jnp.einsum("swu,shuc->hwc", col_place, lifted, preferred_element_type=jnp.float32)
     state = (background.astype(jnp.float32) + summed).astype(jnp.bfloat16)
+    reach = HALO * LAYERS
+    widened = with_halo(state, (("lon", 1),), reach, True)
+    widened = with_halo(widened, (("lat", 0),), reach, False)
+    first_row = own_band * tile_rows
     for layer_index in range(LAYERS):
-        widened = with_halo(state, (("lon", 1),), HALO, True)
-        widened = with_halo(widened, (("lat", 0),), HALO, False)
-        state = layer_apply(
+        widened = layer_apply(
             widened,
             depth_weight[layer_index],
             norm_gain[layer_index],
             up_weight[layer_index],
             down_weight[layer_index],
         )
-    return state
+        margin = (widened.shape[0] - tile_rows) // 2
+        if margin:
+            grid_row = first_row - margin + jnp.arange(widened.shape[0], dtype=jnp.int32)
+            inside = (grid_row >= 0) & (grid_row < bands * tile_rows)
+            widened = jnp.where(inside[:, None, None], widened, jnp.zeros_like(widened))
+    return widened
 
 
 def solution(mesh):

time: 163 us -> 80.7 us (0.50)
  starting transfers between devices: 50.6 us -> 17.4 us
  waiting for transfers between devices: 45 us -> 15.9 us
  matrix products: 39.7 us -> 16.7 us
  other arithmetic: 9.81 us -> 18 us
  local copies, waits for them, and re-layouts: 16.9 us -> 11.8 us
    ppermute x10 -> x2, waiting for transfers between devices: 32.1 us -> 5.4 us  [shifted(): lax.ppermute(value, axis, [(source, source + steps) for source in range(l...]
    ppermute x10 -> x2, starting transfers between devices: 32.6 us -> 6.82 us  [shifted(): lax.ppermute(value, axis, [(source, source + steps) for source in range(l...]
    conv_general_dilated x2 -> x0, matrix products: 18.5 us -> none  [layer_apply(): lax.conv_general_dilated(widened[None], kernel, (1, 1), ((0, 0), (0, 0)),...]
    reduce_sum x0 -> x2, other arithmetic: none -> 11.9 us  [layer_apply(): centered = mixed - jnp.mean(mixed, axis=-1, keepdims=True)]
    reshape x8 -> x1, local copies, waits for them, and re-layouts: 6.36 us -> 0.89 us  [layer_apply(): flat_cells = normed.reshape(height * width, -1)]
    ppermute x4 -> x2, starting transfers between devices: 9.91 us -> 4.82 us  [with_halo(): after = lax.ppermute(leading, axis, down)]
    dot_general x0 -> x1, local copies, waits for them, and re-layouts: none -> 3.46 us  [layer_apply(): jnp.dot(hidden, down_matrix, preferred_element_type=jnp.float32)]
    dot_general x6 -> x2, matrix products: 4.09 us -> 0.84 us  [place_rows(): jnp.dot(onehot.astype(values.dtype), flat_values, preferred_element_type=...]
  transfers between devices with their start and end apart: 18 -> 6, of which waited for: 10 -> 5; matrix products, arithmetic and copies ran while one was open for 9% -> 2% of each run, Pallas kernels for 0% -> 0%
where the time goes in v1:
time: 80.7 us; the launch traced here: 80.4 us
  other arithmetic  18 us (22%)
  starting transfers between devices  17.4 us (22%)
  matrix products  16.7 us (21%)
  waiting for transfers between devices  15.9 us (20%)
  local copies, waits for them, and re-layouts  11.8 us (15%)
    reduce_sum x2, other arithmetic, layer_apply(): centered = mixed - jnp.mean(mixed, axis=-1, keepdims=True)  11.9 us
    ppermute x2, starting transfers between devices, shifted(): lax.ppermute(value, axis, [(source, source + steps) for source in range(l...  6.82 us
    ppermute x2, waiting for transfers between devices, with_halo(): after = lax.ppermute(leading, axis, down)  6.47 us
    unnamed x35, local copies, waits for them, and re-layouts  6.3 us
    ppermute x2, starting transfers between devices, with_halo(): before = lax.ppermute(last, axis, up)  5.79 us
    ppermute x2, waiting for transfers between devices, shifted(): lax.ppermute(value, axis, [(source, source + steps) for source in range(l...  5.4 us
    conv_general_dilated x1, matrix products, per_device(): lax.conv_general_dilated(swath_input, conv_weight, (2, 2), ((1, 1), (1, 1...  5.13 us
    ppermute x2, starting transfers between devices, with_halo(): after = lax.ppermute(leading, axis, down)  4.82 us
  transfers between devices with their start and end apart: 6, of which 5 were waited for; matrix products, arithmetic and copies ran while one was open for 2% of the time, Pallas kernels for 0%

profile of v1, /device:TPU:0, one launch (start us, length us, event | category | flops | bytes accessed | tf_op | source)
XLA Modules:
  0.0 80.4 jit_solution(8860212455000989392)
XLA Ops:
  0.0 4.7 %copy.59 = bf16[2,64,64,256]{3,1,2,0:T(8,128)(2,1)S(1)} copy(bf16[2,64,64,256]{3,2,1,0:T(8,128)(2,1)} %param.13) | data formatting | bytes 8388608 | tf_op args[0]
  4.7 0.7 pad
  5.5 3.3 %fusion.1 = bf16[64,2,8,12,256]{4,0,3,2,1:T(8,128)(2,1)S(1)} fusion(bf16[64,2,7,2,256]{4,0,3,2,1:T(8,128)(2,1)S(1)} %slice.980, bf16[64,2,8,10,256]{4,0,3,2,1:T(8,128)(2,1)S(1)} %bitcast.196), kind=kLoop, calls=%fused_computation.4 | loop fusion | flops 18874368 | bytes 12451840 | tf_op jit(solution)/shard_map/conv_general_dilated | solution.py:105
  8.8 5.1 %fusion.20 = bf16[32,16,5,256]{3,1,2,0:T(8,128)(2,1)S(1)} fusion(bf16[3,3,256,256]{3,2,1,0:T(8,128)(2,1)S(1)} %copy-done, bf16[64,2,8,12,256]{4,0,3,2,1:T(8,128)(2,1)S(1)} %fusion.1, f32[256]{0:T(256)S(1)} %copy-done.11, pred[16,5]{0,1:T(8,128)(4,1)S(1)} %copy-done.13), kind=kOutput, calls=%fused_computation.27 | convolution fusion | flops 2995650560 | bytes 8782928 | tf_op jit(solution)/shard_map/conv_general_dilated | solution.py:105
  14.0 0.4 copy.23
  14.4 0.2 copy-done.8
  14.7 0.3 convolution_bitcast_fusion
  15.0 1.1 %bitcast_select_fusion = (bf16[2,16,16,256]{3,2,1,0:T(8,128)(2,1)S(1)}, bf16[2,16,256,16]{2,3,1,0:T(8,128)(2,1)S(1)}) fusion(pred[2]{0:T(512)(128)(4,1)S(1)} %get-tuple-element.126, bf16[2,16,32]{2,1,0:T(8,128)(2,1)S(1)} %copy-done.4, f32[2,16,32,256]{3,1,2,0:T(8,128)S(1)} %convolution_bitcast_fusion), kind=kOutput, calls=%fused_computation.260 | convolution fusion | flops 50593792 | bytes 1574914 | tf_op jit(solution)/shard_map/nrjc,nuj->nruc/dot_general | solution.py:35
  16.0 0.3 copy.37
  16.3 0.1 fusion.152
  16.5 0.2 select_reduce_fusion.2
  16.6 0.4 convolution_convert_fusion
  17.1 0.1 select_convert_fusion.1
  17.2 1.3 %collective-permute-start.1 = (bf16[2,17,16,256]{3,2,1,0:T(8,128)(2,1)S(1)}, bf16[2,17,16,256]{3,2,1,0:T(8,128)(2,1)S(1)}, u32[]{:S(2)}, u32[]{:S(2)}) collective-permute-start(bf16[2,17,16,256]{3,2,1,0:T(8,128)(2,1)S(1)} %pad_maximum_fusion.2), channel_id=1, source_target_pairs={{8,0},{16,8},{24,16},{9,1},{17,9},{25,17},{10,2},{18,10},{26,18},{... | collective-permute-start | bytes 835592 | tf_op jit(solution)/shard_map/ppermute | solution.py:17
  18.5 0.4 convolution_convert_fusion.1
  19.0 5.5 %collective-permute-start = (bf16[2,17,16,256]{3,2,1,0:T(8,128)(2,1)S(1)}, bf16[2,17,16,256]{3,2,1,0:T(8,128)(2,1)S(1)}, u32[]{:S(2)}, u32[]{:S(2)}) collective-permute-start(bf16[2,17,16,256]{3,2,1,0:T(8,128)(2,1)S(1)} %pad_maximum_fusion.1), channel_id=1, source_target_pairs={{0,8},{8,16},{16,24},{1,9},{9,17},{17,25},{2,10},{10,18},{18,26},{... | collective-permute-start | bytes 835592 | tf_op jit(solution)/shard_map/ppermute | solution.py:17
  24.6 0.1 fusion.159
  24.9 4.7 %collective-permute-done.1 = bf16[2,17,16,256]{3,2,1,0:T(8,128)(2,1)S(1)} collective-permute-done((bf16[2,17,16,256]{3,2,1,0:T(8,128)(2,1)S(1)}, bf16[2,17,16,256]{3,2,1,0:T(8,128)(2,1)S(1)}, u32[]{:S(2)}, u32[]{:S(2)}) %collective-permute-start.1) | collective-permute-done | bytes 278560 | tf_op jit(solution)/shard_map/ppermute | solution.py:17
  29.6 0.2 slice_reduce_fusion
  29.8 0.7 collective-permute-done
  30.5 0.2 slice_reduce_fusion.1
  30.7 0.1 pad_add_fusion
  30.8 0.1 pad_add_fusion.1
  31.0 0.1 pad_maximum_fusion
  31.1 0.8 %convolution_convert_fusion.2 = bf16[6,24,16,256]{3,1,2,0:T(8,128)(2,1)S(1)} fusion(bf16[6,16,16,256]{3,2,1,0:T(8,128)(2,1)S(1)} %pad_maximum_fusion, s32[6,16]{1,0:T(8,128)S(1)} %iota_add_fusion.1), kind=kOutput, calls=%fused_computation.36 | convolution fusion | flops 19466496 | bytes 1966464 | tf_op jit(solution)/shard_map/shr,sruc->shuc/dot_general | solution.py:151
  32.0 0.4 fusion.35
  32.5 3.5 %collective-permute-start.3 = (bf16[24,6,256]{2,1,0:T(8,128)(2,1)S(1)}, bf16[24,6,256]{2,1,0:T(8,128)(2,1)S(1)}, u32[]{:S(2)}, u32[]{:S(2)}) collective-permute-start(bf16[24,6,256]{2,1,0:T(8,128)(2,1)S(1)} %get-tuple-element.21), channel_id=1, source_target_pairs={{1,0},{2,1},{3,2},{4,3},{5,4},{6,5},{7,6},{0,7},{9,8},{10,9},{11,1... | collective-permute-start | bytes 221192 | tf_op jit(solution)/shard_map/ppermute | solution.py:28
  36.0 2.4 %collective-permute-done.2 = bf16[24,6,256]{2,1,0:T(8,128)(2,1)S(1)} collective-permute-done((bf16[24,6,256]{2,1,0:T(8,128)(2,1)S(1)}, bf16[24,6,256]{2,1,0:T(8,128)(2,1)S(1)}, u32[]{:S(2)}, u32[]{:S(2)}) %collective-permute-start.2) | collective-permute-done | bytes 73760 | tf_op jit(solution)/shard_map/ppermute | solution.py:27
  38.4 0.1 pad_maximum_fusion.5
  38.5 5.7 %collective-permute-start.4 = (bf16[6,36,256]{2,1,0:T(8,128)(2,1)S(1)}, bf16[6,36,256]{2,1,0:T(8,128)(2,1)S(1)}, u32[]{:S(2)}, u32[]{:S(2)}) collective-permute-start(bf16[6,36,256]{2,1,0:T(8,128)(2,1)S(1)} %get-tuple-element.18), channel_id=1, source_target_pairs={{0,8},{8,16},{16,24},{1,9},{9,17},{17,25},{2,10},{10,18},{18,26},{... | collective-permute-start | bytes 331784 | tf_op jit(solution)/shard_map/ppermute | solution.py:27
  44.2 1.3 %collective-permute-start.5 = (bf16[6,36,256]{2,1,0:T(8,128)(2,1)S(1)}, bf16[6,36,256]{2,1,0:T(8,128)(2,1)S(1)}, u32[]{:S(2)}, u32[]{:S(2)}) collective-permute-start(bf16[6,36,256]{2,1,0:T(8,128)(2,1)S(1)} %get-tuple-element.19), channel_id=1, source_target_pairs={{8,0},{16,8},{24,16},{9,1},{17,9},{25,17},{10,2},{18,10},{26,18},{... | collective-permute-start | bytes 331784 | tf_op jit(solution)/shard_map/ppermute | solution.py:28
  45.5 0.5 compare_and_fusion.2
  46.0 1.7 %collective-permute-done.4 = bf16[6,36,256]{2,1,0:T(8,128)(2,1)S(1)} collective-permute-done((bf16[6,36,256]{2,1,0:T(8,128)(2,1)S(1)}, bf16[6,36,256]{2,1,0:T(8,128)(2,1)S(1)}, u32[]{:S(2)}, u32[]{:S(2)}) %collective-permute-start.4) | collective-permute-done | bytes 110624 | tf_op jit(solution)/shard_map/ppermute | solution.py:27
  47.7 6.5 %collective-permute-done.5 = bf16[6,36,256]{2,1,0:T(8,128)(2,1)S(1)} collective-permute-done((bf16[6,36,256]{2,1,0:T(8,128)(2,1)S(1)}, bf16[6,36,256]{2,1,0:T(8,128)(2,1)S(1)}, u32[]{:S(2)}, u32[]{:S(2)}) %collective-permute-start.5) | collective-permute-done | bytes 110624 | tf_op jit(solution)/shard_map/ppermute | solution.py:28
  54.2 0.2 maximum_convert_fusion
  54.3 7.4 %fusion.156 = (f32[30,30]{1,0:T(8,128)S(1)}, f32[30,30,256]{2,1,0:T(8,128)S(1)}) fusion(f32[256]{0:T(256)S(1)} %bitcast.259, f32[36,36,256]{2,1,0:T(8,128)S(1)} %maximum_convert_fusion, f32[256]{0:T(256)S(1)} %bitcast.260, f32[256]{0:T(256)S(1)} %bitcast.261, f32[256]{0:T(256)S(1)} %bitcast.262, f32[256]{0:T(256)S(1)} %bitcast.263, f32[256]{0:T(256)S(1)} %bitcast.264, ...), kind=kLoop, calls=%fused_computation.311 | loop fusion | flops 22578300 | bytes 46133776 | tf_op jit(solution)/shard_map/reduce_sum | solution.py:71
  61.8 0.4 multiply_reduce_fusion
  62.2 0.3 multiply_convert_fusion
  62.5 0.9 %reshape.240 = bf16[900,256]{1,0:T(8,128)(2,1)} reshape(bf16[30,30,256]{2,1,0:T(8,128)(2,1)S(1)} %multiply_convert_fusion) | data formatting | bytes 921600 | tf_op jit(solution)/shard_map/reshape | solution.py:74
  63.4 3.8 %fusion.12 = bf16[900,1024]{1,0:T(8,128)(2,1)} fusion(bf16[900,256]{1,0:T(8,128)(2,1)} %reshape.240, bf16[2,256,1024]{2,1,0:T(8,128)(2,1)} %param.24), kind=kOutput, calls=%fused_computation.18 | convolution fusion | flops 480153600 | bytes 2830336 | tf_op jit(solution)/shard_map/dot_general | solution.py:75
  67.1 3.5 %dot_general.44 = bf16[30,30,1024]{2,1,0:T(8,128)(2,1)} reshape(bf16[900,1024]{1,0:T(8,128)(2,1)} %fusion.12) | data formatting | bytes 3686400 | tf_op jit(solution)/shard_map/dot_general | solution.py:78
  70.6 2.3 %fusion.34 = f32[30,30,256]{2,1,0:T(8,128)S(1)} fusion(bf16[30,30,1024]{2,1,0:T(8,128)(2,1)} %dot_general.44, f32[36,36,256]{2,1,0:T(8,128)S(1)} %maximum_convert_fusion, bf16[2,1024,256]{2,1,0:T(8,128)(2,1)} %param.25, pred[30]{0:T(512)(128)(4,1)S(1)} %copy-done.12), kind=kOutput, calls=%fused_computation.44 | convolution fusion | flops 472780800 | bytes 4333598 | tf_op jit(solution)/shard_map/dot_general | solution.py:78
  72.9 4.4 %fusion.154 = (f32[24,24]{1,0:T(8,128)S(1)}, f32[24,24,256]{2,1,0:T(8,128)S(1)}) fusion(f32[256]{0:T(256)S(1)} %bitcast.240, f32[30,30,256]{2,1,0:T(8,128)S(1)} %fusion.34, f32[256]{0:T(256)S(1)} %bitcast.241, f32[256]{0:T(256)S(1)} %bitcast.242, f32[256]{0:T(256)S(1)} %bitcast.243, f32[256]{0:T(256)S(1)} %bitcast.244, f32[256]{0:T(256)S(1)} %bitcast.245, ...), kind=kLoop, calls=%fused_computation.310 | loop fusion | flops 14450112 | bytes 29543680 | tf_op jit(solution)/shard_map/reduce_sum | solution.py:71
  77.4 0.3 multiply_reduce_fusion.1
  77.7 0.2 multiply_convert_fusion.1
  77.9 0.9 %fusion.28 = bf16[576,1024]{1,0:T(8,128)(2,1)S(1)} fusion(bf16[576,256]{1,0:T(8,128)(2,1)S(1)} %bitcast.202, bf16[2,256,1024]{2,1,0:T(8,128)(2,1)S(1)} %copy-done.9), kind=kOutput, calls=%fused_computation.35 | convolution fusion | flops 307298304 | bytes 1998848 | tf_op jit(solution)/shard_map/dot_general | solution.py:75
  78.9 0.3 copy-done.10
  79.1 1.2 %fusion.36 = bf16[24,24,256]{2,1,0:T(8,128)(2,1)} fusion(bf16[24,24,1024]{2,1,0:T(8,128)(2,1)S(1)} %bitcast.309, f32[30,30,256]{2,1,0:T(8,128)S(1)} %fusion.34, bf16[2,1024,256]{2,1,0:T(8,128)(2,1)S(1)} %copy-done.10), kind=kOutput, calls=%fused_computation.46 | convolution fusion | flops 302284800 | bytes 2588672 | tf_op jit(solution)/shard_map/dot_general | solution.py:78
  (58 shorter events, 0.8 us)
Async XLA Ops:
  0.0 8.8 %copy-start = (bf16[3,3,256,256]{3,2,1,0:T(8,128)(2,1)S(1)}, bf16[3,3,256,256]{3,2,1,0:T(8,128)(2,1)}, u32[]{:S(2)}) copy-start(bf16[3,3,256,256]{3,2,1,0:T(8,128)(2,1)} %param.14) | copy-start | bytes 3538948
  5.5 3.3 %copy-start.11 = (f32[256]{0:T(256)S(1)}, f32[256]{0:T(256)}, u32[]{:S(2)}) copy-start(f32[256]{0:T(256)} %param.15) | copy-start | bytes 3076
  5.5 3.3 %copy-start.13 = (pred[16,5]{0,1:T(8,128)(4,1)S(1)}, pred[16,5]{0,1:T(8,128)(4,1)}, u32[]{:S(2)}) copy-start(pred[16,5]{0,1:T(8,128)(4,1)} %constant.63) | copy-start | bytes 244
  13.9 0.7 copy-start.8
  14.0 0.7 copy-start.3
  14.0 1.0 %copy-start.4 = (bf16[2,16,32]{2,1,0:T(8,128)(2,1)S(1)}, bf16[2,16,32]{2,1,0:T(8,128)(2,1)}, u32[]{:S(2)}) copy-start(bf16[2,16,32]{2,1,0:T(8,128)(2,1)} %param.20) | copy-start | bytes 6148
  14.6 1.9 %copy-start.6 = (s32[2]{0:T(128)S(1)}, s32[2]{0:T(128)}, u32[]{:S(2)}) copy-start(s32[2]{0:T(128)} %param.17) | copy-start | bytes 28
  14.6 1.9 %copy-start.7 = (s32[2]{0:T(128)S(1)}, s32[2]{0:T(128)}, u32[]{:S(2)}) copy-start(s32[2]{0:T(128)} %param.18) | copy-start | bytes 28
  16.0 8.5 %copy-start.2 = (f32[2,7,7,256]{3,0,2,1:T(2,128)S(1)}, f32[2,7,7,256]{3,0,2,1:T(2,128)}, u32[]{:S(2)}) copy-start(f32[2,7,7,256]{3,0,2,1:T(2,128)} %param.22) | copy-start | bytes 301060
  17.2 12.4 %collective-permute-start.1 = (bf16[2,17,16,256]{3,2,1,0:T(8,128)(2,1)S(1)}, bf16[2,17,16,256]{3,2,1,0:T(8,128)(2,1)S(1)}, u32[]{:S(2)}, u32[]{:S(2)}) collective-permute-start(bf16[2,17,16,256]{3,2,1,0:T(8,128)(2,1)S(1)} %pad_maximum_fusion.2), channel_id=1, source_target_pairs={{8,0},{16,8},{24,16},{9,1},{17,9},{25,17},{10,2},{18,10},{26,18},{... | collective-permute-start | bytes 835592 | tf_op jit(solution)/shard_map/ppermute | solution.py:17
  19.0 11.4 %collective-permute-start = (bf16[2,17,16,256]{3,2,1,0:T(8,128)(2,1)S(1)}, bf16[2,17,16,256]{3,2,1,0:T(8,128)(2,1)S(1)}, u32[]{:S(2)}, u32[]{:S(2)}) collective-permute-start(bf16[2,17,16,256]{3,2,1,0:T(8,128)(2,1)S(1)} %pad_maximum_fusion.1), channel_id=1, source_target_pairs={{0,8},{8,16},{16,24},{1,9},{9,17},{17,25},{2,10},{10,18},{18,26},{... | collective-permute-start | bytes 835592 | tf_op jit(solution)/shard_map/ppermute | solution.py:17
  24.8 7.2 %copy-start.1 = (bf16[24,24,256]{2,1,0:T(8,128)(2,1)S(1)}, bf16[24,24,256]{2,1,0:T(8,128)(2,1)}, u32[]{:S(2)}) copy-start(bf16[24,24,256]{2,1,0:T(8,128)(2,1)} %param.21) | copy-start | bytes 884740
  31.1 4.9 %copy-start.5 = (f32[2,256]{1,0:T(2,128)S(1)}, f32[2,256]{1,0:T(2,128)}, u32[]{:S(2)}) copy-start(f32[2,256]{1,0:T(2,128)} %param.23) | copy-start | bytes 6148
  32.4 6.0 %collective-permute-start.2 = (bf16[24,6,256]{2,1,0:T(8,128)(2,1)S(1)}, bf16[24,6,256]{2,1,0:T(8,128)(2,1)S(1)}, u32[]{:S(2)}, u32[]{:S(2)}) collective-permute-start(bf16[24,6,256]{2,1,0:T(8,128)(2,1)S(1)} %get-tuple-element.20), channel_id=1, source_target_pairs={{0,1},{1,2},{2,3},{3,4},{4,5},{5,6},{6,7},{7,0},{8,9},{9,10},{10,1... | collective-permute-start | bytes 221192 | tf_op jit(solution)/shard_map/ppermute | solution.py:27
  32.5 5.9 %collective-permute-start.3 = (bf16[24,6,256]{2,1,0:T(8,128)(2,1)S(1)}, bf16[24,6,256]{2,1,0:T(8,128)(2,1)S(1)}, u32[]{:S(2)}, u32[]{:S(2)}) collective-permute-start(bf16[24,6,256]{2,1,0:T(8,128)(2,1)S(1)} %get-tuple-element.21), channel_id=1, source_target_pairs={{1,0},{2,1},{3,2},{4,3},{5,4},{6,5},{7,6},{0,7},{9,8},{10,9},{11,1... | collective-permute-start | bytes 221192 | tf_op jit(solution)/shard_map/ppermute | solution.py:28
  38.5 9.2 %collective-permute-start.4 = (bf16[6,36,256]{2,1,0:T(8,128)(2,1)S(1)}, bf16[6,36,256]{2,1,0:T(8,128)(2,1)S(1)}, u32[]{:S(2)}, u32[]{:S(2)}) collective-permute-start(bf16[6,36,256]{2,1,0:T(8,128)(2,1)S(1)} %get-tuple-element.18), channel_id=1, source_target_pairs={{0,8},{8,16},{16,24},{1,9},{9,17},{17,25},{2,10},{10,18},{18,26},{... | collective-permute-start | bytes 331784 | tf_op jit(solution)/shard_map/ppermute | solution.py:27
  44.2 10.0 %collective-permute-start.5 = (bf16[6,36,256]{2,1,0:T(8,128)(2,1)S(1)}, bf16[6,36,256]{2,1,0:T(8,128)(2,1)S(1)}, u32[]{:S(2)}, u32[]{:S(2)}) collective-permute-start(bf16[6,36,256]{2,1,0:T(8,128)(2,1)S(1)} %get-tuple-element.19), channel_id=1, source_target_pairs={{8,0},{16,8},{24,16},{9,1},{17,9},{25,17},{10,2},{18,10},{26,18},{... | collective-permute-start | bytes 331784 | tf_op jit(solution)/shard_map/ppermute | solution.py:28
  67.1 3.5 %copy-start.12 = (pred[30]{0:T(512)(128)(4,1)S(1)}, pred[30]{0:T(512)(128)(4,1)}, u32[]{:S(2)}) copy-start(pred[30]{0:T(512)(128)(4,1)} %compare_and_fusion.2) | copy-start | bytes 94
  72.9 5.0 %copy-start.9 = (bf16[2,256,1024]{2,1,0:T(8,128)(2,1)S(1)}, bf16[2,256,1024]{2,1,0:T(8,128)(2,1)}, u32[]{:S(2)}) copy-start(bf16[2,256,1024]{2,1,0:T(8,128)(2,1)} %param.24) | copy-start | bytes 3145732
  77.9 1.2 %copy-start.10 = (bf16[2,1024,256]{2,1,0:T(8,128)(2,1)S(1)}, bf16[2,1024,256]{2,1,0:T(8,128)(2,1)}, u32[]{:S(2)}) copy-start(bf16[2,1024,256]{2,1,0:T(8,128)(2,1)} %param.25) | copy-start | bytes 3145732

commit v2 on v1

--- a/solution.py
+++ b/solution.py
@@ -17,17 +17,30 @@
     return lax.ppermute(value, axis, [(source, source + steps) for source in range(leading, last)])
 
 
-def with_halo(value, sides, width, wrap):
-    for axis, dim in sides:
-        size, length = (lax.axis_size(axis), value.shape[dim])
-        up = [(i, (i + 1) % size) for i in range(size if wrap else size - 1)]
-        down = [(j, i) for i, j in up]
-        last = lax.slice_in_dim(value, length - width, length, axis=dim)
-        leading = lax.slice_in_dim(value, 0, width, axis=dim)
-        before = lax.ppermute(last, axis, up)
-        after = lax.ppermute(leading, axis, down)
-        value = jnp.concatenate([before, value, after], axis=dim)
-    return value
+def halo_all(value, reach):
+    bands, tiles = lax.axis_size("lat"), lax.axis_size("lon")
+
+    def send(piece, dlat, dlon):
+        pairs = []
+        for lat in range(bands):
+            if 0 <= lat + dlat < bands:
+                for lon in range(tiles):
+                    pairs.append((lat * tiles + lon, (lat + dlat) * tiles + (lon + dlon) % tiles))
+        return lax.ppermute(piece, ("lat", "lon"), pairs)
+
+    top, bottom = value[:reach], value[-reach:]
+    north = send(bottom, 1, 0)
+    south = send(top, -1, 0)
+    west = send(value[:, -reach:], 0, 1)
+    east = send(value[:, :reach], 0, -1)
+    north_west = send(bottom[:, -reach:], 1, 1)
+    north_east = send(bottom[:, :reach], 1, -1)
+    south_west = send(top[:, -reach:], -1, 1)
+    south_east = send(top[:, :reach], -1, -1)
+    upper = jnp.concatenate([north_west, north, north_east], axis=1)
+    middle = jnp.concatenate([west, value, east], axis=1)
+    lower = jnp.concatenate([south_west, south, south_east], axis=1)
+    return jnp.concatenate([upper, middle, lower], axis=0)
 
 
 def resample_local(blocks, row_mix, col_mix):
@@ -66,20 +79,23 @@
 def layer_apply(padded, depth_kernel, gain, up_matrix, down_matrix):
     height = padded.shape[0] - (KS - 1)
     width = padded.shape[1] - (KS - 1)
+    spare = -width % 8
     widened = padded.astype(jnp.float32)
-    mixed = depthwise(widened, depth_kernel, height, width)
+    if spare:
+        widened = jnp.pad(widened, ((0, 0), (0, spare), (0, 0)))
+    mixed = depthwise(widened, depth_kernel, height, width + spare)
     centered = mixed - jnp.mean(mixed, axis=-1, keepdims=True)
     variance = jnp.mean(centered * centered, axis=-1, keepdims=True)
     normed = (centered * lax.rsqrt(variance + 1e-06) * gain).astype(jnp.bfloat16)
-    flat_cells = normed.reshape(height * width, -1)
+    flat_cells = normed.reshape(height * (width + spare), -1)
     hidden = jax.nn.gelu(jnp.dot(flat_cells, up_matrix, preferred_element_type=jnp.float32)).astype(
         jnp.bfloat16
     )
     output = jnp.dot(hidden, down_matrix, preferred_element_type=jnp.float32).reshape(
-        height, width, -1
-    )
-    residual_part = widened[HALO : HALO + height, HALO : HALO + width]
-    return (residual_part + output).astype(jnp.bfloat16)
+        height, width + spare, -1
+    )
+    residual_part = widened[HALO : HALO + height, HALO : HALO + width + spare]
+    return (residual_part + output).astype(jnp.bfloat16)[:, :width]
 
 
 def per_device(
@@ -154,8 +170,7 @@
     summed = jnp.einsum("swu,shuc->hwc", col_place, lifted, preferred_element_type=jnp.float32)
     state = (background.astype(jnp.float32) + summed).astype(jnp.bfloat16)
     reach = HALO * LAYERS
-    widened = with_halo(state, (("lon", 1),), reach, True)
-    widened = with_halo(widened, (("lat", 0),), reach, False)
+    widened = halo_all(state, reach)
     first_row = own_band * tile_rows
     for layer_index in range(LAYERS):
         widened = layer_apply(

time: 80.7 us -> 81.7 us (1.012); the launches traced: 80.4 us -> 80.3 us
  starting transfers between devices: 17.4 us -> 32.2 us
  waiting for transfers between devices: 15.9 us -> 9.44 us
  local copies, waits for them, and re-layouts: 11.8 us -> 7.81 us
  matrix products: 16.7 us -> 12.8 us
    ppermute x4 -> x8, starting transfers between devices: 10.6 us -> 25.4 us  [send(): return lax.ppermute(piece, ('lat', 'lon'), pairs)]
    ppermute x4 -> x8, waiting for transfers between devices: 10.5 us -> 4.07 us  [send(): return lax.ppermute(piece, ('lat', 'lon'), pairs)]
    dot_general x1 -> x0, local copies, waits for them, and re-layouts: 3.46 us -> none  [layer_apply(): jnp.dot(hidden, down_matrix, preferred_element_type=jnp.float32)]
    dot_general x2, matrix products: 4.69 us -> 2.35 us  [layer_apply(): jnp.dot(flat_cells, up_matrix, preferred_element_type=jnp.float32)]
    dot_general x2, matrix products: 3.51 us -> 1.9 us  [layer_apply(): jnp.dot(hidden, down_matrix, preferred_element_type=jnp.float32)]
    reshape x1 -> x0, local copies, waits for them, and re-layouts: 0.89 us -> none  [layer_apply(): flat_cells = normed.reshape(height * width, -1)]
    unnamed x35 -> x33, local copies, waits for them, and re-layouts: 6.3 us -> 6.51 us
  transfers between devices with their start and end apart: 6 -> 10, of which waited for: 5 -> 4; matrix products, arithmetic and copies ran while one was open for 2% -> 1% of each run, Pallas kernels for 0% -> 0%
where the time goes in v2:
time: 81.7 us; the launch traced here: 80.3 us
  starting transfers between devices  32.2 us (39%)
  other arithmetic  17.4 us (21%)
  matrix products  12.8 us (16%)
  waiting for transfers between devices  9.44 us (12%)
  local copies, waits for them, and re-layouts  7.81 us (10%)
    ppermute x8, starting transfers between devices, send(): return lax.ppermute(piece, ('lat', 'lon'), pairs)  25.4 us
    reduce_sum x2, other arithmetic, layer_apply(): centered = mixed - jnp.mean(mixed, axis=-1, keepdims=True)  11.7 us
    ppermute x2, starting transfers between devices, shifted(): lax.ppermute(value, axis, [(source, source + steps) for source in range(l...  6.82 us
    unnamed x33, local copies, waits for them, and re-layouts  6.51 us
    ppermute x2, waiting for transfers between devices, shifted(): lax.ppermute(value, axis, [(source, source + steps) for source in range(l...  5.37 us
    conv_general_dilated x1, matrix products, per_device(): lax.conv_general_dilated(swath_input, conv_weight, (2, 2), ((1, 1), (1, 1...  5.13 us
    ppermute x8, waiting for transfers between devices, send(): return lax.ppermute(piece, ('lat', 'lon'), pairs)  4.07 us
    conv_general_dilated x1, other arithmetic, per_device(): lax.conv_general_dilated(swath_input, conv_weight, (2, 2), ((1, 1), (1, 1...  3.28 us
  transfers between devices with their start and end apart: 10, of which 4 were waited for; matrix products, arithmetic and copies ran while one was open for 1% of the time, Pallas kernels for 0%

profile of v2, /device:TPU:0, one launch (start us, length us, event | category | flops | bytes accessed | tf_op | source)
XLA Modules:
  0.0 80.3 jit_solution(3647211014486977219)
XLA Ops:
  0.0 4.7 %copy.59 = bf16[2,64,64,256]{3,1,2,0:T(8,128)(2,1)S(1)} copy(bf16[2,64,64,256]{3,2,1,0:T(8,128)(2,1)} %param.13) | data formatting | bytes 8388608 | tf_op args[0]
  4.7 0.7 pad.5
  5.5 3.3 %fusion.1 = bf16[64,2,8,12,256]{4,0,3,2,1:T(8,128)(2,1)S(1)} fusion(bf16[64,2,7,2,256]{4,0,3,2,1:T(8,128)(2,1)S(1)} %slice.1010, bf16[64,2,8,10,256]{4,0,3,2,1:T(8,128)(2,1)S(1)} %bitcast.198), kind=kLoop, calls=%fused_computation.4 | loop fusion | flops 18874368 | bytes 12451840 | tf_op jit(solution)/shard_map/conv_general_dilated | solution.py:121
  8.8 5.1 %fusion.20 = bf16[32,16,5,256]{3,1,2,0:T(8,128)(2,1)S(1)} fusion(bf16[3,3,256,256]{3,2,1,0:T(8,128)(2,1)S(1)} %copy-done, bf16[64,2,8,12,256]{4,0,3,2,1:T(8,128)(2,1)S(1)} %fusion.1, f32[256]{0:T(256)S(1)} %copy-done.11, pred[16,5]{0,1:T(8,128)(4,1)S(1)} %copy-done.12), kind=kOutput, calls=%fused_computation.27 | convolution fusion | flops 2995650560 | bytes 8782928 | tf_op jit(solution)/shard_map/conv_general_dilated | solution.py:121
  14.0 0.4 copy.23
  14.4 0.2 copy-done.8
  14.7 0.3 convolution_bitcast_fusion
  15.0 1.1 %bitcast_select_fusion = (bf16[2,16,16,256]{3,2,1,0:T(8,128)(2,1)S(1)}, bf16[2,16,256,16]{2,3,1,0:T(8,128)(2,1)S(1)}) fusion(pred[2]{0:T(512)(128)(4,1)S(1)} %get-tuple-element.130, bf16[2,16,32]{2,1,0:T(8,128)(2,1)S(1)} %copy-done.4, f32[2,16,32,256]{3,1,2,0:T(8,128)S(1)} %convolution_bitcast_fusion), kind=kOutput, calls=%fused_computation.257 | convolution fusion | flops 50593792 | bytes 1574914 | tf_op jit(solution)/shard_map/nrjc,nuj->nruc/dot_general | solution.py:48
  16.0 0.3 copy.37
  16.3 0.1 fusion.158
  16.5 0.2 select_reduce_fusion.2
  16.7 0.4 convolution_convert_fusion
  17.1 0.1 select_convert_fusion.1
  17.2 1.3 %collective-permute-start.1 = (bf16[2,17,16,256]{3,2,1,0:T(8,128)(2,1)S(1)}, bf16[2,17,16,256]{3,2,1,0:T(8,128)(2,1)S(1)}, u32[]{:S(2)}, u32[]{:S(2)}) collective-permute-start(bf16[2,17,16,256]{3,2,1,0:T(8,128)(2,1)S(1)} %pad_maximum_fusion.2), channel_id=1, source_target_pairs={{8,0},{16,8},{24,16},{9,1},{17,9},{25,17},{10,2},{18,10},{26,18},{... | collective-permute-start | bytes 835592 | tf_op jit(solution)/shard_map/ppermute | solution.py:17
  18.5 0.4 convolution_convert_fusion.1
  19.1 5.5 %collective-permute-start = (bf16[2,17,16,256]{3,2,1,0:T(8,128)(2,1)S(1)}, bf16[2,17,16,256]{3,2,1,0:T(8,128)(2,1)S(1)}, u32[]{:S(2)}, u32[]{:S(2)}) collective-permute-start(bf16[2,17,16,256]{3,2,1,0:T(8,128)(2,1)S(1)} %pad_maximum_fusion.1), channel_id=1, source_target_pairs={{0,8},{8,16},{16,24},{1,9},{9,17},{17,25},{2,10},{10,18},{18,26},{... | collective-permute-start | bytes 835592 | tf_op jit(solution)/shard_map/ppermute | solution.py:17
  24.6 0.1 fusion.167
  24.9 4.7 %collective-permute-done.1 = bf16[2,17,16,256]{3,2,1,0:T(8,128)(2,1)S(1)} collective-permute-done((bf16[2,17,16,256]{3,2,1,0:T(8,128)(2,1)S(1)}, bf16[2,17,16,256]{3,2,1,0:T(8,128)(2,1)S(1)}, u32[]{:S(2)}, u32[]{:S(2)}) %collective-permute-start.1) | collective-permute-done | bytes 278560 | tf_op jit(solution)/shard_map/ppermute | solution.py:17
  29.6 0.2 slice_reduce_fusion
  29.8 0.6 collective-permute-done
  30.5 0.2 slice_reduce_fusion.1
  30.7 0.1 pad_add_fusion
  31.0 0.1 pad_maximum_fusion
  31.1 0.8 %convolution_convert_fusion.2 = bf16[6,24,16,256]{3,1,2,0:T(8,128)(2,1)S(1)} fusion(bf16[6,16,16,256]{3,2,1,0:T(8,128)(2,1)S(1)} %pad_maximum_fusion, s32[6,16]{1,0:T(8,128)S(1)} %iota_add_fusion.1), kind=kOutput, calls=%fused_computation.36 | convolution fusion | flops 19466496 | bytes 1966464 | tf_op jit(solution)/shard_map/shr,sruc->shuc/dot_general | solution.py:167
  32.0 0.4 fusion.32
  32.4 4.6 %collective-permute-start.2 = (bf16[6,6,256]{2,1,0:T(8,128)(2,1)S(1)}, bf16[6,6,256]{2,1,0:T(8,128)(2,1)S(1)}, u32[]{:S(2)}, u32[]{:S(2)}) collective-permute-start(bf16[6,6,256]{2,1,0:T(8,128)(2,1)S(1)} %get-tuple-element.18), channel_id=1, source_target_pairs={{0,9},{1,10},{2,11},{3,12},{4,13},{5,14},{6,15},{7,8},{8,17},{9,18... | collective-permute-start | bytes 55304 | tf_op jit(solution)/shard_map/ppermute | solution.py:29
  37.0 8.8 %collective-permute-start.4 = (bf16[6,6,256]{2,1,0:T(8,128)(2,1)S(1)}, bf16[6,6,256]{2,1,0:T(8,128)(2,1)S(1)}, u32[]{:S(2)}, u32[]{:S(2)}) collective-permute-start(bf16[6,6,256]{2,1,0:T(8,128)(2,1)S(1)} %get-tuple-element.21), channel_id=1, source_target_pairs={{0,15},{1,8},{2,9},{3,10},{4,11},{5,12},{6,13},{7,14},{8,23},{9,16... | collective-permute-start | bytes 55304 | tf_op jit(solution)/shard_map/ppermute | solution.py:29
  45.9 1.3 %collective-permute-start.7 = (bf16[6,6,256]{2,1,0:T(8,128)(2,1)S(1)}, bf16[6,6,256]{2,1,0:T(8,128)(2,1)S(1)}, u32[]{:S(2)}, u32[]{:S(2)}) collective-permute-start(bf16[6,6,256]{2,1,0:T(8,128)(2,1)S(1)} %get-tuple-element.20), channel_id=1, source_target_pairs={{8,1},{9,2},{10,3},{11,4},{12,5},{13,6},{14,7},{15,0},{16,9},{17,1... | collective-permute-start | bytes 55304 | tf_op jit(solution)/shard_map/ppermute | solution.py:29
  47.3 3.5 %collective-permute-start.6 = (bf16[24,6,256]{2,1,0:T(8,128)(2,1)S(1)}, bf16[24,6,256]{2,1,0:T(8,128)(2,1)S(1)}, u32[]{:S(2)}, u32[]{:S(2)}) collective-permute-start(bf16[24,6,256]{2,1,0:T(8,128)(2,1)S(1)} %get-tuple-element.25), channel_id=1, source_target_pairs={{0,7},{1,0},{2,1},{3,2},{4,3},{5,4},{6,5},{7,6},{8,15},{9,8},{10,9... | collective-permute-start | bytes 221192 | tf_op jit(solution)/shard_map/ppermute | solution.py:29
  50.8 4.3 %collective-permute-start.3 = (bf16[6,24,256]{2,1,0:T(8,128)(2,1)S(1)}, bf16[6,24,256]{2,1,0:T(8,128)(2,1)S(1)}, u32[]{:S(2)}, u32[]{:S(2)}) collective-permute-start(bf16[6,24,256]{2,1,0:T(8,128)(2,1)S(1)} %get-tuple-element.22), channel_id=1, source_target_pairs={{0,8},{1,9},{2,10},{3,11},{4,12},{5,13},{6,14},{7,15},{8,16},{9,17... | collective-permute-start | bytes 221192 | tf_op jit(solution)/shard_map/ppermute | solution.py:29
  55.1 1.3 %collective-permute-start.8 = (bf16[6,24,256]{2,1,0:T(8,128)(2,1)S(1)}, bf16[6,24,256]{2,1,0:T(8,128)(2,1)S(1)}, u32[]{:S(2)}, u32[]{:S(2)}) collective-permute-start(bf16[6,24,256]{2,1,0:T(8,128)(2,1)S(1)} %get-tuple-element.23), channel_id=1, source_target_pairs={{8,0},{9,1},{10,2},{11,3},{12,4},{13,5},{14,6},{15,7},{16,8},{17,9... | collective-permute-start | bytes 221192 | tf_op jit(solution)/shard_map/ppermute | solution.py:29
  56.4 1.5 %collective-permute-start.9 = (bf16[6,6,256]{2,1,0:T(8,128)(2,1)S(1)}, bf16[6,6,256]{2,1,0:T(8,128)(2,1)S(1)}, u32[]{:S(2)}, u32[]{:S(2)}) collective-permute-start(bf16[6,6,256]{2,1,0:T(8,128)(2,1)S(1)} %get-tuple-element.19), channel_id=1, source_target_pairs={{8,7},{9,0},{10,1},{11,2},{12,3},{13,4},{14,5},{15,6},{16,15},{17,... | collective-permute-start | bytes 55304 | tf_op jit(solution)/shard_map/ppermute | solution.py:29
  57.9 3.9 %collective-permute-done.9 = bf16[6,6,256]{2,1,0:T(8,128)(2,1)S(1)} collective-permute-done((bf16[6,6,256]{2,1,0:T(8,128)(2,1)S(1)}, bf16[6,6,256]{2,1,0:T(8,128)(2,1)S(1)}, u32[]{:S(2)}, u32[]{:S(2)}) %collective-permute-start.9) | collective-permute-done | bytes 18464 | tf_op jit(solution)/shard_map/ppermute | solution.py:29
  61.8 0.2 collective-permute-done.8
  62.0 0.2 maximum_convert_fusion
  62.2 0.1 slice.1028
  62.4 7.2 %fusion.162 = (f32[30,32]{1,0:T(8,128)S(1)}, f32[30,32,256]{2,1,0:T(8,128)S(1)}) fusion(f32[256]{0:T(256)S(1)} %bitcast.213, f32[256]{0:T(256)S(1)} %bitcast.214, f32[256]{0:T(256)S(1)} %bitcast.215, f32[256]{0:T(256)S(1)} %bitcast.216, f32[256]{0:T(256)S(1)} %bitcast.217, f32[256]{0:T(256)S(1)} %bitcast.218, f32[256]{0:T(256)S(1)} %bitcast.219, ...), kind=kLoop, calls=%fused_computation.305 | loop fusion | flops 24083520 | bytes 36918016 | tf_op jit(solution)/shard_map/reduce_sum | solution.py:87
  69.6 0.4 multiply_reduce_fusion
  70.0 0.3 multiply_convert_fusion
  70.3 0.5 copy-done.9
  70.8 1.4 %fusion.12 = bf16[960,1024]{1,0:T(8,128)(2,1)S(1)} fusion(bf16[960,256]{1,0:T(8,128)(2,1)S(1)} %bitcast.204, bf16[2,256,1024]{2,1,0:T(8,128)(2,1)S(1)} %copy-done.9), kind=kOutput, calls=%fused_computation.17 | convolution fusion | flops 512163840 | bytes 2981888 | tf_op jit(solution)/shard_map/dot_general | solution.py:91
  72.3 0.7 fusion.141
  72.9 0.2 fusion.149
  73.1 4.4 %fusion.160 = (f32[24,24]{1,0:T(8,128)S(1)}, f32[24,24,256]{2,1,0:T(8,128)S(1)}) fusion(f32[256]{0:T(256)S(1)} %bitcast.292, f32[30,30,256]{2,1,0:T(8,128)S(1)} %fusion.149, f32[256]{0:T(256)S(1)} %bitcast.293, f32[256]{0:T(256)S(1)} %bitcast.294, f32[256]{0:T(256)S(1)} %bitcast.295, f32[256]{0:T(256)S(1)} %bitcast.296, f32[256]{0:T(256)S(1)} %bitcast.297, ...), kind=kLoop, calls=%fused_computation.304 | loop fusion | flops 14450112 | bytes 29543680 | tf_op jit(solution)/shard_map/reduce_sum | solution.py:87
  77.6 0.3 multiply_reduce_fusion.1
  77.9 0.2 multiply_convert_fusion.1
  78.1 0.9 %fusion.28 = bf16[576,1024]{1,0:T(8,128)(2,1)S(1)} fusion(bf16[576,256]{1,0:T(8,128)(2,1)S(1)} %bitcast.205, bf16[2,256,1024]{2,1,0:T(8,128)(2,1)S(1)} %copy-done.9), kind=kOutput, calls=%fused_computation.35 | convolution fusion | flops 307298304 | bytes 1998848 | tf_op jit(solution)/shard_map/dot_general | solution.py:91
  79.0 1.2 %fusion.33 = bf16[24,24,256]{2,1,0:T(8,128)(2,1)} fusion(bf16[24,24,1024]{2,1,0:T(8,128)(2,1)S(1)} %bitcast.313, f32[30,30,256]{2,1,0:T(8,128)S(1)} %fusion.149, bf16[2,1024,256]{2,1,0:T(8,128)(2,1)S(1)} %copy-done.10), kind=kOutput, calls=%fused_computation.42 | convolution fusion | flops 302284800 | bytes 2588672 | tf_op jit(solution)/shard_map/dot_general | solution.py:94
  (65 shorter events, 0.9 us)
Async XLA Ops:
  0.0 8.8 %copy-start = (bf16[3,3,256,256]{3,2,1,0:T(8,128)(2,1)S(1)}, bf16[3,3,256,256]{3,2,1,0:T(8,128)(2,1)}, u32[]{:S(2)}) copy-start(bf16[3,3,256,256]{3,2,1,0:T(8,128)(2,1)} %param.14) | copy-start | bytes 3538948
  5.5 3.3 %copy-start.11 = (f32[256]{0:T(256)S(1)}, f32[256]{0:T(256)}, u32[]{:S(2)}) copy-start(f32[256]{0:T(256)} %param.15) | copy-start | bytes 3076
  5.5 3.3 %copy-start.12 = (pred[16,5]{0,1:T(8,128)(4,1)S(1)}, pred[16,5]{0,1:T(8,128)(4,1)}, u32[]{:S(2)}) copy-start(pred[16,5]{0,1:T(8,128)(4,1)} %constant.66) | copy-start | bytes 244
  13.9 0.7 copy-start.8
  14.0 0.7 copy-start.3
  14.0 1.0 %copy-start.4 = (bf16[2,16,32]{2,1,0:T(8,128)(2,1)S(1)}, bf16[2,16,32]{2,1,0:T(8,128)(2,1)}, u32[]{:S(2)}) copy-start(bf16[2,16,32]{2,1,0:T(8,128)(2,1)} %param.20) | copy-start | bytes 6148
  14.6 1.9 %copy-start.6 = (s32[2]{0:T(128)S(1)}, s32[2]{0:T(128)}, u32[]{:S(2)}) copy-start(s32[2]{0:T(128)} %param.17) | copy-start | bytes 28
  14.6 1.9 %copy-start.7 = (s32[2]{0:T(128)S(1)}, s32[2]{0:T(128)}, u32[]{:S(2)}) copy-start(s32[2]{0:T(128)} %param.18) | copy-start | bytes 28
  16.0 8.6 %copy-start.2 = (f32[2,7,7,256]{3,0,2,1:T(2,128)S(1)}, f32[2,7,7,256]{3,0,2,1:T(2,128)}, u32[]{:S(2)}) copy-start(f32[2,7,7,256]{3,0,2,1:T(2,128)} %param.22) | copy-start | bytes 301060
  16.6 8.2 %copy-start.5 = (f32[2,256]{1,0:T(2,128)S(1)}, f32[2,256]{1,0:T(2,128)}, u32[]{:S(2)}) copy-start(f32[2,256]{1,0:T(2,128)} %param.23) | copy-start | bytes 6148
  17.2 12.4 %collective-permute-start.1 = (bf16[2,17,16,256]{3,2,1,0:T(8,128)(2,1)S(1)}, bf16[2,17,16,256]{3,2,1,0:T(8,128)(2,1)S(1)}, u32[]{:S(2)}, u32[]{:S(2)}) collective-permute-start(bf16[2,17,16,256]{3,2,1,0:T(8,128)(2,1)S(1)} %pad_maximum_fusion.2), channel_id=1, source_target_pairs={{8,0},{16,8},{24,16},{9,1},{17,9},{25,17},{10,2},{18,10},{26,18},{... | collective-permute-start | bytes 835592 | tf_op jit(solution)/shard_map/ppermute | solution.py:17
  19.1 11.4 %collective-permute-start = (bf16[2,17,16,256]{3,2,1,0:T(8,128)(2,1)S(1)}, bf16[2,17,16,256]{3,2,1,0:T(8,128)(2,1)S(1)}, u32[]{:S(2)}, u32[]{:S(2)}) collective-permute-start(bf16[2,17,16,256]{3,2,1,0:T(8,128)(2,1)S(1)} %pad_maximum_fusion.1), channel_id=1, source_target_pairs={{0,8},{8,16},{16,24},{1,9},{9,17},{17,25},{2,10},{10,18},{18,26},{... | collective-permute-start | bytes 835592 | tf_op jit(solution)/shard_map/ppermute | solution.py:17
  24.8 7.1 %copy-start.1 = (bf16[24,24,256]{2,1,0:T(8,128)(2,1)S(1)}, bf16[24,24,256]{2,1,0:T(8,128)(2,1)}, u32[]{:S(2)}) copy-start(bf16[24,24,256]{2,1,0:T(8,128)(2,1)} %param.21) | copy-start | bytes 884740
  32.4 18.4 %collective-permute-start.2 = (bf16[6,6,256]{2,1,0:T(8,128)(2,1)S(1)}, bf16[6,6,256]{2,1,0:T(8,128)(2,1)S(1)}, u32[]{:S(2)}, u32[]{:S(2)}) collective-permute-start(bf16[6,6,256]{2,1,0:T(8,128)(2,1)S(1)} %get-tuple-element.18), channel_id=1, source_target_pairs={{0,9},{1,10},{2,11},{3,12},{4,13},{5,14},{6,15},{7,8},{8,17},{9,18... | collective-permute-start | bytes 55304 | tf_op jit(solution)/shard_map/ppermute | solution.py:29
  37.0 18.0 %collective-permute-start.4 = (bf16[6,6,256]{2,1,0:T(8,128)(2,1)S(1)}, bf16[6,6,256]{2,1,0:T(8,128)(2,1)S(1)}, u32[]{:S(2)}, u32[]{:S(2)}) collective-permute-start(bf16[6,6,256]{2,1,0:T(8,128)(2,1)S(1)} %get-tuple-element.21), channel_id=1, source_target_pairs={{0,15},{1,8},{2,9},{3,10},{4,11},{5,12},{6,13},{7,14},{8,23},{9,16... | collective-permute-start | bytes 55304 | tf_op jit(solution)/shard_map/ppermute | solution.py:29
  45.9 10.5 %collective-permute-start.7 = (bf16[6,6,256]{2,1,0:T(8,128)(2,1)S(1)}, bf16[6,6,256]{2,1,0:T(8,128)(2,1)S(1)}, u32[]{:S(2)}, u32[]{:S(2)}) collective-permute-start(bf16[6,6,256]{2,1,0:T(8,128)(2,1)S(1)} %get-tuple-element.20), channel_id=1, source_target_pairs={{8,1},{9,2},{10,3},{11,4},{12,5},{13,6},{14,7},{15,0},{16,9},{17,1... | collective-permute-start | bytes 55304 | tf_op jit(solution)/shard_map/ppermute | solution.py:29
  47.2 14.6 %collective-permute-start.5 = (bf16[24,6,256]{2,1,0:T(8,128)(2,1)S(1)}, bf16[24,6,256]{2,1,0:T(8,128)(2,1)S(1)}, u32[]{:S(2)}, u32[]{:S(2)}) collective-permute-start(bf16[24,6,256]{2,1,0:T(8,128)(2,1)S(1)} %get-tuple-element.24), channel_id=1, source_target_pairs={{0,1},{1,2},{2,3},{3,4},{4,5},{5,6},{6,7},{7,0},{8,9},{9,10},{10,1... | collective-permute-start | bytes 221192 | tf_op jit(solution)/shard_map/ppermute | solution.py:29
  47.3 14.5 %collective-permute-start.6 = (bf16[24,6,256]{2,1,0:T(8,128)(2,1)S(1)}, bf16[24,6,256]{2,1,0:T(8,128)(2,1)S(1)}, u32[]{:S(2)}, u32[]{:S(2)}) collective-permute-start(bf16[24,6,256]{2,1,0:T(8,128)(2,1)S(1)} %get-tuple-element.25), channel_id=1, source_target_pairs={{0,7},{1,0},{2,1},{3,2},{4,3},{5,4},{6,5},{7,6},{8,15},{9,8},{10,9... | collective-permute-start | bytes 221192 | tf_op jit(solution)/shard_map/ppermute | solution.py:29
  50.8 11.0 %collective-permute-start.3 = (bf16[6,24,256]{2,1,0:T(8,128)(2,1)S(1)}, bf16[6,24,256]{2,1,0:T(8,128)(2,1)S(1)}, u32[]{:S(2)}, u32[]{:S(2)}) collective-permute-start(bf16[6,24,256]{2,1,0:T(8,128)(2,1)S(1)} %get-tuple-element.22), channel_id=1, source_target_pairs={{0,8},{1,9},{2,10},{3,11},{4,12},{5,13},{6,14},{7,15},{8,16},{9,17... | collective-permute-start | bytes 221192 | tf_op jit(solution)/shard_map/ppermute | solution.py:29
  55.1 6.9 %collective-permute-start.8 = (bf16[6,24,256]{2,1,0:T(8,128)(2,1)S(1)}, bf16[6,24,256]{2,1,0:T(8,128)(2,1)S(1)}, u32[]{:S(2)}, u32[]{:S(2)}) collective-permute-start(bf16[6,24,256]{2,1,0:T(8,128)(2,1)S(1)} %get-tuple-element.23), channel_id=1, source_target_pairs={{8,0},{9,1},{10,2},{11,3},{12,4},{13,5},{14,6},{15,7},{16,8},{17,9... | collective-permute-start | bytes 221192 | tf_op jit(solution)/shard_map/ppermute | solution.py:29
  56.4 5.4 %collective-permute-start.9 = (bf16[6,6,256]{2,1,0:T(8,128)(2,1)S(1)}, bf16[6,6,256]{2,1,0:T(8,128)(2,1)S(1)}, u32[]{:S(2)}, u32[]{:S(2)}) collective-permute-start(bf16[6,6,256]{2,1,0:T(8,128)(2,1)S(1)} %get-tuple-element.19), channel_id=1, source_target_pairs={{8,7},{9,0},{10,1},{11,2},{12,3},{13,4},{14,5},{15,6},{16,15},{17,... | collective-permute-start | bytes 55304 | tf_op jit(solution)/shard_map/ppermute | solution.py:29
  69.6 1.2 %copy-start.9 = (bf16[2,256,1024]{2,1,0:T(8,128)(2,1)S(1)}, bf16[2,256,1024]{2,1,0:T(8,128)(2,1)}, u32[]{:S(2)}) copy-start(bf16[2,256,1024]{2,1,0:T(8,128)(2,1)} %param.24) | copy-start | bytes 3145732
  70.8 1.4 %copy-start.10 = (bf16[2,1024,256]{2,1,0:T(8,128)(2,1)S(1)}, bf16[2,1024,256]{2,1,0:T(8,128)(2,1)}, u32[]{:S(2)}) copy-start(bf16[2,1024,256]{2,1,0:T(8,128)(2,1)} %param.25) | copy-start | bytes 3145732

commit v3 on v2

--- a/solution.py
+++ b/solution.py
@@ -15,32 +15,6 @@
     count = lax.axis_size(axis)
     leading, last = (max(0, -steps), min(count, count - steps))
     return lax.ppermute(value, axis, [(source, source + steps) for source in range(leading, last)])
-
-
-def halo_all(value, reach):
-    bands, tiles = lax.axis_size("lat"), lax.axis_size("lon")
-
-    def send(piece, dlat, dlon):
-        pairs = []
-        for lat in range(bands):
-            if 0 <= lat + dlat < bands:
-                for lon in range(tiles):
-                    pairs.append((lat * tiles + lon, (lat + dlat) * tiles + (lon + dlon) % tiles))
-        return lax.ppermute(piece, ("lat", "lon"), pairs)
-
-    top, bottom = value[:reach], value[-reach:]
-    north = send(bottom, 1, 0)
-    south = send(top, -1, 0)
-    west = send(value[:, -reach:], 0, 1)
-    east = send(value[:, :reach], 0, -1)
-    north_west = send(bottom[:, -reach:], 1, 1)
-    north_east = send(bottom[:, :reach], 1, -1)
-    south_west = send(top[:, -reach:], -1, 1)
-    south_east = send(top[:, :reach], -1, -1)
-    upper = jnp.concatenate([north_west, north, north_east], axis=1)
-    middle = jnp.concatenate([west, value, east], axis=1)
-    lower = jnp.concatenate([south_west, south, south_east], axis=1)
-    return jnp.concatenate([upper, middle, lower], axis=0)
 
 
 def resample_local(blocks, row_mix, col_mix):
@@ -129,35 +103,62 @@
     features = jax.nn.gelu(convolved + conv_bias).astype(jnp.bfloat16)
     resampled = resample_local(features, row_weights, col_weights)
     own_band = lax.axis_index("lat")
-    offset_band = block_band[:, 0] - own_band
-    staying = offset_band == 0
+    reach = HALO * LAYERS
+    lane = jnp.arange(channels, dtype=jnp.int32)[None, :]
+
+    def with_header(blocks, rows, cols, bands_of):
+        header = jnp.where(
+            lane == 0,
+            rows[:, None],
+            jnp.where(lane == 1, cols[:, None], jnp.where(lane == 2, bands_of[:, None], 0)),
+        ).astype(jnp.bfloat16)
+        header = jnp.broadcast_to(header[:, None, None, :], (blocks.shape[0], 1, RW, channels))
+        return jnp.concatenate([blocks, header], axis=1)
+
+    def split_header(got):
+        got_header = got[:, RB, 0, :].astype(jnp.int32)
+        return got[:, :RB], got_header[:, 0], got_header[:, 1], got_header[:, 2]
+
+    own_bands = block_band[:, 0]
+    mine = with_header(resampled, row_offset, col_offset, own_bands)
+    block_list, row_list, col_list, band_list = [resampled], [row_offset], [col_offset], [own_bands]
     positions = jnp.arange(blocks_here, dtype=jnp.int32)
-    row_list = [row_offset]
-    col_list = [col_offset]
-    block_list = [keep_local(staying, resampled)]
     for step in (1, -1):
-        going = offset_band == step
+        edge = background[-reach:] if step == 1 else background[:reach]
+        near_payload = jnp.concatenate(
+            [mine.reshape(-1, channels), edge.reshape(-1, channels)], axis=0
+        )
+        going = own_bands - own_band == step
         earlier = jnp.sum(going[None, :] & (positions[None, :] < positions[:, None]), axis=1)
         table = (jnp.arange(CAP, dtype=jnp.int32)[:, None] == earlier[None, :]) & going[None, :]
-        sent_blocks = place_rows(table, resampled)
-        sent_rows = place_ints(table, row_offset)
-        sent_cols = place_ints(table, col_offset)
-        lane = jnp.arange(channels, dtype=jnp.int32)[None, :]
-        header = jnp.where(
-            lane == 0, sent_rows[:, None], jnp.where(lane == 1, sent_cols[:, None], 0)
-        ).astype(jnp.bfloat16)
-        header = jnp.broadcast_to(header[:, None, None, :], (CAP, 1, RW, channels))
-        payload = jnp.concatenate([sent_blocks, header], axis=1)
-        got = shifted(payload, "lat", step)
-        block_list.append(got[:, :RB])
-        got_header = got[:, RB, 0, :].astype(jnp.int32)
-        row_list.append(got_header[:, 0])
-        col_list.append(got_header[:, 1])
+        far_payload = with_header(
+            place_rows(table, resampled),
+            place_ints(table, row_offset),
+            place_ints(table, col_offset),
+            place_ints(table, own_bands),
+        )
+        got_near = shifted(near_payload, "lat", step)
+        got_far = shifted(far_payload, "lat", 2 * step)
+        near_blocks = got_near[: mine.shape[0] * mine.shape[1] * RW].reshape(mine.shape)
+        got_edge = got_near[mine.shape[0] * mine.shape[1] * RW :].reshape(edge.shape)
+        for got in (near_blocks, got_far):
+            blocks, rows, cols, bands_of = split_header(got)
+            block_list.append(blocks)
+            row_list.append(rows)
+            col_list.append(cols)
+            band_list.append(bands_of)
+        if step == 1:
+            north_edge = got_edge
+        else:
+            south_edge = got_edge
     arrived = jnp.concatenate(block_list, axis=0)
-    all_rows = jnp.concatenate(row_list, axis=0)
+    all_rows = (jnp.concatenate(band_list, axis=0) - own_band) * tile_rows + jnp.concatenate(
+        row_list, axis=0
+    ) + reach
     all_cols = jnp.concatenate(col_list, axis=0)
+    ext_rows = tile_rows + 2 * reach
     row_place = (
-        jnp.arange(tile_rows, dtype=jnp.int32)[None, :, None]
+        jnp.arange(ext_rows, dtype=jnp.int32)[None, :, None]
         == all_rows[:, None, None] + jnp.arange(RB, dtype=jnp.int32)[None, None, :]
     ).astype(jnp.bfloat16)
     col_place = (
@@ -168,9 +169,12 @@
         "shr,sruc->shuc", row_place, arrived, preferred_element_type=jnp.float32
     ).astype(jnp.bfloat16)
     summed = jnp.einsum("swu,shuc->hwc", col_place, lifted, preferred_element_type=jnp.float32)
-    state = (background.astype(jnp.float32) + summed).astype(jnp.bfloat16)
-    reach = HALO * LAYERS
-    widened = halo_all(state, reach)
+    ground = jnp.concatenate([north_edge, background, south_edge], axis=0)
+    state = (ground.astype(jnp.float32) + summed).astype(jnp.bfloat16)
+    tiles = lax.axis_size("lon")
+    west = lax.ppermute(state[:, -reach:], "lon", [(i, (i + 1) % tiles) for i in range(tiles)])
+    east = lax.ppermute(state[:, :reach], "lon", [((i + 1) % tiles, i) for i in range(tiles)])
+    widened = jnp.concatenate([west, state, east], axis=1)
     first_row = own_band * tile_rows
     for layer_index in range(LAYERS):
         widened = layer_apply(

time: 81.7 us -> 83.2 us (1.018)
  starting transfers between devices: 32.2 us -> 16.1 us
  local copies, waits for them, and re-layouts: 7.81 us -> 18.6 us
  other arithmetic: 17.4 us -> 20.2 us
  waiting for transfers between devices: 9.44 us -> 12 us
    ppermute x8 -> x2, starting transfers between devices: 25.4 us -> 3.59 us  [the longest x1 3.53 us: per_device(): lax.ppermute(state[:, :reach], 'lon', [((i + 1) % tiles, i) for i in rang...]
    ppermute x2 -> x4, starting transfers between devices: 6.82 us -> 12.5 us  [shifted(): lax.ppermute(value, axis, [(source, source + steps) for source in range(l...]
    slice x7 -> x10, local copies, waits for them, and re-layouts: 0.46 us -> 4.64 us  [the longest x2 1.95 us: per_device(): got_near[:mine.shape[0] * mine.shape[1] * RW].reshape(mine.shape)]
    slice x6, local copies, waits for them, and re-layouts: 0.11 us -> 3.83 us  [depthwise(): term = column[a:a + height] * depth_kernel[a, e]]
    ppermute x2 -> x4, waiting for transfers between devices: 5.37 us -> 9.06 us  [shifted(): lax.ppermute(value, axis, [(source, source + steps) for source in range(l...]
    unnamed x33 -> x184, local copies, waits for them, and re-layouts: 6.51 us -> 8.15 us
    convert_element_type x3 -> x5, other arithmetic: 0.09 us -> 1.5 us  [the longest x4 1.42 us: split_header(): got_header = got[:, RB, 0, :].astype(jnp.int32)]
    concatenate x5 -> x4, other arithmetic: 0.29 us -> 1.56 us  [the longest x3 1.51 us: with_header(): return jnp.concatenate([blocks, header], axis=1)]
  transfers between devices with their start and end apart: 10 -> 6, of which waited for: 4 -> 2; matrix products, arithmetic and copies ran while one was open for 1% -> 10% of each run, Pallas kernels for 0% -> 0%
where the time goes in v3:
time: 83.2 us; the launch traced here: 81.8 us
  other arithmetic  20.2 us (24%)
  local copies, waits for them, and re-layouts  18.6 us (22%)
  starting transfers between devices  16.1 us (19%)
  matrix products  13.6 us (16%)
  waiting for transfers between devices  12 us (14%)
  between operations  1.4 us (2%)
    ppermute x4, starting transfers between devices, shifted(): lax.ppermute(value, axis, [(source, source + steps) for source in range(l...  12.5 us
    reduce_sum x2, other arithmetic, layer_apply(): centered = mixed - jnp.mean(mixed, axis=-1, keepdims=True)  11.6 us
    ppermute x4, waiting for transfers between devices, shifted(): lax.ppermute(value, axis, [(source, source + steps) for source in range(l...  9.06 us
    unnamed x184, local copies, waits for them, and re-layouts  8.15 us
    conv_general_dilated x1, matrix products, per_device(): lax.conv_general_dilated(swath_input, conv_weight, (2, 2), ((1, 1), (1, 1...  5.13 us
    slice x6, local copies, waits for them, and re-layouts, depthwise(): term = column[a:a + height] * depth_kernel[a, e]  3.83 us
    ppermute x1, starting transfers between devices, per_device(): lax.ppermute(state[:, :reach], 'lon', [((i + 1) % tiles, i) for i in rang...  3.53 us
    conv_general_dilated x1, other arithmetic, per_device(): lax.conv_general_dilated(swath_input, conv_weight, (2, 2), ((1, 1), (1, 1...  3.28 us
  transfers between devices with their start and end apart: 6, of which 2 were waited for; matrix products, arithmetic and copies ran while one was open for 10% of the time, Pallas kernels for 0%

profile of v3, /device:TPU:0, one launch (start us, length us, event | category | flops | bytes accessed | tf_op | source)
XLA Modules:
  0.0 81.8 jit_solution(15974450229013449492)
XLA Ops:
  0.0 4.7 %copy.67 = bf16[2,64,64,256]{3,1,2,0:T(8,128)(2,1)S(1)} copy(bf16[2,64,64,256]{3,2,1,0:T(8,128)(2,1)} %param.13) | data formatting | bytes 8388608 | tf_op args[0]
  4.7 0.7 pad.5
  5.5 3.3 %fusion.1 = bf16[64,2,8,12,256]{4,0,3,2,1:T(8,128)(2,1)S(1)} fusion(bf16[64,2,7,2,256]{4,0,3,2,1:T(8,128)(2,1)S(1)} %slice.1054, bf16[64,2,8,10,256]{4,0,3,2,1:T(8,128)(2,1)S(1)} %bitcast.209), kind=kLoop, calls=%fused_computation.4 | loop fusion | flops 18874368 | bytes 12451840 | tf_op jit(solution)/shard_map/conv_general_dilated | solution.py:95
  8.8 5.1 %fusion.22 = bf16[32,16,5,256]{3,1,2,0:T(8,128)(2,1)S(1)} fusion(bf16[3,3,256,256]{3,2,1,0:T(8,128)(2,1)S(1)} %copy-done, bf16[64,2,8,12,256]{4,0,3,2,1:T(8,128)(2,1)S(1)} %fusion.1, f32[256]{0:T(256)S(1)} %copy-done.84, pred[16,5]{0,1:T(8,128)(4,1)S(1)} %copy-done.85), kind=kOutput, calls=%fused_computation.29 | convolution fusion | flops 2995650560 | bytes 8782928 | tf_op jit(solution)/shard_map/conv_general_dilated | solution.py:95
  14.0 0.4 copy.23
  14.7 0.3 convolution_bitcast_fusion
  14.9 1.1 %constant_dynamic-update-slice_fusion = (bf16[10,16,16,256]{3,2,1,0:T(8,128)(2,1)S(1)}, bf16[2,16,256,16]{2,3,1,0:T(8,128)(2,1)S(1)}) fusion(bf16[2,16,32]{2,1,0:T(8,128)(2,1)S(1)} %copy-done.5, f32[2,16,32,256]{3,1,2,0:T(8,128)S(1)} %convolution_bitcast_fusion), kind=kOutput, calls=%fused_computation.273 | convolution fusion | flops 50462720 | bytes 1574912 | tf_op jit(solution)/shard_map/nrjc,nuj->nruc/dot_general | solution.py:22
  16.0 0.3 copy.39
  16.7 0.4 convolution_convert_fusion.1
  17.3 0.7 pad_maximum_fusion.3
  18.0 5.6 %collective-permute-start.2 = (bf16[2,17,16,256]{3,2,1,0:T(8,128)(2,1)}, bf16[2,17,16,256]{3,2,1,0:T(8,128)(2,1)}, u32[]{:S(2)}, u32[]{:S(2)}) collective-permute-start(bf16[2,17,16,256]{3,2,1,0:T(8,128)(2,1)} %pad_maximum_fusion.3), channel_id=1, source_target_pairs={{0,16},{8,24},{1,17},{9,25},{2,18},{10,26},{3,19},{11,27},{4,20},{... | collective-permute-start | bytes 835592 | tf_op jit(solution)/shard_map/ppermute | solution.py:17
  23.6 0.4 convolution_convert_fusion
  24.1 0.7 pad_maximum_fusion.4
  24.9 1.3 %collective-permute-start.3 = (bf16[2,17,16,256]{3,2,1,0:T(8,128)(2,1)}, bf16[2,17,16,256]{3,2,1,0:T(8,128)(2,1)}, u32[]{:S(2)}, u32[]{:S(2)}) collective-permute-start(bf16[2,17,16,256]{3,2,1,0:T(8,128)(2,1)} %pad_maximum_fusion.4), channel_id=1, source_target_pairs={{16,0},{24,8},{17,1},{25,9},{18,2},{26,10},{19,3},{27,11},{20,4},{... | collective-permute-start | bytes 835592 | tf_op jit(solution)/shard_map/ppermute | solution.py:17
  26.3 4.1 %collective-permute-start = (bf16[688,256]{1,0:T(8,128)(2,1)S(1)}, bf16[688,256]{1,0:T(8,128)(2,1)}, u32[]{:S(2)}, u32[]{:S(2)}) collective-permute-start(bf16[688,256]{1,0:T(8,128)(2,1)S(1)} %get-tuple-element.33), channel_id=1, source_target_pairs={{0,8},{8,16},{16,24},{1,9},{9,17},{17,25},{2,10},{10,18},{18,26},{... | collective-permute-start | bytes 1056776 | tf_op jit(solution)/shard_map/ppermute | solution.py:17
  30.4 1.5 %collective-permute-start.1 = (bf16[688,256]{1,0:T(8,128)(2,1)S(1)}, bf16[688,256]{1,0:T(8,128)(2,1)}, u32[]{:S(2)}, u32[]{:S(2)}) collective-permute-start(bf16[688,256]{1,0:T(8,128)(2,1)S(1)} %get-tuple-element.34), channel_id=1, source_target_pairs={{8,0},{16,8},{24,16},{9,1},{17,9},{25,17},{10,2},{18,10},{26,18},{... | collective-permute-start | bytes 1056776 | tf_op jit(solution)/shard_map/ppermute | solution.py:17
  32.0 0.6 fusion.176
  32.6 0.7 fusion.177
  33.3 0.6 fusion.178
  33.9 0.7 fusion.174
  34.6 0.7 fusion.173
  35.3 0.6 fusion.175
  35.9 0.7 slice_convert_fusion.2
  36.6 0.7 slice_convert_fusion
  37.5 0.2 slice_reduce_fusion
  37.7 1.0 %slice.1058 = bf16[544,256]{1,0:T(8,128)(2,1)S(1)} slice(bf16[688,256]{1,0:T(8,128)(2,1)} %collective-permute-done), slice={[0:544], [0:256]} | slice | bytes 557056 | tf_op jit(solution)/shard_map/slice | solution.py:142
  39.0 9.1 %collective-permute-done.1 = bf16[688,256]{1,0:T(8,128)(2,1)} collective-permute-done((bf16[688,256]{1,0:T(8,128)(2,1)S(1)}, bf16[688,256]{1,0:T(8,128)(2,1)}, u32[]{:S(2)}, u32[]{:S(2)}) %collective-permute-start.1) | collective-permute-done | bytes 352288 | tf_op jit(solution)/shard_map/ppermute | solution.py:17
  48.0 1.0 %slice.1063 = bf16[544,256]{1,0:T(8,128)(2,1)S(1)} slice(bf16[688,256]{1,0:T(8,128)(2,1)} %collective-permute-done.1), slice={[0:544], [0:256]} | slice | bytes 557056 | tf_op jit(solution)/shard_map/slice | solution.py:142
  49.7 1.0 %slice_dynamic-update-slice_fusion.2 = bf16[10,16,16,256]{3,2,1,0:T(8,128)(2,1)S(1)} fusion(bf16[10,16,16,256]{3,2,1,0:T(8,128)(2,1)S(1)} %slice_dynamic-update-slice_fusion.3, bf16[2,17,16,256]{3,2,1,0:T(8,128)(2,1)} %collective-permute-done.2), kind=kLoop, calls=%fused_computation.261 | loop fusion | bytes 524288
  50.7 1.0 %slice_dynamic-update-slice_fusion = bf16[10,16,16,256]{3,2,1,0:T(8,128)(2,1)S(1)} fusion(bf16[10,16,16,256]{3,2,1,0:T(8,128)(2,1)S(1)} %slice_dynamic-update-slice_fusion.1, bf16[2,17,16,256]{3,2,1,0:T(8,128)(2,1)} %collective-permute-done.3), kind=kLoop, calls=%fused_computation.259 | loop fusion | bytes 524288 | tf_op jit(solution)/shard_map/concatenate | solution.py:154
  51.6 1.3 %convolution_convert_fusion.2 = bf16[10,36,16,256]{3,1,2,0:T(8,128)(2,1)S(1)} fusion(bf16[10,16,16,256]{3,2,1,0:T(8,128)(2,1)S(1)} %slice_dynamic-update-slice_fusion, s32[10,16]{1,0:T(8,128)S(1)} %iota_add_fusion.1), kind=kOutput, calls=%fused_computation.38 | convolution fusion | flops 48666240 | bytes 4260480 | tf_op jit(solution)/shard_map/shr,sruc->shuc/dot_general | solution.py:168
  53.0 0.9 %slice.1056 = bf16[144,256]{1,0:T(8,128)(2,1)S(1)} slice(bf16[688,256]{1,0:T(8,128)(2,1)} %collective-permute-done), slice={[544:688], [0:256]} | slice | bytes 147456 | tf_op jit(solution)/shard_map/slice | solution.py:143
  53.8 0.9 %slice.1057 = bf16[144,256]{1,0:T(8,128)(2,1)S(1)} slice(bf16[688,256]{1,0:T(8,128)(2,1)} %collective-permute-done.1), slice={[544:688], [0:256]} | slice | bytes 147456 | tf_op jit(solution)/shard_map/slice | solution.py:143
  54.7 0.7 add_convert_fusion
  55.9 3.5 %collective-permute-start.5 = (bf16[36,6,256]{2,1,0:T(8,128)(2,1)S(1)}, bf16[36,6,256]{2,1,0:T(8,128)(2,1)S(1)}, u32[]{:S(2)}, u32[]{:S(2)}) collective-permute-start(bf16[36,6,256]{2,1,0:T(8,128)(2,1)S(1)} %get-tuple-element.30), channel_id=1, source_target_pairs={{1,0},{2,1},{3,2},{4,3},{5,4},{6,5},{7,6},{0,7},{9,8},{10,9},{11,1... | collective-permute-start | bytes 331784 | tf_op jit(solution)/shard_map/ppermute | solution.py:176
  59.4 2.9 %collective-permute-done.4 = bf16[36,6,256]{2,1,0:T(8,128)(2,1)S(1)} collective-permute-done((bf16[36,6,256]{2,1,0:T(8,128)(2,1)S(1)}, bf16[36,6,256]{2,1,0:T(8,128)(2,1)S(1)}, u32[]{:S(2)}, u32[]{:S(2)}) %collective-permute-start.4) | collective-permute-done | bytes 110624 | tf_op jit(solution)/shard_map/ppermute | solution.py:175
  62.3 0.2 maximum_convert_fusion
  63.0 7.2 %fusion.168 = (f32[30,32]{1,0:T(8,128)S(1)}, f32[30,32,256]{2,1,0:T(8,128)S(1)}) fusion(f32[256]{0:T(256)S(1)} %bitcast.239, f32[256]{0:T(256)S(1)} %bitcast.240, f32[256]{0:T(256)S(1)} %bitcast.241, f32[256]{0:T(256)S(1)} %bitcast.242, f32[256]{0:T(256)S(1)} %bitcast.243, f32[256]{0:T(256)S(1)} %bitcast.244, f32[256]{0:T(256)S(1)} %bitcast.245, ...), kind=kLoop, calls=%fused_computation.324 | loop fusion | flops 24083520 | bytes 36918016 | tf_op jit(solution)/shard_map/reduce_sum | solution.py:61
  70.3 0.4 multiply_reduce_fusion
  70.7 0.3 multiply_convert_fusion
  71.0 0.5 copy-done.82
  71.5 1.4 %fusion.12 = bf16[960,1024]{1,0:T(8,128)(2,1)S(1)} fusion(bf16[960,256]{1,0:T(8,128)(2,1)S(1)} %bitcast.221, bf16[2,256,1024]{2,1,0:T(8,128)(2,1)S(1)} %copy-done.82), kind=kOutput, calls=%fused_computation.17 | convolution fusion | flops 512163840 | bytes 2981888 | tf_op jit(solution)/shard_map/dot_general | solution.py:65
  72.9 0.7 fusion.143
  74.7 4.4 %fusion.166 = (f32[24,24]{1,0:T(8,128)S(1)}, f32[24,24,256]{2,1,0:T(8,128)S(1)}) fusion(f32[256]{0:T(256)S(1)} %bitcast.307, f32[30,30,256]{2,1,0:T(8,128)S(1)} %fusion.151, f32[256]{0:T(256)S(1)} %bitcast.308, f32[256]{0:T(256)S(1)} %bitcast.309, f32[256]{0:T(256)S(1)} %bitcast.310, f32[256]{0:T(256)S(1)} %bitcast.311, f32[256]{0:T(256)S(1)} %bitcast.312, ...), kind=kLoop, calls=%fused_computation.323 | loop fusion | flops 14450112 | bytes 29543680 | tf_op jit(solution)/shard_map/reduce_sum | solution.py:61
  79.1 0.3 multiply_reduce_fusion.1
  79.4 0.2 multiply_convert_fusion.1
  79.6 0.9 %fusion.30 = bf16[576,1024]{1,0:T(8,128)(2,1)S(1)} fusion(bf16[576,256]{1,0:T(8,128)(2,1)S(1)} %bitcast.224, bf16[2,256,1024]{2,1,0:T(8,128)(2,1)S(1)} %copy-done.82), kind=kOutput, calls=%fused_computation.37 | convolution fusion | flops 307298304 | bytes 1998848 | tf_op jit(solution)/shard_map/dot_general | solution.py:65
  80.6 1.2 %fusion.37 = bf16[24,24,256]{2,1,0:T(8,128)(2,1)} fusion(bf16[24,24,1024]{2,1,0:T(8,128)(2,1)S(1)} %bitcast.339, f32[30,30,256]{2,1,0:T(8,128)S(1)} %fusion.151, bf16[2,1024,256]{2,1,0:T(8,128)(2,1)S(1)} %copy-done.83), kind=kOutput, calls=%fused_computation.43 | convolution fusion | flops 302284800 | bytes 2588672 | tf_op jit(solution)/shard_map/dot_general | solution.py:68
  (219 shorter events, 3.3 us)
Async XLA Ops:
  0.0 8.8 %copy-start = (bf16[3,3,256,256]{3,2,1,0:T(8,128)(2,1)S(1)}, bf16[3,3,256,256]{3,2,1,0:T(8,128)(2,1)}, u32[]{:S(2)}) copy-start(bf16[3,3,256,256]{3,2,1,0:T(8,128)(2,1)} %param.14) | copy-start | bytes 3538948
  5.5 3.3 %copy-start.84 = (f32[256]{0:T(256)S(1)}, f32[256]{0:T(256)}, u32[]{:S(2)}) copy-start(f32[256]{0:T(256)} %param.15) | copy-start | bytes 3076
  5.5 3.3 %copy-start.85 = (pred[16,5]{0,1:T(8,128)(4,1)S(1)}, pred[16,5]{0,1:T(8,128)(4,1)}, u32[]{:S(2)}) copy-start(pred[16,5]{0,1:T(8,128)(4,1)} %constant.69) | copy-start | bytes 244
  14.4 1.9 %copy-start.6 = (s32[2,1]{0,1:T(1,128)S(1)}, s32[2,1]{0,1:T(1,128)}, u32[]{:S(2)}) copy-start(s32[2,1]{0,1:T(1,128)} %param.16) | copy-start | bytes 28
  14.4 2.1 %copy-start.7 = (s32[2]{0:T(128)S(1)}, s32[2]{0:T(128)}, u32[]{:S(2)}) copy-start(s32[2]{0:T(128)} %param.18) | copy-start | bytes 28
  14.4 2.1 %copy-start.8 = (s32[2]{0:T(128)S(1)}, s32[2]{0:T(128)}, u32[]{:S(2)}) copy-start(s32[2]{0:T(128)} %param.17) | copy-start | bytes 28
  16.0 10.1 %copy-start.2 = (bf16[24,24,256]{2,1,0:T(8,128)(2,1)S(1)}, bf16[24,24,256]{2,1,0:T(8,128)(2,1)}, u32[]{:S(2)}) copy-start(bf16[24,24,256]{2,1,0:T(8,128)(2,1)} %param.21) | copy-start | bytes 884740
  17.2 14.7 %copy-start.1 = (f32[2,7,7,256]{3,0,2,1:T(2,128)S(1)}, f32[2,7,7,256]{3,0,2,1:T(2,128)}, u32[]{:S(2)}) copy-start(f32[2,7,7,256]{3,0,2,1:T(2,128)} %param.22) | copy-start | bytes 301060
  18.0 17.9 %collective-permute-start.2 = (bf16[2,17,16,256]{3,2,1,0:T(8,128)(2,1)}, bf16[2,17,16,256]{3,2,1,0:T(8,128)(2,1)}, u32[]{:S(2)}, u32[]{:S(2)}) collective-permute-start(bf16[2,17,16,256]{3,2,1,0:T(8,128)(2,1)} %pad_maximum_fusion.3), channel_id=1, source_target_pairs={{0,16},{8,24},{1,17},{9,25},{2,18},{10,26},{3,19},{11,27},{4,20},{... | collective-permute-start | bytes 835592 | tf_op jit(solution)/shard_map/ppermute | solution.py:17
  23.6 12.2 %copy-start.81 = (f32[2,256]{1,0:T(2,128)S(1)}, f32[2,256]{1,0:T(2,128)}, u32[]{:S(2)}) copy-start(f32[2,256]{1,0:T(2,128)} %param.23) | copy-start | bytes 6148
  24.9 11.7 %collective-permute-start.3 = (bf16[2,17,16,256]{3,2,1,0:T(8,128)(2,1)}, bf16[2,17,16,256]{3,2,1,0:T(8,128)(2,1)}, u32[]{:S(2)}, u32[]{:S(2)}) collective-permute-start(bf16[2,17,16,256]{3,2,1,0:T(8,128)(2,1)} %pad_maximum_fusion.4), channel_id=1, source_target_pairs={{16,0},{24,8},{17,1},{25,9},{18,2},{26,10},{19,3},{27,11},{20,4},{... | collective-permute-start | bytes 835592 | tf_op jit(solution)/shard_map/ppermute | solution.py:17
  26.3 11.5 %collective-permute-start = (bf16[688,256]{1,0:T(8,128)(2,1)S(1)}, bf16[688,256]{1,0:T(8,128)(2,1)}, u32[]{:S(2)}, u32[]{:S(2)}) collective-permute-start(bf16[688,256]{1,0:T(8,128)(2,1)S(1)} %get-tuple-element.33), channel_id=1, source_target_pairs={{0,8},{8,16},{16,24},{1,9},{9,17},{17,25},{2,10},{10,18},{18,26},{... | collective-permute-start | bytes 1056776 | tf_op jit(solution)/shard_map/ppermute | solution.py:17
  30.4 17.6 %collective-permute-start.1 = (bf16[688,256]{1,0:T(8,128)(2,1)S(1)}, bf16[688,256]{1,0:T(8,128)(2,1)}, u32[]{:S(2)}, u32[]{:S(2)}) collective-permute-start(bf16[688,256]{1,0:T(8,128)(2,1)S(1)} %get-tuple-element.34), channel_id=1, source_target_pairs={{8,0},{16,8},{24,16},{9,1},{17,9},{25,17},{10,2},{18,10},{26,18},{... | collective-permute-start | bytes 1056776 | tf_op jit(solution)/shard_map/ppermute | solution.py:17
  51.6 3.1 %copy-start.3 = (bf16[24,24,256]{2,1,0:T(8,128)(2,1)S(1)}, bf16[24,24,256]{2,1,0:T(8,128)(2,1)}, u32[]{:S(2)}) copy-start(bf16[24,24,256]{2,1,0:T(8,128)(2,1)} %param.21) | copy-start | bytes 884740
  55.5 7.3 %copy-start.9 = (f32[1,1,256]{2,1,0:T(1,128)S(1)}, f32[1,1,256]{2,1,0:T(1,128)}, u32[]{:S(2)}) copy-start(f32[1,1,256]{2,1,0:T(1,128)} %get-tuple-element.103) | copy-start | bytes 3076
  55.5 7.3 %copy-start.10 = (f32[1,1,256]{2,1,0:T(1,128)S(1)}, f32[1,1,256]{2,1,0:T(1,128)}, u32[]{:S(2)}) copy-start(f32[1,1,256]{2,1,0:T(1,128)} %get-tuple-element.104) | copy-start | bytes 3076
  55.5 7.3 %copy-start.11 = (f32[1,1,256]{2,1,0:T(1,128)S(1)}, f32[1,1,256]{2,1,0:T(1,128)}, u32[]{:S(2)}) copy-start(f32[1,1,256]{2,1,0:T(1,128)} %get-tuple-element.105) | copy-start | bytes 3076
  55.5 7.3 %copy-start.12 = (f32[1,1,256]{2,1,0:T(1,128)S(1)}, f32[1,1,256]{2,1,0:T(1,128)}, u32[]{:S(2)}) copy-start(f32[1,1,256]{2,1,0:T(1,128)} %get-tuple-element.106) | copy-start | bytes 3076
  55.5 7.3 %copy-start.13 = (f32[1,1,256]{2,1,0:T(1,128)S(1)}, f32[1,1,256]{2,1,0:T(1,128)}, u32[]{:S(2)}) copy-start(f32[1,1,256]{2,1,0:T(1,128)} %get-tuple-element.107) | copy-start | bytes 3076
  55.5 7.3 %copy-start.14 = (f32[1,1,256]{2,1,0:T(1,128)S(1)}, f32[1,1,256]{2,1,0:T(1,128)}, u32[]{:S(2)}) copy-start(f32[1,1,256]{2,1,0:T(1,128)} %get-tuple-element.108) | copy-start | bytes 3076
  55.5 7.3 %copy-start.15 = (f32[1,1,256]{2,1,0:T(1,128)S(1)}, f32[1,1,256]{2,1,0:T(1,128)}, u32[]{:S(2)}) copy-start(f32[1,1,256]{2,1,0:T(1,128)} %get-tuple-element.109) | copy-start | bytes 3076
  55.5 7.3 %copy-start.16 = (f32[1,1,256]{2,1,0:T(1,128)S(1)}, f32[1,1,256]{2,1,0:T(1,128)}, u32[]{:S(2)}) copy-start(f32[1,1,256]{2,1,0:T(1,128)} %get-tuple-element.110) | copy-start | bytes 3076
  55.5 7.3 %copy-start.17 = (f32[1,1,256]{2,1,0:T(1,128)S(1)}, f32[1,1,256]{2,1,0:T(1,128)}, u32[]{:S(2)}) copy-start(f32[1,1,256]{2,1,0:T(1,128)} %get-tuple-element.111) | copy-start | bytes 3076
  55.5 7.3 %copy-start.18 = (f32[1,1,256]{2,1,0:T(1,128)S(1)}, f32[1,1,256]{2,1,0:T(1,128)}, u32[]{:S(2)}) copy-start(f32[1,1,256]{2,1,0:T(1,128)} %get-tuple-element.112) | copy-start | bytes 3076
  55.6 7.3 %copy-start.19 = (f32[1,1,256]{2,1,0:T(1,128)S(1)}, f32[1,1,256]{2,1,0:T(1,128)}, u32[]{:S(2)}) copy-start(f32[1,1,256]{2,1,0:T(1,128)} %get-tuple-element.113) | copy-start | bytes 3076
  55.6 7.3 %copy-start.20 = (f32[1,1,256]{2,1,0:T(1,128)S(1)}, f32[1,1,256]{2,1,0:T(1,128)}, u32[]{:S(2)}) copy-start(f32[1,1,256]{2,1,0:T(1,128)} %get-tuple-element.114) | copy-start | bytes 3076
  55.6 7.3 %copy-start.21 = (f32[1,1,256]{2,1,0:T(1,128)S(1)}, f32[1,1,256]{2,1,0:T(1,128)}, u32[]{:S(2)}) copy-start(f32[1,1,256]{2,1,0:T(1,128)} %get-tuple-element.115) | copy-start | bytes 3076
  55.6 7.3 %copy-start.22 = (f32[1,1,256]{2,1,0:T(1,128)S(1)}, f32[1,1,256]{2,1,0:T(1,128)}, u32[]{:S(2)}) copy-start(f32[1,1,256]{2,1,0:T(1,128)} %get-tuple-element.116) | copy-start | bytes 3076
  55.6 7.3 %copy-start.23 = (f32[1,1,256]{2,1,0:T(1,128)S(1)}, f32[1,1,256]{2,1,0:T(1,128)}, u32[]{:S(2)}) copy-start(f32[1,1,256]{2,1,0:T(1,128)} %get-tuple-element.117) | copy-start | bytes 3076
  55.6 7.3 %copy-start.24 = (f32[1,1,256]{2,1,0:T(1,128)S(1)}, f32[1,1,256]{2,1,0:T(1,128)}, u32[]{:S(2)}) copy-start(f32[1,1,256]{2,1,0:T(1,128)} %get-tuple-element.118) | copy-start | bytes 3076
  55.6 7.3 %copy-start.25 = (f32[1,1,256]{2,1,0:T(1,128)S(1)}, f32[1,1,256]{2,1,0:T(1,128)}, u32[]{:S(2)}) copy-start(f32[1,1,256]{2,1,0:T(1,128)} %get-tuple-element.119) | copy-start | bytes 3076
  55.6 7.3 %copy-start.26 = (f32[1,1,256]{2,1,0:T(1,128)S(1)}, f32[1,1,256]{2,1,0:T(1,128)}, u32[]{:S(2)}) copy-start(f32[1,1,256]{2,1,0:T(1,128)} %get-tuple-element.120) | copy-start | bytes 3076
  55.6 7.3 %copy-start.27 = (f32[1,1,256]{2,1,0:T(1,128)S(1)}, f32[1,1,256]{2,1,0:T(1,128)}, u32[]{:S(2)}) copy-start(f32[1,1,256]{2,1,0:T(1,128)} %get-tuple-element.121) | copy-start | bytes 3076
  55.6 7.3 %copy-start.28 = (f32[1,1,256]{2,1,0:T(1,128)S(1)}, f32[1,1,256]{2,1,0:T(1,128)}, u32[]{:S(2)}) copy-start(f32[1,1,256]{2,1,0:T(1,128)} %get-tuple-element.122) | copy-start | bytes 3076
  55.7 7.3 %copy-start.29 = (f32[1,1,256]{2,1,0:T(1,128)S(1)}, f32[1,1,256]{2,1,0:T(1,128)}, u32[]{:S(2)}) copy-start(f32[1,1,256]{2,1,0:T(1,128)} %get-tuple-element.123) | copy-start | bytes 3076
  55.7 7.3 %copy-start.30 = (f32[1,1,256]{2,1,0:T(1,128)S(1)}, f32[1,1,256]{2,1,0:T(1,128)}, u32[]{:S(2)}) copy-start(f32[1,1,256]{2,1,0:T(1,128)} %get-tuple-element.124) | copy-start | bytes 3076
  55.7 7.3 %copy-start.31 = (f32[1,1,256]{2,1,0:T(1,128)S(1)}, f32[1,1,256]{2,1,0:T(1,128)}, u32[]{:S(2)}) copy-start(f32[1,1,256]{2,1,0:T(1,128)} %get-tuple-element.125) | copy-start | bytes 3076
  55.7 7.3 %copy-start.32 = (f32[1,1,256]{2,1,0:T(1,128)S(1)}, f32[1,1,256]{2,1,0:T(1,128)}, u32[]{:S(2)}) copy-start(f32[1,1,256]{2,1,0:T(1,128)} %get-tuple-element.126) | copy-start | bytes 3076
  55.7 7.3 %copy-start.33 = (f32[1,1,256]{2,1,0:T(1,128)S(1)}, f32[1,1,256]{2,1,0:T(1,128)}, u32[]{:S(2)}) copy-start(f32[1,1,256]{2,1,0:T(1,128)} %get-tuple-element.127) | copy-start | bytes 3076
  55.7 7.3 %copy-start.34 = (f32[1,1,256]{2,1,0:T(1,128)S(1)}, f32[1,1,256]{2,1,0:T(1,128)}, u32[]{:S(2)}) copy-start(f32[1,1,256]{2,1,0:T(1,128)} %get-tuple-element.128) | copy-start | bytes 3076
  55.7 7.3 %copy-start.35 = (f32[1,1,256]{2,1,0:T(1,128)S(1)}, f32[1,1,256]{2,1,0:T(1,128)}, u32[]{:S(2)}) copy-start(f32[1,1,256]{2,1,0:T(1,128)} %get-tuple-element.129) | copy-start | bytes 3076
  55.7 7.3 %copy-start.36 = (f32[1,1,256]{2,1,0:T(1,128)S(1)}, f32[1,1,256]{2,1,0:T(1,128)}, u32[]{:S(2)}) copy-start(f32[1,1,256]{2,1,0:T(1,128)} %get-tuple-element.130) | copy-start | bytes 3076
  55.7 7.3 %copy-start.37 = (f32[1,1,256]{2,1,0:T(1,128)S(1)}, f32[1,1,256]{2,1,0:T(1,128)}, u32[]{:S(2)}) copy-start(f32[1,1,256]{2,1,0:T(1,128)} %get-tuple-element.131) | copy-start | bytes 3076
  55.7 7.3 %copy-start.38 = (f32[1,1,256]{2,1,0:T(1,128)S(1)}, f32[1,1,256]{2,1,0:T(1,128)}, u32[]{:S(2)}) copy-start(f32[1,1,256]{2,1,0:T(1,128)} %get-tuple-element.132) | copy-start | bytes 3076
  55.8 7.3 %copy-start.39 = (f32[1,1,256]{2,1,0:T(1,128)S(1)}, f32[1,1,256]{2,1,0:T(1,128)}, u32[]{:S(2)}) copy-start(f32[1,1,256]{2,1,0:T(1,128)} %get-tuple-element.133) | copy-start | bytes 3076
  55.8 7.3 %copy-start.40 = (f32[1,1,256]{2,1,0:T(1,128)S(1)}, f32[1,1,256]{2,1,0:T(1,128)}, u32[]{:S(2)}) copy-start(f32[1,1,256]{2,1,0:T(1,128)} %get-tuple-element.134) | copy-start | bytes 3076
  55.8 6.5 %collective-permute-start.4 = (bf16[36,6,256]{2,1,0:T(8,128)(2,1)S(1)}, bf16[36,6,256]{2,1,0:T(8,128)(2,1)S(1)}, u32[]{:S(2)}, u32[]{:S(2)}) collective-permute-start(bf16[36,6,256]{2,1,0:T(8,128)(2,1)S(1)} %get-tuple-element.29), channel_id=1, source_target_pairs={{0,1},{1,2},{2,3},{3,4},{4,5},{5,6},{6,7},{7,0},{8,9},{9,10},{10,1... | collective-permute-start | bytes 331784 | tf_op jit(solution)/shard_map/ppermute | solution.py:175
  55.9 6.5 %collective-permute-start.5 = (bf16[36,6,256]{2,1,0:T(8,128)(2,1)S(1)}, bf16[36,6,256]{2,1,0:T(8,128)(2,1)S(1)}, u32[]{:S(2)}, u32[]{:S(2)}) collective-permute-start(bf16[36,6,256]{2,1,0:T(8,128)(2,1)S(1)} %get-tuple-element.30), channel_id=1, source_target_pairs={{1,0},{2,1},{3,2},{4,3},{5,4},{6,5},{7,6},{0,7},{9,8},{10,9},{11,1... | collective-permute-start | bytes 331784 | tf_op jit(solution)/shard_map/ppermute | solution.py:176
  (44 other events, 31.0 us)

commit v4 on v1

--- a/solution.py
+++ b/solution.py
@@ -66,20 +66,23 @@
 def layer_apply(padded, depth_kernel, gain, up_matrix, down_matrix):
     height = padded.shape[0] - (KS - 1)
     width = padded.shape[1] - (KS - 1)
+    spare = -width % 8
     widened = padded.astype(jnp.float32)
-    mixed = depthwise(widened, depth_kernel, height, width)
+    if spare:
+        widened = jnp.pad(widened, ((0, 0), (0, spare), (0, 0)))
+    mixed = depthwise(widened, depth_kernel, height, width + spare)
     centered = mixed - jnp.mean(mixed, axis=-1, keepdims=True)
     variance = jnp.mean(centered * centered, axis=-1, keepdims=True)
     normed = (centered * lax.rsqrt(variance + 1e-06) * gain).astype(jnp.bfloat16)
-    flat_cells = normed.reshape(height * width, -1)
+    flat_cells = normed.reshape(height * (width + spare), -1)
     hidden = jax.nn.gelu(jnp.dot(flat_cells, up_matrix, preferred_element_type=jnp.float32)).astype(
         jnp.bfloat16
     )
     output = jnp.dot(hidden, down_matrix, preferred_element_type=jnp.float32).reshape(
-        height, width, -1
+        height, width + spare, -1
     )
-    residual_part = widened[HALO : HALO + height, HALO : HALO + width]
-    return (residual_part + output).astype(jnp.bfloat16)
+    residual_part = widened[HALO : HALO + height, HALO : HALO + width + spare]
+    return (residual_part + output).astype(jnp.bfloat16)[:, :width]
 
 
 def per_device(

time: 80.7 us -> 72.9 us (0.903)
  local copies, waits for them, and re-layouts: 11.8 us -> 7.78 us
  matrix products: 16.7 us -> 12.8 us
    dot_general x1 -> x0, local copies, waits for them, and re-layouts: 3.46 us -> none  [layer_apply(): jnp.dot(hidden, down_matrix, preferred_element_type=jnp.float32)]
    dot_general x2, matrix products: 4.69 us -> 2.35 us  [layer_apply(): jnp.dot(flat_cells, up_matrix, preferred_element_type=jnp.float32)]
    dot_general x2, matrix products: 3.51 us -> 1.9 us  [layer_apply(): jnp.dot(hidden, down_matrix, preferred_element_type=jnp.float32)]
    reshape x1 -> x0, local copies, waits for them, and re-layouts: 0.89 us -> none  [layer_apply(): flat_cells = normed.reshape(height * width, -1)]
    unnamed x35 -> x33, local copies, waits for them, and re-layouts: 6.3 us -> 6.51 us
  transfers between devices with their start and end apart: 6 -> 6, of which waited for: 5 -> 5; matrix products, arithmetic and copies ran while one was open for 2% -> 1% of each run, Pallas kernels for 0% -> 0%
where the time goes in v4:
time: 72.9 us; the launch traced here: 72.6 us
  other arithmetic  17.7 us (24%)
  starting transfers between devices  17.4 us (24%)
  waiting for transfers between devices  16.4 us (22%)
  matrix products  12.8 us (18%)
  local copies, waits for them, and re-layouts  7.78 us (11%)
    reduce_sum x2, other arithmetic, layer_apply(): centered = mixed - jnp.mean(mixed, axis=-1, keepdims=True)  11.9 us
    ppermute x2, starting transfers between devices, shifted(): lax.ppermute(value, axis, [(source, source + steps) for source in range(l...  6.82 us
    unnamed x33, local copies, waits for them, and re-layouts  6.51 us
    ppermute x2, waiting for transfers between devices, with_halo(): after = lax.ppermute(leading, axis, down)  6.47 us
    ppermute x2, starting transfers between devices, with_halo(): before = lax.ppermute(last, axis, up)  5.79 us
    ppermute x2, waiting for transfers between devices, shifted(): lax.ppermute(value, axis, [(source, source + steps) for source in range(l...  5.4 us
    conv_general_dilated x1, matrix products, per_device(): lax.conv_general_dilated(swath_input, conv_weight, (2, 2), ((1, 1), (1, 1...  5.13 us
    ppermute x2, starting transfers between devices, with_halo(): after = lax.ppermute(leading, axis, down)  4.82 us
  transfers between devices with their start and end apart: 6, of which 5 were waited for; matrix products, arithmetic and copies ran while one was open for 1% of the time, Pallas kernels for 0%

profile of v4, /device:TPU:0, one launch (start us, length us, event | category | flops | bytes accessed | tf_op | source)
XLA Modules:
  0.0 72.6 jit_solution(16988405833613685044)
XLA Ops:
  0.0 4.7 %copy.59 = bf16[2,64,64,256]{3,1,2,0:T(8,128)(2,1)S(1)} copy(bf16[2,64,64,256]{3,2,1,0:T(8,128)(2,1)} %param.13) | data formatting | bytes 8388608 | tf_op args[0]
  4.7 0.7 pad.5
  5.5 3.3 %fusion.1 = bf16[64,2,8,12,256]{4,0,3,2,1:T(8,128)(2,1)S(1)} fusion(bf16[64,2,7,2,256]{4,0,3,2,1:T(8,128)(2,1)S(1)} %slice.990, bf16[64,2,8,10,256]{4,0,3,2,1:T(8,128)(2,1)S(1)} %bitcast.198), kind=kLoop, calls=%fused_computation.4 | loop fusion | flops 18874368 | bytes 12451840 | tf_op jit(solution)/shard_map/conv_general_dilated | solution.py:108
  8.8 5.1 %fusion.20 = bf16[32,16,5,256]{3,1,2,0:T(8,128)(2,1)S(1)} fusion(bf16[3,3,256,256]{3,2,1,0:T(8,128)(2,1)S(1)} %copy-done, bf16[64,2,8,12,256]{4,0,3,2,1:T(8,128)(2,1)S(1)} %fusion.1, f32[256]{0:T(256)S(1)} %copy-done.11, pred[16,5]{0,1:T(8,128)(4,1)S(1)} %copy-done.12), kind=kOutput, calls=%fused_computation.27 | convolution fusion | flops 2995650560 | bytes 8782928 | tf_op jit(solution)/shard_map/conv_general_dilated | solution.py:108
  14.0 0.4 copy.23
  14.4 0.2 copy-done.8
  14.7 0.3 convolution_bitcast_fusion
  15.0 1.1 %bitcast_select_fusion = (bf16[2,16,16,256]{3,2,1,0:T(8,128)(2,1)S(1)}, bf16[2,16,256,16]{2,3,1,0:T(8,128)(2,1)S(1)}) fusion(pred[2]{0:T(512)(128)(4,1)S(1)} %get-tuple-element.126, bf16[2,16,32]{2,1,0:T(8,128)(2,1)S(1)} %copy-done.4, f32[2,16,32,256]{3,1,2,0:T(8,128)S(1)} %convolution_bitcast_fusion), kind=kOutput, calls=%fused_computation.257 | convolution fusion | flops 50593792 | bytes 1574914 | tf_op jit(solution)/shard_map/nrjc,nuj->nruc/dot_general | solution.py:35
  16.0 0.3 copy.37
  16.3 0.1 fusion.158
  16.5 0.2 select_reduce_fusion.2
  16.6 0.4 convolution_convert_fusion
  17.1 0.1 select_convert_fusion.1
  17.2 1.3 %collective-permute-start.1 = (bf16[2,17,16,256]{3,2,1,0:T(8,128)(2,1)S(1)}, bf16[2,17,16,256]{3,2,1,0:T(8,128)(2,1)S(1)}, u32[]{:S(2)}, u32[]{:S(2)}) collective-permute-start(bf16[2,17,16,256]{3,2,1,0:T(8,128)(2,1)S(1)} %pad_maximum_fusion.2), channel_id=1, source_target_pairs={{8,0},{16,8},{24,16},{9,1},{17,9},{25,17},{10,2},{18,10},{26,18},{... | collective-permute-start | bytes 835592 | tf_op jit(solution)/shard_map/ppermute | solution.py:17
  18.5 0.4 convolution_convert_fusion.1
  19.0 5.5 %collective-permute-start = (bf16[2,17,16,256]{3,2,1,0:T(8,128)(2,1)S(1)}, bf16[2,17,16,256]{3,2,1,0:T(8,128)(2,1)S(1)}, u32[]{:S(2)}, u32[]{:S(2)}) collective-permute-start(bf16[2,17,16,256]{3,2,1,0:T(8,128)(2,1)S(1)} %pad_maximum_fusion.1), channel_id=1, source_target_pairs={{0,8},{8,16},{16,24},{1,9},{9,17},{17,25},{2,10},{10,18},{18,26},{... | collective-permute-start | bytes 835592 | tf_op jit(solution)/shard_map/ppermute | solution.py:17
  24.6 0.1 fusion.165
  24.9 4.7 %collective-permute-done.1 = bf16[2,17,16,256]{3,2,1,0:T(8,128)(2,1)S(1)} collective-permute-done((bf16[2,17,16,256]{3,2,1,0:T(8,128)(2,1)S(1)}, bf16[2,17,16,256]{3,2,1,0:T(8,128)(2,1)S(1)}, u32[]{:S(2)}, u32[]{:S(2)}) %collective-permute-start.1) | collective-permute-done | bytes 278560 | tf_op jit(solution)/shard_map/ppermute | solution.py:17
  29.6 0.2 slice_reduce_fusion
  29.8 0.7 collective-permute-done
  30.5 0.2 slice_reduce_fusion.1
  30.7 0.1 pad_add_fusion
  30.7 0.1 iota_add_fusion.1
  30.8 0.1 pad_add_fusion.1
  31.0 0.1 pad_maximum_fusion
  31.1 0.8 %convolution_convert_fusion.2 = bf16[6,24,16,256]{3,1,2,0:T(8,128)(2,1)S(1)} fusion(bf16[6,16,16,256]{3,2,1,0:T(8,128)(2,1)S(1)} %pad_maximum_fusion, s32[6,16]{1,0:T(8,128)S(1)} %iota_add_fusion.1), kind=kOutput, calls=%fused_computation.36 | convolution fusion | flops 19466496 | bytes 1966464 | tf_op jit(solution)/shard_map/shr,sruc->shuc/dot_general | solution.py:154
  32.0 0.4 fusion.32
  32.5 3.5 %collective-permute-start.3 = (bf16[24,6,256]{2,1,0:T(8,128)(2,1)S(1)}, bf16[24,6,256]{2,1,0:T(8,128)(2,1)S(1)}, u32[]{:S(2)}, u32[]{:S(2)}) collective-permute-start(bf16[24,6,256]{2,1,0:T(8,128)(2,1)S(1)} %get-tuple-element.21), channel_id=1, source_target_pairs={{1,0},{2,1},{3,2},{4,3},{5,4},{6,5},{7,6},{0,7},{9,8},{10,9},{11,1... | collective-permute-start | bytes 221192 | tf_op jit(solution)/shard_map/ppermute | solution.py:28
  36.0 2.4 %collective-permute-done.2 = bf16[24,6,256]{2,1,0:T(8,128)(2,1)S(1)} collective-permute-done((bf16[24,6,256]{2,1,0:T(8,128)(2,1)S(1)}, bf16[24,6,256]{2,1,0:T(8,128)(2,1)S(1)}, u32[]{:S(2)}, u32[]{:S(2)}) %collective-permute-start.2) | collective-permute-done | bytes 73760 | tf_op jit(solution)/shard_map/ppermute | solution.py:27
  38.4 0.1 pad_maximum_fusion.5
  38.5 5.7 %collective-permute-start.4 = (bf16[6,36,256]{2,1,0:T(8,128)(2,1)S(1)}, bf16[6,36,256]{2,1,0:T(8,128)(2,1)S(1)}, u32[]{:S(2)}, u32[]{:S(2)}) collective-permute-start(bf16[6,36,256]{2,1,0:T(8,128)(2,1)S(1)} %get-tuple-element.18), channel_id=1, source_target_pairs={{0,8},{8,16},{16,24},{1,9},{9,17},{17,25},{2,10},{10,18},{18,26},{... | collective-permute-start | bytes 331784 | tf_op jit(solution)/shard_map/ppermute | solution.py:27
  44.2 1.3 %collective-permute-start.5 = (bf16[6,36,256]{2,1,0:T(8,128)(2,1)S(1)}, bf16[6,36,256]{2,1,0:T(8,128)(2,1)S(1)}, u32[]{:S(2)}, u32[]{:S(2)}) collective-permute-start(bf16[6,36,256]{2,1,0:T(8,128)(2,1)S(1)} %get-tuple-element.19), channel_id=1, source_target_pairs={{8,0},{16,8},{24,16},{9,1},{17,9},{25,17},{10,2},{18,10},{26,18},{... | collective-permute-start | bytes 331784 | tf_op jit(solution)/shard_map/ppermute | solution.py:28
  45.5 2.2 %collective-permute-done.4 = bf16[6,36,256]{2,1,0:T(8,128)(2,1)S(1)} collective-permute-done((bf16[6,36,256]{2,1,0:T(8,128)(2,1)S(1)}, bf16[6,36,256]{2,1,0:T(8,128)(2,1)S(1)}, u32[]{:S(2)}, u32[]{:S(2)}) %collective-permute-start.4) | collective-permute-done | bytes 110624 | tf_op jit(solution)/shard_map/ppermute | solution.py:27
  47.7 6.5 %collective-permute-done.5 = bf16[6,36,256]{2,1,0:T(8,128)(2,1)S(1)} collective-permute-done((bf16[6,36,256]{2,1,0:T(8,128)(2,1)S(1)}, bf16[6,36,256]{2,1,0:T(8,128)(2,1)S(1)}, u32[]{:S(2)}, u32[]{:S(2)}) %collective-permute-start.5) | collective-permute-done | bytes 110624 | tf_op jit(solution)/shard_map/ppermute | solution.py:28
  54.2 0.2 maximum_convert_fusion
  54.3 0.1 slice.1002
  54.5 7.4 %fusion.162 = (f32[30,32]{1,0:T(8,128)S(1)}, f32[30,32,256]{2,1,0:T(8,128)S(1)}) fusion(f32[256]{0:T(256)S(1)} %bitcast.213, f32[256]{0:T(256)S(1)} %bitcast.214, f32[256]{0:T(256)S(1)} %bitcast.215, f32[256]{0:T(256)S(1)} %bitcast.216, f32[256]{0:T(256)S(1)} %bitcast.217, f32[256]{0:T(256)S(1)} %bitcast.218, f32[256]{0:T(256)S(1)} %bitcast.219, ...), kind=kLoop, calls=%fused_computation.308 | loop fusion | flops 24083520 | bytes 36918016 | tf_op jit(solution)/shard_map/reduce_sum | solution.py:74
  61.9 0.4 multiply_reduce_fusion
  62.3 0.3 multiply_convert_fusion
  62.7 0.5 copy-done.9
  63.2 1.4 %fusion.12 = bf16[960,1024]{1,0:T(8,128)(2,1)S(1)} fusion(bf16[960,256]{1,0:T(8,128)(2,1)S(1)} %bitcast.204, bf16[2,256,1024]{2,1,0:T(8,128)(2,1)S(1)} %copy-done.9), kind=kOutput, calls=%fused_computation.17 | convolution fusion | flops 512163840 | bytes 2981888 | tf_op jit(solution)/shard_map/dot_general | solution.py:78
  64.6 0.7 fusion.141
  65.3 0.2 fusion.149
  65.5 4.5 %fusion.160 = (f32[24,24]{1,0:T(8,128)S(1)}, f32[24,24,256]{2,1,0:T(8,128)S(1)}) fusion(f32[256]{0:T(256)S(1)} %bitcast.292, f32[30,30,256]{2,1,0:T(8,128)S(1)} %fusion.149, f32[256]{0:T(256)S(1)} %bitcast.293, f32[256]{0:T(256)S(1)} %bitcast.294, f32[256]{0:T(256)S(1)} %bitcast.295, f32[256]{0:T(256)S(1)} %bitcast.296, f32[256]{0:T(256)S(1)} %bitcast.297, ...), kind=kLoop, calls=%fused_computation.307 | loop fusion | flops 14450112 | bytes 29543680 | tf_op jit(solution)/shard_map/reduce_sum | solution.py:74
  69.9 0.3 multiply_reduce_fusion.1
  70.2 0.2 multiply_convert_fusion.1
  70.5 0.9 %fusion.28 = bf16[576,1024]{1,0:T(8,128)(2,1)S(1)} fusion(bf16[576,256]{1,0:T(8,128)(2,1)S(1)} %bitcast.205, bf16[2,256,1024]{2,1,0:T(8,128)(2,1)S(1)} %copy-done.9), kind=kOutput, calls=%fused_computation.35 | convolution fusion | flops 307298304 | bytes 1998848 | tf_op jit(solution)/shard_map/dot_general | solution.py:78
  71.4 1.2 %fusion.33 = bf16[24,24,256]{2,1,0:T(8,128)(2,1)} fusion(bf16[24,24,1024]{2,1,0:T(8,128)(2,1)S(1)} %bitcast.313, f32[30,30,256]{2,1,0:T(8,128)S(1)} %fusion.149, bf16[2,1024,256]{2,1,0:T(8,128)(2,1)S(1)} %copy-done.10), kind=kOutput, calls=%fused_computation.42 | convolution fusion | flops 302284800 | bytes 2588672 | tf_op jit(solution)/shard_map/dot_general | solution.py:81
  (56 shorter events, 0.7 us)
Async XLA Ops:
  0.0 8.8 %copy-start = (bf16[3,3,256,256]{3,2,1,0:T(8,128)(2,1)S(1)}, bf16[3,3,256,256]{3,2,1,0:T(8,128)(2,1)}, u32[]{:S(2)}) copy-start(bf16[3,3,256,256]{3,2,1,0:T(8,128)(2,1)} %param.14) | copy-start | bytes 3538948
  5.5 3.3 %copy-start.11 = (f32[256]{0:T(256)S(1)}, f32[256]{0:T(256)}, u32[]{:S(2)}) copy-start(f32[256]{0:T(256)} %param.15) | copy-start | bytes 3076
  5.5 3.3 %copy-start.12 = (pred[16,5]{0,1:T(8,128)(4,1)S(1)}, pred[16,5]{0,1:T(8,128)(4,1)}, u32[]{:S(2)}) copy-start(pred[16,5]{0,1:T(8,128)(4,1)} %constant.66) | copy-start | bytes 244
  13.9 0.7 copy-start.8
  14.0 0.7 copy-start.3
  14.0 1.0 %copy-start.4 = (bf16[2,16,32]{2,1,0:T(8,128)(2,1)S(1)}, bf16[2,16,32]{2,1,0:T(8,128)(2,1)}, u32[]{:S(2)}) copy-start(bf16[2,16,32]{2,1,0:T(8,128)(2,1)} %param.20) | copy-start | bytes 6148
  14.6 1.9 %copy-start.6 = (s32[2]{0:T(128)S(1)}, s32[2]{0:T(128)}, u32[]{:S(2)}) copy-start(s32[2]{0:T(128)} %param.17) | copy-start | bytes 28
  14.6 1.9 %copy-start.7 = (s32[2]{0:T(128)S(1)}, s32[2]{0:T(128)}, u32[]{:S(2)}) copy-start(s32[2]{0:T(128)} %param.18) | copy-start | bytes 28
  16.0 8.5 %copy-start.2 = (f32[2,7,7,256]{3,0,2,1:T(2,128)S(1)}, f32[2,7,7,256]{3,0,2,1:T(2,128)}, u32[]{:S(2)}) copy-start(f32[2,7,7,256]{3,0,2,1:T(2,128)} %param.22) | copy-start | bytes 301060
  17.2 12.4 %collective-permute-start.1 = (bf16[2,17,16,256]{3,2,1,0:T(8,128)(2,1)S(1)}, bf16[2,17,16,256]{3,2,1,0:T(8,128)(2,1)S(1)}, u32[]{:S(2)}, u32[]{:S(2)}) collective-permute-start(bf16[2,17,16,256]{3,2,1,0:T(8,128)(2,1)S(1)} %pad_maximum_fusion.2), channel_id=1, source_target_pairs={{8,0},{16,8},{24,16},{9,1},{17,9},{25,17},{10,2},{18,10},{26,18},{... | collective-permute-start | bytes 835592 | tf_op jit(solution)/shard_map/ppermute | solution.py:17
  19.0 11.4 %collective-permute-start = (bf16[2,17,16,256]{3,2,1,0:T(8,128)(2,1)S(1)}, bf16[2,17,16,256]{3,2,1,0:T(8,128)(2,1)S(1)}, u32[]{:S(2)}, u32[]{:S(2)}) collective-permute-start(bf16[2,17,16,256]{3,2,1,0:T(8,128)(2,1)S(1)} %pad_maximum_fusion.1), channel_id=1, source_target_pairs={{0,8},{8,16},{16,24},{1,9},{9,17},{17,25},{2,10},{10,18},{18,26},{... | collective-permute-start | bytes 835592 | tf_op jit(solution)/shard_map/ppermute | solution.py:17
  24.8 7.2 %copy-start.1 = (bf16[24,24,256]{2,1,0:T(8,128)(2,1)S(1)}, bf16[24,24,256]{2,1,0:T(8,128)(2,1)}, u32[]{:S(2)}) copy-start(bf16[24,24,256]{2,1,0:T(8,128)(2,1)} %param.21) | copy-start | bytes 884740
  31.1 4.9 %copy-start.5 = (f32[2,256]{1,0:T(2,128)S(1)}, f32[2,256]{1,0:T(2,128)}, u32[]{:S(2)}) copy-start(f32[2,256]{1,0:T(2,128)} %param.23) | copy-start | bytes 6148
  32.4 6.0 %collective-permute-start.2 = (bf16[24,6,256]{2,1,0:T(8,128)(2,1)S(1)}, bf16[24,6,256]{2,1,0:T(8,128)(2,1)S(1)}, u32[]{:S(2)}, u32[]{:S(2)}) collective-permute-start(bf16[24,6,256]{2,1,0:T(8,128)(2,1)S(1)} %get-tuple-element.20), channel_id=1, source_target_pairs={{0,1},{1,2},{2,3},{3,4},{4,5},{5,6},{6,7},{7,0},{8,9},{9,10},{10,1... | collective-permute-start | bytes 221192 | tf_op jit(solution)/shard_map/ppermute | solution.py:27
  32.5 5.9 %collective-permute-start.3 = (bf16[24,6,256]{2,1,0:T(8,128)(2,1)S(1)}, bf16[24,6,256]{2,1,0:T(8,128)(2,1)S(1)}, u32[]{:S(2)}, u32[]{:S(2)}) collective-permute-start(bf16[24,6,256]{2,1,0:T(8,128)(2,1)S(1)} %get-tuple-element.21), channel_id=1, source_target_pairs={{1,0},{2,1},{3,2},{4,3},{5,4},{6,5},{7,6},{0,7},{9,8},{10,9},{11,1... | collective-permute-start | bytes 221192 | tf_op jit(solution)/shard_map/ppermute | solution.py:28
  38.5 9.2 %collective-permute-start.4 = (bf16[6,36,256]{2,1,0:T(8,128)(2,1)S(1)}, bf16[6,36,256]{2,1,0:T(8,128)(2,1)S(1)}, u32[]{:S(2)}, u32[]{:S(2)}) collective-permute-start(bf16[6,36,256]{2,1,0:T(8,128)(2,1)S(1)} %get-tuple-element.18), channel_id=1, source_target_pairs={{0,8},{8,16},{16,24},{1,9},{9,17},{17,25},{2,10},{10,18},{18,26},{... | collective-permute-start | bytes 331784 | tf_op jit(solution)/shard_map/ppermute | solution.py:27
  44.2 10.0 %collective-permute-start.5 = (bf16[6,36,256]{2,1,0:T(8,128)(2,1)S(1)}, bf16[6,36,256]{2,1,0:T(8,128)(2,1)S(1)}, u32[]{:S(2)}, u32[]{:S(2)}) collective-permute-start(bf16[6,36,256]{2,1,0:T(8,128)(2,1)S(1)} %get-tuple-element.19), channel_id=1, source_target_pairs={{8,0},{16,8},{24,16},{9,1},{17,9},{25,17},{10,2},{18,10},{26,18},{... | collective-permute-start | bytes 331784 | tf_op jit(solution)/shard_map/ppermute | solution.py:28
  61.9 1.2 %copy-start.9 = (bf16[2,256,1024]{2,1,0:T(8,128)(2,1)S(1)}, bf16[2,256,1024]{2,1,0:T(8,128)(2,1)}, u32[]{:S(2)}) copy-start(bf16[2,256,1024]{2,1,0:T(8,128)(2,1)} %param.24) | copy-start | bytes 3145732
  63.2 1.4 %copy-start.10 = (bf16[2,1024,256]{2,1,0:T(8,128)(2,1)S(1)}, bf16[2,1024,256]{2,1,0:T(8,128)(2,1)}, u32[]{:S(2)}) copy-start(bf16[2,1024,256]{2,1,0:T(8,128)(2,1)} %param.25) | copy-start | bytes 3145732

commit v5 on v4

--- a/solution.py
+++ b/solution.py
@@ -1,6 +1,8 @@
 import jax
 import jax.numpy as jnp
 from jax import lax
+from jax.experimental import pallas as pl
+from jax.experimental.pallas import tpu as pltpu
 from jax.sharding import PartitionSpec as P
 
 KS = 7
@@ -9,6 +11,64 @@
 CAP = 2
 RB = 16
 RW = 16
+
+
+def _conv_body(x_ref, w_ref, b_ref, o_ref, wide_ref):
+    oh, ow, ch = o_ref.shape[1], o_ref.shape[2], o_ref.shape[3]
+    cin = x_ref.shape[3]
+    lanes = wide_ref.shape[3]
+    parts = wide_ref.shape[0]
+    for part in range(parts):
+        wide_ref[part] = x_ref[0, :, :, part * lanes : (part + 1) * lanes].astype(jnp.float32)
+
+    def parity(rp, cp):
+        halves = [
+            wide_ref[part, pl.ds(rp, oh, stride=2), pl.ds(cp, ow, stride=2), :].astype(x_ref.dtype)
+            for part in range(parts)
+        ]
+        v = jnp.concatenate(halves, axis=-1)
+        return v.reshape(oh * ow, cin)
+
+    def tap(v, a, e):
+        return jnp.dot(v, w_ref[a, e], preferred_element_type=jnp.float32)
+
+    even_even, even_odd = parity(0, 0), parity(0, 1)
+    odd_even, odd_odd = parity(1, 0), parity(1, 1)
+    plain = tap(even_even, 1, 1) + tap(even_odd, 1, 2) + tap(odd_even, 2, 1) + tap(odd_odd, 2, 2)
+    row_shift = tap(odd_even, 0, 1) + tap(odd_odd, 0, 2)
+    col_shift = tap(even_odd, 1, 0) + tap(odd_odd, 2, 0)
+    both_shift = tap(odd_odd, 0, 0)
+    plain = plain.reshape(oh, ow, ch)
+    row_shift = row_shift.reshape(oh, ow, ch)
+    col_shift = col_shift.reshape(oh, ow, ch)
+    both_shift = both_shift.reshape(oh, ow, ch)
+    zero_row = jnp.zeros((1, ow, ch), jnp.float32)
+    col_part = col_shift + jnp.concatenate([zero_row, both_shift[:-1]], axis=0)
+    total = plain + jnp.concatenate([zero_row, row_shift[:-1]], axis=0)
+    rolled = pltpu.roll(col_part, 1, 1)
+    first_col = lax.broadcasted_iota(jnp.int32, (oh, ow, ch), 1) == 0
+    total = total + jnp.where(first_col, 0.0, rolled)
+    total = total + b_ref[...]
+    o_ref[0] = jax.nn.gelu(total).astype(o_ref.dtype)
+
+
+def conv_gelu(x, w, b):
+    n, h, wd, cin = x.shape
+    cout = w.shape[3]
+    oh, ow = h // 2, wd // 2
+    return pl.pallas_call(
+        _conv_body,
+        grid=(n,),
+        in_specs=[
+            pl.BlockSpec((1, h, wd, cin), lambda i: (i, 0, 0, 0)),
+            pl.BlockSpec((3, 3, cin, cout), lambda i: (0, 0, 0, 0)),
+            pl.BlockSpec((1, cout), lambda i: (0, 0)),
+        ],
+        out_specs=pl.BlockSpec((1, oh, ow, cout), lambda i: (i, 0, 0, 0)),
+        out_shape=jax.ShapeDtypeStruct((n, oh, ow, cout), jnp.bfloat16),
+        scratch_shapes=[pltpu.VMEM((cin // 128, h, wd, 128), jnp.float32)],
+        compiler_params=pltpu.CompilerParams(dimension_semantics=("arbitrary",)),
+    )(x, w, b.reshape(1, cout))
 
 
 def shifted(value, axis, steps):
@@ -105,15 +165,7 @@
     tile_cols = background.shape[1]
     channels = background.shape[2]
     bands = lax.axis_size("lat")
-    convolved = lax.conv_general_dilated(
-        swath_input,
-        conv_weight,
-        (2, 2),
-        ((1, 1), (1, 1)),
-        dimension_numbers=("NHWC", "HWIO", "NHWC"),
-        preferred_element_type=jnp.float32,
-    )
-    features = jax.nn.gelu(convolved + conv_bias).astype(jnp.bfloat16)
+    features = conv_gelu(swath_input, conv_weight, conv_bias)
     resampled = resample_local(features, row_weights, col_weights)
     own_band = lax.axis_index("lat")
     offset_band = block_band[:, 0] - own_band

time: 72.9 us -> 67.2 us (0.922)
  Pallas kernels: 0 us -> 6.12 us
  local copies, waits for them, and re-layouts: 7.78 us -> 1.66 us
  waiting for transfers between devices: 16.4 us -> 20 us
  matrix products: 12.8 us -> 9.3 us
  other arithmetic: 17.7 us -> 14.8 us
  starting transfers between devices: 17.4 us -> 14.6 us
    pallas_call x0 -> x1, Pallas kernels: none -> 6.12 us  [conv_gelu(): pl.pallas_call(_conv_body, grid=(n,), in_specs=[pl.BlockSpec((1, h, wd, c...]
    ppermute x2, waiting for transfers between devices: 5.4 us -> 11.5 us  [shifted(): lax.ppermute(value, axis, [(source, source + steps) for source in range(l...]
    unnamed x33 -> x23, local copies, waits for them, and re-layouts: 6.51 us -> 0.88 us
    conv_general_dilated x1 -> x0, matrix products: 5.13 us -> none  [per_device(): lax.conv_general_dilated(swath_input, conv_weight, (2, 2), ((1, 1), (1, 1...]
    conv_general_dilated x1 -> x0, other arithmetic: 3.28 us -> none  [per_device(): lax.conv_general_dilated(swath_input, conv_weight, (2, 2), ((1, 1), (1, 1...]
    ppermute x2, waiting for transfers between devices: 6.47 us -> 4.12 us  [with_halo(): after = lax.ppermute(leading, axis, down)]
    ppermute x2, starting transfers between devices: 5.79 us -> 3.46 us  [with_halo(): before = lax.ppermute(last, axis, up)]
    dot_general x1, matrix products: 0.28 us -> 1.92 us  [resample_local(): jnp.einsum('nri,nijc->nrjc', row_mix, blocks, preferred_element_type=jnp....]
where the time goes in v5:
time: 67.2 us; the launch traced here: 66.9 us
  waiting for transfers between devices  20 us (30%)
  other arithmetic  14.8 us (22%)
  starting transfers between devices  14.6 us (22%)
  matrix products  9.3 us (14%)
  Pallas kernels  6.12 us (9%)
  local copies, waits for them, and re-layouts  1.66 us (2%)
    reduce_sum x2, other arithmetic, layer_apply(): centered = mixed - jnp.mean(mixed, axis=-1, keepdims=True)  11.6 us
    ppermute x2, waiting for transfers between devices, shifted(): lax.ppermute(value, axis, [(source, source + steps) for source in range(l...  11.5 us
    ppermute x2, starting transfers between devices, shifted(): lax.ppermute(value, axis, [(source, source + steps) for source in range(l...  6.18 us
    pallas_call x1, Pallas kernels, conv_gelu(): pl.pallas_call(_conv_body, grid=(n,), in_specs=[pl.BlockSpec((1, h, wd, c...  6.12 us
    ppermute x2, starting transfers between devices, with_halo(): after = lax.ppermute(leading, axis, down)  5 us
    ppermute x2, waiting for transfers between devices, with_halo(): before = lax.ppermute(last, axis, up)  4.38 us
    ppermute x2, waiting for transfers between devices, with_halo(): after = lax.ppermute(leading, axis, down)  4.12 us
    ppermute x2, starting transfers between devices, with_halo(): before = lax.ppermute(last, axis, up)  3.46 us
  transfers between devices with their start and end apart: 6, of which 5 were waited for; matrix products, arithmetic and copies ran while one was open for 1% of the time, Pallas kernels for 0%

profile of v5, /device:TPU:0, one launch (start us, length us, event | category | flops | bytes accessed | tf_op | source)
XLA Modules:
  0.0 66.9 jit_solution(1917491753659280644)
XLA Ops:
  0.0 0.7 compare_bitcast_fusion
  0.7 6.1 %shard_map.127 = bf16[2,32,32,256]{3,2,1,0:T(8,128)(2,1)} custom-call(bf16[2,64,64,256]{3,2,1,0:T(8,128)(2,1)} %x_ref.1, bf16[3,3,256,256]{3,2,1,0:T(8,128)(2,1)} %w_ref.1, f32[1,256]{1,0:T(1,128)} %bitcast.295), custom_call_target="tpu_custom_call" | custom-call | tf_op jit(solution)/shard_map/pallas_call | solution.py:59
  6.8 1.9 %convolution_bitcast_fusion = f32[2,16,32,256]{3,1,2,0:T(8,128)S(1)} fusion(bf16[2,32,32,256]{3,2,1,0:T(8,128)(2,1)} %shard_map.127, bf16[2,16,32]{2,1,0:T(8,128)(2,1)S(1)} %copy-done), kind=kOutput, calls=%fused_computation.21 | convolution fusion | flops 16777216 | bytes 2099200 | tf_op jit(solution)/shard_map/nri,nijc->nrjc/dot_general | solution.py:94
  8.7 1.1 %bitcast_select_fusion = (bf16[2,16,16,256]{3,2,1,0:T(8,128)(2,1)S(1)}, bf16[2,16,256,16]{2,3,1,0:T(8,128)(2,1)S(1)}) fusion(pred[2]{0:T(512)(128)(4,1)S(1)} %get-tuple-element.126, bf16[2,16,32]{2,1,0:T(8,128)(2,1)S(1)} %copy-done.3, f32[2,16,32,256]{3,1,2,0:T(8,128)S(1)} %convolution_bitcast_fusion), kind=kOutput, calls=%fused_computation.241 | convolution fusion | flops 50593792 | bytes 1574914 | tf_op jit(solution)/shard_map/nrjc,nuj->nruc/dot_general | solution.py:95
  9.8 0.0 copy-start.2
  9.8 0.3 copy.30
  10.1 0.1 fusion.144
  10.3 0.4 convolution_convert_fusion.1
  10.7 0.2 select_reduce_fusion.2
  10.9 0.1 select_convert_fusion.1
  11.0 4.9 %collective-permute-start = (bf16[2,17,16,256]{3,2,1,0:T(8,128)(2,1)S(1)}, bf16[2,17,16,256]{3,2,1,0:T(8,128)(2,1)S(1)}, u32[]{:S(2)}, u32[]{:S(2)}) collective-permute-start(bf16[2,17,16,256]{3,2,1,0:T(8,128)(2,1)S(1)} %pad_maximum_fusion.1), channel_id=1, source_target_pairs={{0,8},{8,16},{16,24},{1,9},{9,17},{17,25},{2,10},{10,18},{18,26},{... | collective-permute-start | bytes 835592 | tf_op jit(solution)/shard_map/ppermute | solution.py:77
  15.9 0.4 convolution_convert_fusion
  16.4 1.3 %collective-permute-start.1 = (bf16[2,17,16,256]{3,2,1,0:T(8,128)(2,1)S(1)}, bf16[2,17,16,256]{3,2,1,0:T(8,128)(2,1)S(1)}, u32[]{:S(2)}, u32[]{:S(2)}) collective-permute-start(bf16[2,17,16,256]{3,2,1,0:T(8,128)(2,1)S(1)} %pad_maximum_fusion.2), channel_id=1, source_target_pairs={{8,0},{16,8},{24,16},{9,1},{17,9},{25,17},{10,2},{18,10},{26,18},{... | collective-permute-start | bytes 835592 | tf_op jit(solution)/shard_map/ppermute | solution.py:77
  17.7 0.1 fusion.151
  18.0 3.8 %collective-permute-done = bf16[2,17,16,256]{3,2,1,0:T(8,128)(2,1)S(1)} collective-permute-done((bf16[2,17,16,256]{3,2,1,0:T(8,128)(2,1)S(1)}, bf16[2,17,16,256]{3,2,1,0:T(8,128)(2,1)S(1)}, u32[]{:S(2)}, u32[]{:S(2)}) %collective-permute-start) | collective-permute-done | bytes 278560 | tf_op jit(solution)/shard_map/ppermute | solution.py:77
  21.8 0.2 slice_reduce_fusion.1
  22.0 7.7 %collective-permute-done.1 = bf16[2,17,16,256]{3,2,1,0:T(8,128)(2,1)S(1)} collective-permute-done((bf16[2,17,16,256]{3,2,1,0:T(8,128)(2,1)S(1)}, bf16[2,17,16,256]{3,2,1,0:T(8,128)(2,1)S(1)}, u32[]{:S(2)}, u32[]{:S(2)}) %collective-permute-start.1) | collective-permute-done | bytes 278560 | tf_op jit(solution)/shard_map/ppermute | solution.py:77
  29.7 0.2 slice_reduce_fusion
  29.9 0.1 pad_add_fusion
  30.0 0.1 iota_add_fusion.1
  30.1 0.1 pad_add_fusion.1
  30.1 0.1 iota_add_fusion
  30.3 0.1 pad_maximum_fusion
  30.4 0.0 copy-start.4
  30.4 0.8 %convolution_convert_fusion.2 = bf16[6,24,16,256]{3,1,2,0:T(8,128)(2,1)S(1)} fusion(bf16[6,16,16,256]{3,2,1,0:T(8,128)(2,1)S(1)} %pad_maximum_fusion, s32[6,16]{1,0:T(8,128)S(1)} %iota_add_fusion.1), kind=kOutput, calls=%fused_computation.20 | convolution fusion | flops 19466496 | bytes 1966464 | tf_op jit(solution)/shard_map/shr,sruc->shuc/dot_general | solution.py:206
  31.2 0.4 fusion.17
  31.7 0.1 collective-permute-start.2
  31.7 3.5 %collective-permute-start.3 = (bf16[24,6,256]{2,1,0:T(8,128)(2,1)S(1)}, bf16[24,6,256]{2,1,0:T(8,128)(2,1)S(1)}, u32[]{:S(2)}, u32[]{:S(2)}) collective-permute-start(bf16[24,6,256]{2,1,0:T(8,128)(2,1)S(1)} %get-tuple-element.21), channel_id=1, source_target_pairs={{1,0},{2,1},{3,2},{4,3},{5,4},{6,5},{7,6},{0,7},{9,8},{10,9},{11,1... | collective-permute-start | bytes 221192 | tf_op jit(solution)/shard_map/ppermute | solution.py:88
  35.3 2.4 %collective-permute-done.2 = bf16[24,6,256]{2,1,0:T(8,128)(2,1)S(1)} collective-permute-done((bf16[24,6,256]{2,1,0:T(8,128)(2,1)S(1)}, bf16[24,6,256]{2,1,0:T(8,128)(2,1)S(1)}, u32[]{:S(2)}, u32[]{:S(2)}) %collective-permute-start.2) | collective-permute-done | bytes 73760 | tf_op jit(solution)/shard_map/ppermute | solution.py:87
  37.7 0.1 pad_maximum_fusion.5
  37.7 3.4 %collective-permute-start.4 = (bf16[6,36,256]{2,1,0:T(8,128)(2,1)S(1)}, bf16[6,36,256]{2,1,0:T(8,128)(2,1)S(1)}, u32[]{:S(2)}, u32[]{:S(2)}) collective-permute-start(bf16[6,36,256]{2,1,0:T(8,128)(2,1)S(1)} %get-tuple-element.18), channel_id=1, source_target_pairs={{0,8},{8,16},{16,24},{1,9},{9,17},{17,25},{2,10},{10,18},{18,26},{... | collective-permute-start | bytes 331784 | tf_op jit(solution)/shard_map/ppermute | solution.py:87
  41.2 1.5 %collective-permute-start.5 = (bf16[6,36,256]{2,1,0:T(8,128)(2,1)S(1)}, bf16[6,36,256]{2,1,0:T(8,128)(2,1)S(1)}, u32[]{:S(2)}, u32[]{:S(2)}) collective-permute-start(bf16[6,36,256]{2,1,0:T(8,128)(2,1)S(1)} %get-tuple-element.19), channel_id=1, source_target_pairs={{8,0},{16,8},{24,16},{9,1},{17,9},{25,17},{10,2},{18,10},{26,18},{... | collective-permute-start | bytes 331784 | tf_op jit(solution)/shard_map/ppermute | solution.py:88
  42.6 2.0 %collective-permute-done.4 = bf16[6,36,256]{2,1,0:T(8,128)(2,1)S(1)} collective-permute-done((bf16[6,36,256]{2,1,0:T(8,128)(2,1)S(1)}, bf16[6,36,256]{2,1,0:T(8,128)(2,1)S(1)}, u32[]{:S(2)}, u32[]{:S(2)}) %collective-permute-start.4) | collective-permute-done | bytes 110624 | tf_op jit(solution)/shard_map/ppermute | solution.py:87
  44.6 4.1 %collective-permute-done.5 = bf16[6,36,256]{2,1,0:T(8,128)(2,1)S(1)} collective-permute-done((bf16[6,36,256]{2,1,0:T(8,128)(2,1)S(1)}, bf16[6,36,256]{2,1,0:T(8,128)(2,1)S(1)}, u32[]{:S(2)}, u32[]{:S(2)}) %collective-permute-start.5) | collective-permute-done | bytes 110624 | tf_op jit(solution)/shard_map/ppermute | solution.py:88
  48.8 0.2 maximum_convert_fusion
  48.9 0.1 slice.998
  49.1 7.2 %fusion.148 = (f32[30,32]{1,0:T(8,128)S(1)}, f32[30,32,256]{2,1,0:T(8,128)S(1)}) fusion(f32[256]{0:T(256)S(1)} %bitcast.226, f32[256]{0:T(256)S(1)} %bitcast.227, f32[256]{0:T(256)S(1)} %bitcast.228, f32[256]{0:T(256)S(1)} %bitcast.229, f32[256]{0:T(256)S(1)} %bitcast.230, f32[256]{0:T(256)S(1)} %bitcast.231, f32[256]{0:T(256)S(1)} %bitcast.232, ...), kind=kLoop, calls=%fused_computation.292 | loop fusion | flops 24083520 | bytes 36918016 | tf_op jit(solution)/shard_map/reduce_sum | solution.py:134
  56.3 0.4 multiply_reduce_fusion
  56.7 0.3 multiply_convert_fusion
  57.0 0.5 copy-done.7
  57.5 1.4 %fusion.7 = bf16[960,1024]{1,0:T(8,128)(2,1)S(1)} fusion(bf16[960,256]{1,0:T(8,128)(2,1)S(1)} %bitcast.187, bf16[2,256,1024]{2,1,0:T(8,128)(2,1)S(1)} %copy-done.7), kind=kOutput, calls=%fused_computation.10 | convolution fusion | flops 512163840 | bytes 2981888 | tf_op jit(solution)/shard_map/dot_general | solution.py:138
  58.9 0.7 %fusion.127 = f32[30,32,256]{2,1,0:T(8,128)S(1)} fusion(bf16[30,32,1024]{2,1,0:T(8,128)(2,1)S(1)} %bitcast.296, bf16[2,1024,256]{2,1,0:T(8,128)(2,1)S(1)} %copy-done.8), kind=kOutput, calls=%fused_computation.230 | convolution fusion | flops 503316480 | bytes 3473408 | tf_op jit(solution)/shard_map/dot_general | solution.py:141
  59.6 0.2 fusion.135
  59.8 4.4 %fusion.146 = (f32[24,24]{1,0:T(8,128)S(1)}, f32[24,24,256]{2,1,0:T(8,128)S(1)}) fusion(f32[256]{0:T(256)S(1)} %bitcast.275, f32[30,30,256]{2,1,0:T(8,128)S(1)} %fusion.135, f32[256]{0:T(256)S(1)} %bitcast.276, f32[256]{0:T(256)S(1)} %bitcast.277, f32[256]{0:T(256)S(1)} %bitcast.278, f32[256]{0:T(256)S(1)} %bitcast.279, f32[256]{0:T(256)S(1)} %bitcast.280, ...), kind=kLoop, calls=%fused_computation.291 | loop fusion | flops 14450112 | bytes 29543680 | tf_op jit(solution)/shard_map/reduce_sum | solution.py:134
  64.2 0.3 multiply_reduce_fusion.1
  64.5 0.2 multiply_convert_fusion.1
  64.8 0.9 %fusion.15 = bf16[576,1024]{1,0:T(8,128)(2,1)S(1)} fusion(bf16[576,256]{1,0:T(8,128)(2,1)S(1)} %bitcast.188, bf16[2,256,1024]{2,1,0:T(8,128)(2,1)S(1)} %copy-done.7), kind=kOutput, calls=%fused_computation.19 | convolution fusion | flops 307298304 | bytes 1998848 | tf_op jit(solution)/shard_map/dot_general | solution.py:138
  65.7 1.2 %fusion.18 = bf16[24,24,256]{2,1,0:T(8,128)(2,1)} fusion(bf16[24,24,1024]{2,1,0:T(8,128)(2,1)S(1)} %bitcast.297, f32[30,30,256]{2,1,0:T(8,128)S(1)} %fusion.135, bf16[2,1024,256]{2,1,0:T(8,128)(2,1)S(1)} %copy-done.8), kind=kOutput, calls=%fused_computation.26 | convolution fusion | flops 302284800 | bytes 2588672 | tf_op jit(solution)/shard_map/dot_general | solution.py:141
  (43 shorter events, 0.4 us)
Async XLA Ops:
  0.0 6.8 %copy-start = (bf16[2,16,32]{2,1,0:T(8,128)(2,1)S(1)}, bf16[2,16,32]{2,1,0:T(8,128)(2,1)}, u32[]{:S(2)}) copy-start(bf16[2,16,32]{2,1,0:T(8,128)(2,1)} %param.19) | copy-start | bytes 6148
  0.7 8.1 %copy-start.3 = (bf16[2,16,32]{2,1,0:T(8,128)(2,1)S(1)}, bf16[2,16,32]{2,1,0:T(8,128)(2,1)}, u32[]{:S(2)}) copy-start(bf16[2,16,32]{2,1,0:T(8,128)(2,1)} %param.20) | copy-start | bytes 6148
  6.8 3.9 %copy-start.5 = (s32[2]{0:T(128)S(1)}, s32[2]{0:T(128)}, u32[]{:S(2)}) copy-start(s32[2]{0:T(128)} %param.17) | copy-start | bytes 28
  6.8 3.9 %copy-start.6 = (s32[2]{0:T(128)S(1)}, s32[2]{0:T(128)}, u32[]{:S(2)}) copy-start(s32[2]{0:T(128)} %param.18) | copy-start | bytes 28
  9.8 7.9 %copy-start.2 = (f32[2,7,7,256]{3,0,2,1:T(2,128)S(1)}, f32[2,7,7,256]{3,0,2,1:T(2,128)}, u32[]{:S(2)}) copy-start(f32[2,7,7,256]{3,0,2,1:T(2,128)} %param.22) | copy-start | bytes 301060
  11.0 10.8 %collective-permute-start = (bf16[2,17,16,256]{3,2,1,0:T(8,128)(2,1)S(1)}, bf16[2,17,16,256]{3,2,1,0:T(8,128)(2,1)S(1)}, u32[]{:S(2)}, u32[]{:S(2)}) collective-permute-start(bf16[2,17,16,256]{3,2,1,0:T(8,128)(2,1)S(1)} %pad_maximum_fusion.1), channel_id=1, source_target_pairs={{0,8},{8,16},{16,24},{1,9},{9,17},{17,25},{2,10},{10,18},{18,26},{... | collective-permute-start | bytes 835592 | tf_op jit(solution)/shard_map/ppermute | solution.py:77
  16.4 13.3 %collective-permute-start.1 = (bf16[2,17,16,256]{3,2,1,0:T(8,128)(2,1)S(1)}, bf16[2,17,16,256]{3,2,1,0:T(8,128)(2,1)S(1)}, u32[]{:S(2)}, u32[]{:S(2)}) collective-permute-start(bf16[2,17,16,256]{3,2,1,0:T(8,128)(2,1)S(1)} %pad_maximum_fusion.2), channel_id=1, source_target_pairs={{8,0},{16,8},{24,16},{9,1},{17,9},{25,17},{10,2},{18,10},{26,18},{... | collective-permute-start | bytes 835592 | tf_op jit(solution)/shard_map/ppermute | solution.py:77
  18.0 13.3 %copy-start.1 = (bf16[24,24,256]{2,1,0:T(8,128)(2,1)S(1)}, bf16[24,24,256]{2,1,0:T(8,128)(2,1)}, u32[]{:S(2)}) copy-start(bf16[24,24,256]{2,1,0:T(8,128)(2,1)} %param.21) | copy-start | bytes 884740
  30.4 4.9 %copy-start.4 = (f32[2,256]{1,0:T(2,128)S(1)}, f32[2,256]{1,0:T(2,128)}, u32[]{:S(2)}) copy-start(f32[2,256]{1,0:T(2,128)} %param.23) | copy-start | bytes 6148
  31.7 6.0 %collective-permute-start.2 = (bf16[24,6,256]{2,1,0:T(8,128)(2,1)S(1)}, bf16[24,6,256]{2,1,0:T(8,128)(2,1)S(1)}, u32[]{:S(2)}, u32[]{:S(2)}) collective-permute-start(bf16[24,6,256]{2,1,0:T(8,128)(2,1)S(1)} %get-tuple-element.20), channel_id=1, source_target_pairs={{0,1},{1,2},{2,3},{3,4},{4,5},{5,6},{6,7},{7,0},{8,9},{9,10},{10,1... | collective-permute-start | bytes 221192 | tf_op jit(solution)/shard_map/ppermute | solution.py:87
  31.7 5.9 %collective-permute-start.3 = (bf16[24,6,256]{2,1,0:T(8,128)(2,1)S(1)}, bf16[24,6,256]{2,1,0:T(8,128)(2,1)S(1)}, u32[]{:S(2)}, u32[]{:S(2)}) collective-permute-start(bf16[24,6,256]{2,1,0:T(8,128)(2,1)S(1)} %get-tuple-element.21), channel_id=1, source_target_pairs={{1,0},{2,1},{3,2},{4,3},{5,4},{6,5},{7,6},{0,7},{9,8},{10,9},{11,1... | collective-permute-start | bytes 221192 | tf_op jit(solution)/shard_map/ppermute | solution.py:88
  37.7 6.9 %collective-permute-start.4 = (bf16[6,36,256]{2,1,0:T(8,128)(2,1)S(1)}, bf16[6,36,256]{2,1,0:T(8,128)(2,1)S(1)}, u32[]{:S(2)}, u32[]{:S(2)}) collective-permute-start(bf16[6,36,256]{2,1,0:T(8,128)(2,1)S(1)} %get-tuple-element.18), channel_id=1, source_target_pairs={{0,8},{8,16},{16,24},{1,9},{9,17},{17,25},{2,10},{10,18},{18,26},{... | collective-permute-start | bytes 331784 | tf_op jit(solution)/shard_map/ppermute | solution.py:87
  41.2 7.6 %collective-permute-start.5 = (bf16[6,36,256]{2,1,0:T(8,128)(2,1)S(1)}, bf16[6,36,256]{2,1,0:T(8,128)(2,1)S(1)}, u32[]{:S(2)}, u32[]{:S(2)}) collective-permute-start(bf16[6,36,256]{2,1,0:T(8,128)(2,1)S(1)} %get-tuple-element.19), channel_id=1, source_target_pairs={{8,0},{16,8},{24,16},{9,1},{17,9},{25,17},{10,2},{18,10},{26,18},{... | collective-permute-start | bytes 331784 | tf_op jit(solution)/shard_map/ppermute | solution.py:88
  56.3 1.2 %copy-start.7 = (bf16[2,256,1024]{2,1,0:T(8,128)(2,1)S(1)}, bf16[2,256,1024]{2,1,0:T(8,128)(2,1)}, u32[]{:S(2)}) copy-start(bf16[2,256,1024]{2,1,0:T(8,128)(2,1)} %param.24) | copy-start | bytes 3145732
  57.5 1.4 %copy-start.8 = (bf16[2,1024,256]{2,1,0:T(8,128)(2,1)S(1)}, bf16[2,1024,256]{2,1,0:T(8,128)(2,1)}, u32[]{:S(2)}) copy-start(bf16[2,1024,256]{2,1,0:T(8,128)(2,1)} %param.25) | copy-start | bytes 3145732

commit v6 on v5

--- a/solution.py
+++ b/solution.py
@@ -13,8 +13,8 @@
 RW = 16
 
 
-def _conv_body(x_ref, w_ref, b_ref, o_ref, wide_ref):
-    oh, ow, ch = o_ref.shape[1], o_ref.shape[2], o_ref.shape[3]
+def _conv_body(x_ref, w_ref, b_ref, high_ref, low_ref, o_ref, wide_ref):
+    oh, ow, ch = x_ref.shape[1] // 2, x_ref.shape[2] // 2, o_ref.shape[2]
     cin = x_ref.shape[3]
     lanes = wide_ref.shape[3]
     parts = wide_ref.shape[0]
@@ -49,26 +49,39 @@
     first_col = lax.broadcasted_iota(jnp.int32, (oh, ow, ch), 1) == 0
     total = total + jnp.where(first_col, 0.0, rolled)
     total = total + b_ref[...]
-    o_ref[0] = jax.nn.gelu(total).astype(o_ref.dtype)
-
-
-def conv_gelu(x, w, b):
+    features = jax.nn.gelu(total).astype(x_ref.dtype).reshape(oh * ow, ch)
+    mixed = jnp.dot(high_ref[0], features, preferred_element_type=jnp.float32) + jnp.dot(
+        low_ref[0], features, preferred_element_type=jnp.float32
+    )
+    o_ref[0] = mixed.astype(o_ref.dtype)
+
+
+def conv_resample(x, w, b, row_mix, col_mix):
     n, h, wd, cin = x.shape
     cout = w.shape[3]
     oh, ow = h // 2, wd // 2
-    return pl.pallas_call(
+    rb, rw = row_mix.shape[1], col_mix.shape[1]
+    both = (
+        row_mix.astype(jnp.float32)[:, :, None, :, None] * col_mix.astype(jnp.float32)[:, None, :, None, :]
+    ).reshape(n, rb * rw, oh * ow)
+    high = both.astype(x.dtype)
+    low = (both - high.astype(jnp.float32)).astype(x.dtype)
+    out = pl.pallas_call(
         _conv_body,
         grid=(n,),
         in_specs=[
             pl.BlockSpec((1, h, wd, cin), lambda i: (i, 0, 0, 0)),
             pl.BlockSpec((3, 3, cin, cout), lambda i: (0, 0, 0, 0)),
             pl.BlockSpec((1, cout), lambda i: (0, 0)),
+            pl.BlockSpec((1, rb * rw, oh * ow), lambda i: (i, 0, 0)),
+            pl.BlockSpec((1, rb * rw, oh * ow), lambda i: (i, 0, 0)),
         ],
-        out_specs=pl.BlockSpec((1, oh, ow, cout), lambda i: (i, 0, 0, 0)),
-        out_shape=jax.ShapeDtypeStruct((n, oh, ow, cout), jnp.bfloat16),
+        out_specs=pl.BlockSpec((1, rb * rw, cout), lambda i: (i, 0, 0)),
+        out_shape=jax.ShapeDtypeStruct((n, rb * rw, cout), jnp.bfloat16),
         scratch_shapes=[pltpu.VMEM((cin // 128, h, wd, 128), jnp.float32)],
         compiler_params=pltpu.CompilerParams(dimension_semantics=("arbitrary",)),
-    )(x, w, b.reshape(1, cout))
+    )(x, w, b.reshape(1, cout), high, low)
+    return out.reshape(n, rb, rw, cout)
 
 
 def shifted(value, axis, steps):
@@ -88,14 +101,6 @@
         after = lax.ppermute(leading, axis, down)
         value = jnp.concatenate([before, value, after], axis=dim)
     return value
-
-
-def resample_local(blocks, row_mix, col_mix):
-    row_mixed = jnp.einsum("nri,nijc->nrjc", row_mix, blocks, preferred_element_type=jnp.float32)
-    both_mixed = jnp.einsum(
-        "nrjc,nuj->nruc", row_mixed, col_mix.astype(jnp.float32), precision=lax.Precision.HIGHEST
-    )
-    return both_mixed.astype(jnp.bfloat16)
 
 
 def place_rows(onehot, values):
@@ -165,8 +170,7 @@
     tile_cols = background.shape[1]
     channels = background.shape[2]
     bands = lax.axis_size("lat")
-    features = conv_gelu(swath_input, conv_weight, conv_bias)
-    resampled = resample_local(features, row_weights, col_weights)
+    resampled = conv_resample(swath_input, conv_weight, conv_bias, row_weights, col_weights)
     own_band = lax.axis_index("lat")
     offset_band = block_band[:, 0] - own_band
     staying = offset_band == 0

time: 67.2 us -> 79.7 us (1.19)
  local copies, waits for them, and re-layouts: 1.66 us -> 9.27 us
  other arithmetic: 14.8 us -> 21.8 us
  waiting for transfers between devices: 20 us -> 16.2 us
  starting transfers between devices: 14.6 us -> 17.6 us
  matrix products: 9.3 us -> 6.32 us
  Pallas kernels: 6.12 us -> 7.72 us
    mul x0 -> x1, local copies, waits for them, and re-layouts: none -> 6.63 us  [conv_resample(): row_mix.astype(jnp.float32)[:, :, None, :, None]]
    ppermute x2, waiting for transfers between devices: 11.5 us -> 5.29 us  [shifted(): lax.ppermute(value, axis, [(source, source + steps) for source in range(l...]
    mul x0 -> x1, other arithmetic: none -> 4.38 us  [conv_resample(): row_mix.astype(jnp.float32)[:, :, None, :, None]]
    convert_element_type x0 -> x3, other arithmetic: none -> 3.17 us  [the longest x1 1.77 us: conv_resample(): low = (both - high.astype(jnp.float32)).astype(x.dtype)]
    dot_general x2 -> x0, matrix products: 2.99 us -> none  [the longest x1 1.92 us: resample_local(): jnp.einsum('nri,nijc->nrjc', row_mix, blocks, preferred_element_type=jnp....]
    ppermute x2, waiting for transfers between devices: 4.12 us -> 6.48 us  [with_halo(): after = lax.ppermute(leading, axis, down)]
    ppermute x2, starting transfers between devices: 3.46 us -> 5.78 us  [with_halo(): before = lax.ppermute(last, axis, up)]
    pallas_call x1, Pallas kernels: 6.12 us -> 7.72 us  [conv_resample(): pl.pallas_call(_conv_body, grid=(n,), in_specs=[pl.BlockSpec((1, h, wd, c...]
where the time goes in v6:
time: 79.7 us; the launch traced here: 79.3 us
  other arithmetic  21.8 us (27%)
  starting transfers between devices  17.6 us (22%)
  waiting for transfers between devices  16.2 us (20%)
  local copies, waits for them, and re-layouts  9.27 us (12%)
  Pallas kernels  7.72 us (10%)
  matrix products  6.32 us (8%)
    reduce_sum x2, other arithmetic, layer_apply(): centered = mixed - jnp.mean(mixed, axis=-1, keepdims=True)  11.7 us
    pallas_call x1, Pallas kernels, conv_resample(): pl.pallas_call(_conv_body, grid=(n,), in_specs=[pl.BlockSpec((1, h, wd, c...  7.72 us
    ppermute x2, starting transfers between devices, shifted(): lax.ppermute(value, axis, [(source, source + steps) for source in range(l...  6.81 us
    mul x1, local copies, waits for them, and re-layouts, conv_resample(): row_mix.astype(jnp.float32)[:, :, None, :, None]  6.63 us
    ppermute x2, waiting for transfers between devices, with_halo(): after = lax.ppermute(leading, axis, down)  6.48 us
    ppermute x2, starting transfers between devices, with_halo(): before = lax.ppermute(last, axis, up)  5.78 us
    ppermute x2, waiting for transfers between devices, shifted(): lax.ppermute(value, axis, [(source, source + steps) for source in range(l...  5.29 us
    ppermute x2, starting transfers between devices, with_halo(): after = lax.ppermute(leading, axis, down)  5 us
  transfers between devices with their start and end apart: 6, of which 5 were waited for; matrix products, arithmetic and copies ran while one was open for 1% of the time, Pallas kernels for 0%

profile of v6, /device:TPU:0, one launch (start us, length us, event | category | flops | bytes accessed | tf_op | source)
XLA Modules:
  0.0 79.3 jit_solution(8919281853978162932)
XLA Ops:
  0.0 0.7 convert_element_type.94
  0.7 0.7 convert_element_type.95
  1.4 4.4 %broadcast_multiply_fusion = f32[2,16,16,32,32]{4,3,2,1,0:T(8,128)} fusion(f32[2,16,32]{2,1,0:T(8,128)S(1)} %convert_element_type.95, f32[2,16,32]{2,1,0:T(8,128)S(1)} %convert_element_type.94), kind=kLoop, calls=%fused_computation.3 | loop fusion | flops 524288 | bytes 2105344 | tf_op jit(solution)/shard_map/mul | solution.py:65
  5.8 6.6 %mul.1088 = f32[2,256,1024]{2,1,0:T(8,128)S(1)} reshape(f32[2,16,16,32,32]{4,3,2,1,0:T(8,128)} %broadcast_multiply_fusion) | data formatting | bytes 4194304 | tf_op jit(solution)/shard_map/mul | solution.py:65
  12.4 1.8 %subtract_convert_fusion = (bf16[2,256,1024]{2,1,0:T(8,128)(2,1)}, bf16[2,256,1024]{2,1,0:T(8,128)(2,1)}) fusion(f32[2,256,1024]{2,1,0:T(8,128)S(1)} %mul.1088), kind=kLoop, calls=%fused_computation.21 | loop fusion | flops 2097152 | bytes 4194304 | tf_op jit(solution)/shard_map/convert_element_type | solution.py:68
  14.2 7.7 %shard_map.127 = bf16[2,256,256]{2,1,0:T(8,128)(2,1)} custom-call(bf16[2,64,64,256]{3,2,1,0:T(8,128)(2,1)} %x_ref.1, bf16[3,3,256,256]{3,2,1,0:T(8,128)(2,1)} %w_ref.1, f32[1,256]{1,0:T(1,128)} %bitcast.282, bf16[2,256,1024]{2,1,0:T(8,128)(2,1)} %get-tuple-element.18.high_ref, bf16[2,256,1024]{2,1,0:T(8,128)(2,1)} %get-tuple-element.17.low_ref), custom_call_target="tpu_custom_call" | custom-call | tf_op jit(solution)/shard_map/pallas_call | solution.py:69
  21.9 1.3 %copy.40 = bf16[1,2,256,256]{3,1,2,0:T(2,128)(2,1)S(1)} copy(bf16[1,2,256,256]{3,2,1,0:T(8,128)(2,1)} %bitcast.170) | data formatting | bytes 524288
  23.2 0.1 fusion.140
  23.4 0.2 select_reduce_fusion.2
  23.5 0.4 convolution_convert_fusion
  24.0 0.1 select_convert_fusion.1
  24.1 1.3 %collective-permute-start.1 = (bf16[2,17,16,256]{3,2,1,0:T(8,128)(2,1)S(1)}, bf16[2,17,16,256]{3,2,1,0:T(8,128)(2,1)S(1)}, u32[]{:S(2)}, u32[]{:S(2)}) collective-permute-start(bf16[2,17,16,256]{3,2,1,0:T(8,128)(2,1)S(1)} %pad_maximum_fusion.2), channel_id=1, source_target_pairs={{8,0},{16,8},{24,16},{9,1},{17,9},{25,17},{10,2},{18,10},{26,18},{... | collective-permute-start | bytes 835592 | tf_op jit(solution)/shard_map/ppermute | solution.py:90
  25.4 0.4 convolution_convert_fusion.1
  25.9 5.5 %collective-permute-start = (bf16[2,17,16,256]{3,2,1,0:T(8,128)(2,1)S(1)}, bf16[2,17,16,256]{3,2,1,0:T(8,128)(2,1)S(1)}, u32[]{:S(2)}, u32[]{:S(2)}) collective-permute-start(bf16[2,17,16,256]{3,2,1,0:T(8,128)(2,1)S(1)} %pad_maximum_fusion.1), channel_id=1, source_target_pairs={{0,8},{8,16},{16,24},{1,9},{9,17},{17,25},{2,10},{10,18},{18,26},{... | collective-permute-start | bytes 835592 | tf_op jit(solution)/shard_map/ppermute | solution.py:90
  31.5 0.1 fusion.147
  31.8 0.1 broadcast_select_fusion
  31.9 4.6 %collective-permute-done.1 = bf16[2,17,16,256]{3,2,1,0:T(8,128)(2,1)S(1)} collective-permute-done((bf16[2,17,16,256]{3,2,1,0:T(8,128)(2,1)S(1)}, bf16[2,17,16,256]{3,2,1,0:T(8,128)(2,1)S(1)}, u32[]{:S(2)}, u32[]{:S(2)}) %collective-permute-start.1) | collective-permute-done | bytes 278560 | tf_op jit(solution)/shard_map/ppermute | solution.py:90
  36.5 0.2 slice_reduce_fusion
  36.7 0.6 collective-permute-done
  37.4 0.2 slice_reduce_fusion.1
  37.5 0.1 pad_add_fusion
  37.6 0.1 iota_add_fusion.1
  37.7 0.1 pad_add_fusion.1
  37.8 0.1 iota_add_fusion
  37.9 0.1 pad_maximum_fusion
  38.0 0.8 %convolution_convert_fusion.2 = bf16[6,24,16,256]{3,1,2,0:T(8,128)(2,1)S(1)} fusion(bf16[6,16,16,256]{3,2,1,0:T(8,128)(2,1)S(1)} %pad_maximum_fusion, s32[6,16]{1,0:T(8,128)S(1)} %iota_add_fusion.1), kind=kOutput, calls=%fused_computation.22 | convolution fusion | flops 19466496 | bytes 1966464 | tf_op jit(solution)/shard_map/shr,sruc->shuc/dot_general | solution.py:210
  38.9 0.4 fusion.17
  39.4 3.5 %collective-permute-start.3 = (bf16[24,6,256]{2,1,0:T(8,128)(2,1)S(1)}, bf16[24,6,256]{2,1,0:T(8,128)(2,1)S(1)}, u32[]{:S(2)}, u32[]{:S(2)}) collective-permute-start(bf16[24,6,256]{2,1,0:T(8,128)(2,1)S(1)} %get-tuple-element.23), channel_id=1, source_target_pairs={{1,0},{2,1},{3,2},{4,3},{5,4},{6,5},{7,6},{0,7},{9,8},{10,9},{11,1... | collective-permute-start | bytes 221192 | tf_op jit(solution)/shard_map/ppermute | solution.py:101
  42.9 2.4 %collective-permute-done.2 = bf16[24,6,256]{2,1,0:T(8,128)(2,1)S(1)} collective-permute-done((bf16[24,6,256]{2,1,0:T(8,128)(2,1)S(1)}, bf16[24,6,256]{2,1,0:T(8,128)(2,1)S(1)}, u32[]{:S(2)}, u32[]{:S(2)}) %collective-permute-start.2) | collective-permute-done | bytes 73760 | tf_op jit(solution)/shard_map/ppermute | solution.py:100
  45.3 0.1 pad_maximum_fusion.5
  45.4 5.7 %collective-permute-start.4 = (bf16[6,36,256]{2,1,0:T(8,128)(2,1)S(1)}, bf16[6,36,256]{2,1,0:T(8,128)(2,1)S(1)}, u32[]{:S(2)}, u32[]{:S(2)}) collective-permute-start(bf16[6,36,256]{2,1,0:T(8,128)(2,1)S(1)} %get-tuple-element.20), channel_id=1, source_target_pairs={{0,8},{8,16},{16,24},{1,9},{9,17},{17,25},{2,10},{10,18},{18,26},{... | collective-permute-start | bytes 331784 | tf_op jit(solution)/shard_map/ppermute | solution.py:100
  51.1 1.5 %collective-permute-start.5 = (bf16[6,36,256]{2,1,0:T(8,128)(2,1)S(1)}, bf16[6,36,256]{2,1,0:T(8,128)(2,1)S(1)}, u32[]{:S(2)}, u32[]{:S(2)}) collective-permute-start(bf16[6,36,256]{2,1,0:T(8,128)(2,1)S(1)} %get-tuple-element.21), channel_id=1, source_target_pairs={{8,0},{16,8},{24,16},{9,1},{17,9},{25,17},{10,2},{18,10},{26,18},{... | collective-permute-start | bytes 331784 | tf_op jit(solution)/shard_map/ppermute | solution.py:101
  52.6 2.0 %collective-permute-done.4 = bf16[6,36,256]{2,1,0:T(8,128)(2,1)S(1)} collective-permute-done((bf16[6,36,256]{2,1,0:T(8,128)(2,1)S(1)}, bf16[6,36,256]{2,1,0:T(8,128)(2,1)S(1)}, u32[]{:S(2)}, u32[]{:S(2)}) %collective-permute-start.4) | collective-permute-done | bytes 110624 | tf_op jit(solution)/shard_map/ppermute | solution.py:100
  54.6 6.5 %collective-permute-done.5 = bf16[6,36,256]{2,1,0:T(8,128)(2,1)S(1)} collective-permute-done((bf16[6,36,256]{2,1,0:T(8,128)(2,1)S(1)}, bf16[6,36,256]{2,1,0:T(8,128)(2,1)S(1)}, u32[]{:S(2)}, u32[]{:S(2)}) %collective-permute-start.5) | collective-permute-done | bytes 110624 | tf_op jit(solution)/shard_map/ppermute | solution.py:101
  61.1 0.2 maximum_convert_fusion
  61.2 0.1 slice.998
  61.4 7.2 %fusion.144 = (f32[30,32]{1,0:T(8,128)S(1)}, f32[30,32,256]{2,1,0:T(8,128)S(1)}) fusion(f32[256]{0:T(256)S(1)} %bitcast.183, f32[256]{0:T(256)S(1)} %bitcast.184, f32[256]{0:T(256)S(1)} %bitcast.185, f32[256]{0:T(256)S(1)} %bitcast.186, f32[256]{0:T(256)S(1)} %bitcast.187, f32[256]{0:T(256)S(1)} %bitcast.188, f32[256]{0:T(256)S(1)} %bitcast.189, ...), kind=kLoop, calls=%fused_computation.288 | loop fusion | flops 24083520 | bytes 36918016 | tf_op jit(solution)/shard_map/reduce_sum | solution.py:139
  68.6 0.4 multiply_reduce_fusion
  69.0 0.3 multiply_convert_fusion
  69.3 0.5 copy-done.7
  69.8 1.4 %fusion.7 = bf16[960,1024]{1,0:T(8,128)(2,1)S(1)} fusion(bf16[960,256]{1,0:T(8,128)(2,1)S(1)} %bitcast.174, bf16[2,256,1024]{2,1,0:T(8,128)(2,1)S(1)} %copy-done.7), kind=kOutput, calls=%fused_computation.11 | convolution fusion | flops 512163840 | bytes 2981888 | tf_op jit(solution)/shard_map/dot_general | solution.py:143
  71.3 0.7 fusion.125
  71.9 0.2 fusion.133
  72.1 4.4 %fusion.142 = (f32[24,24]{1,0:T(8,128)S(1)}, f32[24,24,256]{2,1,0:T(8,128)S(1)}) fusion(f32[256]{0:T(256)S(1)} %bitcast.232, f32[30,30,256]{2,1,0:T(8,128)S(1)} %fusion.133, f32[256]{0:T(256)S(1)} %bitcast.233, f32[256]{0:T(256)S(1)} %bitcast.234, f32[256]{0:T(256)S(1)} %bitcast.235, f32[256]{0:T(256)S(1)} %bitcast.236, f32[256]{0:T(256)S(1)} %bitcast.237, ...), kind=kLoop, calls=%fused_computation.287 | loop fusion | flops 14450112 | bytes 29543680 | tf_op jit(solution)/shard_map/reduce_sum | solution.py:139
  76.6 0.3 multiply_reduce_fusion.1
  76.9 0.2 multiply_convert_fusion.1
  77.1 0.9 %fusion.15 = bf16[576,1024]{1,0:T(8,128)(2,1)S(1)} fusion(bf16[576,256]{1,0:T(8,128)(2,1)S(1)} %bitcast.175, bf16[2,256,1024]{2,1,0:T(8,128)(2,1)S(1)} %copy-done.7), kind=kOutput, calls=%fused_computation.20 | convolution fusion | flops 307298304 | bytes 1998848 | tf_op jit(solution)/shard_map/dot_general | solution.py:143
  78.1 1.2 %fusion.18 = bf16[24,24,256]{2,1,0:T(8,128)(2,1)} fusion(bf16[24,24,1024]{2,1,0:T(8,128)(2,1)S(1)} %bitcast.284, f32[30,30,256]{2,1,0:T(8,128)S(1)} %fusion.133, bf16[2,1024,256]{2,1,0:T(8,128)(2,1)S(1)} %copy-done.8), kind=kOutput, calls=%fused_computation.27 | convolution fusion | flops 302284800 | bytes 2588672 | tf_op jit(solution)/shard_map/dot_general | solution.py:146
  (47 shorter events, 0.5 us)
Async XLA Ops:
  14.2 9.0 %copy-start.6 = (s32[2,1]{0,1:T(1,128)S(1)}, s32[2,1]{0,1:T(1,128)}, u32[]{:S(2)}) copy-start(s32[2,1]{0,1:T(1,128)} %param.16) | copy-start | bytes 28
  14.2 9.2 %copy-start.4 = (s32[2]{0:T(128)S(1)}, s32[2]{0:T(128)}, u32[]{:S(2)}) copy-start(s32[2]{0:T(128)} %param.17) | copy-start | bytes 28
  14.2 9.2 %copy-start.5 = (s32[2]{0:T(128)S(1)}, s32[2]{0:T(128)}, u32[]{:S(2)}) copy-start(s32[2]{0:T(128)} %param.18) | copy-start | bytes 28
  21.9 9.5 %copy-start.2 = (f32[2,7,7,256]{3,0,2,1:T(2,128)S(1)}, f32[2,7,7,256]{3,0,2,1:T(2,128)}, u32[]{:S(2)}) copy-start(f32[2,7,7,256]{3,0,2,1:T(2,128)} %param.22) | copy-start | bytes 301060
  23.5 8.2 %copy-start = (bf16[2,256,256]{2,1,0:T(8,128)(2,1)S(1)}, bf16[2,256,256]{2,1,0:T(8,128)(2,1)}, u32[]{:S(2)}) copy-start(bf16[2,256,256]{2,1,0:T(8,128)(2,1)} %shard_map.127) | copy-start | bytes 786436
  24.1 12.4 %collective-permute-start.1 = (bf16[2,17,16,256]{3,2,1,0:T(8,128)(2,1)S(1)}, bf16[2,17,16,256]{3,2,1,0:T(8,128)(2,1)S(1)}, u32[]{:S(2)}, u32[]{:S(2)}) collective-permute-start(bf16[2,17,16,256]{3,2,1,0:T(8,128)(2,1)S(1)} %pad_maximum_fusion.2), channel_id=1, source_target_pairs={{8,0},{16,8},{24,16},{9,1},{17,9},{25,17},{10,2},{18,10},{26,18},{... | collective-permute-start | bytes 835592 | tf_op jit(solution)/shard_map/ppermute | solution.py:90
  25.9 11.4 %collective-permute-start = (bf16[2,17,16,256]{3,2,1,0:T(8,128)(2,1)S(1)}, bf16[2,17,16,256]{3,2,1,0:T(8,128)(2,1)S(1)}, u32[]{:S(2)}, u32[]{:S(2)}) collective-permute-start(bf16[2,17,16,256]{3,2,1,0:T(8,128)(2,1)S(1)} %pad_maximum_fusion.1), channel_id=1, source_target_pairs={{0,8},{8,16},{16,24},{1,9},{9,17},{17,25},{2,10},{10,18},{18,26},{... | collective-permute-start | bytes 835592 | tf_op jit(solution)/shard_map/ppermute | solution.py:90
  31.8 7.0 %copy-start.1 = (bf16[24,24,256]{2,1,0:T(8,128)(2,1)S(1)}, bf16[24,24,256]{2,1,0:T(8,128)(2,1)}, u32[]{:S(2)}) copy-start(bf16[24,24,256]{2,1,0:T(8,128)(2,1)} %param.21) | copy-start | bytes 884740
  38.0 4.9 %copy-start.3 = (f32[2,256]{1,0:T(2,128)S(1)}, f32[2,256]{1,0:T(2,128)}, u32[]{:S(2)}) copy-start(f32[2,256]{1,0:T(2,128)} %param.23) | copy-start | bytes 6148
  39.3 6.0 %collective-permute-start.2 = (bf16[24,6,256]{2,1,0:T(8,128)(2,1)S(1)}, bf16[24,6,256]{2,1,0:T(8,128)(2,1)S(1)}, u32[]{:S(2)}, u32[]{:S(2)}) collective-permute-start(bf16[24,6,256]{2,1,0:T(8,128)(2,1)S(1)} %get-tuple-element.22), channel_id=1, source_target_pairs={{0,1},{1,2},{2,3},{3,4},{4,5},{5,6},{6,7},{7,0},{8,9},{9,10},{10,1... | collective-permute-start | bytes 221192 | tf_op jit(solution)/shard_map/ppermute | solution.py:100
  39.4 5.9 %collective-permute-start.3 = (bf16[24,6,256]{2,1,0:T(8,128)(2,1)S(1)}, bf16[24,6,256]{2,1,0:T(8,128)(2,1)S(1)}, u32[]{:S(2)}, u32[]{:S(2)}) collective-permute-start(bf16[24,6,256]{2,1,0:T(8,128)(2,1)S(1)} %get-tuple-element.23), channel_id=1, source_target_pairs={{1,0},{2,1},{3,2},{4,3},{5,4},{6,5},{7,6},{0,7},{9,8},{10,9},{11,1... | collective-permute-start | bytes 221192 | tf_op jit(solution)/shard_map/ppermute | solution.py:101
  45.4 9.2 %collective-permute-start.4 = (bf16[6,36,256]{2,1,0:T(8,128)(2,1)S(1)}, bf16[6,36,256]{2,1,0:T(8,128)(2,1)S(1)}, u32[]{:S(2)}, u32[]{:S(2)}) collective-permute-start(bf16[6,36,256]{2,1,0:T(8,128)(2,1)S(1)} %get-tuple-element.20), channel_id=1, source_target_pairs={{0,8},{8,16},{16,24},{1,9},{9,17},{17,25},{2,10},{10,18},{18,26},{... | collective-permute-start | bytes 331784 | tf_op jit(solution)/shard_map/ppermute | solution.py:100
  51.1 10.0 %collective-permute-start.5 = (bf16[6,36,256]{2,1,0:T(8,128)(2,1)S(1)}, bf16[6,36,256]{2,1,0:T(8,128)(2,1)S(1)}, u32[]{:S(2)}, u32[]{:S(2)}) collective-permute-start(bf16[6,36,256]{2,1,0:T(8,128)(2,1)S(1)} %get-tuple-element.21), channel_id=1, source_target_pairs={{8,0},{16,8},{24,16},{9,1},{17,9},{25,17},{10,2},{18,10},{26,18},{... | collective-permute-start | bytes 331784 | tf_op jit(solution)/shard_map/ppermute | solution.py:101
  68.6 1.2 %copy-start.7 = (bf16[2,256,1024]{2,1,0:T(8,128)(2,1)S(1)}, bf16[2,256,1024]{2,1,0:T(8,128)(2,1)}, u32[]{:S(2)}) copy-start(bf16[2,256,1024]{2,1,0:T(8,128)(2,1)} %param.24) | copy-start | bytes 3145732
  69.8 1.4 %copy-start.8 = (bf16[2,1024,256]{2,1,0:T(8,128)(2,1)S(1)}, bf16[2,1024,256]{2,1,0:T(8,128)(2,1)}, u32[]{:S(2)}) copy-start(bf16[2,1024,256]{2,1,0:T(8,128)(2,1)} %param.25) | copy-start | bytes 3145732

commit v7 on v5

--- a/solution.py
+++ b/solution.py
@@ -209,10 +209,28 @@
     summed = jnp.einsum("swu,shuc->hwc", col_place, lifted, preferred_element_type=jnp.float32)
     state = (background.astype(jnp.float32) + summed).astype(jnp.bfloat16)
     reach = HALO * LAYERS
-    widened = with_halo(state, (("lon", 1),), reach, True)
-    widened = with_halo(widened, (("lat", 0),), reach, False)
+    lon_wide = with_halo(state, (("lon", 1),), reach, True)
+    size, length = lax.axis_size("lat"), lon_wide.shape[0]
+    up = [(i, i + 1) for i in range(size - 1)]
+    down = [(j, i) for i, j in up]
+    north = lax.ppermute(lon_wide[length - reach :], "lat", up)
+    south = lax.ppermute(lon_wide[:reach], "lat", down)
+    first = (
+        depth_weight[0],
+        norm_gain[0],
+        up_weight[0],
+        down_weight[0],
+    )
+    middle = layer_apply(lon_wide, *first)
+    top = layer_apply(jnp.concatenate([north, lon_wide[:reach]], axis=0), *first)
+    bottom = layer_apply(jnp.concatenate([lon_wide[length - reach :], south], axis=0), *first)
+    widened = jnp.concatenate([top, middle, bottom], axis=0)
     first_row = own_band * tile_rows
-    for layer_index in range(LAYERS):
+    margin = (widened.shape[0] - tile_rows) // 2
+    grid_row = first_row - margin + jnp.arange(widened.shape[0], dtype=jnp.int32)
+    inside = (grid_row >= 0) & (grid_row < bands * tile_rows)
+    widened = jnp.where(inside[:, None, None], widened, jnp.zeros_like(widened))
+    for layer_index in range(1, LAYERS):
         widened = layer_apply(
             widened,
             depth_weight[layer_index],
@@ -220,11 +238,6 @@
             up_weight[layer_index],
             down_weight[layer_index],
         )
-        margin = (widened.shape[0] - tile_rows) // 2
-        if margin:
-            grid_row = first_row - margin + jnp.arange(widened.shape[0], dtype=jnp.int32)
-            inside = (grid_row >= 0) & (grid_row < bands * tile_rows)
-            widened = jnp.where(inside[:, None, None], widened, jnp.zeros_like(widened))
     return widened
 
 

time: 67.2 us -> 62.2 us (0.926)
  waiting for transfers between devices: 20 us -> 13.9 us
  matrix products: 9.3 us -> 10 us
    ppermute x0 -> x2, starting transfers between devices: none -> 4.88 us  [the longest x1 3.4 us: per_device(): north = lax.ppermute(lon_wide[length - reach:], 'lat', up)]
    ppermute x2 -> x1, waiting for transfers between devices: 4.12 us -> 0.01 us  [with_halo(): after = lax.ppermute(leading, axis, down)]
    ppermute x2 -> x1, starting transfers between devices: 3.46 us -> 0.06 us  [with_halo(): before = lax.ppermute(last, axis, up)]
    ppermute x2 -> x1, waiting for transfers between devices: 4.38 us -> 2.39 us  [with_halo(): before = lax.ppermute(last, axis, up)]
    ppermute x2 -> x1, starting transfers between devices: 5 us -> 3.53 us  [with_halo(): after = lax.ppermute(leading, axis, down)]
    dot_general x2 -> x4, matrix products: 1.89 us -> 2.25 us  [layer_apply(): jnp.dot(hidden, down_matrix, preferred_element_type=jnp.float32)]
    dot_general x2 -> x4, matrix products: 2.36 us -> 2.7 us  [layer_apply(): jnp.dot(flat_cells, up_matrix, preferred_element_type=jnp.float32)]
    reduce_sum x2 -> x4, other arithmetic: 11.6 us -> 11.6 us  [layer_apply(): centered = mixed - jnp.mean(mixed, axis=-1, keepdims=True)]
  transfers between devices with their start and end apart: 6 -> 6, of which waited for: 5 -> 3; matrix products, arithmetic and copies ran while one was open for 1% -> 14% of each run, Pallas kernels for 0% -> 0%
where the time goes in v7:
time: 62.2 us; the launch traced here: 61.9 us
  other arithmetic  15.2 us (24%)
  starting transfers between devices  14.6 us (23%)
  waiting for transfers between devices  13.9 us (22%)
  matrix products  10 us (16%)
  Pallas kernels  6.12 us (10%)
  local copies, waits for them, and re-layouts  1.44 us (2%)
    reduce_sum x4, other arithmetic, layer_apply(): centered = mixed - jnp.mean(mixed, axis=-1, keepdims=True)  11.6 us
    ppermute x2, waiting for transfers between devices, shifted(): lax.ppermute(value, axis, [(source, source + steps) for source in range(l...  11.5 us
    ppermute x2, starting transfers between devices, shifted(): lax.ppermute(value, axis, [(source, source + steps) for source in range(l...  6.18 us
    pallas_call x1, Pallas kernels, conv_gelu(): pl.pallas_call(_conv_body, grid=(n,), in_specs=[pl.BlockSpec((1, h, wd, c...  6.12 us
    ppermute x1, starting transfers between devices, with_halo(): after = lax.ppermute(leading, axis, down)  3.53 us
    ppermute x1, starting transfers between devices, per_device(): north = lax.ppermute(lon_wide[length - reach:], 'lat', up)  3.4 us
    dot_general x4, matrix products, layer_apply(): jnp.dot(flat_cells, up_matrix, preferred_element_type=jnp.float32)  2.7 us
    ppermute x1, waiting for transfers between devices, with_halo(): before = lax.ppermute(last, axis, up)  2.39 us
  transfers between devices with their start and end apart: 6, of which 3 were waited for; matrix products, arithmetic and copies ran while one was open for 14% of the time, Pallas kernels for 0%

profile of v7, /device:TPU:0, one launch (start us, length us, event | category | flops | bytes accessed | tf_op | source)
XLA Modules:
  0.0 61.9 jit_solution(9348074145523555771)
XLA Ops:
  0.0 0.7 %compare_bitcast_fusion = (pred[2]{0:T(512)(128)(4,1)S(1)}, pred[2]{0:T(512)(128)(4,1)S(1)}, pred[2]{0:T(512)(128)(4,1)S(1)}) fusion(s32[2,1]{0,1:T(1,128)} %param.16, s32[]{:T(128)S(6)} %axis_index.15), kind=kLoop, calls=%fused_computation.514 | loop fusion | flops 8 | bytes 18 | tf_op jit(solution)/shard_map/eq | solution.py:172
  0.7 6.1 %shard_map.127 = bf16[2,32,32,256]{3,2,1,0:T(8,128)(2,1)} custom-call(bf16[2,64,64,256]{3,2,1,0:T(8,128)(2,1)} %x_ref.1, bf16[3,3,256,256]{3,2,1,0:T(8,128)(2,1)} %w_ref.1, f32[1,256]{1,0:T(1,128)} %bitcast.418), custom_call_target="tpu_custom_call" | custom-call | tf_op jit(solution)/shard_map/pallas_call | solution.py:59
  6.8 1.9 %convolution_bitcast_fusion = f32[2,16,32,256]{3,1,2,0:T(8,128)S(1)} fusion(bf16[2,32,32,256]{3,2,1,0:T(8,128)(2,1)} %shard_map.127, bf16[2,16,32]{2,1,0:T(8,128)(2,1)S(1)} %copy-done), kind=kOutput, calls=%fused_computation.21 | convolution fusion | flops 16777216 | bytes 2099200 | tf_op jit(solution)/shard_map/nri,nijc->nrjc/dot_general | solution.py:94
  8.7 1.1 %bitcast_select_fusion = (bf16[2,16,16,256]{3,2,1,0:T(8,128)(2,1)S(1)}, bf16[2,16,256,16]{2,3,1,0:T(8,128)(2,1)S(1)}) fusion(pred[2]{0:T(512)(128)(4,1)S(1)} %get-tuple-element.134, bf16[2,16,32]{2,1,0:T(8,128)(2,1)S(1)} %copy-done.4, f32[2,16,32,256]{3,1,2,0:T(8,128)S(1)} %convolution_bitcast_fusion), kind=kOutput, calls=%fused_computation.273 | convolution fusion | flops 50593792 | bytes 1574914 | tf_op jit(solution)/shard_map/nrjc,nuj->nruc/dot_general | solution.py:95
  9.8 0.3 copy.30
  10.1 0.1 fusion.294
  10.3 0.4 convolution_convert_fusion.1
  10.8 0.2 select_reduce_fusion.2
  10.9 0.1 select_convert_fusion.1
  11.0 4.9 %collective-permute-start = (bf16[2,17,16,256]{3,2,1,0:T(8,128)(2,1)S(1)}, bf16[2,17,16,256]{3,2,1,0:T(8,128)(2,1)S(1)}, u32[]{:S(2)}, u32[]{:S(2)}) collective-permute-start(bf16[2,17,16,256]{3,2,1,0:T(8,128)(2,1)S(1)} %pad_maximum_fusion.2), channel_id=1, source_target_pairs={{0,8},{8,16},{16,24},{1,9},{9,17},{17,25},{2,10},{10,18},{18,26},{... | collective-permute-start | bytes 835592 | tf_op jit(solution)/shard_map/ppermute | solution.py:77
  15.9 0.4 convolution_convert_fusion
  16.4 1.3 %collective-permute-start.1 = (bf16[2,17,16,256]{3,2,1,0:T(8,128)(2,1)S(1)}, bf16[2,17,16,256]{3,2,1,0:T(8,128)(2,1)S(1)}, u32[]{:S(2)}, u32[]{:S(2)}) collective-permute-start(bf16[2,17,16,256]{3,2,1,0:T(8,128)(2,1)S(1)} %pad_maximum_fusion.3), channel_id=1, source_target_pairs={{8,0},{16,8},{24,16},{9,1},{17,9},{25,17},{10,2},{18,10},{26,18},{... | collective-permute-start | bytes 835592 | tf_op jit(solution)/shard_map/ppermute | solution.py:77
  17.7 0.1 fusion.307
  18.1 3.8 %collective-permute-done = bf16[2,17,16,256]{3,2,1,0:T(8,128)(2,1)S(1)} collective-permute-done((bf16[2,17,16,256]{3,2,1,0:T(8,128)(2,1)S(1)}, bf16[2,17,16,256]{3,2,1,0:T(8,128)(2,1)S(1)}, u32[]{:S(2)}, u32[]{:S(2)}) %collective-permute-start) | collective-permute-done | bytes 278560 | tf_op jit(solution)/shard_map/ppermute | solution.py:77
  21.8 0.2 slice_reduce_fusion.1
  22.0 7.7 %collective-permute-done.1 = bf16[2,17,16,256]{3,2,1,0:T(8,128)(2,1)S(1)} collective-permute-done((bf16[2,17,16,256]{3,2,1,0:T(8,128)(2,1)S(1)}, bf16[2,17,16,256]{3,2,1,0:T(8,128)(2,1)S(1)}, u32[]{:S(2)}, u32[]{:S(2)}) %collective-permute-start.1) | collective-permute-done | bytes 278560 | tf_op jit(solution)/shard_map/ppermute | solution.py:77
  29.7 0.2 slice_reduce_fusion
  29.9 0.1 pad_add_fusion
  30.3 0.1 pad_maximum_fusion
  30.4 0.8 %convolution_convert_fusion.2 = bf16[6,24,16,256]{3,1,2,0:T(8,128)(2,1)S(1)} fusion(bf16[6,16,16,256]{3,2,1,0:T(8,128)(2,1)S(1)} %pad_maximum_fusion, s32[6,16]{1,0:T(8,128)S(1)} %iota_add_fusion.1), kind=kOutput, calls=%fused_computation.20 | convolution fusion | flops 19466496 | bytes 1966464 | tf_op jit(solution)/shard_map/shr,sruc->shuc/dot_general | solution.py:206
  31.2 0.4 fusion.17
  31.7 3.5 %collective-permute-start.3 = (bf16[24,6,256]{2,1,0:T(8,128)(2,1)S(1)}, bf16[24,6,256]{2,1,0:T(8,128)(2,1)S(1)}, u32[]{:S(2)}, u32[]{:S(2)}) collective-permute-start(bf16[24,6,256]{2,1,0:T(8,128)(2,1)S(1)} %get-tuple-element.27), channel_id=1, source_target_pairs={{1,0},{2,1},{3,2},{4,3},{5,4},{6,5},{7,6},{0,7},{9,8},{10,9},{11,1... | collective-permute-start | bytes 221192 | tf_op jit(solution)/shard_map/ppermute | solution.py:88
  35.3 2.4 %collective-permute-done.2 = bf16[24,6,256]{2,1,0:T(8,128)(2,1)S(1)} collective-permute-done((bf16[24,6,256]{2,1,0:T(8,128)(2,1)S(1)}, bf16[24,6,256]{2,1,0:T(8,128)(2,1)S(1)}, u32[]{:S(2)}, u32[]{:S(2)}) %collective-permute-start.2) | collective-permute-done | bytes 73760 | tf_op jit(solution)/shard_map/ppermute | solution.py:87
  37.6 0.2 fusion.296
  37.9 3.4 %collective-permute-start.4 = (bf16[6,36,256]{2,1,0:T(8,128)(2,1)S(1)}, bf16[6,36,256]{2,1,0:T(8,128)(2,1)S(1)}, u32[]{:S(2)}, u32[]{:S(2)}) collective-permute-start(bf16[6,36,256]{2,1,0:T(8,128)(2,1)S(1)} %get-tuple-element.24), channel_id=1, source_target_pairs={{0,8},{8,16},{16,24},{1,9},{9,17},{17,25},{2,10},{10,18},{18,26},{... | collective-permute-start | bytes 331784 | tf_op jit(solution)/shard_map/ppermute | solution.py:216
  41.3 1.5 %collective-permute-start.5 = (bf16[6,36,256]{2,1,0:T(8,128)(2,1)S(1)}, bf16[6,36,256]{2,1,0:T(8,128)(2,1)S(1)}, u32[]{:S(2)}, u32[]{:S(2)}) collective-permute-start(bf16[6,36,256]{2,1,0:T(8,128)(2,1)S(1)} %get-tuple-element.25), channel_id=1, source_target_pairs={{8,0},{16,8},{24,16},{9,1},{17,9},{25,17},{10,2},{18,10},{26,18},{... | collective-permute-start | bytes 331784 | tf_op jit(solution)/shard_map/ppermute | solution.py:217
  42.8 4.4 %fusion.301 = (f32[18,32]{1,0:T(8,128)S(1)}, f32[18,32,256]{2,1,0:T(8,128)S(1)}) fusion(f32[256]{0:T(256)S(1)} %bitcast.310, f32[256]{0:T(256)S(1)} %bitcast.313, f32[256]{0:T(256)S(1)} %bitcast.316, f32[256]{0:T(256)S(1)} %bitcast.319, f32[256]{0:T(256)S(1)} %bitcast.322, f32[256]{0:T(256)S(1)} %bitcast.325, f32[256]{0:T(256)S(1)} %bitcast.328, ...), kind=kLoop, calls=%fused_computation.541 | loop fusion | flops 14450112 | bytes 22269184 | tf_op jit(solution)/shard_map/reduce_sum | solution.py:134
  47.3 0.3 multiply_reduce_fusion.1
  47.6 0.2 multiply_convert_fusion.1
  47.8 0.9 %fusion.7 = bf16[576,1024]{1,0:T(8,128)(2,1)S(1)} fusion(bf16[576,256]{1,0:T(8,128)(2,1)S(1)} %bitcast.210, bf16[2,256,1024]{2,1,0:T(8,128)(2,1)S(1)} %copy-done.8), kind=kOutput, calls=%fused_computation.11 | convolution fusion | flops 307298304 | bytes 1998848 | tf_op jit(solution)/shard_map/dot_general | solution.py:138
  48.7 0.3 copy-done.1
  49.0 0.5 fusion.146
  49.5 0.1 fusion.87
  49.7 1.4 %fusion.303 = (f32[6,32]{1,0:T(8,128)S(1)}, f32[6,32,256]{2,1,0:T(8,128)S(1)}) fusion(f32[256]{0:T(256)S(1)} %bitcast.311, f32[256]{0:T(256)S(1)} %bitcast.314, f32[256]{0:T(256)S(1)} %bitcast.317, f32[256]{0:T(256)S(1)} %bitcast.320, f32[256]{0:T(256)S(1)} %bitcast.323, f32[256]{0:T(256)S(1)} %bitcast.326, f32[256]{0:T(256)S(1)} %bitcast.329, ...), kind=kLoop, calls=%fused_computation.542 | loop fusion | flops 4816704 | bytes 7620352 | tf_op jit(solution)/shard_map/reduce_sum | solution.py:134
  51.2 1.4 %fusion.299 = (f32[6,32]{1,0:T(8,128)S(1)}, f32[6,32,256]{2,1,0:T(8,128)S(1)}) fusion(f32[256]{0:T(256)S(1)} %bitcast.312, f32[256]{0:T(256)S(1)} %bitcast.315, f32[256]{0:T(256)S(1)} %bitcast.318, f32[256]{0:T(256)S(1)} %bitcast.321, f32[256]{0:T(256)S(1)} %bitcast.324, f32[256]{0:T(256)S(1)} %bitcast.327, f32[256]{0:T(256)S(1)} %bitcast.330, ...), kind=kLoop, calls=%fused_computation.540 | loop fusion | flops 4816704 | bytes 7620352 | tf_op jit(solution)/shard_map/reduce_sum | solution.py:134
  52.6 0.2 multiply_reduce_fusion.2
  52.8 0.2 multiply_reduce_fusion.3
  52.9 0.2 multiply_convert_fusion.3
  53.1 0.4 fusion.37
  53.6 0.3 fusion.144
  53.8 0.4 fusion.29
  54.3 0.3 fusion.148
  54.6 0.1 fusion.161
  54.8 4.4 %fusion.297 = (f32[24,24]{1,0:T(8,128)S(1)}, f32[24,24,256]{2,1,0:T(8,128)S(1)}) fusion(f32[256]{0:T(256)S(1)} %bitcast.399, f32[30,30,256]{2,1,0:T(8,128)S(1)} %fusion.161, f32[256]{0:T(256)S(1)} %bitcast.400, f32[256]{0:T(256)S(1)} %bitcast.401, f32[256]{0:T(256)S(1)} %bitcast.402, f32[256]{0:T(256)S(1)} %bitcast.403, f32[256]{0:T(256)S(1)} %bitcast.404, ...), kind=kLoop, calls=%fused_computation.539 | loop fusion | flops 14450112 | bytes 29543680 | tf_op jit(solution)/shard_map/reduce_sum | solution.py:134
  59.2 0.3 multiply_reduce_fusion
  59.5 0.2 multiply_convert_fusion
  59.7 0.9 %fusion.15 = bf16[576,1024]{1,0:T(8,128)(2,1)S(1)} fusion(bf16[576,256]{1,0:T(8,128)(2,1)S(1)} %bitcast.209, bf16[2,256,1024]{2,1,0:T(8,128)(2,1)S(1)} %copy-done.8), kind=kOutput, calls=%fused_computation.19 | convolution fusion | flops 307298304 | bytes 1998848 | tf_op jit(solution)/shard_map/dot_general | solution.py:138
  60.7 1.2 %fusion.18 = bf16[24,24,256]{2,1,0:T(8,128)(2,1)} fusion(bf16[24,24,1024]{2,1,0:T(8,128)(2,1)S(1)} %bitcast.419, f32[30,30,256]{2,1,0:T(8,128)S(1)} %fusion.161, bf16[2,1024,256]{2,1,0:T(8,128)(2,1)S(1)} %copy-done.1), kind=kOutput, calls=%fused_computation.26 | convolution fusion | flops 302284800 | bytes 2588672 | tf_op jit(solution)/shard_map/dot_general | solution.py:141
  (63 shorter events, 1.0 us)
Async XLA Ops:
  0.0 6.8 %copy-start = (bf16[2,16,32]{2,1,0:T(8,128)(2,1)S(1)}, bf16[2,16,32]{2,1,0:T(8,128)(2,1)}, u32[]{:S(2)}) copy-start(bf16[2,16,32]{2,1,0:T(8,128)(2,1)} %param.19) | copy-start | bytes 6148
  0.7 8.1 %copy-start.4 = (bf16[2,16,32]{2,1,0:T(8,128)(2,1)S(1)}, bf16[2,16,32]{2,1,0:T(8,128)(2,1)}, u32[]{:S(2)}) copy-start(bf16[2,16,32]{2,1,0:T(8,128)(2,1)} %param.20) | copy-start | bytes 6148
  6.8 3.9 %copy-start.6 = (s32[2]{0:T(128)S(1)}, s32[2]{0:T(128)}, u32[]{:S(2)}) copy-start(s32[2]{0:T(128)} %param.17) | copy-start | bytes 28
  6.8 3.9 %copy-start.7 = (s32[2]{0:T(128)S(1)}, s32[2]{0:T(128)}, u32[]{:S(2)}) copy-start(s32[2]{0:T(128)} %param.18) | copy-start | bytes 28
  9.8 7.9 %copy-start.3 = (f32[2,7,7,256]{3,0,2,1:T(2,128)S(1)}, f32[2,7,7,256]{3,0,2,1:T(2,128)}, u32[]{:S(2)}) copy-start(f32[2,7,7,256]{3,0,2,1:T(2,128)} %param.22) | copy-start | bytes 301060
  10.3 7.7 %copy-start.5 = (f32[2,256]{1,0:T(2,128)S(1)}, f32[2,256]{1,0:T(2,128)}, u32[]{:S(2)}) copy-start(f32[2,256]{1,0:T(2,128)} %param.23) | copy-start | bytes 6148
  11.0 10.8 %collective-permute-start = (bf16[2,17,16,256]{3,2,1,0:T(8,128)(2,1)S(1)}, bf16[2,17,16,256]{3,2,1,0:T(8,128)(2,1)S(1)}, u32[]{:S(2)}, u32[]{:S(2)}) collective-permute-start(bf16[2,17,16,256]{3,2,1,0:T(8,128)(2,1)S(1)} %pad_maximum_fusion.2), channel_id=1, source_target_pairs={{0,8},{8,16},{16,24},{1,9},{9,17},{17,25},{2,10},{10,18},{18,26},{... | collective-permute-start | bytes 835592 | tf_op jit(solution)/shard_map/ppermute | solution.py:77
  16.4 13.3 %collective-permute-start.1 = (bf16[2,17,16,256]{3,2,1,0:T(8,128)(2,1)S(1)}, bf16[2,17,16,256]{3,2,1,0:T(8,128)(2,1)S(1)}, u32[]{:S(2)}, u32[]{:S(2)}) collective-permute-start(bf16[2,17,16,256]{3,2,1,0:T(8,128)(2,1)S(1)} %pad_maximum_fusion.3), channel_id=1, source_target_pairs={{8,0},{16,8},{24,16},{9,1},{17,9},{25,17},{10,2},{18,10},{26,18},{... | collective-permute-start | bytes 835592 | tf_op jit(solution)/shard_map/ppermute | solution.py:77
  18.0 13.3 %copy-start.2 = (bf16[24,24,256]{2,1,0:T(8,128)(2,1)S(1)}, bf16[24,24,256]{2,1,0:T(8,128)(2,1)}, u32[]{:S(2)}) copy-start(bf16[24,24,256]{2,1,0:T(8,128)(2,1)} %param.21) | copy-start | bytes 884740
  31.7 6.0 %collective-permute-start.2 = (bf16[24,6,256]{2,1,0:T(8,128)(2,1)S(1)}, bf16[24,6,256]{2,1,0:T(8,128)(2,1)S(1)}, u32[]{:S(2)}, u32[]{:S(2)}) collective-permute-start(bf16[24,6,256]{2,1,0:T(8,128)(2,1)S(1)} %get-tuple-element.26), channel_id=1, source_target_pairs={{0,1},{1,2},{2,3},{3,4},{4,5},{5,6},{6,7},{7,0},{8,9},{9,10},{10,1... | collective-permute-start | bytes 221192 | tf_op jit(solution)/shard_map/ppermute | solution.py:87
  31.7 5.9 %collective-permute-start.3 = (bf16[24,6,256]{2,1,0:T(8,128)(2,1)S(1)}, bf16[24,6,256]{2,1,0:T(8,128)(2,1)S(1)}, u32[]{:S(2)}, u32[]{:S(2)}) collective-permute-start(bf16[24,6,256]{2,1,0:T(8,128)(2,1)S(1)} %get-tuple-element.27), channel_id=1, source_target_pairs={{1,0},{2,1},{3,2},{4,3},{5,4},{6,5},{7,6},{0,7},{9,8},{10,9},{11,1... | collective-permute-start | bytes 221192 | tf_op jit(solution)/shard_map/ppermute | solution.py:88
  37.9 13.2 %collective-permute-start.4 = (bf16[6,36,256]{2,1,0:T(8,128)(2,1)S(1)}, bf16[6,36,256]{2,1,0:T(8,128)(2,1)S(1)}, u32[]{:S(2)}, u32[]{:S(2)}) collective-permute-start(bf16[6,36,256]{2,1,0:T(8,128)(2,1)S(1)} %get-tuple-element.24), channel_id=1, source_target_pairs={{0,8},{8,16},{16,24},{1,9},{9,17},{17,25},{2,10},{10,18},{18,26},{... | collective-permute-start | bytes 331784 | tf_op jit(solution)/shard_map/ppermute | solution.py:216
  41.3 8.4 %collective-permute-start.5 = (bf16[6,36,256]{2,1,0:T(8,128)(2,1)S(1)}, bf16[6,36,256]{2,1,0:T(8,128)(2,1)S(1)}, u32[]{:S(2)}, u32[]{:S(2)}) collective-permute-start(bf16[6,36,256]{2,1,0:T(8,128)(2,1)S(1)} %get-tuple-element.25), channel_id=1, source_target_pairs={{8,0},{16,8},{24,16},{9,1},{17,9},{25,17},{10,2},{18,10},{26,18},{... | collective-permute-start | bytes 331784 | tf_op jit(solution)/shard_map/ppermute | solution.py:217
  42.8 5.0 %copy-start.8 = (bf16[2,256,1024]{2,1,0:T(8,128)(2,1)S(1)}, bf16[2,256,1024]{2,1,0:T(8,128)(2,1)}, u32[]{:S(2)}) copy-start(bf16[2,256,1024]{2,1,0:T(8,128)(2,1)} %param.24) | copy-start | bytes 3145732
  47.8 1.2 %copy-start.1 = (bf16[2,1024,256]{2,1,0:T(8,128)(2,1)S(1)}, bf16[2,1024,256]{2,1,0:T(8,128)(2,1)}, u32[]{:S(2)}) copy-start(bf16[2,1024,256]{2,1,0:T(8,128)(2,1)} %param.25) | copy-start | bytes 3145732

commit v8 on v7

--- a/solution.py
+++ b/solution.py
@@ -13,8 +13,16 @@
 RW = 16
 
 
-def _conv_body(x_ref, w_ref, b_ref, o_ref, wide_ref):
-    oh, ow, ch = o_ref.shape[1], o_ref.shape[2], o_ref.shape[3]
+def _expand(count, size, by_block):
+    rows = lax.broadcasted_iota(jnp.int32, (count, size), 0)
+    cols = lax.broadcasted_iota(jnp.int32, (count, size), 1)
+    group = count // size if by_block else 1
+    picked = rows // group if by_block else rows % size
+    return (picked == cols).astype(jnp.bfloat16)
+
+
+def _conv_body(x_ref, w_ref, b_ref, r_ref, c_ref, o_ref, wide_ref):
+    oh, ow, ch = x_ref.shape[1] // 2, x_ref.shape[2] // 2, o_ref.shape[2]
     cin = x_ref.shape[3]
     lanes = wide_ref.shape[3]
     parts = wide_ref.shape[0]
@@ -49,26 +57,48 @@
     first_col = lax.broadcasted_iota(jnp.int32, (oh, ow, ch), 1) == 0
     total = total + jnp.where(first_col, 0.0, rolled)
     total = total + b_ref[...]
-    o_ref[0] = jax.nn.gelu(total).astype(o_ref.dtype)
-
-
-def conv_gelu(x, w, b):
+    features = jax.nn.gelu(total).astype(x_ref.dtype).reshape(oh * ow, ch)
+    row_mix, col_mix = r_ref[0], c_ref[0]
+    rb, rw = row_mix.shape[0], col_mix.shape[0]
+    cells = rb * rw
+    by_row = jnp.dot(_expand(cells, rb, True), row_mix, preferred_element_type=jnp.float32)
+    by_col = jnp.dot(_expand(cells, rw, False), col_mix, preferred_element_type=jnp.float32)
+    spread_row = jnp.dot(
+        by_row.astype(x_ref.dtype), _expand(oh * ow, oh, True).T, preferred_element_type=jnp.float32
+    )
+    spread_col = jnp.dot(
+        by_col.astype(x_ref.dtype), _expand(oh * ow, ow, False).T, preferred_element_type=jnp.float32
+    )
+    both = spread_row * spread_col
+    high = both.astype(x_ref.dtype)
+    low = (both - high.astype(jnp.float32)).astype(x_ref.dtype)
+    mixed = jnp.dot(high, features, preferred_element_type=jnp.float32) + jnp.dot(
+        low, features, preferred_element_type=jnp.float32
+    )
+    o_ref[0] = mixed.astype(o_ref.dtype)
+
+
+def conv_resample(x, w, b, row_mix, col_mix):
     n, h, wd, cin = x.shape
     cout = w.shape[3]
     oh, ow = h // 2, wd // 2
-    return pl.pallas_call(
+    rb, rw = row_mix.shape[1], col_mix.shape[1]
+    out = pl.pallas_call(
         _conv_body,
         grid=(n,),
         in_specs=[
             pl.BlockSpec((1, h, wd, cin), lambda i: (i, 0, 0, 0)),
             pl.BlockSpec((3, 3, cin, cout), lambda i: (0, 0, 0, 0)),
             pl.BlockSpec((1, cout), lambda i: (0, 0)),
+            pl.BlockSpec((1, rb, oh), lambda i: (i, 0, 0)),
+            pl.BlockSpec((1, rw, ow), lambda i: (i, 0, 0)),
         ],
-        out_specs=pl.BlockSpec((1, oh, ow, cout), lambda i: (i, 0, 0, 0)),
-        out_shape=jax.ShapeDtypeStruct((n, oh, ow, cout), jnp.bfloat16),
+        out_specs=pl.BlockSpec((1, rb * rw, cout), lambda i: (i, 0, 0)),
+        out_shape=jax.ShapeDtypeStruct((n, rb * rw, cout), jnp.bfloat16),
         scratch_shapes=[pltpu.VMEM((cin // 128, h, wd, 128), jnp.float32)],
         compiler_params=pltpu.CompilerParams(dimension_semantics=("arbitrary",)),
-    )(x, w, b.reshape(1, cout))
+    )(x, w, b.reshape(1, cout), row_mix, col_mix)
+    return out.reshape(n, rb, rw, cout)
 
 
 def shifted(value, axis, steps):
@@ -88,14 +118,6 @@
         after = lax.ppermute(leading, axis, down)
         value = jnp.concatenate([before, value, after], axis=dim)
     return value
-
-
-def resample_local(blocks, row_mix, col_mix):
-    row_mixed = jnp.einsum("nri,nijc->nrjc", row_mix, blocks, preferred_element_type=jnp.float32)
-    both_mixed = jnp.einsum(
-        "nrjc,nuj->nruc", row_mixed, col_mix.astype(jnp.float32), precision=lax.Precision.HIGHEST
-    )
-    return both_mixed.astype(jnp.bfloat16)
 
 
 def place_rows(onehot, values):
@@ -165,8 +187,7 @@
     tile_cols = background.shape[1]
     channels = background.shape[2]
     bands = lax.axis_size("lat")
-    features = conv_gelu(swath_input, conv_weight, conv_bias)
-    resampled = resample_local(features, row_weights, col_weights)
+    resampled = conv_resample(swath_input, conv_weight, conv_bias, row_weights, col_weights)
     own_band = lax.axis_index("lat")
     offset_band = block_band[:, 0] - own_band
     staying = offset_band == 0

time: 62.2 us -> 61.7 us (level)
  matrix products: 10 us -> 7 us
  Pallas kernels: 6.12 us -> 8.19 us
  local copies, waits for them, and re-layouts: 1.44 us -> 2.41 us
    dot_general x2 -> x0, matrix products: 2.99 us -> none  [the longest x1 1.92 us: resample_local(): jnp.einsum('nri,nijc->nrjc', row_mix, blocks, preferred_element_type=jnp....]
    pallas_call x1, Pallas kernels: 6.12 us -> 8.19 us  [conv_resample(): pl.pallas_call(_conv_body, grid=(n,), in_specs=[pl.BlockSpec((1, h, wd, c...]
    unnamed x23, local copies, waits for them, and re-layouts: 0.66 us -> 1.64 us
    eq x1, other arithmetic: 0.67 us -> 0.01 us  [per_device(): staying = offset_band == 0]
  transfers between devices with their start and end apart: 6 -> 6, of which waited for: 3 -> 3; matrix products, arithmetic and copies ran while one was open for 14% -> 15% of each run, Pallas kernels for 0% -> 0%
where the time goes in v8:
time: 61.7 us; the launch traced here: 61.4 us
  other arithmetic  14.8 us (24%)
  starting transfers between devices  14.7 us (24%)
  waiting for transfers between devices  13.8 us (22%)
  Pallas kernels  8.19 us (13%)
  matrix products  7 us (11%)
  local copies, waits for them, and re-layouts  2.41 us (4%)
    reduce_sum x4, other arithmetic, layer_apply(): centered = mixed - jnp.mean(mixed, axis=-1, keepdims=True)  11.7 us
    ppermute x2, waiting for transfers between devices, shifted(): lax.ppermute(value, axis, [(source, source + steps) for source in range(l...  11.4 us
    pallas_call x1, Pallas kernels, conv_resample(): pl.pallas_call(_conv_body, grid=(n,), in_specs=[pl.BlockSpec((1, h, wd, c...  8.19 us
    ppermute x2, starting transfers between devices, shifted(): lax.ppermute(value, axis, [(source, source + steps) for source in range(l...  6.18 us
    ppermute x1, starting transfers between devices, with_halo(): after = lax.ppermute(leading, axis, down)  3.53 us
    ppermute x1, starting transfers between devices, per_device(): north = lax.ppermute(lon_wide[length - reach:], 'lat', up)  3.4 us
    dot_general x4, matrix products, layer_apply(): jnp.dot(flat_cells, up_matrix, preferred_element_type=jnp.float32)  2.71 us
    ppermute x1, waiting for transfers between devices, with_halo(): before = lax.ppermute(last, axis, up)  2.39 us
  transfers between devices with their start and end apart: 6, of which 3 were waited for; matrix products, arithmetic and copies ran while one was open for 15% of the time, Pallas kernels for 0%

profile of v8, /device:TPU:0, one launch (start us, length us, event | category | flops | bytes accessed | tf_op | source)
XLA Modules:
  0.0 61.4 jit_solution(15907517238520039068)
XLA Ops:
  0.0 8.2 %shard_map.127 = bf16[2,256,256]{2,1,0:T(8,128)(2,1)} custom-call(bf16[2,64,64,256]{3,2,1,0:T(8,128)(2,1)} %x_ref.1, bf16[3,3,256,256]{3,2,1,0:T(8,128)(2,1)} %w_ref.1, f32[1,256]{1,0:T(1,128)} %bitcast.403, bf16[2,16,32]{2,1,0:T(8,128)(2,1)} %r_ref.1, bf16[2,16,32]{2,1,0:T(8,128)(2,1)} %c_ref.1), custom_call_target="tpu_custom_call" | custom-call | tf_op jit(solution)/shard_map/pallas_call | solution.py:86
  8.2 1.3 %copy.40 = bf16[1,2,256,256]{3,1,2,0:T(2,128)(2,1)S(1)} copy(bf16[1,2,256,256]{3,2,1,0:T(8,128)(2,1)} %bitcast.188) | data formatting | bytes 524288
  9.5 0.1 fusion.290
  9.7 0.4 convolution_convert_fusion.1
  10.1 0.2 select_reduce_fusion.2
  10.3 0.1 select_convert_fusion.1
  10.4 4.9 %collective-permute-start = (bf16[2,17,16,256]{3,2,1,0:T(8,128)(2,1)S(1)}, bf16[2,17,16,256]{3,2,1,0:T(8,128)(2,1)S(1)}, u32[]{:S(2)}, u32[]{:S(2)}) collective-permute-start(bf16[2,17,16,256]{3,2,1,0:T(8,128)(2,1)S(1)} %pad_maximum_fusion.2), channel_id=1, source_target_pairs={{0,8},{8,16},{16,24},{1,9},{9,17},{17,25},{2,10},{10,18},{18,26},{... | collective-permute-start | bytes 835592 | tf_op jit(solution)/shard_map/ppermute | solution.py:107
  15.3 0.4 convolution_convert_fusion
  15.8 1.3 %collective-permute-start.1 = (bf16[2,17,16,256]{3,2,1,0:T(8,128)(2,1)S(1)}, bf16[2,17,16,256]{3,2,1,0:T(8,128)(2,1)S(1)}, u32[]{:S(2)}, u32[]{:S(2)}) collective-permute-start(bf16[2,17,16,256]{3,2,1,0:T(8,128)(2,1)S(1)} %pad_maximum_fusion.3), channel_id=1, source_target_pairs={{8,0},{16,8},{24,16},{9,1},{17,9},{25,17},{10,2},{18,10},{26,18},{... | collective-permute-start | bytes 835592 | tf_op jit(solution)/shard_map/ppermute | solution.py:107
  17.1 0.1 fusion.303
  17.4 0.1 broadcast_select_fusion
  17.6 3.6 %collective-permute-done = bf16[2,17,16,256]{3,2,1,0:T(8,128)(2,1)S(1)} collective-permute-done((bf16[2,17,16,256]{3,2,1,0:T(8,128)(2,1)S(1)}, bf16[2,17,16,256]{3,2,1,0:T(8,128)(2,1)S(1)}, u32[]{:S(2)}, u32[]{:S(2)}) %collective-permute-start) | collective-permute-done | bytes 278560 | tf_op jit(solution)/shard_map/ppermute | solution.py:107
  21.2 0.2 slice_reduce_fusion.1
  21.4 7.7 %collective-permute-done.1 = bf16[2,17,16,256]{3,2,1,0:T(8,128)(2,1)S(1)} collective-permute-done((bf16[2,17,16,256]{3,2,1,0:T(8,128)(2,1)S(1)}, bf16[2,17,16,256]{3,2,1,0:T(8,128)(2,1)S(1)}, u32[]{:S(2)}, u32[]{:S(2)}) %collective-permute-start.1) | collective-permute-done | bytes 278560 | tf_op jit(solution)/shard_map/ppermute | solution.py:107
  29.1 0.2 slice_reduce_fusion
  29.3 0.1 pad_add_fusion
  29.4 0.1 iota_add_fusion.1
  29.5 0.1 pad_add_fusion.1
  29.7 0.1 pad_maximum_fusion
  29.8 0.8 %convolution_convert_fusion.2 = bf16[6,24,16,256]{3,1,2,0:T(8,128)(2,1)S(1)} fusion(bf16[6,16,16,256]{3,2,1,0:T(8,128)(2,1)S(1)} %pad_maximum_fusion, s32[6,16]{1,0:T(8,128)S(1)} %iota_add_fusion.1), kind=kOutput, calls=%fused_computation.20 | convolution fusion | flops 19466496 | bytes 1966464 | tf_op jit(solution)/shard_map/shr,sruc->shuc/dot_general | solution.py:227
  30.6 0.4 fusion.17
  31.1 3.5 %collective-permute-start.3 = (bf16[24,6,256]{2,1,0:T(8,128)(2,1)S(1)}, bf16[24,6,256]{2,1,0:T(8,128)(2,1)S(1)}, u32[]{:S(2)}, u32[]{:S(2)}) collective-permute-start(bf16[24,6,256]{2,1,0:T(8,128)(2,1)S(1)} %get-tuple-element.27), channel_id=1, source_target_pairs={{1,0},{2,1},{3,2},{4,3},{5,4},{6,5},{7,6},{0,7},{9,8},{10,9},{11,1... | collective-permute-start | bytes 221192 | tf_op jit(solution)/shard_map/ppermute | solution.py:118
  34.7 2.4 %collective-permute-done.2 = bf16[24,6,256]{2,1,0:T(8,128)(2,1)S(1)} collective-permute-done((bf16[24,6,256]{2,1,0:T(8,128)(2,1)S(1)}, bf16[24,6,256]{2,1,0:T(8,128)(2,1)S(1)}, u32[]{:S(2)}, u32[]{:S(2)}) %collective-permute-start.2) | collective-permute-done | bytes 73760 | tf_op jit(solution)/shard_map/ppermute | solution.py:117
  37.0 0.2 fusion.292
  37.2 3.4 %collective-permute-start.4 = (bf16[6,36,256]{2,1,0:T(8,128)(2,1)S(1)}, bf16[6,36,256]{2,1,0:T(8,128)(2,1)S(1)}, u32[]{:S(2)}, u32[]{:S(2)}) collective-permute-start(bf16[6,36,256]{2,1,0:T(8,128)(2,1)S(1)} %get-tuple-element.24), channel_id=1, source_target_pairs={{0,8},{8,16},{16,24},{1,9},{9,17},{17,25},{2,10},{10,18},{18,26},{... | collective-permute-start | bytes 331784 | tf_op jit(solution)/shard_map/ppermute | solution.py:237
  40.7 1.5 %collective-permute-start.5 = (bf16[6,36,256]{2,1,0:T(8,128)(2,1)S(1)}, bf16[6,36,256]{2,1,0:T(8,128)(2,1)S(1)}, u32[]{:S(2)}, u32[]{:S(2)}) collective-permute-start(bf16[6,36,256]{2,1,0:T(8,128)(2,1)S(1)} %get-tuple-element.25), channel_id=1, source_target_pairs={{8,0},{16,8},{24,16},{9,1},{17,9},{25,17},{10,2},{18,10},{26,18},{... | collective-permute-start | bytes 331784 | tf_op jit(solution)/shard_map/ppermute | solution.py:238
  42.2 4.4 %fusion.297 = (f32[18,32]{1,0:T(8,128)S(1)}, f32[18,32,256]{2,1,0:T(8,128)S(1)}) fusion(f32[256]{0:T(256)S(1)} %bitcast.295, f32[256]{0:T(256)S(1)} %bitcast.298, f32[256]{0:T(256)S(1)} %bitcast.301, f32[256]{0:T(256)S(1)} %bitcast.304, f32[256]{0:T(256)S(1)} %bitcast.307, f32[256]{0:T(256)S(1)} %bitcast.310, f32[256]{0:T(256)S(1)} %bitcast.313, ...), kind=kLoop, calls=%fused_computation.535 | loop fusion | flops 14450112 | bytes 22269184 | tf_op jit(solution)/shard_map/reduce_sum | solution.py:156
  46.7 0.3 multiply_reduce_fusion.1
  47.0 0.2 multiply_convert_fusion.1
  47.2 0.9 %fusion.7 = bf16[576,1024]{1,0:T(8,128)(2,1)S(1)} fusion(bf16[576,256]{1,0:T(8,128)(2,1)S(1)} %bitcast.195, bf16[2,256,1024]{2,1,0:T(8,128)(2,1)S(1)} %copy-done.8), kind=kOutput, calls=%fused_computation.11 | convolution fusion | flops 307298304 | bytes 1998848 | tf_op jit(solution)/shard_map/dot_general | solution.py:160
  48.2 0.3 copy-done.1
  48.4 0.5 fusion.144
  48.9 0.1 fusion.85
  49.1 1.4 %fusion.299 = (f32[6,32]{1,0:T(8,128)S(1)}, f32[6,32,256]{2,1,0:T(8,128)S(1)}) fusion(f32[256]{0:T(256)S(1)} %bitcast.296, f32[256]{0:T(256)S(1)} %bitcast.299, f32[256]{0:T(256)S(1)} %bitcast.302, f32[256]{0:T(256)S(1)} %bitcast.305, f32[256]{0:T(256)S(1)} %bitcast.308, f32[256]{0:T(256)S(1)} %bitcast.311, f32[256]{0:T(256)S(1)} %bitcast.314, ...), kind=kLoop, calls=%fused_computation.536 | loop fusion | flops 4816704 | bytes 7620352 | tf_op jit(solution)/shard_map/reduce_sum | solution.py:156
  50.6 1.4 %fusion.295 = (f32[6,32]{1,0:T(8,128)S(1)}, f32[6,32,256]{2,1,0:T(8,128)S(1)}) fusion(f32[256]{0:T(256)S(1)} %bitcast.297, f32[256]{0:T(256)S(1)} %bitcast.300, f32[256]{0:T(256)S(1)} %bitcast.303, f32[256]{0:T(256)S(1)} %bitcast.306, f32[256]{0:T(256)S(1)} %bitcast.309, f32[256]{0:T(256)S(1)} %bitcast.312, f32[256]{0:T(256)S(1)} %bitcast.315, ...), kind=kLoop, calls=%fused_computation.534 | loop fusion | flops 4816704 | bytes 7620352 | tf_op jit(solution)/shard_map/reduce_sum | solution.py:156
  52.1 0.2 multiply_reduce_fusion.2
  52.3 0.2 multiply_reduce_fusion.3
  52.4 0.2 multiply_convert_fusion.3
  52.6 0.4 fusion.35
  53.1 0.3 fusion.142
  53.3 0.4 fusion.27
  53.8 0.3 fusion.146
  54.1 0.1 fusion.159
  54.3 4.4 %fusion.293 = (f32[24,24]{1,0:T(8,128)S(1)}, f32[24,24,256]{2,1,0:T(8,128)S(1)}) fusion(f32[256]{0:T(256)S(1)} %bitcast.384, f32[30,30,256]{2,1,0:T(8,128)S(1)} %fusion.159, f32[256]{0:T(256)S(1)} %bitcast.385, f32[256]{0:T(256)S(1)} %bitcast.386, f32[256]{0:T(256)S(1)} %bitcast.387, f32[256]{0:T(256)S(1)} %bitcast.388, f32[256]{0:T(256)S(1)} %bitcast.389, ...), kind=kLoop, calls=%fused_computation.533 | loop fusion | flops 14450112 | bytes 29543680 | tf_op jit(solution)/shard_map/reduce_sum | solution.py:156
  58.7 0.3 multiply_reduce_fusion
  59.0 0.2 multiply_convert_fusion
  59.2 0.9 %fusion.15 = bf16[576,1024]{1,0:T(8,128)(2,1)S(1)} fusion(bf16[576,256]{1,0:T(8,128)(2,1)S(1)} %bitcast.194, bf16[2,256,1024]{2,1,0:T(8,128)(2,1)S(1)} %copy-done.8), kind=kOutput, calls=%fused_computation.19 | convolution fusion | flops 307298304 | bytes 1998848 | tf_op jit(solution)/shard_map/dot_general | solution.py:160
  60.2 1.2 %fusion.18 = bf16[24,24,256]{2,1,0:T(8,128)(2,1)} fusion(bf16[24,24,1024]{2,1,0:T(8,128)(2,1)S(1)} %bitcast.404, f32[30,30,256]{2,1,0:T(8,128)S(1)} %fusion.159, bf16[2,1024,256]{2,1,0:T(8,128)(2,1)S(1)} %copy-done.1), kind=kOutput, calls=%fused_computation.25 | convolution fusion | flops 302284800 | bytes 2588672 | tf_op jit(solution)/shard_map/dot_general | solution.py:163
  (62 shorter events, 0.8 us)
Async XLA Ops:
  0.0 9.5 %copy-start.7 = (s32[2,1]{0,1:T(1,128)S(1)}, s32[2,1]{0,1:T(1,128)}, u32[]{:S(2)}) copy-start(s32[2,1]{0,1:T(1,128)} %param.16) | copy-start | bytes 28
  0.0 10.1 %copy-start.5 = (s32[2]{0:T(128)S(1)}, s32[2]{0:T(128)}, u32[]{:S(2)}) copy-start(s32[2]{0:T(128)} %param.17) | copy-start | bytes 28
  0.0 10.1 %copy-start.6 = (s32[2]{0:T(128)S(1)}, s32[2]{0:T(128)}, u32[]{:S(2)}) copy-start(s32[2]{0:T(128)} %param.18) | copy-start | bytes 28
  8.2 8.9 %copy-start.3 = (f32[2,7,7,256]{3,0,2,1:T(2,128)S(1)}, f32[2,7,7,256]{3,0,2,1:T(2,128)}, u32[]{:S(2)}) copy-start(f32[2,7,7,256]{3,0,2,1:T(2,128)} %param.22) | copy-start | bytes 301060
  9.6 7.8 %copy-start.4 = (f32[2,256]{1,0:T(2,128)S(1)}, f32[2,256]{1,0:T(2,128)}, u32[]{:S(2)}) copy-start(f32[2,256]{1,0:T(2,128)} %param.23) | copy-start | bytes 6148
  9.6 7.8 %copy-start = (bf16[2,256,256]{2,1,0:T(8,128)(2,1)S(1)}, bf16[2,256,256]{2,1,0:T(8,128)(2,1)}, u32[]{:S(2)}) copy-start(bf16[2,256,256]{2,1,0:T(8,128)(2,1)} %shard_map.127) | copy-start | bytes 786436
  10.4 10.8 %collective-permute-start = (bf16[2,17,16,256]{3,2,1,0:T(8,128)(2,1)S(1)}, bf16[2,17,16,256]{3,2,1,0:T(8,128)(2,1)S(1)}, u32[]{:S(2)}, u32[]{:S(2)}) collective-permute-start(bf16[2,17,16,256]{3,2,1,0:T(8,128)(2,1)S(1)} %pad_maximum_fusion.2), channel_id=1, source_target_pairs={{0,8},{8,16},{16,24},{1,9},{9,17},{17,25},{2,10},{10,18},{18,26},{... | collective-permute-start | bytes 835592 | tf_op jit(solution)/shard_map/ppermute | solution.py:107
  15.8 13.3 %collective-permute-start.1 = (bf16[2,17,16,256]{3,2,1,0:T(8,128)(2,1)S(1)}, bf16[2,17,16,256]{3,2,1,0:T(8,128)(2,1)S(1)}, u32[]{:S(2)}, u32[]{:S(2)}) collective-permute-start(bf16[2,17,16,256]{3,2,1,0:T(8,128)(2,1)S(1)} %pad_maximum_fusion.3), channel_id=1, source_target_pairs={{8,0},{16,8},{24,16},{9,1},{17,9},{25,17},{10,2},{18,10},{26,18},{... | collective-permute-start | bytes 835592 | tf_op jit(solution)/shard_map/ppermute | solution.py:107
  17.5 13.1 %copy-start.2 = (bf16[24,24,256]{2,1,0:T(8,128)(2,1)S(1)}, bf16[24,24,256]{2,1,0:T(8,128)(2,1)}, u32[]{:S(2)}) copy-start(bf16[24,24,256]{2,1,0:T(8,128)(2,1)} %param.21) | copy-start | bytes 884740
  31.0 6.0 %collective-permute-start.2 = (bf16[24,6,256]{2,1,0:T(8,128)(2,1)S(1)}, bf16[24,6,256]{2,1,0:T(8,128)(2,1)S(1)}, u32[]{:S(2)}, u32[]{:S(2)}) collective-permute-start(bf16[24,6,256]{2,1,0:T(8,128)(2,1)S(1)} %get-tuple-element.26), channel_id=1, source_target_pairs={{0,1},{1,2},{2,3},{3,4},{4,5},{5,6},{6,7},{7,0},{8,9},{9,10},{10,1... | collective-permute-start | bytes 221192 | tf_op jit(solution)/shard_map/ppermute | solution.py:117
  31.1 5.9 %collective-permute-start.3 = (bf16[24,6,256]{2,1,0:T(8,128)(2,1)S(1)}, bf16[24,6,256]{2,1,0:T(8,128)(2,1)S(1)}, u32[]{:S(2)}, u32[]{:S(2)}) collective-permute-start(bf16[24,6,256]{2,1,0:T(8,128)(2,1)S(1)} %get-tuple-element.27), channel_id=1, source_target_pairs={{1,0},{2,1},{3,2},{4,3},{5,4},{6,5},{7,6},{0,7},{9,8},{10,9},{11,1... | collective-permute-start | bytes 221192 | tf_op jit(solution)/shard_map/ppermute | solution.py:118
  37.2 13.3 %collective-permute-start.4 = (bf16[6,36,256]{2,1,0:T(8,128)(2,1)S(1)}, bf16[6,36,256]{2,1,0:T(8,128)(2,1)S(1)}, u32[]{:S(2)}, u32[]{:S(2)}) collective-permute-start(bf16[6,36,256]{2,1,0:T(8,128)(2,1)S(1)} %get-tuple-element.24), channel_id=1, source_target_pairs={{0,8},{8,16},{16,24},{1,9},{9,17},{17,25},{2,10},{10,18},{18,26},{... | collective-permute-start | bytes 331784 | tf_op jit(solution)/shard_map/ppermute | solution.py:237
  40.7 8.4 %collective-permute-start.5 = (bf16[6,36,256]{2,1,0:T(8,128)(2,1)S(1)}, bf16[6,36,256]{2,1,0:T(8,128)(2,1)S(1)}, u32[]{:S(2)}, u32[]{:S(2)}) collective-permute-start(bf16[6,36,256]{2,1,0:T(8,128)(2,1)S(1)} %get-tuple-element.25), channel_id=1, source_target_pairs={{8,0},{16,8},{24,16},{9,1},{17,9},{25,17},{10,2},{18,10},{26,18},{... | collective-permute-start | bytes 331784 | tf_op jit(solution)/shard_map/ppermute | solution.py:238
  42.2 5.0 %copy-start.8 = (bf16[2,256,1024]{2,1,0:T(8,128)(2,1)S(1)}, bf16[2,256,1024]{2,1,0:T(8,128)(2,1)}, u32[]{:S(2)}) copy-start(bf16[2,256,1024]{2,1,0:T(8,128)(2,1)} %param.24) | copy-start | bytes 3145732
  47.2 1.2 %copy-start.1 = (bf16[2,1024,256]{2,1,0:T(8,128)(2,1)S(1)}, bf16[2,1024,256]{2,1,0:T(8,128)(2,1)}, u32[]{:S(2)}) copy-start(bf16[2,1024,256]{2,1,0:T(8,128)(2,1)} %param.25) | copy-start | bytes 3145732

commit v9 on v8

--- a/solution.py
+++ b/solution.py
@@ -121,9 +121,8 @@
 
 
 def place_rows(onehot, values):
-    flat_values = values.reshape(values.shape[0], -1)
-    placed = jnp.dot(onehot.astype(values.dtype), flat_values, preferred_element_type=jnp.float32)
-    return placed.astype(values.dtype).reshape((onehot.shape[0],) + values.shape[1:])
+    shaped = onehot.reshape(onehot.shape + (1,) * (values.ndim - 1))
+    return jnp.sum(jnp.where(shaped, values[None], jnp.zeros_like(values[None])), axis=1)
 
 
 def place_ints(onehot, values):

time: 61.7 us -> 62.3 us (level)
  the two profiles are of different devices: /device:TPU:0 before, /device:TPU:5 now
where the time goes in v9:
time: 62.3 us; the launch traced here: 62 us
  other arithmetic  17.5 us (28%)
  starting transfers between devices  14.4 us (23%)
  waiting for transfers between devices  14.2 us (23%)
  Pallas kernels  8.21 us (13%)
  matrix products  6.16 us (10%)
  local copies, waits for them, and re-layouts  1.1 us (2%)
    reduce_sum x4, other arithmetic, layer_apply(): centered = mixed - jnp.mean(mixed, axis=-1, keepdims=True)  11.7 us
    ppermute x2, waiting for transfers between devices, shifted(): lax.ppermute(value, axis, [(source, source + steps) for source in range(l...  9.39 us
    pallas_call x1, Pallas kernels, conv_resample(): pl.pallas_call(_conv_body, grid=(n,), in_specs=[pl.BlockSpec((1, h, wd, c...  8.21 us
    ppermute x2, starting transfers between devices, shifted(): lax.ppermute(value, axis, [(source, source + steps) for source in range(l...  5.3 us
    ppermute x1, starting transfers between devices, per_device(): north = lax.ppermute(lon_wide[length - reach:], 'lat', up)  3.37 us
    ppermute x1, waiting for transfers between devices, with_halo(): after = lax.ppermute(leading, axis, down)  3.13 us
    ppermute x1, starting transfers between devices, per_device(): south = lax.ppermute(lon_wide[:reach], 'lat', down)  3 us
    ppermute x1, starting transfers between devices, with_halo(): before = lax.ppermute(last, axis, up)  2.74 us
  transfers between devices with their start and end apart: 6, of which 4 were waited for; matrix products, arithmetic and copies ran while one was open for 14% of the time, Pallas kernels for 0%

profile of v9, /device:TPU:5, one launch (start us, length us, event | category | flops | bytes accessed | tf_op | source)
XLA Modules:
  0.0 62.0 jit_solution(17145327204627286344)
XLA Ops:
  0.0 0.7 %compare_bitcast_fusion = (pred[2]{0:T(512)(128)(4,1)S(1)}, pred[2]{0:T(512)(128)(4,1)S(1)}, pred[2]{0:T(512)(128)(4,1)S(1)}) fusion(s32[2,1]{0,1:T(1,128)} %param.16, s32[]{:T(128)S(6)} %axis_index.15), kind=kLoop, calls=%fused_computation.508 | loop fusion | flops 8 | bytes 18 | tf_op jit(solution)/shard_map/eq | solution.py:192
  0.7 0.1 fusion.290
  0.8 0.8 %select_reduce_fusion.4 = (s32[2]{0:T(128)S(1)}, s32[2]{0:T(128)S(1)}, s32[2]{0:T(128)S(1)}, s32[2]{0:T(128)S(1)}, pred[2,2]{1,0:T(4,128)(4,1)S(1)}, /*index=5*/pred[2,2]{1,0:T(4,128)(4,1)S(1)}) fusion(s32[2]{0:T(128)} %param.18, s32[2]{0:T(128)} %param.17, pred[2]{0:T(512)(128)(4,1)S(1)} %get-tuple-element.138, s32[2]{0:T(128)S(1)} %get-tuple-element.141, ...), kind=kLoop, calls=%fused_computation.524 | loop fusion | flops 40 | bytes 76 | tf_op jit(solution)/shard_map/reduce_sum | solution.py:129
  1.7 8.2 %shard_map.127 = bf16[2,256,256]{2,1,0:T(8,128)(2,1)} custom-call(bf16[2,64,64,256]{3,2,1,0:T(8,128)(2,1)} %x_ref.1, bf16[3,3,256,256]{3,2,1,0:T(8,128)(2,1)} %w_ref.1, f32[1,256]{1,0:T(1,128)} %bitcast.386, bf16[2,16,32]{2,1,0:T(8,128)(2,1)} %r_ref.1, bf16[2,16,32]{2,1,0:T(8,128)(2,1)} %c_ref.1), custom_call_target="tpu_custom_call" | custom-call | tf_op jit(solution)/shard_map/pallas_call | solution.py:86
  9.9 1.3 %select_reduce_fusion.1 = (bf16[2,16,16,256]{3,2,1,0:T(8,128)(2,1)S(1)}, bf16[2,16,16,256]{3,2,1,0:T(8,128)(2,1)S(1)}) fusion(pred[2,2]{1,0:T(4,128)(4,1)S(1)} %get-tuple-element.24, bf16[2,16,16,256]{3,2,1,0:T(8,128)(2,1)} %bitcast.178, pred[2,2]{1,0:T(4,128)(4,1)S(1)} %get-tuple-element.23), kind=kLoop, calls=%fused_computation.257 | loop fusion | flops 786432 | bytes 786440 | tf_op jit(solution)/shard_map/reduce_sum | solution.py:125
  11.2 0.1 select_convert_fusion.1
  11.3 3.1 %collective-permute-start.1 = (bf16[2,17,16,256]{3,2,1,0:T(8,128)(2,1)S(1)}, bf16[2,17,16,256]{3,2,1,0:T(8,128)(2,1)S(1)}, u32[]{:S(2)}, u32[]{:S(2)}) collective-permute-start(bf16[2,17,16,256]{3,2,1,0:T(8,128)(2,1)S(1)} %pad_maximum_fusion.3), channel_id=1, source_target_pairs={{8,0},{16,8},{24,16},{9,1},{17,9},{25,17},{10,2},{18,10},{26,18},{... | collective-permute-start | bytes 835592 | tf_op jit(solution)/shard_map/ppermute | solution.py:107
  14.5 2.2 %collective-permute-start = (bf16[2,17,16,256]{3,2,1,0:T(8,128)(2,1)S(1)}, bf16[2,17,16,256]{3,2,1,0:T(8,128)(2,1)S(1)}, u32[]{:S(2)}, u32[]{:S(2)}) collective-permute-start(bf16[2,17,16,256]{3,2,1,0:T(8,128)(2,1)S(1)} %pad_maximum_fusion.2), channel_id=1, source_target_pairs={{0,8},{8,16},{16,24},{1,9},{9,17},{17,25},{2,10},{10,18},{18,26},{... | collective-permute-start | bytes 835592 | tf_op jit(solution)/shard_map/ppermute | solution.py:107
  16.7 0.1 fusion.303
  17.0 0.1 broadcast_select_fusion
  17.1 3.7 %collective-permute-done.1 = bf16[2,17,16,256]{3,2,1,0:T(8,128)(2,1)S(1)} collective-permute-done((bf16[2,17,16,256]{3,2,1,0:T(8,128)(2,1)S(1)}, bf16[2,17,16,256]{3,2,1,0:T(8,128)(2,1)S(1)}, u32[]{:S(2)}, u32[]{:S(2)}) %collective-permute-start.1) | collective-permute-done | bytes 278560 | tf_op jit(solution)/shard_map/ppermute | solution.py:107
  20.8 0.2 slice_reduce_fusion
  21.0 5.7 %collective-permute-done = bf16[2,17,16,256]{3,2,1,0:T(8,128)(2,1)S(1)} collective-permute-done((bf16[2,17,16,256]{3,2,1,0:T(8,128)(2,1)S(1)}, bf16[2,17,16,256]{3,2,1,0:T(8,128)(2,1)S(1)}, u32[]{:S(2)}, u32[]{:S(2)}) %collective-permute-start) | collective-permute-done | bytes 278560 | tf_op jit(solution)/shard_map/ppermute | solution.py:107
  26.7 0.2 slice_reduce_fusion.1
  26.9 0.1 pad_add_fusion
  27.0 0.1 iota_add_fusion.1
  27.1 0.1 pad_add_fusion.1
  27.3 0.1 pad_maximum_fusion
  27.4 0.8 %convolution_convert_fusion = bf16[6,24,16,256]{3,1,2,0:T(8,128)(2,1)S(1)} fusion(bf16[6,16,16,256]{3,2,1,0:T(8,128)(2,1)S(1)} %pad_maximum_fusion, s32[6,16]{1,0:T(8,128)S(1)} %iota_add_fusion.1), kind=kOutput, calls=%fused_computation.18 | convolution fusion | flops 19466496 | bytes 1966464 | tf_op jit(solution)/shard_map/shr,sruc->shuc/dot_general | solution.py:226
  28.2 0.4 fusion.17
  28.7 2.7 %collective-permute-start.2 = (bf16[24,6,256]{2,1,0:T(8,128)(2,1)S(1)}, bf16[24,6,256]{2,1,0:T(8,128)(2,1)S(1)}, u32[]{:S(2)}, u32[]{:S(2)}) collective-permute-start(bf16[24,6,256]{2,1,0:T(8,128)(2,1)S(1)} %get-tuple-element.29), channel_id=1, source_target_pairs={{0,1},{1,2},{2,3},{3,4},{4,5},{5,6},{6,7},{7,0},{8,9},{9,10},{10,1... | collective-permute-start | bytes 221192 | tf_op jit(solution)/shard_map/ppermute | solution.py:117
  31.4 1.6 %collective-permute-done.2 = bf16[24,6,256]{2,1,0:T(8,128)(2,1)S(1)} collective-permute-done((bf16[24,6,256]{2,1,0:T(8,128)(2,1)S(1)}, bf16[24,6,256]{2,1,0:T(8,128)(2,1)S(1)}, u32[]{:S(2)}, u32[]{:S(2)}) %collective-permute-start.2) | collective-permute-done | bytes 73760 | tf_op jit(solution)/shard_map/ppermute | solution.py:117
  33.0 3.1 %collective-permute-done.3 = bf16[24,6,256]{2,1,0:T(8,128)(2,1)S(1)} collective-permute-done((bf16[24,6,256]{2,1,0:T(8,128)(2,1)S(1)}, bf16[24,6,256]{2,1,0:T(8,128)(2,1)S(1)}, u32[]{:S(2)}, u32[]{:S(2)}) %collective-permute-start.3) | collective-permute-done | bytes 73760 | tf_op jit(solution)/shard_map/ppermute | solution.py:118
  36.2 0.2 fusion.292
  36.4 3.4 %collective-permute-start.4 = (bf16[6,36,256]{2,1,0:T(8,128)(2,1)S(1)}, bf16[6,36,256]{2,1,0:T(8,128)(2,1)S(1)}, u32[]{:S(2)}, u32[]{:S(2)}) collective-permute-start(bf16[6,36,256]{2,1,0:T(8,128)(2,1)S(1)} %get-tuple-element.27), channel_id=1, source_target_pairs={{0,8},{8,16},{16,24},{1,9},{9,17},{17,25},{2,10},{10,18},{18,26},{... | collective-permute-start | bytes 331784 | tf_op jit(solution)/shard_map/ppermute | solution.py:236
  39.7 3.0 %collective-permute-start.5 = (bf16[6,36,256]{2,1,0:T(8,128)(2,1)S(1)}, bf16[6,36,256]{2,1,0:T(8,128)(2,1)S(1)}, u32[]{:S(2)}, u32[]{:S(2)}) collective-permute-start(bf16[6,36,256]{2,1,0:T(8,128)(2,1)S(1)} %get-tuple-element.28), channel_id=1, source_target_pairs={{8,0},{16,8},{24,16},{9,1},{17,9},{25,17},{10,2},{18,10},{26,18},{... | collective-permute-start | bytes 331784 | tf_op jit(solution)/shard_map/ppermute | solution.py:237
  42.8 4.4 %fusion.297 = (f32[18,32]{1,0:T(8,128)S(1)}, f32[18,32,256]{2,1,0:T(8,128)S(1)}) fusion(f32[256]{0:T(256)S(1)} %bitcast.278, f32[256]{0:T(256)S(1)} %bitcast.281, f32[256]{0:T(256)S(1)} %bitcast.284, f32[256]{0:T(256)S(1)} %bitcast.287, f32[256]{0:T(256)S(1)} %bitcast.290, f32[256]{0:T(256)S(1)} %bitcast.293, f32[256]{0:T(256)S(1)} %bitcast.296, ...), kind=kLoop, calls=%fused_computation.535 | loop fusion | flops 14450112 | bytes 22269184 | tf_op jit(solution)/shard_map/reduce_sum | solution.py:155
  47.3 0.3 multiply_reduce_fusion.1
  47.6 0.2 multiply_convert_fusion.1
  47.8 0.9 %fusion.7 = bf16[576,1024]{1,0:T(8,128)(2,1)S(1)} fusion(bf16[576,256]{1,0:T(8,128)(2,1)S(1)} %bitcast.182, bf16[2,256,1024]{2,1,0:T(8,128)(2,1)S(1)} %copy-done.7), kind=kOutput, calls=%fused_computation.9 | convolution fusion | flops 307298304 | bytes 1998848 | tf_op jit(solution)/shard_map/dot_general | solution.py:159
  48.8 0.3 copy-done.1
  49.0 0.5 fusion.144
  49.5 0.1 fusion.85
  49.7 1.4 %fusion.299 = (f32[6,32]{1,0:T(8,128)S(1)}, f32[6,32,256]{2,1,0:T(8,128)S(1)}) fusion(f32[256]{0:T(256)S(1)} %bitcast.279, f32[256]{0:T(256)S(1)} %bitcast.282, f32[256]{0:T(256)S(1)} %bitcast.285, f32[256]{0:T(256)S(1)} %bitcast.288, f32[256]{0:T(256)S(1)} %bitcast.291, f32[256]{0:T(256)S(1)} %bitcast.294, f32[256]{0:T(256)S(1)} %bitcast.297, ...), kind=kLoop, calls=%fused_computation.536 | loop fusion | flops 4816704 | bytes 7620352 | tf_op jit(solution)/shard_map/reduce_sum | solution.py:155
  51.2 1.4 %fusion.295 = (f32[6,32]{1,0:T(8,128)S(1)}, f32[6,32,256]{2,1,0:T(8,128)S(1)}) fusion(f32[256]{0:T(256)S(1)} %bitcast.280, f32[256]{0:T(256)S(1)} %bitcast.283, f32[256]{0:T(256)S(1)} %bitcast.286, f32[256]{0:T(256)S(1)} %bitcast.289, f32[256]{0:T(256)S(1)} %bitcast.292, f32[256]{0:T(256)S(1)} %bitcast.295, f32[256]{0:T(256)S(1)} %bitcast.298, ...), kind=kLoop, calls=%fused_computation.534 | loop fusion | flops 4816704 | bytes 7620352 | tf_op jit(solution)/shard_map/reduce_sum | solution.py:155
  52.7 0.2 multiply_reduce_fusion.2
  52.9 0.2 multiply_reduce_fusion.3
  53.1 0.2 multiply_convert_fusion.3
  53.2 0.4 fusion.35
  53.7 0.3 fusion.142
  53.9 0.4 fusion.27
  54.4 0.3 fusion.146
  54.7 0.1 fusion.159
  54.9 4.4 %fusion.293 = (f32[24,24]{1,0:T(8,128)S(1)}, f32[24,24,256]{2,1,0:T(8,128)S(1)}) fusion(f32[256]{0:T(256)S(1)} %bitcast.367, f32[30,30,256]{2,1,0:T(8,128)S(1)} %fusion.159, f32[256]{0:T(256)S(1)} %bitcast.368, f32[256]{0:T(256)S(1)} %bitcast.369, f32[256]{0:T(256)S(1)} %bitcast.370, f32[256]{0:T(256)S(1)} %bitcast.371, f32[256]{0:T(256)S(1)} %bitcast.372, ...), kind=kLoop, calls=%fused_computation.533 | loop fusion | flops 14450112 | bytes 29543680 | tf_op jit(solution)/shard_map/reduce_sum | solution.py:155
  59.3 0.3 multiply_reduce_fusion
  59.6 0.2 multiply_convert_fusion
  59.8 0.9 %fusion.15 = bf16[576,1024]{1,0:T(8,128)(2,1)S(1)} fusion(bf16[576,256]{1,0:T(8,128)(2,1)S(1)} %bitcast.181, bf16[2,256,1024]{2,1,0:T(8,128)(2,1)S(1)} %copy-done.7), kind=kOutput, calls=%fused_computation.17 | convolution fusion | flops 307298304 | bytes 1998848 | tf_op jit(solution)/shard_map/dot_general | solution.py:159
  60.8 1.2 %fusion.18 = bf16[24,24,256]{2,1,0:T(8,128)(2,1)} fusion(bf16[24,24,1024]{2,1,0:T(8,128)(2,1)S(1)} %bitcast.387, f32[30,30,256]{2,1,0:T(8,128)S(1)} %fusion.159, bf16[2,1024,256]{2,1,0:T(8,128)(2,1)S(1)} %copy-done.1), kind=kOutput, calls=%fused_computation.23 | convolution fusion | flops 302284800 | bytes 2588672 | tf_op jit(solution)/shard_map/dot_general | solution.py:162
  (56 shorter events, 0.7 us)
Async XLA Ops:
  1.6 15.1 %copy-start.3 = (f32[2,7,7,256]{3,0,2,1:T(2,128)S(1)}, f32[2,7,7,256]{3,0,2,1:T(2,128)}, u32[]{:S(2)}) copy-start(f32[2,7,7,256]{3,0,2,1:T(2,128)} %param.22) | copy-start | bytes 301060
  9.9 7.1 %copy-start.4 = (f32[2,256]{1,0:T(2,128)S(1)}, f32[2,256]{1,0:T(2,128)}, u32[]{:S(2)}) copy-start(f32[2,256]{1,0:T(2,128)} %param.23) | copy-start | bytes 6148
  9.9 7.1 %copy-start = (bf16[2,256,256]{2,1,0:T(8,128)(2,1)S(1)}, bf16[2,256,256]{2,1,0:T(8,128)(2,1)}, u32[]{:S(2)}) copy-start(bf16[2,256,256]{2,1,0:T(8,128)(2,1)} %shard_map.127) | copy-start | bytes 786436
  9.9 17.1 %copy-start.5 = (s32[2]{0:T(128)S(1)}, s32[2]{0:T(128)}, u32[]{:S(2)}) copy-start(s32[2]{0:T(128)} %param.17) | copy-start | bytes 28
  9.9 17.2 %copy-start.6 = (s32[2]{0:T(128)S(1)}, s32[2]{0:T(128)}, u32[]{:S(2)}) copy-start(s32[2]{0:T(128)} %param.18) | copy-start | bytes 28
  11.3 9.4 %collective-permute-start.1 = (bf16[2,17,16,256]{3,2,1,0:T(8,128)(2,1)S(1)}, bf16[2,17,16,256]{3,2,1,0:T(8,128)(2,1)S(1)}, u32[]{:S(2)}, u32[]{:S(2)}) collective-permute-start(bf16[2,17,16,256]{3,2,1,0:T(8,128)(2,1)S(1)} %pad_maximum_fusion.3), channel_id=1, source_target_pairs={{8,0},{16,8},{24,16},{9,1},{17,9},{25,17},{10,2},{18,10},{26,18},{... | collective-permute-start | bytes 835592 | tf_op jit(solution)/shard_map/ppermute | solution.py:107
  14.5 12.3 %collective-permute-start = (bf16[2,17,16,256]{3,2,1,0:T(8,128)(2,1)S(1)}, bf16[2,17,16,256]{3,2,1,0:T(8,128)(2,1)S(1)}, u32[]{:S(2)}, u32[]{:S(2)}) collective-permute-start(bf16[2,17,16,256]{3,2,1,0:T(8,128)(2,1)S(1)} %pad_maximum_fusion.2), channel_id=1, source_target_pairs={{0,8},{8,16},{16,24},{1,9},{9,17},{17,25},{2,10},{10,18},{18,26},{... | collective-permute-start | bytes 835592 | tf_op jit(solution)/shard_map/ppermute | solution.py:107
  17.1 11.1 %copy-start.2 = (bf16[24,24,256]{2,1,0:T(8,128)(2,1)S(1)}, bf16[24,24,256]{2,1,0:T(8,128)(2,1)}, u32[]{:S(2)}) copy-start(bf16[24,24,256]{2,1,0:T(8,128)(2,1)} %param.21) | copy-start | bytes 884740
  28.7 4.4 %collective-permute-start.2 = (bf16[24,6,256]{2,1,0:T(8,128)(2,1)S(1)}, bf16[24,6,256]{2,1,0:T(8,128)(2,1)S(1)}, u32[]{:S(2)}, u32[]{:S(2)}) collective-permute-start(bf16[24,6,256]{2,1,0:T(8,128)(2,1)S(1)} %get-tuple-element.29), channel_id=1, source_target_pairs={{0,1},{1,2},{2,3},{3,4},{4,5},{5,6},{6,7},{7,0},{8,9},{9,10},{10,1... | collective-permute-start | bytes 221192 | tf_op jit(solution)/shard_map/ppermute | solution.py:117
  31.4 4.8 %collective-permute-start.3 = (bf16[24,6,256]{2,1,0:T(8,128)(2,1)S(1)}, bf16[24,6,256]{2,1,0:T(8,128)(2,1)S(1)}, u32[]{:S(2)}, u32[]{:S(2)}) collective-permute-start(bf16[24,6,256]{2,1,0:T(8,128)(2,1)S(1)} %get-tuple-element.30), channel_id=1, source_target_pairs={{1,0},{2,1},{3,2},{4,3},{5,4},{6,5},{7,6},{0,7},{9,8},{10,9},{11,1... | collective-permute-start | bytes 221192 | tf_op jit(solution)/shard_map/ppermute | solution.py:118
  36.4 14.8 %collective-permute-start.4 = (bf16[6,36,256]{2,1,0:T(8,128)(2,1)S(1)}, bf16[6,36,256]{2,1,0:T(8,128)(2,1)S(1)}, u32[]{:S(2)}, u32[]{:S(2)}) collective-permute-start(bf16[6,36,256]{2,1,0:T(8,128)(2,1)S(1)} %get-tuple-element.27), channel_id=1, source_target_pairs={{0,8},{8,16},{16,24},{1,9},{9,17},{17,25},{2,10},{10,18},{18,26},{... | collective-permute-start | bytes 331784 | tf_op jit(solution)/shard_map/ppermute | solution.py:236
  39.7 9.9 %collective-permute-start.5 = (bf16[6,36,256]{2,1,0:T(8,128)(2,1)S(1)}, bf16[6,36,256]{2,1,0:T(8,128)(2,1)S(1)}, u32[]{:S(2)}, u32[]{:S(2)}) collective-permute-start(bf16[6,36,256]{2,1,0:T(8,128)(2,1)S(1)} %get-tuple-element.28), channel_id=1, source_target_pairs={{8,0},{16,8},{24,16},{9,1},{17,9},{25,17},{10,2},{18,10},{26,18},{... | collective-permute-start | bytes 331784 | tf_op jit(solution)/shard_map/ppermute | solution.py:237
  42.8 5.0 %copy-start.7 = (bf16[2,256,1024]{2,1,0:T(8,128)(2,1)S(1)}, bf16[2,256,1024]{2,1,0:T(8,128)(2,1)}, u32[]{:S(2)}) copy-start(bf16[2,256,1024]{2,1,0:T(8,128)(2,1)} %param.24) | copy-start | bytes 3145732
  47.8 1.2 %copy-start.1 = (bf16[2,1024,256]{2,1,0:T(8,128)(2,1)S(1)}, bf16[2,1024,256]{2,1,0:T(8,128)(2,1)}, u32[]{:S(2)}) copy-start(bf16[2,1024,256]{2,1,0:T(8,128)(2,1)} %param.25) | copy-start | bytes 3145732

commit v10 on v9

--- a/solution.py
+++ b/solution.py
@@ -241,7 +241,10 @@
         up_weight[0],
         down_weight[0],
     )
-    middle = layer_apply(lon_wide, *first)
+    inner = layer_apply(state, *first)
+    west_part = layer_apply(lon_wide[:, : 4 * HALO], *first)
+    east_part = layer_apply(lon_wide[:, lon_wide.shape[1] - 4 * HALO :], *first)
+    middle = jnp.concatenate([west_part, inner, east_part], axis=1)
     top = layer_apply(jnp.concatenate([north, lon_wide[:reach]], axis=0), *first)
     bottom = layer_apply(jnp.concatenate([lon_wide[length - reach :], south], axis=0), *first)
     widened = jnp.concatenate([top, middle, bottom], axis=0)

time: 62.3 us -> 64.8 us (1.040)
  the two profiles are of different devices: /device:TPU:5 before, /device:TPU:0 now
where the time goes in v10:
time: 64.8 us; the launch traced here: 64.5 us
  other arithmetic  18.8 us (29%)
  starting transfers between devices  18.1 us (28%)
  matrix products  8.98 us (14%)
  waiting for transfers between devices  8.44 us (13%)
  Pallas kernels  8.17 us (13%)
  local copies, waits for them, and re-layouts  1.33 us (2%)
    reduce_sum x6, other arithmetic, layer_apply(): centered = mixed - jnp.mean(mixed, axis=-1, keepdims=True)  12.8 us
    pallas_call x1, Pallas kernels, conv_resample(): pl.pallas_call(_conv_body, grid=(n,), in_specs=[pl.BlockSpec((1, h, wd, c...  8.17 us
    ppermute x2, starting transfers between devices, shifted(): lax.ppermute(value, axis, [(source, source + steps) for source in range(l...  6.81 us
    ppermute x1, starting transfers between devices, per_device(): north = lax.ppermute(lon_wide[length - reach:], 'lat', up)  6.2 us
    dot_general x6, matrix products, layer_apply(): jnp.dot(hidden, down_matrix, preferred_element_type=jnp.float32)  5.27 us
    ppermute x2, waiting for transfers between devices, shifted(): lax.ppermute(value, axis, [(source, source + steps) for source in range(l...  5.26 us
    ppermute x1, starting transfers between devices, with_halo(): after = lax.ppermute(leading, axis, down)  3.53 us
    ppermute x1, waiting for transfers between devices, per_device(): south = lax.ppermute(lon_wide[:reach], 'lat', down)  3.17 us
  transfers between devices with their start and end apart: 6, of which 3 were waited for; matrix products, arithmetic and copies ran while one was open for 16% of the time, Pallas kernels for 0%

profile of v10, /device:TPU:0, one launch (start us, length us, event | category | flops | bytes accessed | tf_op | source)
XLA Modules:
  0.0 64.5 jit_solution(462987220402282760)
XLA Ops:
  0.0 0.7 %compare_bitcast_fusion = (pred[2]{0:T(512)(128)(4,1)S(1)}, pred[2]{0:T(512)(128)(4,1)S(1)}, pred[2]{0:T(512)(128)(4,1)S(1)}) fusion(s32[2,1]{0,1:T(1,128)} %param.16, s32[]{:T(128)S(6)} %axis_index.15), kind=kLoop, calls=%fused_computation.822 | loop fusion | flops 8 | bytes 18 | tf_op jit(solution)/shard_map/eq | solution.py:192
  0.7 0.1 fusion.515
  0.8 0.8 %select_reduce_fusion.4 = (s32[2]{0:T(128)S(1)}, s32[2]{0:T(128)S(1)}, s32[2]{0:T(128)S(1)}, s32[2]{0:T(128)S(1)}, pred[2,2]{1,0:T(4,128)(4,1)S(1)}, /*index=5*/pred[2,2]{1,0:T(4,128)(4,1)S(1)}) fusion(s32[2]{0:T(128)} %param.18, s32[2]{0:T(128)} %param.17, pred[2]{0:T(512)(128)(4,1)S(1)} %get-tuple-element.142, s32[2]{0:T(128)S(1)} %get-tuple-element.147, ...), kind=kLoop, calls=%fused_computation.838 | loop fusion | flops 40 | bytes 76 | tf_op jit(solution)/shard_map/reduce_sum | solution.py:129
  1.6 8.2 %shard_map.127 = bf16[2,256,256]{2,1,0:T(8,128)(2,1)} custom-call(bf16[2,64,64,256]{3,2,1,0:T(8,128)(2,1)} %x_ref.1, bf16[3,3,256,256]{3,2,1,0:T(8,128)(2,1)} %w_ref.1, f32[1,256]{1,0:T(1,128)} %bitcast.524, bf16[2,16,32]{2,1,0:T(8,128)(2,1)} %r_ref.1, bf16[2,16,32]{2,1,0:T(8,128)(2,1)} %c_ref.1), custom_call_target="tpu_custom_call" | custom-call | tf_op jit(solution)/shard_map/pallas_call | solution.py:86
  9.9 1.3 %select_reduce_fusion.1 = (bf16[2,16,16,256]{3,2,1,0:T(8,128)(2,1)S(1)}, bf16[2,16,16,256]{3,2,1,0:T(8,128)(2,1)S(1)}) fusion(pred[2,2]{1,0:T(4,128)(4,1)S(1)} %get-tuple-element.28, bf16[2,16,16,256]{3,2,1,0:T(8,128)(2,1)} %bitcast.216, pred[2,2]{1,0:T(4,128)(4,1)S(1)} %get-tuple-element.27), kind=kLoop, calls=%fused_computation.229 | loop fusion | flops 786432 | bytes 786440 | tf_op jit(solution)/shard_map/reduce_sum | solution.py:125
  11.3 1.3 %collective-permute-start.1 = (bf16[2,17,16,256]{3,2,1,0:T(8,128)(2,1)S(1)}, bf16[2,17,16,256]{3,2,1,0:T(8,128)(2,1)S(1)}, u32[]{:S(2)}, u32[]{:S(2)}) collective-permute-start(bf16[2,17,16,256]{3,2,1,0:T(8,128)(2,1)S(1)} %pad_maximum_fusion.2), channel_id=1, source_target_pairs={{8,0},{16,8},{24,16},{9,1},{17,9},{25,17},{10,2},{18,10},{26,18},{... | collective-permute-start | bytes 835592 | tf_op jit(solution)/shard_map/ppermute | solution.py:107
  12.7 5.5 %collective-permute-start = (bf16[2,17,16,256]{3,2,1,0:T(8,128)(2,1)S(1)}, bf16[2,17,16,256]{3,2,1,0:T(8,128)(2,1)S(1)}, u32[]{:S(2)}, u32[]{:S(2)}) collective-permute-start(bf16[2,17,16,256]{3,2,1,0:T(8,128)(2,1)S(1)} %pad_maximum_fusion.1), channel_id=1, source_target_pairs={{0,8},{8,16},{16,24},{1,9},{9,17},{17,25},{2,10},{10,18},{18,26},{... | collective-permute-start | bytes 835592 | tf_op jit(solution)/shard_map/ppermute | solution.py:107
  18.5 0.1 broadcast_select_fusion
  18.6 5.1 %collective-permute-done.1 = bf16[2,17,16,256]{3,2,1,0:T(8,128)(2,1)S(1)} collective-permute-done((bf16[2,17,16,256]{3,2,1,0:T(8,128)(2,1)S(1)}, bf16[2,17,16,256]{3,2,1,0:T(8,128)(2,1)S(1)}, u32[]{:S(2)}, u32[]{:S(2)}) %collective-permute-start.1) | collective-permute-done | bytes 278560 | tf_op jit(solution)/shard_map/ppermute | solution.py:107
  23.7 0.2 slice_reduce_fusion
  23.9 0.2 collective-permute-done
  24.1 0.2 slice_reduce_fusion.1
  24.6 0.1 pad_maximum_fusion
  24.7 0.8 %convolution_convert_fusion = bf16[6,24,16,256]{3,1,2,0:T(8,128)(2,1)S(1)} fusion(bf16[6,16,16,256]{3,2,1,0:T(8,128)(2,1)S(1)} %pad_maximum_fusion, s32[6,16]{1,0:T(8,128)S(1)} %iota_add_fusion.1), kind=kOutput, calls=%fused_computation.60 | convolution fusion | flops 19466496 | bytes 1966464 | tf_op jit(solution)/shard_map/shr,sruc->shuc/dot_general | solution.py:226
  25.6 0.4 fusion.546
  26.1 3.5 %collective-permute-start.3 = (bf16[24,6,256]{2,1,0:T(8,128)(2,1)S(1)}, bf16[24,6,256]{2,1,0:T(8,128)(2,1)S(1)}, u32[]{:S(2)}, u32[]{:S(2)}) collective-permute-start(bf16[24,6,256]{2,1,0:T(8,128)(2,1)S(1)} %get-tuple-element.34), channel_id=1, source_target_pairs={{1,0},{2,1},{3,2},{4,3},{5,4},{6,5},{7,6},{0,7},{9,8},{10,9},{11,1... | collective-permute-start | bytes 221192 | tf_op jit(solution)/shard_map/ppermute | solution.py:118
  29.7 3.4 %fusion.531 = (f32[18,24]{1,0:T(8,128)S(1)}, f32[18,24,256]{2,1,0:T(8,128)S(1)}) fusion(f32[256]{0:T(256)S(1)} %bitcast.378, f32[256]{0:T(256)S(1)} %bitcast.383, f32[256]{0:T(256)S(1)} %bitcast.388, f32[256]{0:T(256)S(1)} %bitcast.393, f32[256]{0:T(256)S(1)} %bitcast.398, f32[256]{0:T(256)S(1)} %bitcast.403, f32[256]{0:T(256)S(1)} %bitcast.408, ...), kind=kLoop, calls=%fused_computation.857 | loop fusion | flops 10837584 | bytes 4180672 | tf_op jit(solution)/shard_map/reduce_sum | solution.py:155
  33.1 0.2 multiply_reduce_fusion.1
  33.3 0.2 multiply_convert_fusion.1
  33.6 0.7 %fusion.15 = bf16[432,1024]{1,0:T(8,128)(2,1)S(1)} fusion(bf16[432,256]{1,0:T(8,128)(2,1)S(1)} %bitcast.220, bf16[2,256,1024]{2,1,0:T(8,128)(2,1)S(1)} %copy-done.7), kind=kOutput, calls=%fused_computation.59 | convolution fusion | flops 230473728 | bytes 1630208 | tf_op jit(solution)/shard_map/dot_general | solution.py:159
  34.3 0.5 copy-done.1
  34.8 0.4 fusion.107
  35.3 0.1 fusion.303
  35.4 1.1 %fusion.529 = (f32[18,8]{1,0:T(8,128)S(1)}, f32[18,8,256]{2,1,0:T(8,128)S(1)}) fusion(f32[256]{0:T(256)S(1)} %bitcast.379, f32[256]{0:T(256)S(1)} %bitcast.384, f32[256]{0:T(256)S(1)} %bitcast.389, f32[256]{0:T(256)S(1)} %bitcast.394, f32[256]{0:T(256)S(1)} %bitcast.399, f32[256]{0:T(256)S(1)} %bitcast.404, f32[256]{0:T(256)S(1)} %bitcast.409, ...), kind=kLoop, calls=%fused_computation.856 | loop fusion | flops 3612528 | bytes 5752384 | tf_op jit(solution)/shard_map/reduce_sum | solution.py:155
  36.5 1.1 %fusion.533 = (f32[18,8]{1,0:T(8,128)S(1)}, f32[18,8,256]{2,1,0:T(8,128)S(1)}) fusion(f32[256]{0:T(256)S(1)} %bitcast.380, f32[256]{0:T(256)S(1)} %bitcast.385, f32[256]{0:T(256)S(1)} %bitcast.390, f32[256]{0:T(256)S(1)} %bitcast.395, f32[256]{0:T(256)S(1)} %bitcast.400, f32[256]{0:T(256)S(1)} %bitcast.405, f32[256]{0:T(256)S(1)} %bitcast.410, ...), kind=kLoop, calls=%fused_computation.858 | loop fusion | flops 3612528 | bytes 5752384 | tf_op jit(solution)/shard_map/reduce_sum | solution.py:155
  37.6 0.1 pad_maximum_fusion.7
  37.7 6.2 %collective-permute-start.4 = (bf16[6,36,256]{2,1,0:T(8,128)(2,1)S(1)}, bf16[6,36,256]{2,1,0:T(8,128)(2,1)S(1)}, u32[]{:S(2)}, u32[]{:S(2)}) collective-permute-start(bf16[6,36,256]{2,1,0:T(8,128)(2,1)S(1)} %get-tuple-element.29), channel_id=1, source_target_pairs={{0,8},{8,16},{16,24},{1,9},{9,17},{17,25},{2,10},{10,18},{18,26},{... | collective-permute-start | bytes 331784 | tf_op jit(solution)/shard_map/ppermute | solution.py:236
  43.9 1.5 %collective-permute-start.5 = (bf16[6,36,256]{2,1,0:T(8,128)(2,1)S(1)}, bf16[6,36,256]{2,1,0:T(8,128)(2,1)S(1)}, u32[]{:S(2)}, u32[]{:S(2)}) collective-permute-start(bf16[6,36,256]{2,1,0:T(8,128)(2,1)S(1)} %get-tuple-element.30), channel_id=1, source_target_pairs={{8,0},{16,8},{24,16},{9,1},{17,9},{25,17},{10,2},{18,10},{26,18},{... | collective-permute-start | bytes 331784 | tf_op jit(solution)/shard_map/ppermute | solution.py:237
  45.4 0.2 multiply_reduce_fusion.5
  45.6 1.5 %fusion.109 = f32[18,8,256]{2,1,0:T(8,128)S(1)} fusion(bf16[2,1024,256]{2,1,0:T(8,128)(2,1)S(1)} %copy-done.1, bf16[2,256,1024]{2,1,0:T(8,128)(2,1)} %param.24, f32[18,8,256]{2,1,0:T(8,128)S(1)} %get-tuple-element.20, f32[256]{0:T(256)S(1)} %bitcast.469, f32[18,8]{1,0:T(8,128)S(1)} %add_rsqrt_fusion.3, f32[18,8]{1,0:T(8,128)S(1)} %broadcast_multiply_fusion.3), kind=kOutput, calls=%fused_computation.211 | convolution fusion | flops 152469504 | bytes 1369088 | tf_op jit(solution)/shard_map/dot_general | solution.py:162
  47.2 0.2 multiply_reduce_fusion.4
  47.3 1.5 %fusion.105 = f32[18,8,256]{2,1,0:T(8,128)S(1)} fusion(bf16[2,1024,256]{2,1,0:T(8,128)(2,1)S(1)} %copy-done.1, bf16[2,256,1024]{2,1,0:T(8,128)(2,1)} %param.24, f32[18,8,256]{2,1,0:T(8,128)S(1)} %get-tuple-element.24, f32[18,8]{1,0:T(8,128)S(1)} %add_rsqrt_fusion.1, f32[18,8]{1,0:T(8,128)S(1)} %broadcast_multiply_fusion.2, f32[256]{0:T(256)S(1)} %bitcast.470), kind=kOutput, calls=%fused_computation.207 | convolution fusion | flops 152469504 | bytes 1369088 | tf_op jit(solution)/shard_map/dot_general | solution.py:162
  48.9 3.2 %collective-permute-done.5 = bf16[6,36,256]{2,1,0:T(8,128)(2,1)S(1)} collective-permute-done((bf16[6,36,256]{2,1,0:T(8,128)(2,1)S(1)}, bf16[6,36,256]{2,1,0:T(8,128)(2,1)S(1)}, u32[]{:S(2)}, u32[]{:S(2)}) %collective-permute-start.5) | collective-permute-done | bytes 110624 | tf_op jit(solution)/shard_map/ppermute | solution.py:237
  52.1 1.4 %fusion.535 = (f32[6,32]{1,0:T(8,128)S(1)}, f32[6,32,256]{2,1,0:T(8,128)S(1)}) fusion(f32[256]{0:T(256)S(1)} %bitcast.381, f32[256]{0:T(256)S(1)} %bitcast.386, f32[256]{0:T(256)S(1)} %bitcast.391, f32[256]{0:T(256)S(1)} %bitcast.396, f32[256]{0:T(256)S(1)} %bitcast.401, f32[256]{0:T(256)S(1)} %bitcast.406, f32[256]{0:T(256)S(1)} %bitcast.411, ...), kind=kLoop, calls=%fused_computation.859 | loop fusion | flops 4816704 | bytes 7620352 | tf_op jit(solution)/shard_map/reduce_sum | solution.py:155
  53.7 1.4 %fusion.527 = (f32[6,32]{1,0:T(8,128)S(1)}, f32[6,32,256]{2,1,0:T(8,128)S(1)}) fusion(f32[256]{0:T(256)S(1)} %bitcast.382, f32[256]{0:T(256)S(1)} %bitcast.387, f32[256]{0:T(256)S(1)} %bitcast.392, f32[256]{0:T(256)S(1)} %bitcast.397, f32[256]{0:T(256)S(1)} %bitcast.402, f32[256]{0:T(256)S(1)} %bitcast.407, f32[256]{0:T(256)S(1)} %bitcast.412, ...), kind=kLoop, calls=%fused_computation.855 | loop fusion | flops 4816704 | bytes 7620352 | tf_op jit(solution)/shard_map/reduce_sum | solution.py:155
  55.1 0.2 multiply_reduce_fusion.2
  55.3 0.2 multiply_reduce_fusion.3
  55.5 0.2 multiply_convert_fusion.3
  55.7 0.4 fusion.35
  56.1 0.3 fusion.103
  56.4 0.4 fusion.27
  56.9 0.3 fusion.111
  57.2 0.2 fusion.142
  57.4 4.4 %fusion.525 = (f32[24,24]{1,0:T(8,128)S(1)}, f32[24,24,256]{2,1,0:T(8,128)S(1)}) fusion(f32[256]{0:T(256)S(1)} %bitcast.505, f32[30,30,256]{2,1,0:T(8,128)S(1)} %fusion.142, f32[256]{0:T(256)S(1)} %bitcast.506, f32[256]{0:T(256)S(1)} %bitcast.507, f32[256]{0:T(256)S(1)} %bitcast.508, f32[256]{0:T(256)S(1)} %bitcast.509, f32[256]{0:T(256)S(1)} %bitcast.510, ...), kind=kLoop, calls=%fused_computation.854 | loop fusion | flops 14450112 | bytes 29543680 | tf_op jit(solution)/shard_map/reduce_sum | solution.py:155
  61.8 0.3 multiply_reduce_fusion
  62.1 0.2 multiply_convert_fusion
  62.3 0.9 %fusion.7 = bf16[576,1024]{1,0:T(8,128)(2,1)S(1)} fusion(bf16[576,256]{1,0:T(8,128)(2,1)S(1)} %bitcast.219, bf16[2,256,1024]{2,1,0:T(8,128)(2,1)S(1)} %copy-done.8), kind=kOutput, calls=%fused_computation.51 | convolution fusion | flops 307298304 | bytes 1998848 | tf_op jit(solution)/shard_map/dot_general | solution.py:159
  63.2 1.2 %fusion.18 = bf16[24,24,256]{2,1,0:T(8,128)(2,1)} fusion(bf16[24,24,1024]{2,1,0:T(8,128)(2,1)S(1)} %bitcast.525, f32[30,30,256]{2,1,0:T(8,128)S(1)} %fusion.142, bf16[2,1024,256]{2,1,0:T(8,128)(2,1)S(1)} %copy-done.1), kind=kOutput, calls=%fused_computation.65 | convolution fusion | flops 302284800 | bytes 2588672 | tf_op jit(solution)/shard_map/dot_general | solution.py:162
  (72 shorter events, 1.3 us)
Async XLA Ops:
  9.8 8.4 %copy-start.3 = (f32[2,7,7,256]{3,0,2,1:T(2,128)S(1)}, f32[2,7,7,256]{3,0,2,1:T(2,128)}, u32[]{:S(2)}) copy-start(f32[2,7,7,256]{3,0,2,1:T(2,128)} %param.22) | copy-start | bytes 301060
  9.8 8.6 %copy-start.4 = (f32[2,256]{1,0:T(2,128)S(1)}, f32[2,256]{1,0:T(2,128)}, u32[]{:S(2)}) copy-start(f32[2,256]{1,0:T(2,128)} %param.23) | copy-start | bytes 6148
  9.8 8.7 %copy-start = (bf16[2,256,256]{2,1,0:T(8,128)(2,1)S(1)}, bf16[2,256,256]{2,1,0:T(8,128)(2,1)}, u32[]{:S(2)}) copy-start(bf16[2,256,256]{2,1,0:T(8,128)(2,1)} %shard_map.127) | copy-start | bytes 786436
  9.8 14.4 %copy-start.5 = (s32[2]{0:T(128)S(1)}, s32[2]{0:T(128)}, u32[]{:S(2)}) copy-start(s32[2]{0:T(128)} %param.17) | copy-start | bytes 28
  9.8 14.6 %copy-start.6 = (s32[2]{0:T(128)S(1)}, s32[2]{0:T(128)}, u32[]{:S(2)}) copy-start(s32[2]{0:T(128)} %param.18) | copy-start | bytes 28
  11.3 12.4 %collective-permute-start.1 = (bf16[2,17,16,256]{3,2,1,0:T(8,128)(2,1)S(1)}, bf16[2,17,16,256]{3,2,1,0:T(8,128)(2,1)S(1)}, u32[]{:S(2)}, u32[]{:S(2)}) collective-permute-start(bf16[2,17,16,256]{3,2,1,0:T(8,128)(2,1)S(1)} %pad_maximum_fusion.2), channel_id=1, source_target_pairs={{8,0},{16,8},{24,16},{9,1},{17,9},{25,17},{10,2},{18,10},{26,18},{... | collective-permute-start | bytes 835592 | tf_op jit(solution)/shard_map/ppermute | solution.py:107
  12.7 11.4 %collective-permute-start = (bf16[2,17,16,256]{3,2,1,0:T(8,128)(2,1)S(1)}, bf16[2,17,16,256]{3,2,1,0:T(8,128)(2,1)S(1)}, u32[]{:S(2)}, u32[]{:S(2)}) collective-permute-start(bf16[2,17,16,256]{3,2,1,0:T(8,128)(2,1)S(1)} %pad_maximum_fusion.1), channel_id=1, source_target_pairs={{0,8},{8,16},{16,24},{1,9},{9,17},{17,25},{2,10},{10,18},{18,26},{... | collective-permute-start | bytes 835592 | tf_op jit(solution)/shard_map/ppermute | solution.py:107
  24.6 1.0 %copy-start.2 = (bf16[24,24,256]{2,1,0:T(8,128)(2,1)S(1)}, bf16[24,24,256]{2,1,0:T(8,128)(2,1)}, u32[]{:S(2)}) copy-start(bf16[24,24,256]{2,1,0:T(8,128)(2,1)} %param.21) | copy-start | bytes 884740
  26.0 9.2 %collective-permute-start.2 = (bf16[24,6,256]{2,1,0:T(8,128)(2,1)S(1)}, bf16[24,6,256]{2,1,0:T(8,128)(2,1)S(1)}, u32[]{:S(2)}, u32[]{:S(2)}) collective-permute-start(bf16[24,6,256]{2,1,0:T(8,128)(2,1)S(1)} %get-tuple-element.33), channel_id=1, source_target_pairs={{0,1},{1,2},{2,3},{3,4},{4,5},{5,6},{6,7},{7,0},{8,9},{9,10},{10,1... | collective-permute-start | bytes 221192 | tf_op jit(solution)/shard_map/ppermute | solution.py:117
  26.1 9.2 %collective-permute-start.3 = (bf16[24,6,256]{2,1,0:T(8,128)(2,1)S(1)}, bf16[24,6,256]{2,1,0:T(8,128)(2,1)S(1)}, u32[]{:S(2)}, u32[]{:S(2)}) collective-permute-start(bf16[24,6,256]{2,1,0:T(8,128)(2,1)S(1)} %get-tuple-element.34), channel_id=1, source_target_pairs={{1,0},{2,1},{3,2},{4,3},{5,4},{6,5},{7,6},{0,7},{9,8},{10,9},{11,1... | collective-permute-start | bytes 221192 | tf_op jit(solution)/shard_map/ppermute | solution.py:118
  29.7 3.9 %copy-start.7 = (bf16[2,256,1024]{2,1,0:T(8,128)(2,1)S(1)}, bf16[2,256,1024]{2,1,0:T(8,128)(2,1)}, u32[]{:S(2)}) copy-start(bf16[2,256,1024]{2,1,0:T(8,128)(2,1)} %param.24) | copy-start | bytes 3145732
  33.5 1.2 %copy-start.1 = (bf16[2,1024,256]{2,1,0:T(8,128)(2,1)S(1)}, bf16[2,1024,256]{2,1,0:T(8,128)(2,1)}, u32[]{:S(2)}) copy-start(bf16[2,1024,256]{2,1,0:T(8,128)(2,1)} %param.25) | copy-start | bytes 3145732
  37.7 15.9 %collective-permute-start.4 = (bf16[6,36,256]{2,1,0:T(8,128)(2,1)S(1)}, bf16[6,36,256]{2,1,0:T(8,128)(2,1)S(1)}, u32[]{:S(2)}, u32[]{:S(2)}) collective-permute-start(bf16[6,36,256]{2,1,0:T(8,128)(2,1)S(1)} %get-tuple-element.29), channel_id=1, source_target_pairs={{0,8},{8,16},{16,24},{1,9},{9,17},{17,25},{2,10},{10,18},{18,26},{... | collective-permute-start | bytes 331784 | tf_op jit(solution)/shard_map/ppermute | solution.py:236
  43.9 8.2 %collective-permute-start.5 = (bf16[6,36,256]{2,1,0:T(8,128)(2,1)S(1)}, bf16[6,36,256]{2,1,0:T(8,128)(2,1)S(1)}, u32[]{:S(2)}, u32[]{:S(2)}) collective-permute-start(bf16[6,36,256]{2,1,0:T(8,128)(2,1)S(1)} %get-tuple-element.30), channel_id=1, source_target_pairs={{8,0},{16,8},{24,16},{9,1},{17,9},{25,17},{10,2},{18,10},{26,18},{... | collective-permute-start | bytes 331784 | tf_op jit(solution)/shard_map/ppermute | solution.py:237
  53.7 2.0 %copy-start.8 = (bf16[2,256,1024]{2,1,0:T(8,128)(2,1)S(1)}, bf16[2,256,1024]{2,1,0:T(8,128)(2,1)}, u32[]{:S(2)}) copy-start(bf16[2,256,1024]{2,1,0:T(8,128)(2,1)} %param.24) | copy-start | bytes 3145732

commit v11 on v9

--- a/solution.py
+++ b/solution.py
@@ -137,33 +137,31 @@
 def depthwise(widened, depth_kernel, height, width):
     mixed = None
     for e in range(KS):
-        column = widened[:, e : e + width]
+        column = widened[..., e : e + width, :]
         for a in range(KS):
-            term = column[a : a + height] * depth_kernel[a, e]
+            term = column[..., a : a + height, :, :] * depth_kernel[a, e]
             mixed = term if mixed is None else mixed + term
     return mixed
 
 
 def layer_apply(padded, depth_kernel, gain, up_matrix, down_matrix):
-    height = padded.shape[0] - (KS - 1)
-    width = padded.shape[1] - (KS - 1)
+    height = padded.shape[-3] - (KS - 1)
+    width = padded.shape[-2] - (KS - 1)
     spare = -width % 8
     widened = padded.astype(jnp.float32)
     if spare:
-        widened = jnp.pad(widened, ((0, 0), (0, spare), (0, 0)))
+        widened = jnp.pad(widened, [(0, 0)] * (widened.ndim - 2) + [(0, spare), (0, 0)])
     mixed = depthwise(widened, depth_kernel, height, width + spare)
     centered = mixed - jnp.mean(mixed, axis=-1, keepdims=True)
     variance = jnp.mean(centered * centered, axis=-1, keepdims=True)
     normed = (centered * lax.rsqrt(variance + 1e-06) * gain).astype(jnp.bfloat16)
-    flat_cells = normed.reshape(height * (width + spare), -1)
+    flat_cells = normed.reshape(-1, normed.shape[-1])
     hidden = jax.nn.gelu(jnp.dot(flat_cells, up_matrix, preferred_element_type=jnp.float32)).astype(
         jnp.bfloat16
     )
-    output = jnp.dot(hidden, down_matrix, preferred_element_type=jnp.float32).reshape(
-        height, width + spare, -1
-    )
-    residual_part = widened[HALO : HALO + height, HALO : HALO + width + spare]
-    return (residual_part + output).astype(jnp.bfloat16)[:, :width]
+    output = jnp.dot(hidden, down_matrix, preferred_element_type=jnp.float32).reshape(normed.shape)
+    residual_part = widened[..., HALO : HALO + height, HALO : HALO + width + spare, :]
+    return (residual_part + output).astype(jnp.bfloat16)[..., :width, :]
 
 
 def per_device(
@@ -235,29 +233,34 @@
     down = [(j, i) for i, j in up]
     north = lax.ppermute(lon_wide[length - reach :], "lat", up)
     south = lax.ppermute(lon_wide[:reach], "lat", down)
-    first = (
-        depth_weight[0],
-        norm_gain[0],
-        up_weight[0],
-        down_weight[0],
-    )
+    first = (depth_weight[0], norm_gain[0], up_weight[0], down_weight[0])
+    second = (depth_weight[1], norm_gain[1], up_weight[1], down_weight[1])
     middle = layer_apply(lon_wide, *first)
-    top = layer_apply(jnp.concatenate([north, lon_wide[:reach]], axis=0), *first)
-    bottom = layer_apply(jnp.concatenate([lon_wide[length - reach :], south], axis=0), *first)
-    widened = jnp.concatenate([top, middle, bottom], axis=0)
+    later_middle = layer_apply(middle, *second)
+    edges = jnp.stack(
+        [
+            jnp.concatenate([north, lon_wide[:reach]], axis=0),
+            jnp.concatenate([lon_wide[length - reach :], south], axis=0),
+        ]
+    )
+    outer = layer_apply(edges, *first)
     first_row = own_band * tile_rows
-    margin = (widened.shape[0] - tile_rows) // 2
-    grid_row = first_row - margin + jnp.arange(widened.shape[0], dtype=jnp.int32)
-    inside = (grid_row >= 0) & (grid_row < bands * tile_rows)
-    widened = jnp.where(inside[:, None, None], widened, jnp.zeros_like(widened))
-    for layer_index in range(1, LAYERS):
-        widened = layer_apply(
-            widened,
-            depth_weight[layer_index],
-            norm_gain[layer_index],
-            up_weight[layer_index],
-            down_weight[layer_index],
-        )
+    outer_rows = jnp.stack(
+        [
+            first_row - HALO + jnp.arange(reach, dtype=jnp.int32),
+            first_row + tile_rows + HALO - reach + jnp.arange(reach, dtype=jnp.int32),
+        ]
+    )
+    inside = (outer_rows >= 0) & (outer_rows < bands * tile_rows)
+    outer = jnp.where(inside[:, :, None, None], outer, jnp.zeros_like(outer))
+    later_edges = jnp.stack(
+        [
+            jnp.concatenate([outer[0], middle[:reach]], axis=0),
+            jnp.concatenate([middle[middle.shape[0] - reach :], outer[1]], axis=0),
+        ]
+    )
+    later_outer = layer_apply(later_edges, *second)
+    widened = jnp.concatenate([later_outer[0], later_middle, later_outer[1]], axis=0)
     return widened
 
 

time: 62.3 us -> 68.5 us (1.100)
  the two profiles are of different devices: /device:TPU:5 before, /device:TPU:0 now
where the time goes in v11:
time: 68.5 us; the launch traced here: 68.1 us
  other arithmetic  18.7 us (27%)
  starting transfers between devices  18.1 us (26%)
  waiting for transfers between devices  15.4 us (22%)
  Pallas kernels  8.17 us (12%)
  matrix products  5.41 us (8%)
  local copies, waits for them, and re-layouts  1.89 us (3%)
    reduce_sum x4, other arithmetic, layer_apply(): centered = mixed - jnp.mean(mixed, axis=-1, keepdims=True)  12.1 us
    pallas_call x1, Pallas kernels, conv_resample(): pl.pallas_call(_conv_body, grid=(n,), in_specs=[pl.BlockSpec((1, h, wd, c...  8.17 us
    ppermute x1, waiting for transfers between devices, per_device(): south = lax.ppermute(lon_wide[:reach], 'lat', down)  7.75 us
    ppermute x2, starting transfers between devices, shifted(): lax.ppermute(value, axis, [(source, source + steps) for source in range(l...  6.81 us
    ppermute x1, starting transfers between devices, per_device(): north = lax.ppermute(lon_wide[length - reach:], 'lat', up)  6.21 us
    ppermute x2, waiting for transfers between devices, shifted(): lax.ppermute(value, axis, [(source, source + steps) for source in range(l...  5.26 us
    ppermute x1, starting transfers between devices, with_halo(): after = lax.ppermute(leading, axis, down)  3.53 us
    dot_general x4, matrix products, layer_apply(): jnp.dot(flat_cells, up_matrix, preferred_element_type=jnp.float32)  2.66 us
  transfers between devices with their start and end apart: 6, of which 4 were waited for; matrix products, arithmetic and copies ran while one was open for 15% of the time, Pallas kernels for 0%

profile of v11, /device:TPU:0, one launch (start us, length us, event | category | flops | bytes accessed | tf_op | source)
XLA Modules:
  0.0 68.1 jit_solution(2802733928693973375)
XLA Ops:
  0.0 0.7 compare_bitcast_fusion
  0.7 0.1 fusion.278
  0.8 0.8 %select_reduce_fusion.4 = (s32[2]{0:T(128)S(1)}, s32[2]{0:T(128)S(1)}, s32[2]{0:T(128)S(1)}, s32[2]{0:T(128)S(1)}, pred[2,2]{1,0:T(4,128)(4,1)S(1)}, /*index=5*/pred[2,2]{1,0:T(4,128)(4,1)S(1)}) fusion(s32[2]{0:T(128)} %param.18, s32[2]{0:T(128)} %param.17, pred[2]{0:T(512)(128)(4,1)S(1)} %get-tuple-element.142, s32[2]{0:T(128)S(1)} %get-tuple-element.145, ...), kind=kLoop, calls=%fused_computation.525 | loop fusion | flops 40 | bytes 76 | tf_op jit(solution)/shard_map/reduce_sum | solution.py:129
  1.6 8.2 %shard_map.127 = bf16[2,256,256]{2,1,0:T(8,128)(2,1)} custom-call(bf16[2,64,64,256]{3,2,1,0:T(8,128)(2,1)} %x_ref.1, bf16[3,3,256,256]{3,2,1,0:T(8,128)(2,1)} %w_ref.1, f32[1,256]{1,0:T(1,128)} %bitcast.409, bf16[2,16,32]{2,1,0:T(8,128)(2,1)} %r_ref.1, bf16[2,16,32]{2,1,0:T(8,128)(2,1)} %c_ref.1), custom_call_target="tpu_custom_call" | custom-call | tf_op jit(solution)/shard_map/pallas_call | solution.py:86
  9.8 1.4 %select_reduce_fusion.1 = (bf16[2,16,16,256]{3,2,1,0:T(8,128)(2,1)S(1)}, bf16[2,16,16,256]{3,2,1,0:T(8,128)(2,1)S(1)}) fusion(pred[2,2]{1,0:T(4,128)(4,1)S(1)} %get-tuple-element.24, bf16[2,16,16,256]{3,2,1,0:T(8,128)(2,1)} %bitcast.202, pred[2,2]{1,0:T(4,128)(4,1)S(1)} %get-tuple-element.23), kind=kLoop, calls=%fused_computation.157 | loop fusion | flops 786432 | bytes 786440 | tf_op jit(solution)/shard_map/reduce_sum | solution.py:125
  11.2 0.1 select_convert_fusion.1
  11.3 1.3 %collective-permute-start.1 = (bf16[2,17,16,256]{3,2,1,0:T(8,128)(2,1)S(1)}, bf16[2,17,16,256]{3,2,1,0:T(8,128)(2,1)S(1)}, u32[]{:S(2)}, u32[]{:S(2)}) collective-permute-start(bf16[2,17,16,256]{3,2,1,0:T(8,128)(2,1)S(1)} %pad_maximum_fusion.4), channel_id=1, source_target_pairs={{8,0},{16,8},{24,16},{9,1},{17,9},{25,17},{10,2},{18,10},{26,18},{... | collective-permute-start | bytes 835592 | tf_op jit(solution)/shard_map/ppermute | solution.py:107
  12.7 5.5 %collective-permute-start = (bf16[2,17,16,256]{3,2,1,0:T(8,128)(2,1)S(1)}, bf16[2,17,16,256]{3,2,1,0:T(8,128)(2,1)S(1)}, u32[]{:S(2)}, u32[]{:S(2)}) collective-permute-start(bf16[2,17,16,256]{3,2,1,0:T(8,128)(2,1)S(1)} %pad_maximum_fusion.3), channel_id=1, source_target_pairs={{0,8},{8,16},{16,24},{1,9},{9,17},{17,25},{2,10},{10,18},{18,26},{... | collective-permute-start | bytes 835592 | tf_op jit(solution)/shard_map/ppermute | solution.py:107
  18.2 0.1 fusion.292
  18.5 0.1 broadcast_select_fusion
  18.6 5.1 %collective-permute-done.1 = bf16[2,17,16,256]{3,2,1,0:T(8,128)(2,1)S(1)} collective-permute-done((bf16[2,17,16,256]{3,2,1,0:T(8,128)(2,1)S(1)}, bf16[2,17,16,256]{3,2,1,0:T(8,128)(2,1)S(1)}, u32[]{:S(2)}, u32[]{:S(2)}) %collective-permute-start.1) | collective-permute-done | bytes 278560 | tf_op jit(solution)/shard_map/ppermute | solution.py:107
  23.7 0.2 slice_reduce_fusion
  23.9 0.2 collective-permute-done
  24.1 0.2 slice_reduce_fusion.1
  24.6 0.1 pad_maximum_fusion
  24.7 0.8 %convolution_convert_fusion = bf16[6,24,16,256]{3,1,2,0:T(8,128)(2,1)S(1)} fusion(bf16[6,16,16,256]{3,2,1,0:T(8,128)(2,1)S(1)} %pad_maximum_fusion, s32[6,16]{1,0:T(8,128)S(1)} %iota_add_fusion.1), kind=kOutput, calls=%fused_computation.20 | convolution fusion | flops 19466496 | bytes 1966464 | tf_op jit(solution)/shard_map/shr,sruc->shuc/dot_general | solution.py:224
  25.6 0.1 copy-done.1
  25.7 0.4 fusion.17
  26.2 3.5 %collective-permute-start.3 = (bf16[24,6,256]{2,1,0:T(8,128)(2,1)S(1)}, bf16[24,6,256]{2,1,0:T(8,128)(2,1)S(1)}, u32[]{:S(2)}, u32[]{:S(2)}) collective-permute-start(bf16[24,6,256]{2,1,0:T(8,128)(2,1)S(1)} %get-tuple-element.32), channel_id=1, source_target_pairs={{1,0},{2,1},{3,2},{4,3},{5,4},{6,5},{7,6},{0,7},{9,8},{10,9},{11,1... | collective-permute-start | bytes 221192 | tf_op jit(solution)/shard_map/ppermute | solution.py:118
  29.7 2.3 %collective-permute-done.2 = bf16[24,6,256]{2,1,0:T(8,128)(2,1)S(1)} collective-permute-done((bf16[24,6,256]{2,1,0:T(8,128)(2,1)S(1)}, bf16[24,6,256]{2,1,0:T(8,128)(2,1)S(1)}, u32[]{:S(2)}, u32[]{:S(2)}) %collective-permute-start.2) | collective-permute-done | bytes 73760 | tf_op jit(solution)/shard_map/ppermute | solution.py:117
  32.1 0.2 fusion.280
  32.3 6.2 %collective-permute-start.4 = (bf16[6,36,256]{2,1,0:T(8,128)(2,1)S(1)}, bf16[6,36,256]{2,1,0:T(8,128)(2,1)S(1)}, u32[]{:S(2)}, u32[]{:S(2)}) collective-permute-start(bf16[6,36,256]{2,1,0:T(8,128)(2,1)S(1)} %get-tuple-element.27), channel_id=1, source_target_pairs={{0,8},{8,16},{16,24},{1,9},{9,17},{17,25},{2,10},{10,18},{18,26},{... | collective-permute-start | bytes 331784 | tf_op jit(solution)/shard_map/ppermute | solution.py:234
  38.5 4.4 %fusion.285 = (f32[18,32]{1,0:T(8,128)S(1)}, f32[18,32,256]{2,1,0:T(8,128)S(1)}) fusion(f32[256]{0:T(256)S(1)} %bitcast.367, f32[256]{0:T(256)S(1)} %bitcast.369, f32[256]{0:T(256)S(1)} %bitcast.371, f32[256]{0:T(256)S(1)} %bitcast.373, f32[256]{0:T(256)S(1)} %bitcast.375, f32[256]{0:T(256)S(1)} %bitcast.377, f32[256]{0:T(256)S(1)} %bitcast.379, ...), kind=kLoop, calls=%fused_computation.538 | loop fusion | flops 14450112 | bytes 22269184 | tf_op jit(solution)/shard_map/reduce_sum | solution.py:155
  42.9 0.3 multiply_reduce_fusion
  43.2 0.2 multiply_convert_fusion
  43.5 0.7 %copy-done.6 = bf16[2,256,1024]{2,1,0:T(8,128)(2,1)S(1)} copy-done((bf16[2,256,1024]{2,1,0:T(8,128)(2,1)S(1)}, bf16[2,256,1024]{2,1,0:T(8,128)(2,1)}, u32[]{:S(2)}) %copy-start.6) | copy-done | bytes 1048600
  44.2 0.9 %fusion.7 = bf16[576,1024]{1,0:T(8,128)(2,1)S(1)} fusion(bf16[576,256]{1,0:T(8,128)(2,1)S(1)} %bitcast.203, bf16[2,256,1024]{2,1,0:T(8,128)(2,1)S(1)} %copy-done.6), kind=kOutput, calls=%fused_computation.9 | convolution fusion | flops 307298304 | bytes 1998848 | tf_op jit(solution)/shard_map/dot_general | solution.py:159
  45.1 0.3 copy-done.7
  45.4 0.5 fusion.18
  45.9 2.3 %fusion.281 = (f32[12,24]{1,0:T(8,128)S(1)}, f32[12,24,256]{2,1,0:T(8,128)S(1)}) fusion(f32[256]{0:T(256)S(1)} %bitcast.269, f32[18,30,256]{2,1,0:T(8,128)S(1)} %slice_convert_fusion, f32[256]{0:T(256)S(1)} %bitcast.271, f32[256]{0:T(256)S(1)} %bitcast.273, f32[256]{0:T(256)S(1)} %bitcast.275, f32[256]{0:T(256)S(1)} %bitcast.277, f32[256]{0:T(256)S(1)} %bitcast.279, ...), kind=kLoop, calls=%fused_computation.536 | loop fusion | flops 7225056 | bytes 14796928 | tf_op jit(solution)/shard_map/reduce_sum | solution.py:155
  48.2 0.2 multiply_reduce_fusion.2
  48.5 0.1 multiply_convert_fusion.2
  48.6 0.5 fusion.34
  49.2 0.3 fusion.37
  49.5 1.5 %collective-permute-start.5 = (bf16[6,36,256]{2,1,0:T(8,128)(2,1)S(1)}, bf16[6,36,256]{2,1,0:T(8,128)(2,1)S(1)}, u32[]{:S(2)}, u32[]{:S(2)}) collective-permute-start(bf16[6,36,256]{2,1,0:T(8,128)(2,1)S(1)} %get-tuple-element.28), channel_id=1, source_target_pairs={{8,0},{16,8},{24,16},{9,1},{17,9},{25,17},{10,2},{18,10},{26,18},{... | collective-permute-start | bytes 331784 | tf_op jit(solution)/shard_map/ppermute | solution.py:235
  51.0 7.7 %collective-permute-done.5 = bf16[6,36,256]{2,1,0:T(8,128)(2,1)S(1)} collective-permute-done((bf16[6,36,256]{2,1,0:T(8,128)(2,1)S(1)}, bf16[6,36,256]{2,1,0:T(8,128)(2,1)S(1)}, u32[]{:S(2)}, u32[]{:S(2)}) %collective-permute-start.5) | collective-permute-done | bytes 110624 | tf_op jit(solution)/shard_map/ppermute | solution.py:235
  59.0 3.1 %fusion.287 = (f32[2,6,32]{2,1,0:T(8,128)S(1)}, f32[2,6,32,256]{3,2,1,0:T(8,128)S(1)}) fusion(f32[256]{0:T(256)S(1)} %bitcast.368, f32[256]{0:T(256)S(1)} %bitcast.370, f32[256]{0:T(256)S(1)} %bitcast.372, f32[256]{0:T(256)S(1)} %bitcast.374, f32[256]{0:T(256)S(1)} %bitcast.376, f32[256]{0:T(256)S(1)} %bitcast.378, f32[256]{0:T(256)S(1)} %bitcast.380, ...), kind=kLoop, calls=%fused_computation.539 | loop fusion | flops 9633408 | bytes 15190528 | tf_op jit(solution)/shard_map/reduce_sum | solution.py:155
  62.0 0.2 multiply_reduce_fusion.1
  62.3 0.2 multiply_convert_fusion.1
  62.5 0.7 fusion.15
  63.1 0.4 fusion.94
  63.5 0.1 fusion.271
  63.8 2.3 %fusion.283 = (f32[2,6,24]{2,1,0:T(8,128)S(1)}, f32[2,6,24,256]{3,2,1,0:T(8,128)S(1)}) fusion(f32[256]{0:T(256)S(1)} %bitcast.270, f32[2,12,30,256]{3,2,1,0:T(8,128)S(1)} %maximum_convert_fusion.1, f32[256]{0:T(256)S(1)} %bitcast.272, f32[256]{0:T(256)S(1)} %bitcast.274, f32[256]{0:T(256)S(1)} %bitcast.276, f32[256]{0:T(256)S(1)} %bitcast.278, ...), kind=kLoop, calls=%fused_computation.537 | loop fusion | flops 7225056 | bytes 14796928 | tf_op jit(solution)/shard_map/reduce_sum | solution.py:155
  66.1 0.2 multiply_reduce_fusion.3
  66.3 0.1 multiply_convert_fusion.3
  66.5 0.5 fusion.26
  67.0 0.3 fusion.36
  67.4 0.8 %pad_maximum_fusion.2 = bf16[24,24,256]{2,1,0:T(8,128)(2,1)} fusion(bf16[6,24,256]{2,1,0:T(8,128)(2,1)S(1)} %get-tuple-element.36, bf16[12,24,256]{2,1,0:T(8,128)(2,1)S(1)} %fusion.37, bf16[6,24,256]{2,1,0:T(8,128)(2,1)S(1)} %get-tuple-element.35), kind=kLoop, calls=%fused_computation.468 | loop fusion | flops 294912 | bytes 589824 | tf_op jit(solution)/shard_map/concatenate | solution.py:263
  (62 shorter events, 1.1 us)
Async XLA Ops:
  9.8 8.4 %copy-start.2 = (f32[2,7,7,256]{3,0,2,1:T(2,128)S(1)}, f32[2,7,7,256]{3,0,2,1:T(2,128)}, u32[]{:S(2)}) copy-start(f32[2,7,7,256]{3,0,2,1:T(2,128)} %param.22) | copy-start | bytes 301060
  9.8 8.7 %copy-start.3 = (f32[2,256]{1,0:T(2,128)S(1)}, f32[2,256]{1,0:T(2,128)}, u32[]{:S(2)}) copy-start(f32[2,256]{1,0:T(2,128)} %param.23) | copy-start | bytes 6148
  9.8 8.7 %copy-start = (bf16[2,256,256]{2,1,0:T(8,128)(2,1)S(1)}, bf16[2,256,256]{2,1,0:T(8,128)(2,1)}, u32[]{:S(2)}) copy-start(bf16[2,256,256]{2,1,0:T(8,128)(2,1)} %shard_map.127) | copy-start | bytes 786436
  11.2 13.1 %copy-start.4 = (s32[2]{0:T(128)S(1)}, s32[2]{0:T(128)}, u32[]{:S(2)}) copy-start(s32[2]{0:T(128)} %param.17) | copy-start | bytes 28
  11.3 13.1 %copy-start.5 = (s32[2]{0:T(128)S(1)}, s32[2]{0:T(128)}, u32[]{:S(2)}) copy-start(s32[2]{0:T(128)} %param.18) | copy-start | bytes 28
  11.3 12.4 %collective-permute-start.1 = (bf16[2,17,16,256]{3,2,1,0:T(8,128)(2,1)S(1)}, bf16[2,17,16,256]{3,2,1,0:T(8,128)(2,1)S(1)}, u32[]{:S(2)}, u32[]{:S(2)}) collective-permute-start(bf16[2,17,16,256]{3,2,1,0:T(8,128)(2,1)S(1)} %pad_maximum_fusion.4), channel_id=1, source_target_pairs={{8,0},{16,8},{24,16},{9,1},{17,9},{25,17},{10,2},{18,10},{26,18},{... | collective-permute-start | bytes 835592 | tf_op jit(solution)/shard_map/ppermute | solution.py:107
  12.7 11.4 %collective-permute-start = (bf16[2,17,16,256]{3,2,1,0:T(8,128)(2,1)S(1)}, bf16[2,17,16,256]{3,2,1,0:T(8,128)(2,1)S(1)}, u32[]{:S(2)}, u32[]{:S(2)}) collective-permute-start(bf16[2,17,16,256]{3,2,1,0:T(8,128)(2,1)S(1)} %pad_maximum_fusion.3), channel_id=1, source_target_pairs={{0,8},{8,16},{16,24},{1,9},{9,17},{17,25},{2,10},{10,18},{18,26},{... | collective-permute-start | bytes 835592 | tf_op jit(solution)/shard_map/ppermute | solution.py:107
  24.7 1.0 %copy-start.1 = (bf16[24,24,256]{2,1,0:T(8,128)(2,1)S(1)}, bf16[24,24,256]{2,1,0:T(8,128)(2,1)}, u32[]{:S(2)}) copy-start(bf16[24,24,256]{2,1,0:T(8,128)(2,1)} %param.21) | copy-start | bytes 884740
  26.1 6.0 %collective-permute-start.2 = (bf16[24,6,256]{2,1,0:T(8,128)(2,1)S(1)}, bf16[24,6,256]{2,1,0:T(8,128)(2,1)S(1)}, u32[]{:S(2)}, u32[]{:S(2)}) collective-permute-start(bf16[24,6,256]{2,1,0:T(8,128)(2,1)S(1)} %get-tuple-element.31), channel_id=1, source_target_pairs={{0,1},{1,2},{2,3},{3,4},{4,5},{5,6},{6,7},{7,0},{8,9},{9,10},{10,1... | collective-permute-start | bytes 221192 | tf_op jit(solution)/shard_map/ppermute | solution.py:117
  26.2 5.9 %collective-permute-start.3 = (bf16[24,6,256]{2,1,0:T(8,128)(2,1)S(1)}, bf16[24,6,256]{2,1,0:T(8,128)(2,1)S(1)}, u32[]{:S(2)}, u32[]{:S(2)}) collective-permute-start(bf16[24,6,256]{2,1,0:T(8,128)(2,1)S(1)} %get-tuple-element.32), channel_id=1, source_target_pairs={{1,0},{2,1},{3,2},{4,3},{5,4},{6,5},{7,6},{0,7},{9,8},{10,9},{11,1... | collective-permute-start | bytes 221192 | tf_op jit(solution)/shard_map/ppermute | solution.py:118
  32.3 18.7 %collective-permute-start.4 = (bf16[6,36,256]{2,1,0:T(8,128)(2,1)S(1)}, bf16[6,36,256]{2,1,0:T(8,128)(2,1)S(1)}, u32[]{:S(2)}, u32[]{:S(2)}) collective-permute-start(bf16[6,36,256]{2,1,0:T(8,128)(2,1)S(1)} %get-tuple-element.27), channel_id=1, source_target_pairs={{0,8},{8,16},{16,24},{1,9},{9,17},{17,25},{2,10},{10,18},{18,26},{... | collective-permute-start | bytes 331784 | tf_op jit(solution)/shard_map/ppermute | solution.py:234
  42.9 1.2 %copy-start.6 = (bf16[2,256,1024]{2,1,0:T(8,128)(2,1)S(1)}, bf16[2,256,1024]{2,1,0:T(8,128)(2,1)}, u32[]{:S(2)}) copy-start(bf16[2,256,1024]{2,1,0:T(8,128)(2,1)} %param.24) | copy-start | bytes 3145732
  44.2 1.2 %copy-start.7 = (bf16[2,1024,256]{2,1,0:T(8,128)(2,1)S(1)}, bf16[2,1024,256]{2,1,0:T(8,128)(2,1)}, u32[]{:S(2)}) copy-start(bf16[2,1024,256]{2,1,0:T(8,128)(2,1)} %param.25) | copy-start | bytes 3145732
  49.5 9.3 %collective-permute-start.5 = (bf16[6,36,256]{2,1,0:T(8,128)(2,1)S(1)}, bf16[6,36,256]{2,1,0:T(8,128)(2,1)S(1)}, u32[]{:S(2)}, u32[]{:S(2)}) collective-permute-start(bf16[6,36,256]{2,1,0:T(8,128)(2,1)S(1)} %get-tuple-element.28), channel_id=1, source_target_pairs={{8,0},{16,8},{24,16},{9,1},{17,9},{25,17},{10,2},{18,10},{26,18},{... | collective-permute-start | bytes 331784 | tf_op jit(solution)/shard_map/ppermute | solution.py:235

commit v12 on v8

--- a/solution.py
+++ b/solution.py
@@ -13,9 +13,10 @@
 RW = 16
 
 
-def _expand(count, size, by_block):
-    rows = lax.broadcasted_iota(jnp.int32, (count, size), 0)
-    cols = lax.broadcasted_iota(jnp.int32, (count, size), 1)
+def _expand(count, size, by_block, across=False):
+    shape = (size, count) if across else (count, size)
+    rows = lax.broadcasted_iota(jnp.int32, shape, 1 if across else 0)
+    cols = lax.broadcasted_iota(jnp.int32, shape, 0 if across else 1)
     group = count // size if by_block else 1
     picked = rows // group if by_block else rows % size
     return (picked == cols).astype(jnp.bfloat16)
@@ -64,10 +65,10 @@
     by_row = jnp.dot(_expand(cells, rb, True), row_mix, preferred_element_type=jnp.float32)
     by_col = jnp.dot(_expand(cells, rw, False), col_mix, preferred_element_type=jnp.float32)
     spread_row = jnp.dot(
-        by_row.astype(x_ref.dtype), _expand(oh * ow, oh, True).T, preferred_element_type=jnp.float32
+        by_row.astype(x_ref.dtype), _expand(oh * ow, oh, True, True), preferred_element_type=jnp.float32
     )
     spread_col = jnp.dot(
-        by_col.astype(x_ref.dtype), _expand(oh * ow, ow, False).T, preferred_element_type=jnp.float32
+        by_col.astype(x_ref.dtype), _expand(oh * ow, ow, False, True), preferred_element_type=jnp.float32
     )
     both = spread_row * spread_col
     high = both.astype(x_ref.dtype)

time: 61.7 us -> 61.7 us (level)
  no operation moved by 1% of the time
where the time goes in v12:
time: 61.7 us; the launch traced here: 61.4 us
  other arithmetic  14.8 us (24%)
  starting transfers between devices  14.6 us (24%)
  waiting for transfers between devices  13.8 us (22%)
  Pallas kernels  8.17 us (13%)
  matrix products  7 us (11%)
  local copies, waits for them, and re-layouts  2.42 us (4%)
    reduce_sum x4, other arithmetic, layer_apply(): centered = mixed - jnp.mean(mixed, axis=-1, keepdims=True)  11.7 us
    ppermute x2, waiting for transfers between devices, shifted(): lax.ppermute(value, axis, [(source, source + steps) for source in range(l...  11.4 us
    pallas_call x1, Pallas kernels, conv_resample(): pl.pallas_call(_conv_body, grid=(n,), in_specs=[pl.BlockSpec((1, h, wd, c...  8.17 us
    ppermute x2, starting transfers between devices, shifted(): lax.ppermute(value, axis, [(source, source + steps) for source in range(l...  6.19 us
    ppermute x1, starting transfers between devices, with_halo(): after = lax.ppermute(leading, axis, down)  3.53 us
    ppermute x1, starting transfers between devices, per_device(): north = lax.ppermute(lon_wide[length - reach:], 'lat', up)  3.4 us
    dot_general x4, matrix products, layer_apply(): jnp.dot(flat_cells, up_matrix, preferred_element_type=jnp.float32)  2.7 us
    ppermute x1, waiting for transfers between devices, with_halo(): before = lax.ppermute(last, axis, up)  2.39 us
  transfers between devices with their start and end apart: 6, of which 3 were waited for; matrix products, arithmetic and copies ran while one was open for 15% of the time, Pallas kernels for 0%

profile of v12, /device:TPU:0, one launch (start us, length us, event | category | flops | bytes accessed | tf_op | source)
XLA Modules:
  0.0 61.4 jit_solution(817514258878825093)
XLA Ops:
  0.0 8.2 %shard_map.127 = bf16[2,256,256]{2,1,0:T(8,128)(2,1)} custom-call(bf16[2,64,64,256]{3,2,1,0:T(8,128)(2,1)} %x_ref.1, bf16[3,3,256,256]{3,2,1,0:T(8,128)(2,1)} %w_ref.1, f32[1,256]{1,0:T(1,128)} %bitcast.403, bf16[2,16,32]{2,1,0:T(8,128)(2,1)} %r_ref.1, bf16[2,16,32]{2,1,0:T(8,128)(2,1)} %c_ref.1), custom_call_target="tpu_custom_call" | custom-call | tf_op jit(solution)/shard_map/pallas_call | solution.py:87
  8.2 1.3 %copy.40 = bf16[1,2,256,256]{3,1,2,0:T(2,128)(2,1)S(1)} copy(bf16[1,2,256,256]{3,2,1,0:T(8,128)(2,1)} %bitcast.188) | data formatting | bytes 524288
  9.5 0.1 fusion.290
  9.6 0.4 convolution_convert_fusion.1
  10.1 0.2 select_reduce_fusion.2
  10.3 0.1 select_convert_fusion.1
  10.4 4.9 %collective-permute-start = (bf16[2,17,16,256]{3,2,1,0:T(8,128)(2,1)S(1)}, bf16[2,17,16,256]{3,2,1,0:T(8,128)(2,1)S(1)}, u32[]{:S(2)}, u32[]{:S(2)}) collective-permute-start(bf16[2,17,16,256]{3,2,1,0:T(8,128)(2,1)S(1)} %pad_maximum_fusion.2), channel_id=1, source_target_pairs={{0,8},{8,16},{16,24},{1,9},{9,17},{17,25},{2,10},{10,18},{18,26},{... | collective-permute-start | bytes 835592 | tf_op jit(solution)/shard_map/ppermute | solution.py:108
  15.3 0.4 convolution_convert_fusion
  15.8 1.3 %collective-permute-start.1 = (bf16[2,17,16,256]{3,2,1,0:T(8,128)(2,1)S(1)}, bf16[2,17,16,256]{3,2,1,0:T(8,128)(2,1)S(1)}, u32[]{:S(2)}, u32[]{:S(2)}) collective-permute-start(bf16[2,17,16,256]{3,2,1,0:T(8,128)(2,1)S(1)} %pad_maximum_fusion.3), channel_id=1, source_target_pairs={{8,0},{16,8},{24,16},{9,1},{17,9},{25,17},{10,2},{18,10},{26,18},{... | collective-permute-start | bytes 835592 | tf_op jit(solution)/shard_map/ppermute | solution.py:108
  17.1 0.1 fusion.303
  17.4 0.1 broadcast_select_fusion
  17.5 3.6 %collective-permute-done = bf16[2,17,16,256]{3,2,1,0:T(8,128)(2,1)S(1)} collective-permute-done((bf16[2,17,16,256]{3,2,1,0:T(8,128)(2,1)S(1)}, bf16[2,17,16,256]{3,2,1,0:T(8,128)(2,1)S(1)}, u32[]{:S(2)}, u32[]{:S(2)}) %collective-permute-start) | collective-permute-done | bytes 278560 | tf_op jit(solution)/shard_map/ppermute | solution.py:108
  21.2 0.2 slice_reduce_fusion.1
  21.4 7.7 %collective-permute-done.1 = bf16[2,17,16,256]{3,2,1,0:T(8,128)(2,1)S(1)} collective-permute-done((bf16[2,17,16,256]{3,2,1,0:T(8,128)(2,1)S(1)}, bf16[2,17,16,256]{3,2,1,0:T(8,128)(2,1)S(1)}, u32[]{:S(2)}, u32[]{:S(2)}) %collective-permute-start.1) | collective-permute-done | bytes 278560 | tf_op jit(solution)/shard_map/ppermute | solution.py:108
  29.1 0.2 slice_reduce_fusion
  29.3 0.1 pad_add_fusion
  29.4 0.1 iota_add_fusion.1
  29.5 0.1 pad_add_fusion.1
  29.7 0.1 pad_maximum_fusion
  29.8 0.8 %convolution_convert_fusion.2 = bf16[6,24,16,256]{3,1,2,0:T(8,128)(2,1)S(1)} fusion(bf16[6,16,16,256]{3,2,1,0:T(8,128)(2,1)S(1)} %pad_maximum_fusion, s32[6,16]{1,0:T(8,128)S(1)} %iota_add_fusion.1), kind=kOutput, calls=%fused_computation.20 | convolution fusion | flops 19466496 | bytes 1966464 | tf_op jit(solution)/shard_map/shr,sruc->shuc/dot_general | solution.py:228
  30.6 0.4 fusion.17
  31.1 3.5 %collective-permute-start.3 = (bf16[24,6,256]{2,1,0:T(8,128)(2,1)S(1)}, bf16[24,6,256]{2,1,0:T(8,128)(2,1)S(1)}, u32[]{:S(2)}, u32[]{:S(2)}) collective-permute-start(bf16[24,6,256]{2,1,0:T(8,128)(2,1)S(1)} %get-tuple-element.27), channel_id=1, source_target_pairs={{1,0},{2,1},{3,2},{4,3},{5,4},{6,5},{7,6},{0,7},{9,8},{10,9},{11,1... | collective-permute-start | bytes 221192 | tf_op jit(solution)/shard_map/ppermute | solution.py:119
  34.6 2.4 %collective-permute-done.2 = bf16[24,6,256]{2,1,0:T(8,128)(2,1)S(1)} collective-permute-done((bf16[24,6,256]{2,1,0:T(8,128)(2,1)S(1)}, bf16[24,6,256]{2,1,0:T(8,128)(2,1)S(1)}, u32[]{:S(2)}, u32[]{:S(2)}) %collective-permute-start.2) | collective-permute-done | bytes 73760 | tf_op jit(solution)/shard_map/ppermute | solution.py:118
  37.0 0.2 fusion.292
  37.2 3.4 %collective-permute-start.4 = (bf16[6,36,256]{2,1,0:T(8,128)(2,1)S(1)}, bf16[6,36,256]{2,1,0:T(8,128)(2,1)S(1)}, u32[]{:S(2)}, u32[]{:S(2)}) collective-permute-start(bf16[6,36,256]{2,1,0:T(8,128)(2,1)S(1)} %get-tuple-element.24), channel_id=1, source_target_pairs={{0,8},{8,16},{16,24},{1,9},{9,17},{17,25},{2,10},{10,18},{18,26},{... | collective-permute-start | bytes 331784 | tf_op jit(solution)/shard_map/ppermute | solution.py:238
  40.6 1.5 %collective-permute-start.5 = (bf16[6,36,256]{2,1,0:T(8,128)(2,1)S(1)}, bf16[6,36,256]{2,1,0:T(8,128)(2,1)S(1)}, u32[]{:S(2)}, u32[]{:S(2)}) collective-permute-start(bf16[6,36,256]{2,1,0:T(8,128)(2,1)S(1)} %get-tuple-element.25), channel_id=1, source_target_pairs={{8,0},{16,8},{24,16},{9,1},{17,9},{25,17},{10,2},{18,10},{26,18},{... | collective-permute-start | bytes 331784 | tf_op jit(solution)/shard_map/ppermute | solution.py:239
  42.2 4.4 %fusion.297 = (f32[18,32]{1,0:T(8,128)S(1)}, f32[18,32,256]{2,1,0:T(8,128)S(1)}) fusion(f32[256]{0:T(256)S(1)} %bitcast.295, f32[256]{0:T(256)S(1)} %bitcast.298, f32[256]{0:T(256)S(1)} %bitcast.301, f32[256]{0:T(256)S(1)} %bitcast.304, f32[256]{0:T(256)S(1)} %bitcast.307, f32[256]{0:T(256)S(1)} %bitcast.310, f32[256]{0:T(256)S(1)} %bitcast.313, ...), kind=kLoop, calls=%fused_computation.535 | loop fusion | flops 14450112 | bytes 22269184 | tf_op jit(solution)/shard_map/reduce_sum | solution.py:157
  46.6 0.3 multiply_reduce_fusion.1
  46.9 0.2 multiply_convert_fusion.1
  47.2 0.9 %fusion.7 = bf16[576,1024]{1,0:T(8,128)(2,1)S(1)} fusion(bf16[576,256]{1,0:T(8,128)(2,1)S(1)} %bitcast.195, bf16[2,256,1024]{2,1,0:T(8,128)(2,1)S(1)} %copy-done.8), kind=kOutput, calls=%fused_computation.11 | convolution fusion | flops 307298304 | bytes 1998848 | tf_op jit(solution)/shard_map/dot_general | solution.py:161
  48.1 0.3 copy-done.1
  48.4 0.5 fusion.144
  48.9 0.1 fusion.85
  49.1 1.4 %fusion.299 = (f32[6,32]{1,0:T(8,128)S(1)}, f32[6,32,256]{2,1,0:T(8,128)S(1)}) fusion(f32[256]{0:T(256)S(1)} %bitcast.296, f32[256]{0:T(256)S(1)} %bitcast.299, f32[256]{0:T(256)S(1)} %bitcast.302, f32[256]{0:T(256)S(1)} %bitcast.305, f32[256]{0:T(256)S(1)} %bitcast.308, f32[256]{0:T(256)S(1)} %bitcast.311, f32[256]{0:T(256)S(1)} %bitcast.314, ...), kind=kLoop, calls=%fused_computation.536 | loop fusion | flops 4816704 | bytes 7620352 | tf_op jit(solution)/shard_map/reduce_sum | solution.py:157
  50.6 1.4 %fusion.295 = (f32[6,32]{1,0:T(8,128)S(1)}, f32[6,32,256]{2,1,0:T(8,128)S(1)}) fusion(f32[256]{0:T(256)S(1)} %bitcast.297, f32[256]{0:T(256)S(1)} %bitcast.300, f32[256]{0:T(256)S(1)} %bitcast.303, f32[256]{0:T(256)S(1)} %bitcast.306, f32[256]{0:T(256)S(1)} %bitcast.309, f32[256]{0:T(256)S(1)} %bitcast.312, f32[256]{0:T(256)S(1)} %bitcast.315, ...), kind=kLoop, calls=%fused_computation.534 | loop fusion | flops 4816704 | bytes 7620352 | tf_op jit(solution)/shard_map/reduce_sum | solution.py:157
  52.0 0.2 multiply_reduce_fusion.2
  52.2 0.2 multiply_reduce_fusion.3
  52.4 0.2 multiply_convert_fusion.3
  52.6 0.4 fusion.35
  53.0 0.3 fusion.142
  53.3 0.4 fusion.27
  53.7 0.3 fusion.146
  54.1 0.1 fusion.159
  54.2 4.4 %fusion.293 = (f32[24,24]{1,0:T(8,128)S(1)}, f32[24,24,256]{2,1,0:T(8,128)S(1)}) fusion(f32[256]{0:T(256)S(1)} %bitcast.384, f32[30,30,256]{2,1,0:T(8,128)S(1)} %fusion.159, f32[256]{0:T(256)S(1)} %bitcast.385, f32[256]{0:T(256)S(1)} %bitcast.386, f32[256]{0:T(256)S(1)} %bitcast.387, f32[256]{0:T(256)S(1)} %bitcast.388, f32[256]{0:T(256)S(1)} %bitcast.389, ...), kind=kLoop, calls=%fused_computation.533 | loop fusion | flops 14450112 | bytes 29543680 | tf_op jit(solution)/shard_map/reduce_sum | solution.py:157
  58.7 0.3 multiply_reduce_fusion
  59.0 0.2 multiply_convert_fusion
  59.2 0.9 %fusion.15 = bf16[576,1024]{1,0:T(8,128)(2,1)S(1)} fusion(bf16[576,256]{1,0:T(8,128)(2,1)S(1)} %bitcast.194, bf16[2,256,1024]{2,1,0:T(8,128)(2,1)S(1)} %copy-done.8), kind=kOutput, calls=%fused_computation.19 | convolution fusion | flops 307298304 | bytes 1998848 | tf_op jit(solution)/shard_map/dot_general | solution.py:161
  60.1 1.2 %fusion.18 = bf16[24,24,256]{2,1,0:T(8,128)(2,1)} fusion(bf16[24,24,1024]{2,1,0:T(8,128)(2,1)S(1)} %bitcast.404, f32[30,30,256]{2,1,0:T(8,128)S(1)} %fusion.159, bf16[2,1024,256]{2,1,0:T(8,128)(2,1)S(1)} %copy-done.1), kind=kOutput, calls=%fused_computation.25 | convolution fusion | flops 302284800 | bytes 2588672 | tf_op jit(solution)/shard_map/dot_general | solution.py:164
  (62 shorter events, 0.8 us)
Async XLA Ops:
  0.0 9.4 %copy-start.7 = (s32[2,1]{0,1:T(1,128)S(1)}, s32[2,1]{0,1:T(1,128)}, u32[]{:S(2)}) copy-start(s32[2,1]{0,1:T(1,128)} %param.16) | copy-start | bytes 28
  0.0 10.1 %copy-start.5 = (s32[2]{0:T(128)S(1)}, s32[2]{0:T(128)}, u32[]{:S(2)}) copy-start(s32[2]{0:T(128)} %param.17) | copy-start | bytes 28
  0.0 10.1 %copy-start.6 = (s32[2]{0:T(128)S(1)}, s32[2]{0:T(128)}, u32[]{:S(2)}) copy-start(s32[2]{0:T(128)} %param.18) | copy-start | bytes 28
  8.2 8.9 %copy-start.3 = (f32[2,7,7,256]{3,0,2,1:T(2,128)S(1)}, f32[2,7,7,256]{3,0,2,1:T(2,128)}, u32[]{:S(2)}) copy-start(f32[2,7,7,256]{3,0,2,1:T(2,128)} %param.22) | copy-start | bytes 301060
  9.6 7.8 %copy-start.4 = (f32[2,256]{1,0:T(2,128)S(1)}, f32[2,256]{1,0:T(2,128)}, u32[]{:S(2)}) copy-start(f32[2,256]{1,0:T(2,128)} %param.23) | copy-start | bytes 6148
  9.6 7.8 %copy-start = (bf16[2,256,256]{2,1,0:T(8,128)(2,1)S(1)}, bf16[2,256,256]{2,1,0:T(8,128)(2,1)}, u32[]{:S(2)}) copy-start(bf16[2,256,256]{2,1,0:T(8,128)(2,1)} %shard_map.127) | copy-start | bytes 786436
  10.4 10.8 %collective-permute-start = (bf16[2,17,16,256]{3,2,1,0:T(8,128)(2,1)S(1)}, bf16[2,17,16,256]{3,2,1,0:T(8,128)(2,1)S(1)}, u32[]{:S(2)}, u32[]{:S(2)}) collective-permute-start(bf16[2,17,16,256]{3,2,1,0:T(8,128)(2,1)S(1)} %pad_maximum_fusion.2), channel_id=1, source_target_pairs={{0,8},{8,16},{16,24},{1,9},{9,17},{17,25},{2,10},{10,18},{18,26},{... | collective-permute-start | bytes 835592 | tf_op jit(solution)/shard_map/ppermute | solution.py:108
  15.8 13.3 %collective-permute-start.1 = (bf16[2,17,16,256]{3,2,1,0:T(8,128)(2,1)S(1)}, bf16[2,17,16,256]{3,2,1,0:T(8,128)(2,1)S(1)}, u32[]{:S(2)}, u32[]{:S(2)}) collective-permute-start(bf16[2,17,16,256]{3,2,1,0:T(8,128)(2,1)S(1)} %pad_maximum_fusion.3), channel_id=1, source_target_pairs={{8,0},{16,8},{24,16},{9,1},{17,9},{25,17},{10,2},{18,10},{26,18},{... | collective-permute-start | bytes 835592 | tf_op jit(solution)/shard_map/ppermute | solution.py:108
  17.5 13.1 %copy-start.2 = (bf16[24,24,256]{2,1,0:T(8,128)(2,1)S(1)}, bf16[24,24,256]{2,1,0:T(8,128)(2,1)}, u32[]{:S(2)}) copy-start(bf16[24,24,256]{2,1,0:T(8,128)(2,1)} %param.21) | copy-start | bytes 884740
  31.0 6.0 %collective-permute-start.2 = (bf16[24,6,256]{2,1,0:T(8,128)(2,1)S(1)}, bf16[24,6,256]{2,1,0:T(8,128)(2,1)S(1)}, u32[]{:S(2)}, u32[]{:S(2)}) collective-permute-start(bf16[24,6,256]{2,1,0:T(8,128)(2,1)S(1)} %get-tuple-element.26), channel_id=1, source_target_pairs={{0,1},{1,2},{2,3},{3,4},{4,5},{5,6},{6,7},{7,0},{8,9},{9,10},{10,1... | collective-permute-start | bytes 221192 | tf_op jit(solution)/shard_map/ppermute | solution.py:118
  31.1 5.9 %collective-permute-start.3 = (bf16[24,6,256]{2,1,0:T(8,128)(2,1)S(1)}, bf16[24,6,256]{2,1,0:T(8,128)(2,1)S(1)}, u32[]{:S(2)}, u32[]{:S(2)}) collective-permute-start(bf16[24,6,256]{2,1,0:T(8,128)(2,1)S(1)} %get-tuple-element.27), channel_id=1, source_target_pairs={{1,0},{2,1},{3,2},{4,3},{5,4},{6,5},{7,6},{0,7},{9,8},{10,9},{11,1... | collective-permute-start | bytes 221192 | tf_op jit(solution)/shard_map/ppermute | solution.py:119
  37.2 13.3 %collective-permute-start.4 = (bf16[6,36,256]{2,1,0:T(8,128)(2,1)S(1)}, bf16[6,36,256]{2,1,0:T(8,128)(2,1)S(1)}, u32[]{:S(2)}, u32[]{:S(2)}) collective-permute-start(bf16[6,36,256]{2,1,0:T(8,128)(2,1)S(1)} %get-tuple-element.24), channel_id=1, source_target_pairs={{0,8},{8,16},{16,24},{1,9},{9,17},{17,25},{2,10},{10,18},{18,26},{... | collective-permute-start | bytes 331784 | tf_op jit(solution)/shard_map/ppermute | solution.py:238
  40.6 8.4 %collective-permute-start.5 = (bf16[6,36,256]{2,1,0:T(8,128)(2,1)S(1)}, bf16[6,36,256]{2,1,0:T(8,128)(2,1)S(1)}, u32[]{:S(2)}, u32[]{:S(2)}) collective-permute-start(bf16[6,36,256]{2,1,0:T(8,128)(2,1)S(1)} %get-tuple-element.25), channel_id=1, source_target_pairs={{8,0},{16,8},{24,16},{9,1},{17,9},{25,17},{10,2},{18,10},{26,18},{... | collective-permute-start | bytes 331784 | tf_op jit(solution)/shard_map/ppermute | solution.py:239
  42.2 5.0 %copy-start.8 = (bf16[2,256,1024]{2,1,0:T(8,128)(2,1)S(1)}, bf16[2,256,1024]{2,1,0:T(8,128)(2,1)}, u32[]{:S(2)}) copy-start(bf16[2,256,1024]{2,1,0:T(8,128)(2,1)} %param.24) | copy-start | bytes 3145732
  47.2 1.2 %copy-start.1 = (bf16[2,1024,256]{2,1,0:T(8,128)(2,1)S(1)}, bf16[2,1024,256]{2,1,0:T(8,128)(2,1)}, u32[]{:S(2)}) copy-start(bf16[2,1024,256]{2,1,0:T(8,128)(2,1)} %param.25) | copy-start | bytes 3145732

commit v13 on v12

--- a/solution.py
+++ b/solution.py
@@ -190,32 +190,27 @@
     bands = lax.axis_size("lat")
     resampled = conv_resample(swath_input, conv_weight, conv_bias, row_weights, col_weights)
     own_band = lax.axis_index("lat")
-    offset_band = block_band[:, 0] - own_band
-    staying = offset_band == 0
-    positions = jnp.arange(blocks_here, dtype=jnp.int32)
-    row_list = [row_offset]
-    col_list = [col_offset]
-    block_list = [keep_local(staying, resampled)]
+    own_bands = block_band[:, 0]
+    lane = jnp.arange(channels, dtype=jnp.int32)[None, :]
+    header = jnp.where(
+        lane == 0,
+        row_offset[:, None],
+        jnp.where(lane == 1, col_offset[:, None], jnp.where(lane == 2, own_bands[:, None], 0)),
+    ).astype(jnp.bfloat16)
+    header = jnp.broadcast_to(header[:, None, None, :], (blocks_here, 1, RW, channels))
+    payload = jnp.concatenate([resampled, header], axis=1)
+    block_list, row_list, col_list, band_list = [resampled], [row_offset], [col_offset], [own_bands]
     for step in (1, -1):
-        going = offset_band == step
-        earlier = jnp.sum(going[None, :] & (positions[None, :] < positions[:, None]), axis=1)
-        table = (jnp.arange(CAP, dtype=jnp.int32)[:, None] == earlier[None, :]) & going[None, :]
-        sent_blocks = place_rows(table, resampled)
-        sent_rows = place_ints(table, row_offset)
-        sent_cols = place_ints(table, col_offset)
-        lane = jnp.arange(channels, dtype=jnp.int32)[None, :]
-        header = jnp.where(
-            lane == 0, sent_rows[:, None], jnp.where(lane == 1, sent_cols[:, None], 0)
-        ).astype(jnp.bfloat16)
-        header = jnp.broadcast_to(header[:, None, None, :], (CAP, 1, RW, channels))
-        payload = jnp.concatenate([sent_blocks, header], axis=1)
         got = shifted(payload, "lat", step)
+        got_header = got[:, RB, 0, :].astype(jnp.int32)
         block_list.append(got[:, :RB])
-        got_header = got[:, RB, 0, :].astype(jnp.int32)
         row_list.append(got_header[:, 0])
         col_list.append(got_header[:, 1])
+        band_list.append(got_header[:, 2])
     arrived = jnp.concatenate(block_list, axis=0)
-    all_rows = jnp.concatenate(row_list, axis=0)
+    all_rows = (jnp.concatenate(band_list, axis=0) - own_band) * tile_rows + jnp.concatenate(
+        row_list, axis=0
+    )
     all_cols = jnp.concatenate(col_list, axis=0)
     row_place = (
         jnp.arange(tile_rows, dtype=jnp.int32)[None, :, None]

time: 61.7 us -> 60.3 us (0.977)
  the two profiles are of different devices: /device:TPU:0 before, /device:TPU:5 now
where the time goes in v13:
time: 60.3 us; the launch traced here: 60.1 us
  other arithmetic  15.4 us (26%)
  starting transfers between devices  14.4 us (24%)
  waiting for transfers between devices  14.3 us (24%)
  Pallas kernels  8.19 us (14%)
  matrix products  6.17 us (10%)
  local copies, waits for them, and re-layouts  1.17 us (2%)
    reduce_sum x4, other arithmetic, layer_apply(): centered = mixed - jnp.mean(mixed, axis=-1, keepdims=True)  11.8 us
    ppermute x2, waiting for transfers between devices, shifted(): lax.ppermute(value, axis, [(source, source + steps) for source in range(l...  9.53 us
    pallas_call x1, Pallas kernels, conv_resample(): pl.pallas_call(_conv_body, grid=(n,), in_specs=[pl.BlockSpec((1, h, wd, c...  8.19 us
    ppermute x2, starting transfers between devices, shifted(): lax.ppermute(value, axis, [(source, source + steps) for source in range(l...  5.3 us
    ppermute x1, starting transfers between devices, per_device(): north = lax.ppermute(lon_wide[length - reach:], 'lat', up)  3.36 us
    ppermute x1, waiting for transfers between devices, with_halo(): after = lax.ppermute(leading, axis, down)  3.14 us
    ppermute x1, starting transfers between devices, per_device(): south = lax.ppermute(lon_wide[:reach], 'lat', down)  3.01 us
    ppermute x1, starting transfers between devices, with_halo(): before = lax.ppermute(last, axis, up)  2.73 us
  transfers between devices with their start and end apart: 6, of which 4 were waited for; matrix products, arithmetic and copies ran while one was open for 14% of the time, Pallas kernels for 0%

profile of v13, /device:TPU:5, one launch (start us, length us, event | category | flops | bytes accessed | tf_op | source)
XLA Modules:
  0.0 60.1 jit_solution(8742433400506227499)
XLA Ops:
  0.0 0.0 copy-start.3
  0.1 0.0 copy-start.4
  0.1 8.2 %shard_map.127 = bf16[2,256,256]{2,1,0:T(8,128)(2,1)} custom-call(bf16[2,64,64,256]{3,2,1,0:T(8,128)(2,1)} %x_ref.1, bf16[3,3,256,256]{3,2,1,0:T(8,128)(2,1)} %w_ref.1, f32[1,256]{1,0:T(1,128)} %bitcast.383, bf16[2,16,32]{2,1,0:T(8,128)(2,1)} %r_ref.1, bf16[2,16,32]{2,1,0:T(8,128)(2,1)} %c_ref.1), custom_call_target="tpu_custom_call" | custom-call | tf_op jit(solution)/shard_map/pallas_call | solution.py:87
  8.3 0.1 select_convert_fusion
  8.4 1.0 %pad_maximum_fusion.2 = bf16[2,17,16,256]{3,2,1,0:T(8,128)(2,1)S(1)} fusion(bf16[2,1,16,256]{3,2,1,0:T(8,128)(2,1)S(1)} %broadcast_in_dim.89, bf16[2,16,16,256]{3,2,1,0:T(8,128)(2,1)} %bitcast.172), kind=kLoop, calls=%fused_computation.265 | loop fusion | flops 139264 | bytes 557056 | tf_op jit(solution)/shard_map/concatenate | solution.py:201
  9.4 3.1 %collective-permute-start.1 = (bf16[2,17,16,256]{3,2,1,0:T(8,128)(2,1)S(1)}, bf16[2,17,16,256]{3,2,1,0:T(8,128)(2,1)S(1)}, u32[]{:S(2)}, u32[]{:S(2)}) collective-permute-start(bf16[2,17,16,256]{3,2,1,0:T(8,128)(2,1)S(1)} %pad_maximum_fusion.2), channel_id=1, source_target_pairs={{8,0},{16,8},{24,16},{9,1},{17,9},{25,17},{10,2},{18,10},{26,18},{... | collective-permute-start | bytes 835592 | tf_op jit(solution)/shard_map/ppermute | solution.py:108
  12.4 2.2 %collective-permute-start = (bf16[2,17,16,256]{3,2,1,0:T(8,128)(2,1)S(1)}, bf16[2,17,16,256]{3,2,1,0:T(8,128)(2,1)S(1)}, u32[]{:S(2)}, u32[]{:S(2)}) collective-permute-start(bf16[2,17,16,256]{3,2,1,0:T(8,128)(2,1)S(1)} %pad_maximum_fusion.2), channel_id=1, source_target_pairs={{0,8},{8,16},{16,24},{1,9},{9,17},{17,25},{2,10},{10,18},{18,26},{... | collective-permute-start | bytes 835592 | tf_op jit(solution)/shard_map/ppermute | solution.py:108
  14.7 0.1 fusion.303
  15.0 3.8 %collective-permute-done.1 = bf16[2,17,16,256]{3,2,1,0:T(8,128)(2,1)S(1)} collective-permute-done((bf16[2,17,16,256]{3,2,1,0:T(8,128)(2,1)S(1)}, bf16[2,17,16,256]{3,2,1,0:T(8,128)(2,1)S(1)}, u32[]{:S(2)}, u32[]{:S(2)}) %collective-permute-start.1) | collective-permute-done | bytes 278560 | tf_op jit(solution)/shard_map/ppermute | solution.py:108
  18.8 0.2 slice_reduce_fusion
  19.0 5.7 %collective-permute-done = bf16[2,17,16,256]{3,2,1,0:T(8,128)(2,1)S(1)} collective-permute-done((bf16[2,17,16,256]{3,2,1,0:T(8,128)(2,1)S(1)}, bf16[2,17,16,256]{3,2,1,0:T(8,128)(2,1)S(1)}, u32[]{:S(2)}, u32[]{:S(2)}) %collective-permute-start) | collective-permute-done | bytes 278560 | tf_op jit(solution)/shard_map/ppermute | solution.py:108
  24.8 0.2 slice_reduce_fusion.1
  25.0 0.1 pad_add_fusion
  25.0 0.1 iota_add_fusion
  25.1 0.1 fusion.291
  25.2 0.1 iota_add_fusion.1
  25.3 0.1 pad_maximum_fusion
  25.4 0.8 %convolution_convert_fusion = bf16[6,24,16,256]{3,1,2,0:T(8,128)(2,1)S(1)} fusion(bf16[6,16,16,256]{3,2,1,0:T(8,128)(2,1)S(1)} %pad_maximum_fusion, s32[6,16]{1,0:T(8,128)S(1)} %iota_add_fusion.1), kind=kOutput, calls=%fused_computation.18 | convolution fusion | flops 19466496 | bytes 1966464 | tf_op jit(solution)/shard_map/shr,sruc->shuc/dot_general | solution.py:223
  26.3 0.4 fusion.17
  26.7 2.7 %collective-permute-start.2 = (bf16[24,6,256]{2,1,0:T(8,128)(2,1)S(1)}, bf16[24,6,256]{2,1,0:T(8,128)(2,1)S(1)}, u32[]{:S(2)}, u32[]{:S(2)}) collective-permute-start(bf16[24,6,256]{2,1,0:T(8,128)(2,1)S(1)} %get-tuple-element.23), channel_id=1, source_target_pairs={{0,1},{1,2},{2,3},{3,4},{4,5},{5,6},{6,7},{7,0},{8,9},{9,10},{10,1... | collective-permute-start | bytes 221192 | tf_op jit(solution)/shard_map/ppermute | solution.py:118
  29.5 1.6 %collective-permute-done.2 = bf16[24,6,256]{2,1,0:T(8,128)(2,1)S(1)} collective-permute-done((bf16[24,6,256]{2,1,0:T(8,128)(2,1)S(1)}, bf16[24,6,256]{2,1,0:T(8,128)(2,1)S(1)}, u32[]{:S(2)}, u32[]{:S(2)}) %collective-permute-start.2) | collective-permute-done | bytes 73760 | tf_op jit(solution)/shard_map/ppermute | solution.py:118
  31.1 3.1 %collective-permute-done.3 = bf16[24,6,256]{2,1,0:T(8,128)(2,1)S(1)} collective-permute-done((bf16[24,6,256]{2,1,0:T(8,128)(2,1)S(1)}, bf16[24,6,256]{2,1,0:T(8,128)(2,1)S(1)}, u32[]{:S(2)}, u32[]{:S(2)}) %collective-permute-start.3) | collective-permute-done | bytes 73760 | tf_op jit(solution)/shard_map/ppermute | solution.py:119
  34.2 0.2 fusion.292
  34.4 3.4 %collective-permute-start.4 = (bf16[6,36,256]{2,1,0:T(8,128)(2,1)S(1)}, bf16[6,36,256]{2,1,0:T(8,128)(2,1)S(1)}, u32[]{:S(2)}, u32[]{:S(2)}) collective-permute-start(bf16[6,36,256]{2,1,0:T(8,128)(2,1)S(1)} %get-tuple-element.21), channel_id=1, source_target_pairs={{0,8},{8,16},{16,24},{1,9},{9,17},{17,25},{2,10},{10,18},{18,26},{... | collective-permute-start | bytes 331784 | tf_op jit(solution)/shard_map/ppermute | solution.py:233
  37.8 3.0 %collective-permute-start.5 = (bf16[6,36,256]{2,1,0:T(8,128)(2,1)S(1)}, bf16[6,36,256]{2,1,0:T(8,128)(2,1)S(1)}, u32[]{:S(2)}, u32[]{:S(2)}) collective-permute-start(bf16[6,36,256]{2,1,0:T(8,128)(2,1)S(1)} %get-tuple-element.22), channel_id=1, source_target_pairs={{8,0},{16,8},{24,16},{9,1},{17,9},{25,17},{10,2},{18,10},{26,18},{... | collective-permute-start | bytes 331784 | tf_op jit(solution)/shard_map/ppermute | solution.py:234
  40.8 0.1 slice.1722
  40.9 4.4 %fusion.297 = (f32[18,32]{1,0:T(8,128)S(1)}, f32[18,32,256]{2,1,0:T(8,128)S(1)}) fusion(f32[256]{0:T(256)S(1)} %bitcast.273, f32[256]{0:T(256)S(1)} %bitcast.276, f32[256]{0:T(256)S(1)} %bitcast.279, f32[256]{0:T(256)S(1)} %bitcast.282, f32[256]{0:T(256)S(1)} %bitcast.285, f32[256]{0:T(256)S(1)} %bitcast.288, f32[256]{0:T(256)S(1)} %bitcast.291, ...), kind=kLoop, calls=%fused_computation.520 | loop fusion | flops 14450112 | bytes 22269184 | tf_op jit(solution)/shard_map/reduce_sum | solution.py:157
  45.3 0.3 multiply_reduce_fusion.1
  45.6 0.2 multiply_convert_fusion.1
  45.9 0.9 %fusion.7 = bf16[576,1024]{1,0:T(8,128)(2,1)S(1)} fusion(bf16[576,256]{1,0:T(8,128)(2,1)S(1)} %bitcast.177, bf16[2,256,1024]{2,1,0:T(8,128)(2,1)S(1)} %copy-done.8), kind=kOutput, calls=%fused_computation.9 | convolution fusion | flops 307298304 | bytes 1998848 | tf_op jit(solution)/shard_map/dot_general | solution.py:161
  46.8 0.3 copy-done.1
  47.1 0.5 fusion.144
  47.6 0.1 fusion.85
  47.8 1.4 %fusion.299 = (f32[6,32]{1,0:T(8,128)S(1)}, f32[6,32,256]{2,1,0:T(8,128)S(1)}) fusion(f32[256]{0:T(256)S(1)} %bitcast.274, f32[256]{0:T(256)S(1)} %bitcast.277, f32[256]{0:T(256)S(1)} %bitcast.280, f32[256]{0:T(256)S(1)} %bitcast.283, f32[256]{0:T(256)S(1)} %bitcast.286, f32[256]{0:T(256)S(1)} %bitcast.289, f32[256]{0:T(256)S(1)} %bitcast.292, ...), kind=kLoop, calls=%fused_computation.521 | loop fusion | flops 4816704 | bytes 7620352 | tf_op jit(solution)/shard_map/reduce_sum | solution.py:157
  49.3 1.4 %fusion.295 = (f32[6,32]{1,0:T(8,128)S(1)}, f32[6,32,256]{2,1,0:T(8,128)S(1)}) fusion(f32[256]{0:T(256)S(1)} %bitcast.275, f32[256]{0:T(256)S(1)} %bitcast.278, f32[256]{0:T(256)S(1)} %bitcast.281, f32[256]{0:T(256)S(1)} %bitcast.284, f32[256]{0:T(256)S(1)} %bitcast.287, f32[256]{0:T(256)S(1)} %bitcast.290, f32[256]{0:T(256)S(1)} %bitcast.293, ...), kind=kLoop, calls=%fused_computation.519 | loop fusion | flops 4816704 | bytes 7620352 | tf_op jit(solution)/shard_map/reduce_sum | solution.py:157
  50.7 0.2 multiply_reduce_fusion.2
  50.9 0.2 multiply_reduce_fusion.3
  51.1 0.2 multiply_convert_fusion.3
  51.3 0.4 fusion.35
  51.7 0.3 fusion.142
  52.0 0.4 fusion.27
  52.4 0.3 fusion.146
  52.8 0.1 fusion.159
  52.9 4.5 %fusion.293 = (f32[24,24]{1,0:T(8,128)S(1)}, f32[24,24,256]{2,1,0:T(8,128)S(1)}) fusion(f32[256]{0:T(256)S(1)} %bitcast.362, f32[30,30,256]{2,1,0:T(8,128)S(1)} %fusion.159, f32[256]{0:T(256)S(1)} %bitcast.363, f32[256]{0:T(256)S(1)} %bitcast.364, f32[256]{0:T(256)S(1)} %bitcast.365, f32[256]{0:T(256)S(1)} %bitcast.366, f32[256]{0:T(256)S(1)} %bitcast.367, ...), kind=kLoop, calls=%fused_computation.518 | loop fusion | flops 14450112 | bytes 29543680 | tf_op jit(solution)/shard_map/reduce_sum | solution.py:157
  57.4 0.3 multiply_reduce_fusion
  57.7 0.2 multiply_convert_fusion
  57.9 0.9 %fusion.15 = bf16[576,1024]{1,0:T(8,128)(2,1)S(1)} fusion(bf16[576,256]{1,0:T(8,128)(2,1)S(1)} %bitcast.176, bf16[2,256,1024]{2,1,0:T(8,128)(2,1)S(1)} %copy-done.8), kind=kOutput, calls=%fused_computation.17 | convolution fusion | flops 307298304 | bytes 1998848 | tf_op jit(solution)/shard_map/dot_general | solution.py:161
  58.9 1.2 %fusion.18 = bf16[24,24,256]{2,1,0:T(8,128)(2,1)} fusion(bf16[24,24,1024]{2,1,0:T(8,128)(2,1)S(1)} %bitcast.384, f32[30,30,256]{2,1,0:T(8,128)S(1)} %fusion.159, bf16[2,1024,256]{2,1,0:T(8,128)(2,1)S(1)} %copy-done.1), kind=kOutput, calls=%fused_computation.23 | convolution fusion | flops 302284800 | bytes 2588672 | tf_op jit(solution)/shard_map/dot_general | solution.py:164
  (52 shorter events, 0.5 us)
Async XLA Ops:
  0.0 8.3 %copy-start.5 = (s32[2]{0:T(128)S(1)}, s32[2]{0:T(128)}, u32[]{:S(2)}) copy-start(s32[2]{0:T(128)} %param.18) | copy-start | bytes 28
  0.0 8.2 %copy-start.6 = (s32[2]{0:T(128)S(1)}, s32[2]{0:T(128)}, u32[]{:S(2)}) copy-start(s32[2]{0:T(128)} %param.17) | copy-start | bytes 28
  0.0 8.2 %copy-start.7 = (s32[2,1]{0,1:T(1,128)S(1)}, s32[2,1]{0,1:T(1,128)}, u32[]{:S(2)}) copy-start(s32[2,1]{0,1:T(1,128)} %param.16) | copy-start | bytes 28
  0.0 14.6 %copy-start.3 = (f32[2,7,7,256]{3,0,2,1:T(2,128)S(1)}, f32[2,7,7,256]{3,0,2,1:T(2,128)}, u32[]{:S(2)}) copy-start(f32[2,7,7,256]{3,0,2,1:T(2,128)} %param.22) | copy-start | bytes 301060
  0.1 14.9 %copy-start.4 = (f32[2,256]{1,0:T(2,128)S(1)}, f32[2,256]{1,0:T(2,128)}, u32[]{:S(2)}) copy-start(f32[2,256]{1,0:T(2,128)} %param.23) | copy-start | bytes 6148
  8.3 17.1 %copy-start = (bf16[2,256,256]{2,1,0:T(8,128)(2,1)S(1)}, bf16[2,256,256]{2,1,0:T(8,128)(2,1)}, u32[]{:S(2)}) copy-start(bf16[2,256,256]{2,1,0:T(8,128)(2,1)} %shard_map.127) | copy-start | bytes 786436
  9.4 9.4 %collective-permute-start.1 = (bf16[2,17,16,256]{3,2,1,0:T(8,128)(2,1)S(1)}, bf16[2,17,16,256]{3,2,1,0:T(8,128)(2,1)S(1)}, u32[]{:S(2)}, u32[]{:S(2)}) collective-permute-start(bf16[2,17,16,256]{3,2,1,0:T(8,128)(2,1)S(1)} %pad_maximum_fusion.2), channel_id=1, source_target_pairs={{8,0},{16,8},{24,16},{9,1},{17,9},{25,17},{10,2},{18,10},{26,18},{... | collective-permute-start | bytes 835592 | tf_op jit(solution)/shard_map/ppermute | solution.py:108
  12.4 12.3 %collective-permute-start = (bf16[2,17,16,256]{3,2,1,0:T(8,128)(2,1)S(1)}, bf16[2,17,16,256]{3,2,1,0:T(8,128)(2,1)S(1)}, u32[]{:S(2)}, u32[]{:S(2)}) collective-permute-start(bf16[2,17,16,256]{3,2,1,0:T(8,128)(2,1)S(1)} %pad_maximum_fusion.2), channel_id=1, source_target_pairs={{0,8},{8,16},{16,24},{1,9},{9,17},{17,25},{2,10},{10,18},{18,26},{... | collective-permute-start | bytes 835592 | tf_op jit(solution)/shard_map/ppermute | solution.py:108
  14.9 11.3 %copy-start.2 = (bf16[24,24,256]{2,1,0:T(8,128)(2,1)S(1)}, bf16[24,24,256]{2,1,0:T(8,128)(2,1)}, u32[]{:S(2)}) copy-start(bf16[24,24,256]{2,1,0:T(8,128)(2,1)} %param.21) | copy-start | bytes 884740
  26.7 4.4 %collective-permute-start.2 = (bf16[24,6,256]{2,1,0:T(8,128)(2,1)S(1)}, bf16[24,6,256]{2,1,0:T(8,128)(2,1)S(1)}, u32[]{:S(2)}, u32[]{:S(2)}) collective-permute-start(bf16[24,6,256]{2,1,0:T(8,128)(2,1)S(1)} %get-tuple-element.23), channel_id=1, source_target_pairs={{0,1},{1,2},{2,3},{3,4},{4,5},{5,6},{6,7},{7,0},{8,9},{9,10},{10,1... | collective-permute-start | bytes 221192 | tf_op jit(solution)/shard_map/ppermute | solution.py:118
  29.4 4.8 %collective-permute-start.3 = (bf16[24,6,256]{2,1,0:T(8,128)(2,1)S(1)}, bf16[24,6,256]{2,1,0:T(8,128)(2,1)S(1)}, u32[]{:S(2)}, u32[]{:S(2)}) collective-permute-start(bf16[24,6,256]{2,1,0:T(8,128)(2,1)S(1)} %get-tuple-element.24), channel_id=1, source_target_pairs={{1,0},{2,1},{3,2},{4,3},{5,4},{6,5},{7,6},{0,7},{9,8},{10,9},{11,1... | collective-permute-start | bytes 221192 | tf_op jit(solution)/shard_map/ppermute | solution.py:119
  34.4 14.8 %collective-permute-start.4 = (bf16[6,36,256]{2,1,0:T(8,128)(2,1)S(1)}, bf16[6,36,256]{2,1,0:T(8,128)(2,1)S(1)}, u32[]{:S(2)}, u32[]{:S(2)}) collective-permute-start(bf16[6,36,256]{2,1,0:T(8,128)(2,1)S(1)} %get-tuple-element.21), channel_id=1, source_target_pairs={{0,8},{8,16},{16,24},{1,9},{9,17},{17,25},{2,10},{10,18},{18,26},{... | collective-permute-start | bytes 331784 | tf_op jit(solution)/shard_map/ppermute | solution.py:233
  37.8 9.9 %collective-permute-start.5 = (bf16[6,36,256]{2,1,0:T(8,128)(2,1)S(1)}, bf16[6,36,256]{2,1,0:T(8,128)(2,1)S(1)}, u32[]{:S(2)}, u32[]{:S(2)}) collective-permute-start(bf16[6,36,256]{2,1,0:T(8,128)(2,1)S(1)} %get-tuple-element.22), channel_id=1, source_target_pairs={{8,0},{16,8},{24,16},{9,1},{17,9},{25,17},{10,2},{18,10},{26,18},{... | collective-permute-start | bytes 331784 | tf_op jit(solution)/shard_map/ppermute | solution.py:234
  40.9 5.0 %copy-start.8 = (bf16[2,256,1024]{2,1,0:T(8,128)(2,1)S(1)}, bf16[2,256,1024]{2,1,0:T(8,128)(2,1)}, u32[]{:S(2)}) copy-start(bf16[2,256,1024]{2,1,0:T(8,128)(2,1)} %param.24) | copy-start | bytes 3145732
  45.9 1.2 %copy-start.1 = (bf16[2,1024,256]{2,1,0:T(8,128)(2,1)S(1)}, bf16[2,1024,256]{2,1,0:T(8,128)(2,1)}, u32[]{:S(2)}) copy-start(bf16[2,1024,256]{2,1,0:T(8,128)(2,1)} %param.25) | copy-start | bytes 3145732

commit v14 on v13

--- a/solution.py
+++ b/solution.py
@@ -22,7 +22,7 @@
     return (picked == cols).astype(jnp.bfloat16)
 
 
-def _conv_body(x_ref, w_ref, b_ref, r_ref, c_ref, o_ref, wide_ref):
+def _conv_body(x_ref, w_ref, b_ref, r_ref, c_ref, h_ref, o_ref, wide_ref):
     oh, ow, ch = x_ref.shape[1] // 2, x_ref.shape[2] // 2, o_ref.shape[2]
     cin = x_ref.shape[3]
     lanes = wide_ref.shape[3]
@@ -76,10 +76,11 @@
     mixed = jnp.dot(high, features, preferred_element_type=jnp.float32) + jnp.dot(
         low, features, preferred_element_type=jnp.float32
     )
-    o_ref[0] = mixed.astype(o_ref.dtype)
-
-
-def conv_resample(x, w, b, row_mix, col_mix):
+    o_ref[0, :cells] = mixed.astype(o_ref.dtype)
+    o_ref[0, cells:] = jnp.broadcast_to(h_ref[0], (o_ref.shape[1] - cells, ch))
+
+
+def conv_resample(x, w, b, row_mix, col_mix, header):
     n, h, wd, cin = x.shape
     cout = w.shape[3]
     oh, ow = h // 2, wd // 2
@@ -93,13 +94,14 @@
             pl.BlockSpec((1, cout), lambda i: (0, 0)),
             pl.BlockSpec((1, rb, oh), lambda i: (i, 0, 0)),
             pl.BlockSpec((1, rw, ow), lambda i: (i, 0, 0)),
+            pl.BlockSpec((1, 1, cout), lambda i: (i, 0, 0)),
         ],
-        out_specs=pl.BlockSpec((1, rb * rw, cout), lambda i: (i, 0, 0)),
-        out_shape=jax.ShapeDtypeStruct((n, rb * rw, cout), jnp.bfloat16),
+        out_specs=pl.BlockSpec((1, (rb + 1) * rw, cout), lambda i: (i, 0, 0)),
+        out_shape=jax.ShapeDtypeStruct((n, (rb + 1) * rw, cout), jnp.bfloat16),
         scratch_shapes=[pltpu.VMEM((cin // 128, h, wd, 128), jnp.float32)],
         compiler_params=pltpu.CompilerParams(dimension_semantics=("arbitrary",)),
-    )(x, w, b.reshape(1, cout), row_mix, col_mix)
-    return out.reshape(n, rb, rw, cout)
+    )(x, w, b.reshape(1, cout), row_mix, col_mix, header)
+    return out.reshape(n, rb + 1, rw, cout)
 
 
 def shifted(value, axis, steps):
@@ -188,7 +190,6 @@
     tile_cols = background.shape[1]
     channels = background.shape[2]
     bands = lax.axis_size("lat")
-    resampled = conv_resample(swath_input, conv_weight, conv_bias, row_weights, col_weights)
     own_band = lax.axis_index("lat")
     own_bands = block_band[:, 0]
     lane = jnp.arange(channels, dtype=jnp.int32)[None, :]
@@ -197,8 +198,10 @@
         row_offset[:, None],
         jnp.where(lane == 1, col_offset[:, None], jnp.where(lane == 2, own_bands[:, None], 0)),
     ).astype(jnp.bfloat16)
-    header = jnp.broadcast_to(header[:, None, None, :], (blocks_here, 1, RW, channels))
-    payload = jnp.concatenate([resampled, header], axis=1)
+    payload = conv_resample(
+        swath_input, conv_weight, conv_bias, row_weights, col_weights, header[:, None, :]
+    )
+    resampled = payload[:, :RB]
     block_list, row_list, col_list, band_list = [resampled], [row_offset], [col_offset], [own_bands]
     for step in (1, -1):
         got = shifted(payload, "lat", step)

time: 60.3 us -> 61.5 us (1.020)
  local copies, waits for them, and re-layouts: 1.17 us -> 2.12 us
  waiting for transfers between devices: 14.3 us -> 13.5 us
  Pallas kernels: 8.19 us -> 8.88 us
    convert_element_type x1, other arithmetic: 0.08 us -> 1.36 us  [per_device(): header = jnp.where(lane == 0, row_offset[:, None], jnp.where(lane == 1, c...]
    concatenate x1 -> x0, other arithmetic: 0.98 us -> none  [per_device(): payload = jnp.concatenate([resampled, header], axis=1)]
    slice x0 -> x1, local copies, waits for them, and re-layouts: none -> 0.97 us  [per_device(): resampled = payload[:, :RB]]
    ppermute x2, waiting for transfers between devices: 9.53 us -> 8.77 us  [shifted(): lax.ppermute(value, axis, [(source, source + steps) for source in range(l...]
    pallas_call x1, Pallas kernels: 8.19 us -> 8.88 us  [conv_resample(): pl.pallas_call(_conv_body, grid=(n,), in_specs=[pl.BlockSpec((1, h, wd, c...]
  transfers between devices with their start and end apart: 6 -> 6, of which waited for: 4 -> 4; matrix products, arithmetic and copies ran while one was open for 14% -> 15% of each run, Pallas kernels for 0% -> 0%
where the time goes in v14:
time: 61.5 us; the launch traced here: 61.2 us
  other arithmetic  15.7 us (26%)
  starting transfers between devices  14.4 us (23%)
  waiting for transfers between devices  13.5 us (22%)
  Pallas kernels  8.88 us (14%)
  matrix products  6.15 us (10%)
  local copies, waits for them, and re-layouts  2.12 us (3%)
    reduce_sum x4, other arithmetic, layer_apply(): centered = mixed - jnp.mean(mixed, axis=-1, keepdims=True)  11.8 us
    pallas_call x1, Pallas kernels, conv_resample(): pl.pallas_call(_conv_body, grid=(n,), in_specs=[pl.BlockSpec((1, h, wd, c...  8.88 us
    ppermute x2, waiting for transfers between devices, shifted(): lax.ppermute(value, axis, [(source, source + steps) for source in range(l...  8.77 us
    ppermute x2, starting transfers between devices, shifted(): lax.ppermute(value, axis, [(source, source + steps) for source in range(l...  5.28 us
    ppermute x1, starting transfers between devices, per_device(): north = lax.ppermute(lon_wide[length - reach:], 'lat', up)  3.37 us
    ppermute x1, waiting for transfers between devices, with_halo(): after = lax.ppermute(leading, axis, down)  3.14 us
    ppermute x1, starting transfers between devices, per_device(): south = lax.ppermute(lon_wide[:reach], 'lat', down)  3 us
    ppermute x1, starting transfers between devices, with_halo(): before = lax.ppermute(last, axis, up)  2.72 us
  transfers between devices with their start and end apart: 6, of which 4 were waited for; matrix products, arithmetic and copies ran while one was open for 15% of the time, Pallas kernels for 0%

profile of v14, /device:TPU:5, one launch (start us, length us, event | category | flops | bytes accessed | tf_op | source)
XLA Modules:
  0.0 61.2 jit_solution(5691281712504577442)
XLA Ops:
  0.0 1.4 %fusion.290.h_ref = bf16[2,1,256]{2,1,0:T(2,128)(2,1)} fusion(pred[256]{0:T(512)(128)(4,1)S(1)} %iota_compare_fusion.4, pred[256]{0:T(512)(128)(4,1)S(1)} %get-tuple-element.130, pred[256]{0:T(512)(128)(4,1)S(1)} %get-tuple-element.129, s32[2]{0:T(128)} %param.18, s32[2]{0:T(128)} %param.17, s32[2]{0:T(128)} %bitcast.382), kind=kLoop, calls=%fused_computation.498 | loop fusion | flops 2048 | bytes 1816 | tf_op jit(solution)/shard_map/convert_element_type | solution.py:200
  1.4 0.0 copy-start.6
  1.4 8.9 %shard_map.127 = bf16[2,272,256]{2,1,0:T(8,128)(2,1)} custom-call(bf16[2,64,64,256]{3,2,1,0:T(8,128)(2,1)} %x_ref.1, bf16[3,3,256,256]{3,2,1,0:T(8,128)(2,1)} %w_ref.1, f32[1,256]{1,0:T(1,128)} %bitcast.384, bf16[2,16,32]{2,1,0:T(8,128)(2,1)} %r_ref.1, bf16[2,16,32]{2,1,0:T(8,128)(2,1)} %c_ref.1, bf16[2,1,256]{2,1,0:T(2,128)(2,1)} %fusion.290.h_ref), custom_call_target="tpu_custom_call" | custom-call | tf_op jit(solution)/shard_map/pallas_call | solution.py:88
  10.3 3.1 %collective-permute-start.1 = (bf16[2,17,16,256]{3,2,1,0:T(8,128)(2,1)}, bf16[2,17,16,256]{3,2,1,0:T(8,128)(2,1)S(1)}, u32[]{:S(2)}, u32[]{:S(2)}) collective-permute-start(bf16[2,17,16,256]{3,2,1,0:T(8,128)(2,1)} %bitcast.172), channel_id=1, source_target_pairs={{8,0},{16,8},{24,16},{9,1},{17,9},{25,17},{10,2},{18,10},{26,18},{... | collective-permute-start | bytes 835592 | tf_op jit(solution)/shard_map/ppermute | solution.py:110
  13.3 2.2 %collective-permute-start = (bf16[2,17,16,256]{3,2,1,0:T(8,128)(2,1)}, bf16[2,17,16,256]{3,2,1,0:T(8,128)(2,1)S(1)}, u32[]{:S(2)}, u32[]{:S(2)}) collective-permute-start(bf16[2,17,16,256]{3,2,1,0:T(8,128)(2,1)} %bitcast.173), channel_id=1, source_target_pairs={{0,8},{8,16},{16,24},{1,9},{9,17},{17,25},{2,10},{10,18},{18,26},{... | collective-permute-start | bytes 835592 | tf_op jit(solution)/shard_map/ppermute | solution.py:110
  15.6 0.1 fusion.304
  15.8 1.0 %slice.1632 = bf16[2,16,16,256]{3,2,1,0:T(8,128)(2,1)S(1)} slice(bf16[2,17,16,256]{3,2,1,0:T(8,128)(2,1)} %bitcast.174), slice={[0:2], [0:16], [0:16], [0:256]} | slice | bytes 524288 | tf_op jit(solution)/shard_map/slice | solution.py:204
  16.9 3.0 %collective-permute-done.1 = bf16[2,17,16,256]{3,2,1,0:T(8,128)(2,1)S(1)} collective-permute-done((bf16[2,17,16,256]{3,2,1,0:T(8,128)(2,1)}, bf16[2,17,16,256]{3,2,1,0:T(8,128)(2,1)S(1)}, u32[]{:S(2)}, u32[]{:S(2)}) %collective-permute-start.1) | collective-permute-done | bytes 278560 | tf_op jit(solution)/shard_map/ppermute | solution.py:110
  19.9 0.2 slice_reduce_fusion
  20.1 5.7 %collective-permute-done = bf16[2,17,16,256]{3,2,1,0:T(8,128)(2,1)S(1)} collective-permute-done((bf16[2,17,16,256]{3,2,1,0:T(8,128)(2,1)}, bf16[2,17,16,256]{3,2,1,0:T(8,128)(2,1)S(1)}, u32[]{:S(2)}, u32[]{:S(2)}) %collective-permute-start) | collective-permute-done | bytes 278560 | tf_op jit(solution)/shard_map/ppermute | solution.py:110
  25.9 0.2 slice_reduce_fusion.1
  26.1 0.1 pad_add_fusion
  26.2 0.1 iota_add_fusion
  26.3 0.1 fusion.292
  26.3 0.1 iota_add_fusion.1
  26.5 0.1 pad_maximum_fusion
  26.6 0.8 %convolution_convert_fusion = bf16[6,24,16,256]{3,1,2,0:T(8,128)(2,1)S(1)} fusion(bf16[6,16,16,256]{3,2,1,0:T(8,128)(2,1)S(1)} %pad_maximum_fusion, s32[6,16]{1,0:T(8,128)S(1)} %iota_add_fusion.1), kind=kOutput, calls=%fused_computation.18 | convolution fusion | flops 19466496 | bytes 1966464 | tf_op jit(solution)/shard_map/shr,sruc->shuc/dot_general | solution.py:226
  27.4 0.4 fusion.17
  27.8 2.7 %collective-permute-start.2 = (bf16[24,6,256]{2,1,0:T(8,128)(2,1)S(1)}, bf16[24,6,256]{2,1,0:T(8,128)(2,1)S(1)}, u32[]{:S(2)}, u32[]{:S(2)}) collective-permute-start(bf16[24,6,256]{2,1,0:T(8,128)(2,1)S(1)} %get-tuple-element.23), channel_id=1, source_target_pairs={{0,1},{1,2},{2,3},{3,4},{4,5},{5,6},{6,7},{7,0},{8,9},{9,10},{10,1... | collective-permute-start | bytes 221192 | tf_op jit(solution)/shard_map/ppermute | solution.py:120
  30.6 1.6 %collective-permute-done.2 = bf16[24,6,256]{2,1,0:T(8,128)(2,1)S(1)} collective-permute-done((bf16[24,6,256]{2,1,0:T(8,128)(2,1)S(1)}, bf16[24,6,256]{2,1,0:T(8,128)(2,1)S(1)}, u32[]{:S(2)}, u32[]{:S(2)}) %collective-permute-start.2) | collective-permute-done | bytes 73760 | tf_op jit(solution)/shard_map/ppermute | solution.py:120
  32.2 3.1 %collective-permute-done.3 = bf16[24,6,256]{2,1,0:T(8,128)(2,1)S(1)} collective-permute-done((bf16[24,6,256]{2,1,0:T(8,128)(2,1)S(1)}, bf16[24,6,256]{2,1,0:T(8,128)(2,1)S(1)}, u32[]{:S(2)}, u32[]{:S(2)}) %collective-permute-start.3) | collective-permute-done | bytes 73760 | tf_op jit(solution)/shard_map/ppermute | solution.py:121
  35.3 0.2 fusion.293
  35.6 3.4 %collective-permute-start.4 = (bf16[6,36,256]{2,1,0:T(8,128)(2,1)S(1)}, bf16[6,36,256]{2,1,0:T(8,128)(2,1)S(1)}, u32[]{:S(2)}, u32[]{:S(2)}) collective-permute-start(bf16[6,36,256]{2,1,0:T(8,128)(2,1)S(1)} %get-tuple-element.21), channel_id=1, source_target_pairs={{0,8},{8,16},{16,24},{1,9},{9,17},{17,25},{2,10},{10,18},{18,26},{... | collective-permute-start | bytes 331784 | tf_op jit(solution)/shard_map/ppermute | solution.py:236
  38.9 3.0 %collective-permute-start.5 = (bf16[6,36,256]{2,1,0:T(8,128)(2,1)S(1)}, bf16[6,36,256]{2,1,0:T(8,128)(2,1)S(1)}, u32[]{:S(2)}, u32[]{:S(2)}) collective-permute-start(bf16[6,36,256]{2,1,0:T(8,128)(2,1)S(1)} %get-tuple-element.22), channel_id=1, source_target_pairs={{8,0},{16,8},{24,16},{9,1},{17,9},{25,17},{10,2},{18,10},{26,18},{... | collective-permute-start | bytes 331784 | tf_op jit(solution)/shard_map/ppermute | solution.py:237
  41.9 0.1 slice.1727
  42.0 4.4 %fusion.298 = (f32[18,32]{1,0:T(8,128)S(1)}, f32[18,32,256]{2,1,0:T(8,128)S(1)}) fusion(f32[256]{0:T(256)S(1)} %bitcast.274, f32[256]{0:T(256)S(1)} %bitcast.277, f32[256]{0:T(256)S(1)} %bitcast.280, f32[256]{0:T(256)S(1)} %bitcast.283, f32[256]{0:T(256)S(1)} %bitcast.286, f32[256]{0:T(256)S(1)} %bitcast.289, f32[256]{0:T(256)S(1)} %bitcast.292, ...), kind=kLoop, calls=%fused_computation.522 | loop fusion | flops 14450112 | bytes 22269184 | tf_op jit(solution)/shard_map/reduce_sum | solution.py:159
  46.4 0.3 multiply_reduce_fusion.1
  46.7 0.2 multiply_convert_fusion.1
  47.0 0.0 copy-start
  47.0 0.9 %fusion.7 = bf16[576,1024]{1,0:T(8,128)(2,1)S(1)} fusion(bf16[576,256]{1,0:T(8,128)(2,1)S(1)} %bitcast.178, bf16[2,256,1024]{2,1,0:T(8,128)(2,1)S(1)} %copy-done.7), kind=kOutput, calls=%fused_computation.9 | convolution fusion | flops 307298304 | bytes 1998848 | tf_op jit(solution)/shard_map/dot_general | solution.py:163
  47.9 0.3 copy-done
  48.2 0.5 fusion.144
  48.7 0.1 fusion.85
  48.9 1.4 %fusion.300 = (f32[6,32]{1,0:T(8,128)S(1)}, f32[6,32,256]{2,1,0:T(8,128)S(1)}) fusion(f32[256]{0:T(256)S(1)} %bitcast.275, f32[256]{0:T(256)S(1)} %bitcast.278, f32[256]{0:T(256)S(1)} %bitcast.281, f32[256]{0:T(256)S(1)} %bitcast.284, f32[256]{0:T(256)S(1)} %bitcast.287, f32[256]{0:T(256)S(1)} %bitcast.290, f32[256]{0:T(256)S(1)} %bitcast.293, ...), kind=kLoop, calls=%fused_computation.523 | loop fusion | flops 4816704 | bytes 7620352 | tf_op jit(solution)/shard_map/reduce_sum | solution.py:159
  50.4 1.4 %fusion.296 = (f32[6,32]{1,0:T(8,128)S(1)}, f32[6,32,256]{2,1,0:T(8,128)S(1)}) fusion(f32[256]{0:T(256)S(1)} %bitcast.276, f32[256]{0:T(256)S(1)} %bitcast.279, f32[256]{0:T(256)S(1)} %bitcast.282, f32[256]{0:T(256)S(1)} %bitcast.285, f32[256]{0:T(256)S(1)} %bitcast.288, f32[256]{0:T(256)S(1)} %bitcast.291, f32[256]{0:T(256)S(1)} %bitcast.294, ...), kind=kLoop, calls=%fused_computation.521 | loop fusion | flops 4816704 | bytes 7620352 | tf_op jit(solution)/shard_map/reduce_sum | solution.py:159
  51.9 0.2 multiply_reduce_fusion.2
  52.1 0.2 multiply_reduce_fusion.3
  52.2 0.2 multiply_convert_fusion.3
  52.4 0.4 fusion.35
  52.9 0.3 fusion.142
  53.1 0.4 fusion.27
  53.6 0.3 fusion.146
  53.9 0.1 fusion.159
  54.1 4.5 %fusion.294 = (f32[24,24]{1,0:T(8,128)S(1)}, f32[24,24,256]{2,1,0:T(8,128)S(1)}) fusion(f32[256]{0:T(256)S(1)} %bitcast.363, f32[30,30,256]{2,1,0:T(8,128)S(1)} %fusion.159, f32[256]{0:T(256)S(1)} %bitcast.364, f32[256]{0:T(256)S(1)} %bitcast.365, f32[256]{0:T(256)S(1)} %bitcast.366, f32[256]{0:T(256)S(1)} %bitcast.367, f32[256]{0:T(256)S(1)} %bitcast.368, ...), kind=kLoop, calls=%fused_computation.520 | loop fusion | flops 14450112 | bytes 29543680 | tf_op jit(solution)/shard_map/reduce_sum | solution.py:159
  58.5 0.3 multiply_reduce_fusion
  58.8 0.2 multiply_convert_fusion
  59.1 0.9 %fusion.15 = bf16[576,1024]{1,0:T(8,128)(2,1)S(1)} fusion(bf16[576,256]{1,0:T(8,128)(2,1)S(1)} %bitcast.177, bf16[2,256,1024]{2,1,0:T(8,128)(2,1)S(1)} %copy-done.7), kind=kOutput, calls=%fused_computation.17 | convolution fusion | flops 307298304 | bytes 1998848 | tf_op jit(solution)/shard_map/dot_general | solution.py:163
  60.0 1.2 %fusion.18 = bf16[24,24,256]{2,1,0:T(8,128)(2,1)} fusion(bf16[24,24,1024]{2,1,0:T(8,128)(2,1)S(1)} %bitcast.385, f32[30,30,256]{2,1,0:T(8,128)S(1)} %fusion.159, bf16[2,1024,256]{2,1,0:T(8,128)(2,1)S(1)} %copy-done), kind=kOutput, calls=%fused_computation.23 | convolution fusion | flops 302284800 | bytes 2588672 | tf_op jit(solution)/shard_map/dot_general | solution.py:166
  (49 shorter events, 0.5 us)
Async XLA Ops:
  1.4 14.2 %copy-start.2 = (f32[2,7,7,256]{3,0,2,1:T(2,128)S(1)}, f32[2,7,7,256]{3,0,2,1:T(2,128)}, u32[]{:S(2)}) copy-start(f32[2,7,7,256]{3,0,2,1:T(2,128)} %param.22) | copy-start | bytes 301060
  1.4 14.5 %copy-start.3 = (f32[2,256]{1,0:T(2,128)S(1)}, f32[2,256]{1,0:T(2,128)}, u32[]{:S(2)}) copy-start(f32[2,256]{1,0:T(2,128)} %param.23) | copy-start | bytes 6148
  1.4 24.7 %copy-start.4 = (s32[2]{0:T(128)S(1)}, s32[2]{0:T(128)}, u32[]{:S(2)}) copy-start(s32[2]{0:T(128)} %param.18) | copy-start | bytes 28
  1.4 24.9 %copy-start.5 = (s32[2]{0:T(128)S(1)}, s32[2]{0:T(128)}, u32[]{:S(2)}) copy-start(s32[2]{0:T(128)} %param.17) | copy-start | bytes 28
  1.4 24.9 %copy-start.6 = (s32[2,1]{0,1:T(1,128)S(1)}, s32[2,1]{0,1:T(1,128)}, u32[]{:S(2)}) copy-start(s32[2,1]{0,1:T(1,128)} %param.16) | copy-start | bytes 28
  10.3 9.6 %collective-permute-start.1 = (bf16[2,17,16,256]{3,2,1,0:T(8,128)(2,1)}, bf16[2,17,16,256]{3,2,1,0:T(8,128)(2,1)S(1)}, u32[]{:S(2)}, u32[]{:S(2)}) collective-permute-start(bf16[2,17,16,256]{3,2,1,0:T(8,128)(2,1)} %bitcast.172), channel_id=1, source_target_pairs={{8,0},{16,8},{24,16},{9,1},{17,9},{25,17},{10,2},{18,10},{26,18},{... | collective-permute-start | bytes 835592 | tf_op jit(solution)/shard_map/ppermute | solution.py:110
  13.3 12.5 %collective-permute-start = (bf16[2,17,16,256]{3,2,1,0:T(8,128)(2,1)}, bf16[2,17,16,256]{3,2,1,0:T(8,128)(2,1)S(1)}, u32[]{:S(2)}, u32[]{:S(2)}) collective-permute-start(bf16[2,17,16,256]{3,2,1,0:T(8,128)(2,1)} %bitcast.173), channel_id=1, source_target_pairs={{0,8},{8,16},{16,24},{1,9},{9,17},{17,25},{2,10},{10,18},{18,26},{... | collective-permute-start | bytes 835592 | tf_op jit(solution)/shard_map/ppermute | solution.py:110
  16.8 10.6 %copy-start.1 = (bf16[24,24,256]{2,1,0:T(8,128)(2,1)S(1)}, bf16[24,24,256]{2,1,0:T(8,128)(2,1)}, u32[]{:S(2)}) copy-start(bf16[24,24,256]{2,1,0:T(8,128)(2,1)} %param.21) | copy-start | bytes 884740
  27.8 4.4 %collective-permute-start.2 = (bf16[24,6,256]{2,1,0:T(8,128)(2,1)S(1)}, bf16[24,6,256]{2,1,0:T(8,128)(2,1)S(1)}, u32[]{:S(2)}, u32[]{:S(2)}) collective-permute-start(bf16[24,6,256]{2,1,0:T(8,128)(2,1)S(1)} %get-tuple-element.23), channel_id=1, source_target_pairs={{0,1},{1,2},{2,3},{3,4},{4,5},{5,6},{6,7},{7,0},{8,9},{9,10},{10,1... | collective-permute-start | bytes 221192 | tf_op jit(solution)/shard_map/ppermute | solution.py:120
  30.6 4.8 %collective-permute-start.3 = (bf16[24,6,256]{2,1,0:T(8,128)(2,1)S(1)}, bf16[24,6,256]{2,1,0:T(8,128)(2,1)S(1)}, u32[]{:S(2)}, u32[]{:S(2)}) collective-permute-start(bf16[24,6,256]{2,1,0:T(8,128)(2,1)S(1)} %get-tuple-element.24), channel_id=1, source_target_pairs={{1,0},{2,1},{3,2},{4,3},{5,4},{6,5},{7,6},{0,7},{9,8},{10,9},{11,1... | collective-permute-start | bytes 221192 | tf_op jit(solution)/shard_map/ppermute | solution.py:121
  35.6 14.8 %collective-permute-start.4 = (bf16[6,36,256]{2,1,0:T(8,128)(2,1)S(1)}, bf16[6,36,256]{2,1,0:T(8,128)(2,1)S(1)}, u32[]{:S(2)}, u32[]{:S(2)}) collective-permute-start(bf16[6,36,256]{2,1,0:T(8,128)(2,1)S(1)} %get-tuple-element.21), channel_id=1, source_target_pairs={{0,8},{8,16},{16,24},{1,9},{9,17},{17,25},{2,10},{10,18},{18,26},{... | collective-permute-start | bytes 331784 | tf_op jit(solution)/shard_map/ppermute | solution.py:236
  38.9 9.9 %collective-permute-start.5 = (bf16[6,36,256]{2,1,0:T(8,128)(2,1)S(1)}, bf16[6,36,256]{2,1,0:T(8,128)(2,1)S(1)}, u32[]{:S(2)}, u32[]{:S(2)}) collective-permute-start(bf16[6,36,256]{2,1,0:T(8,128)(2,1)S(1)} %get-tuple-element.22), channel_id=1, source_target_pairs={{8,0},{16,8},{24,16},{9,1},{17,9},{25,17},{10,2},{18,10},{26,18},{... | collective-permute-start | bytes 331784 | tf_op jit(solution)/shard_map/ppermute | solution.py:237
  42.0 5.0 %copy-start.7 = (bf16[2,256,1024]{2,1,0:T(8,128)(2,1)S(1)}, bf16[2,256,1024]{2,1,0:T(8,128)(2,1)}, u32[]{:S(2)}) copy-start(bf16[2,256,1024]{2,1,0:T(8,128)(2,1)} %param.24) | copy-start | bytes 3145732
  47.0 1.2 %copy-start = (bf16[2,1024,256]{2,1,0:T(8,128)(2,1)S(1)}, bf16[2,1024,256]{2,1,0:T(8,128)(2,1)}, u32[]{:S(2)}) copy-start(bf16[2,1024,256]{2,1,0:T(8,128)(2,1)} %param.25) | copy-start | bytes 3145732

commit v15 on v13

--- a/solution.py
+++ b/solution.py
@@ -76,7 +76,8 @@
     mixed = jnp.dot(high, features, preferred_element_type=jnp.float32) + jnp.dot(
         low, features, preferred_element_type=jnp.float32
     )
-    o_ref[0] = mixed.astype(o_ref.dtype)
+    o_ref[0, :cells] = mixed.astype(o_ref.dtype)
+    o_ref[0, cells:] = jnp.zeros((o_ref.shape[1] - cells, ch), o_ref.dtype)
 
 
 def conv_resample(x, w, b, row_mix, col_mix):
@@ -94,12 +95,12 @@
             pl.BlockSpec((1, rb, oh), lambda i: (i, 0, 0)),
             pl.BlockSpec((1, rw, ow), lambda i: (i, 0, 0)),
         ],
-        out_specs=pl.BlockSpec((1, rb * rw, cout), lambda i: (i, 0, 0)),
-        out_shape=jax.ShapeDtypeStruct((n, rb * rw, cout), jnp.bfloat16),
+        out_specs=pl.BlockSpec((1, (rb + 1) * rw, cout), lambda i: (i, 0, 0)),
+        out_shape=jax.ShapeDtypeStruct((n, (rb + 1) * rw, cout), jnp.bfloat16),
         scratch_shapes=[pltpu.VMEM((cin // 128, h, wd, 128), jnp.float32)],
         compiler_params=pltpu.CompilerParams(dimension_semantics=("arbitrary",)),
     )(x, w, b.reshape(1, cout), row_mix, col_mix)
-    return out.reshape(n, rb, rw, cout)
+    return out.reshape(n, rb + 1, rw, cout)
 
 
 def shifted(value, axis, steps):
@@ -197,13 +198,12 @@
         row_offset[:, None],
         jnp.where(lane == 1, col_offset[:, None], jnp.where(lane == 2, own_bands[:, None], 0)),
     ).astype(jnp.bfloat16)
-    header = jnp.broadcast_to(header[:, None, None, :], (blocks_here, 1, RW, channels))
-    payload = jnp.concatenate([resampled, header], axis=1)
-    block_list, row_list, col_list, band_list = [resampled], [row_offset], [col_offset], [own_bands]
+    payload = resampled.at[:, RB, 0, :].set(header)
+    block_list, row_list, col_list, band_list = [payload], [row_offset], [col_offset], [own_bands]
     for step in (1, -1):
         got = shifted(payload, "lat", step)
         got_header = got[:, RB, 0, :].astype(jnp.int32)
-        block_list.append(got[:, :RB])
+        block_list.append(got)
         row_list.append(got_header[:, 0])
         col_list.append(got_header[:, 1])
         band_list.append(got_header[:, 2])
@@ -214,8 +214,9 @@
     all_cols = jnp.concatenate(col_list, axis=0)
     row_place = (
         jnp.arange(tile_rows, dtype=jnp.int32)[None, :, None]
-        == all_rows[:, None, None] + jnp.arange(RB, dtype=jnp.int32)[None, None, :]
-    ).astype(jnp.bfloat16)
+        == all_rows[:, None, None] + jnp.arange(RB + 1, dtype=jnp.int32)[None, None, :]
+    ) & (jnp.arange(RB + 1, dtype=jnp.int32) < RB)[None, None, :]
+    row_place = row_place.astype(jnp.bfloat16)
     col_place = (
         jnp.arange(tile_cols, dtype=jnp.int32)[None, :, None]
         == all_cols[:, None, None] + jnp.arange(RW, dtype=jnp.int32)[None, None, :]

time: 60.3 us -> 61.7 us (1.023)
  local copies, waits for them, and re-layouts: 1.17 us -> 2.42 us
    scatter x0 -> x1, local copies, waits for them, and re-layouts: none -> 1.31 us  [per_device(): payload = resampled.at[:, RB, 0, :].set(header)]
    concatenate x1 -> x0, other arithmetic: 0.98 us -> none  [per_device(): payload = jnp.concatenate([resampled, header], axis=1)]
    concatenate x1, other arithmetic: 0.09 us -> 1.06 us  [per_device(): arrived = jnp.concatenate(block_list, axis=0)]
where the time goes in v15:
time: 61.7 us; the launch traced here: 61.4 us
  other arithmetic  15.4 us (25%)
  starting transfers between devices  14.5 us (24%)
  waiting for transfers between devices  14.5 us (24%)
  Pallas kernels  8.19 us (13%)
  matrix products  5.94 us (10%)
  local copies, waits for them, and re-layouts  2.42 us (4%)
    reduce_sum x4, other arithmetic, layer_apply(): centered = mixed - jnp.mean(mixed, axis=-1, keepdims=True)  11.8 us
    ppermute x2, waiting for transfers between devices, shifted(): lax.ppermute(value, axis, [(source, source + steps) for source in range(l...  9.75 us
    pallas_call x1, Pallas kernels, conv_resample(): pl.pallas_call(_conv_body, grid=(n,), in_specs=[pl.BlockSpec((1, h, wd, c...  8.19 us
    ppermute x2, starting transfers between devices, shifted(): lax.ppermute(value, axis, [(source, source + steps) for source in range(l...  5.41 us
    ppermute x1, starting transfers between devices, per_device(): north = lax.ppermute(lon_wide[length - reach:], 'lat', up)  3.36 us
    ppermute x1, waiting for transfers between devices, with_halo(): after = lax.ppermute(leading, axis, down)  3.14 us
    ppermute x1, starting transfers between devices, per_device(): south = lax.ppermute(lon_wide[:reach], 'lat', down)  3 us
    ppermute x1, starting transfers between devices, with_halo(): before = lax.ppermute(last, axis, up)  2.72 us
  transfers between devices with their start and end apart: 6, of which 4 were waited for; matrix products, arithmetic and copies ran while one was open for 14% of the time, Pallas kernels for 0%

profile of v15, /device:TPU:5, one launch (start us, length us, event | category | flops | bytes accessed | tf_op | source)
XLA Modules:
  0.0 61.4 jit_solution(17298749535919464031)
XLA Ops:
  0.0 0.0 copy-start.2
  0.1 0.0 copy-start.3
  0.1 8.2 %shard_map.127 = bf16[2,272,256]{2,1,0:T(8,128)(2,1)} custom-call(bf16[2,64,64,256]{3,2,1,0:T(8,128)(2,1)} %x_ref.1, bf16[3,3,256,256]{3,2,1,0:T(8,128)(2,1)} %w_ref.1, f32[1,256]{1,0:T(1,128)} %bitcast.382, bf16[2,16,32]{2,1,0:T(8,128)(2,1)} %r_ref.1, bf16[2,16,32]{2,1,0:T(8,128)(2,1)} %c_ref.1), custom_call_target="tpu_custom_call" | custom-call | tf_op jit(solution)/shard_map/pallas_call | solution.py:88
  8.3 0.1 fusion.292
  8.4 1.3 %scatter.4 = bf16[2,17,16,256]{3,2,1,0:T(8,128)(2,1)} dynamic-update-slice(bf16[2,17,16,256]{3,2,1,0:T(8,128)(2,1)} %bitcast.172, bf16[2,1,1,256]{3,2,1,0:T(2,128)(2,1)S(1)} %fusion.292, s32[]{:T(128)} %constant.74.clone.1, s32[]{:T(128)} %constant.78.clone.1, s32[]{:T(128)} %constant.74.clone.1, s32[]{:T(128)} %constant.74.clone.1) | dynamic-update-slice | bytes 2052 | tf_op jit(solution)/shard_map/scatter | solution.py:201
  9.7 3.2 %collective-permute-start.1 = (bf16[2,17,16,256]{3,2,1,0:T(8,128)(2,1)}, bf16[2,17,16,256]{3,2,1,0:T(8,128)(2,1)S(1)}, u32[]{:S(2)}, u32[]{:S(2)}) collective-permute-start(bf16[2,17,16,256]{3,2,1,0:T(8,128)(2,1)} %scatter.4), channel_id=1, source_target_pairs={{8,0},{16,8},{24,16},{9,1},{17,9},{25,17},{10,2},{18,10},{26,18},{... | collective-permute-start | bytes 835592 | tf_op jit(solution)/shard_map/ppermute | solution.py:109
  12.9 2.2 %collective-permute-start = (bf16[2,17,16,256]{3,2,1,0:T(8,128)(2,1)}, bf16[2,17,16,256]{3,2,1,0:T(8,128)(2,1)S(1)}, u32[]{:S(2)}, u32[]{:S(2)}) collective-permute-start(bf16[2,17,16,256]{3,2,1,0:T(8,128)(2,1)} %scatter.4), channel_id=1, source_target_pairs={{0,8},{8,16},{16,24},{1,9},{9,17},{17,25},{2,10},{10,18},{18,26},{... | collective-permute-start | bytes 835592 | tf_op jit(solution)/shard_map/ppermute | solution.py:109
  15.1 0.1 fusion.306
  15.4 4.0 %collective-permute-done.1 = bf16[2,17,16,256]{3,2,1,0:T(8,128)(2,1)S(1)} collective-permute-done((bf16[2,17,16,256]{3,2,1,0:T(8,128)(2,1)}, bf16[2,17,16,256]{3,2,1,0:T(8,128)(2,1)S(1)}, u32[]{:S(2)}, u32[]{:S(2)}) %collective-permute-start.1) | collective-permute-done | bytes 278560 | tf_op jit(solution)/shard_map/ppermute | solution.py:109
  19.5 0.2 slice_reduce_fusion
  19.7 5.7 %collective-permute-done = bf16[2,17,16,256]{3,2,1,0:T(8,128)(2,1)S(1)} collective-permute-done((bf16[2,17,16,256]{3,2,1,0:T(8,128)(2,1)}, bf16[2,17,16,256]{3,2,1,0:T(8,128)(2,1)S(1)}, u32[]{:S(2)}, u32[]{:S(2)}) %collective-permute-start) | collective-permute-done | bytes 278560 | tf_op jit(solution)/shard_map/ppermute | solution.py:109
  25.4 0.2 slice_reduce_fusion.1
  25.6 0.1 pad_add_fusion
  25.7 0.1 iota_add_fusion
  25.8 0.1 fusion.294
  25.9 0.1 iota_add_fusion.1
  25.9 1.1 %pad_maximum_fusion = bf16[6,17,16,256]{3,2,1,0:T(8,128)(2,1)S(1)} fusion(bf16[2,17,16,256]{3,2,1,0:T(8,128)(2,1)S(1)} %collective-permute-done.1, bf16[2,17,16,256]{3,2,1,0:T(8,128)(2,1)S(1)} %collective-permute-done, bf16[2,17,16,256]{3,2,1,0:T(8,128)(2,1)} %scatter.4), kind=kLoop, calls=%fused_computation.28 | loop fusion | flops 835584 | bytes 1671168 | tf_op jit(solution)/shard_map/concatenate | solution.py:210
  27.0 0.6 convolution_convert_fusion
  27.6 0.4 fusion.17
  28.1 2.7 %collective-permute-start.2 = (bf16[24,6,256]{2,1,0:T(8,128)(2,1)S(1)}, bf16[24,6,256]{2,1,0:T(8,128)(2,1)S(1)}, u32[]{:S(2)}, u32[]{:S(2)}) collective-permute-start(bf16[24,6,256]{2,1,0:T(8,128)(2,1)S(1)} %get-tuple-element.35), channel_id=1, source_target_pairs={{0,1},{1,2},{2,3},{3,4},{4,5},{5,6},{6,7},{7,0},{8,9},{9,10},{10,1... | collective-permute-start | bytes 221192 | tf_op jit(solution)/shard_map/ppermute | solution.py:119
  30.8 1.6 %collective-permute-done.2 = bf16[24,6,256]{2,1,0:T(8,128)(2,1)S(1)} collective-permute-done((bf16[24,6,256]{2,1,0:T(8,128)(2,1)S(1)}, bf16[24,6,256]{2,1,0:T(8,128)(2,1)S(1)}, u32[]{:S(2)}, u32[]{:S(2)}) %collective-permute-start.2) | collective-permute-done | bytes 73760 | tf_op jit(solution)/shard_map/ppermute | solution.py:119
  32.4 3.1 %collective-permute-done.3 = bf16[24,6,256]{2,1,0:T(8,128)(2,1)S(1)} collective-permute-done((bf16[24,6,256]{2,1,0:T(8,128)(2,1)S(1)}, bf16[24,6,256]{2,1,0:T(8,128)(2,1)S(1)}, u32[]{:S(2)}, u32[]{:S(2)}) %collective-permute-start.3) | collective-permute-done | bytes 73760 | tf_op jit(solution)/shard_map/ppermute | solution.py:120
  35.6 0.2 fusion.295
  35.8 3.4 %collective-permute-start.4 = (bf16[6,36,256]{2,1,0:T(8,128)(2,1)S(1)}, bf16[6,36,256]{2,1,0:T(8,128)(2,1)S(1)}, u32[]{:S(2)}, u32[]{:S(2)}) collective-permute-start(bf16[6,36,256]{2,1,0:T(8,128)(2,1)S(1)} %get-tuple-element.33), channel_id=1, source_target_pairs={{0,8},{8,16},{16,24},{1,9},{9,17},{17,25},{2,10},{10,18},{18,26},{... | collective-permute-start | bytes 331784 | tf_op jit(solution)/shard_map/ppermute | solution.py:234
  39.1 3.0 %collective-permute-start.5 = (bf16[6,36,256]{2,1,0:T(8,128)(2,1)S(1)}, bf16[6,36,256]{2,1,0:T(8,128)(2,1)S(1)}, u32[]{:S(2)}, u32[]{:S(2)}) collective-permute-start(bf16[6,36,256]{2,1,0:T(8,128)(2,1)S(1)} %get-tuple-element.34), channel_id=1, source_target_pairs={{8,0},{16,8},{24,16},{9,1},{17,9},{25,17},{10,2},{18,10},{26,18},{... | collective-permute-start | bytes 331784 | tf_op jit(solution)/shard_map/ppermute | solution.py:235
  42.1 0.1 slice.1741
  42.2 4.4 %fusion.300 = (f32[18,32]{1,0:T(8,128)S(1)}, f32[18,32,256]{2,1,0:T(8,128)S(1)}) fusion(f32[256]{0:T(256)S(1)} %bitcast.272, f32[256]{0:T(256)S(1)} %bitcast.275, f32[256]{0:T(256)S(1)} %bitcast.278, f32[256]{0:T(256)S(1)} %bitcast.281, f32[256]{0:T(256)S(1)} %bitcast.284, f32[256]{0:T(256)S(1)} %bitcast.287, f32[256]{0:T(256)S(1)} %bitcast.290, ...), kind=kLoop, calls=%fused_computation.525 | loop fusion | flops 14450112 | bytes 22269184 | tf_op jit(solution)/shard_map/reduce_sum | solution.py:158
  46.7 0.3 multiply_reduce_fusion.1
  47.0 0.2 multiply_convert_fusion.1
  47.2 0.9 %fusion.7 = bf16[576,1024]{1,0:T(8,128)(2,1)S(1)} fusion(bf16[576,256]{1,0:T(8,128)(2,1)S(1)} %bitcast.176, bf16[2,256,1024]{2,1,0:T(8,128)(2,1)S(1)} %copy-done.7), kind=kOutput, calls=%fused_computation.9 | convolution fusion | flops 307298304 | bytes 1998848 | tf_op jit(solution)/shard_map/dot_general | solution.py:162
  48.2 0.3 copy-done
  48.4 0.5 fusion.144
  48.9 0.1 fusion.85
  49.1 1.4 %fusion.302 = (f32[6,32]{1,0:T(8,128)S(1)}, f32[6,32,256]{2,1,0:T(8,128)S(1)}) fusion(f32[256]{0:T(256)S(1)} %bitcast.273, f32[256]{0:T(256)S(1)} %bitcast.276, f32[256]{0:T(256)S(1)} %bitcast.279, f32[256]{0:T(256)S(1)} %bitcast.282, f32[256]{0:T(256)S(1)} %bitcast.285, f32[256]{0:T(256)S(1)} %bitcast.288, f32[256]{0:T(256)S(1)} %bitcast.291, ...), kind=kLoop, calls=%fused_computation.526 | loop fusion | flops 4816704 | bytes 7620352 | tf_op jit(solution)/shard_map/reduce_sum | solution.py:158
  50.6 1.4 %fusion.298 = (f32[6,32]{1,0:T(8,128)S(1)}, f32[6,32,256]{2,1,0:T(8,128)S(1)}) fusion(f32[256]{0:T(256)S(1)} %bitcast.274, f32[256]{0:T(256)S(1)} %bitcast.277, f32[256]{0:T(256)S(1)} %bitcast.280, f32[256]{0:T(256)S(1)} %bitcast.283, f32[256]{0:T(256)S(1)} %bitcast.286, f32[256]{0:T(256)S(1)} %bitcast.289, f32[256]{0:T(256)S(1)} %bitcast.292, ...), kind=kLoop, calls=%fused_computation.524 | loop fusion | flops 4816704 | bytes 7620352 | tf_op jit(solution)/shard_map/reduce_sum | solution.py:158
  52.1 0.2 multiply_reduce_fusion.2
  52.3 0.2 multiply_reduce_fusion.3
  52.5 0.2 multiply_convert_fusion.3
  52.6 0.4 fusion.36
  53.1 0.3 fusion.142
  53.3 0.4 fusion.28
  53.8 0.3 fusion.146
  54.1 0.1 fusion.159
  54.3 4.5 %fusion.296 = (f32[24,24]{1,0:T(8,128)S(1)}, f32[24,24,256]{2,1,0:T(8,128)S(1)}) fusion(f32[256]{0:T(256)S(1)} %bitcast.361, f32[30,30,256]{2,1,0:T(8,128)S(1)} %fusion.159, f32[256]{0:T(256)S(1)} %bitcast.362, f32[256]{0:T(256)S(1)} %bitcast.363, f32[256]{0:T(256)S(1)} %bitcast.364, f32[256]{0:T(256)S(1)} %bitcast.365, f32[256]{0:T(256)S(1)} %bitcast.366, ...), kind=kLoop, calls=%fused_computation.523 | loop fusion | flops 14450112 | bytes 29543680 | tf_op jit(solution)/shard_map/reduce_sum | solution.py:158
  58.7 0.3 multiply_reduce_fusion
  59.0 0.2 multiply_convert_fusion
  59.3 0.9 %fusion.15 = bf16[576,1024]{1,0:T(8,128)(2,1)S(1)} fusion(bf16[576,256]{1,0:T(8,128)(2,1)S(1)} %bitcast.175, bf16[2,256,1024]{2,1,0:T(8,128)(2,1)S(1)} %copy-done.7), kind=kOutput, calls=%fused_computation.17 | convolution fusion | flops 307298304 | bytes 1998848 | tf_op jit(solution)/shard_map/dot_general | solution.py:162
  60.2 1.2 %fusion.18 = bf16[24,24,256]{2,1,0:T(8,128)(2,1)} fusion(bf16[24,24,1024]{2,1,0:T(8,128)(2,1)S(1)} %bitcast.383, f32[30,30,256]{2,1,0:T(8,128)S(1)} %fusion.159, bf16[2,1024,256]{2,1,0:T(8,128)(2,1)S(1)} %copy-done), kind=kOutput, calls=%fused_computation.23 | convolution fusion | flops 302284800 | bytes 2588672 | tf_op jit(solution)/shard_map/dot_general | solution.py:165
  (48 shorter events, 0.5 us)
Async XLA Ops:
  0.0 8.3 %copy-start.4 = (s32[2]{0:T(128)S(1)}, s32[2]{0:T(128)}, u32[]{:S(2)}) copy-start(s32[2]{0:T(128)} %param.20) | copy-start | bytes 28
  0.0 8.2 %copy-start.5 = (s32[2]{0:T(128)S(1)}, s32[2]{0:T(128)}, u32[]{:S(2)}) copy-start(s32[2]{0:T(128)} %param.19) | copy-start | bytes 28
  0.0 8.2 %copy-start.6 = (s32[2,1]{0,1:T(1,128)S(1)}, s32[2,1]{0,1:T(1,128)}, u32[]{:S(2)}) copy-start(s32[2,1]{0,1:T(1,128)} %param.18) | copy-start | bytes 28
  0.0 15.1 %copy-start.2 = (f32[2,7,7,256]{3,0,2,1:T(2,128)S(1)}, f32[2,7,7,256]{3,0,2,1:T(2,128)}, u32[]{:S(2)}) copy-start(f32[2,7,7,256]{3,0,2,1:T(2,128)} %param.24) | copy-start | bytes 301060
  0.1 15.3 %copy-start.3 = (f32[2,256]{1,0:T(2,128)S(1)}, f32[2,256]{1,0:T(2,128)}, u32[]{:S(2)}) copy-start(f32[2,256]{1,0:T(2,128)} %param.25) | copy-start | bytes 6148
  9.7 17.9 %copy-start.1 = (bf16[24,24,256]{2,1,0:T(8,128)(2,1)S(1)}, bf16[24,24,256]{2,1,0:T(8,128)(2,1)}, u32[]{:S(2)}) copy-start(bf16[24,24,256]{2,1,0:T(8,128)(2,1)} %param.23) | copy-start | bytes 884740
  9.7 9.8 %collective-permute-start.1 = (bf16[2,17,16,256]{3,2,1,0:T(8,128)(2,1)}, bf16[2,17,16,256]{3,2,1,0:T(8,128)(2,1)S(1)}, u32[]{:S(2)}, u32[]{:S(2)}) collective-permute-start(bf16[2,17,16,256]{3,2,1,0:T(8,128)(2,1)} %scatter.4), channel_id=1, source_target_pairs={{8,0},{16,8},{24,16},{9,1},{17,9},{25,17},{10,2},{18,10},{26,18},{... | collective-permute-start | bytes 835592 | tf_op jit(solution)/shard_map/ppermute | solution.py:109
  12.9 12.5 %collective-permute-start = (bf16[2,17,16,256]{3,2,1,0:T(8,128)(2,1)}, bf16[2,17,16,256]{3,2,1,0:T(8,128)(2,1)S(1)}, u32[]{:S(2)}, u32[]{:S(2)}) collective-permute-start(bf16[2,17,16,256]{3,2,1,0:T(8,128)(2,1)} %scatter.4), channel_id=1, source_target_pairs={{0,8},{8,16},{16,24},{1,9},{9,17},{17,25},{2,10},{10,18},{18,26},{... | collective-permute-start | bytes 835592 | tf_op jit(solution)/shard_map/ppermute | solution.py:109
  28.1 4.4 %collective-permute-start.2 = (bf16[24,6,256]{2,1,0:T(8,128)(2,1)S(1)}, bf16[24,6,256]{2,1,0:T(8,128)(2,1)S(1)}, u32[]{:S(2)}, u32[]{:S(2)}) collective-permute-start(bf16[24,6,256]{2,1,0:T(8,128)(2,1)S(1)} %get-tuple-element.35), channel_id=1, source_target_pairs={{0,1},{1,2},{2,3},{3,4},{4,5},{5,6},{6,7},{7,0},{8,9},{9,10},{10,1... | collective-permute-start | bytes 221192 | tf_op jit(solution)/shard_map/ppermute | solution.py:119
  30.8 4.8 %collective-permute-start.3 = (bf16[24,6,256]{2,1,0:T(8,128)(2,1)S(1)}, bf16[24,6,256]{2,1,0:T(8,128)(2,1)S(1)}, u32[]{:S(2)}, u32[]{:S(2)}) collective-permute-start(bf16[24,6,256]{2,1,0:T(8,128)(2,1)S(1)} %get-tuple-element.36), channel_id=1, source_target_pairs={{1,0},{2,1},{3,2},{4,3},{5,4},{6,5},{7,6},{0,7},{9,8},{10,9},{11,1... | collective-permute-start | bytes 221192 | tf_op jit(solution)/shard_map/ppermute | solution.py:120
  35.8 14.8 %collective-permute-start.4 = (bf16[6,36,256]{2,1,0:T(8,128)(2,1)S(1)}, bf16[6,36,256]{2,1,0:T(8,128)(2,1)S(1)}, u32[]{:S(2)}, u32[]{:S(2)}) collective-permute-start(bf16[6,36,256]{2,1,0:T(8,128)(2,1)S(1)} %get-tuple-element.33), channel_id=1, source_target_pairs={{0,8},{8,16},{16,24},{1,9},{9,17},{17,25},{2,10},{10,18},{18,26},{... | collective-permute-start | bytes 331784 | tf_op jit(solution)/shard_map/ppermute | solution.py:234
  39.1 9.9 %collective-permute-start.5 = (bf16[6,36,256]{2,1,0:T(8,128)(2,1)S(1)}, bf16[6,36,256]{2,1,0:T(8,128)(2,1)S(1)}, u32[]{:S(2)}, u32[]{:S(2)}) collective-permute-start(bf16[6,36,256]{2,1,0:T(8,128)(2,1)S(1)} %get-tuple-element.34), channel_id=1, source_target_pairs={{8,0},{16,8},{24,16},{9,1},{17,9},{25,17},{10,2},{18,10},{26,18},{... | collective-permute-start | bytes 331784 | tf_op jit(solution)/shard_map/ppermute | solution.py:235
  42.2 5.0 %copy-start.7 = (bf16[2,256,1024]{2,1,0:T(8,128)(2,1)S(1)}, bf16[2,256,1024]{2,1,0:T(8,128)(2,1)}, u32[]{:S(2)}) copy-start(bf16[2,256,1024]{2,1,0:T(8,128)(2,1)} %param.26) | copy-start | bytes 3145732
  47.2 1.2 %copy-start = (bf16[2,1024,256]{2,1,0:T(8,128)(2,1)S(1)}, bf16[2,1024,256]{2,1,0:T(8,128)(2,1)}, u32[]{:S(2)}) copy-start(bf16[2,1024,256]{2,1,0:T(8,128)(2,1)} %param.27) | copy-start | bytes 3145732

commit v16 on v15

--- a/solution.py
+++ b/solution.py
@@ -22,7 +22,7 @@
     return (picked == cols).astype(jnp.bfloat16)
 
 
-def _conv_body(x_ref, w_ref, b_ref, r_ref, c_ref, o_ref, wide_ref):
+def _conv_body(s_ref, x_ref, w_ref, b_ref, r_ref, c_ref, o_ref, wide_ref):
     oh, ow, ch = x_ref.shape[1] // 2, x_ref.shape[2] // 2, o_ref.shape[2]
     cin = x_ref.shape[3]
     lanes = wide_ref.shape[3]
@@ -77,29 +77,39 @@
         low, features, preferred_element_type=jnp.float32
     )
     o_ref[0, :cells] = mixed.astype(o_ref.dtype)
-    o_ref[0, cells:] = jnp.zeros((o_ref.shape[1] - cells, ch), o_ref.dtype)
-
-
-def conv_resample(x, w, b, row_mix, col_mix):
+    step = pl.program_id(0)
+    lane = lax.broadcasted_iota(jnp.int32, (o_ref.shape[1] - cells, ch), 1)
+    header = jnp.where(
+        lane == 0,
+        s_ref[3 * step],
+        jnp.where(lane == 1, s_ref[3 * step + 1], jnp.where(lane == 2, s_ref[3 * step + 2], 0)),
+    )
+    o_ref[0, cells:] = header.astype(jnp.float32).astype(o_ref.dtype)
+
+
+def conv_resample(x, w, b, row_mix, col_mix, table):
     n, h, wd, cin = x.shape
     cout = w.shape[3]
     oh, ow = h // 2, wd // 2
     rb, rw = row_mix.shape[1], col_mix.shape[1]
     out = pl.pallas_call(
         _conv_body,
-        grid=(n,),
-        in_specs=[
-            pl.BlockSpec((1, h, wd, cin), lambda i: (i, 0, 0, 0)),
-            pl.BlockSpec((3, 3, cin, cout), lambda i: (0, 0, 0, 0)),
-            pl.BlockSpec((1, cout), lambda i: (0, 0)),
-            pl.BlockSpec((1, rb, oh), lambda i: (i, 0, 0)),
-            pl.BlockSpec((1, rw, ow), lambda i: (i, 0, 0)),
-        ],
-        out_specs=pl.BlockSpec((1, (rb + 1) * rw, cout), lambda i: (i, 0, 0)),
+        grid_spec=pltpu.PrefetchScalarGridSpec(
+            num_scalar_prefetch=1,
+            grid=(n,),
+            in_specs=[
+                pl.BlockSpec((1, h, wd, cin), lambda i, s: (i, 0, 0, 0)),
+                pl.BlockSpec((3, 3, cin, cout), lambda i, s: (0, 0, 0, 0)),
+                pl.BlockSpec((1, cout), lambda i, s: (0, 0)),
+                pl.BlockSpec((1, rb, oh), lambda i, s: (i, 0, 0)),
+                pl.BlockSpec((1, rw, ow), lambda i, s: (i, 0, 0)),
+            ],
+            out_specs=pl.BlockSpec((1, (rb + 1) * rw, cout), lambda i, s: (i, 0, 0)),
+            scratch_shapes=[pltpu.VMEM((cin // 128, h, wd, 128), jnp.float32)],
+        ),
         out_shape=jax.ShapeDtypeStruct((n, (rb + 1) * rw, cout), jnp.bfloat16),
-        scratch_shapes=[pltpu.VMEM((cin // 128, h, wd, 128), jnp.float32)],
         compiler_params=pltpu.CompilerParams(dimension_semantics=("arbitrary",)),
-    )(x, w, b.reshape(1, cout), row_mix, col_mix)
+    )(table, x, w, b.reshape(1, cout), row_mix, col_mix)
     return out.reshape(n, rb + 1, rw, cout)
 
 
@@ -189,16 +199,10 @@
     tile_cols = background.shape[1]
     channels = background.shape[2]
     bands = lax.axis_size("lat")
-    resampled = conv_resample(swath_input, conv_weight, conv_bias, row_weights, col_weights)
     own_band = lax.axis_index("lat")
     own_bands = block_band[:, 0]
-    lane = jnp.arange(channels, dtype=jnp.int32)[None, :]
-    header = jnp.where(
-        lane == 0,
-        row_offset[:, None],
-        jnp.where(lane == 1, col_offset[:, None], jnp.where(lane == 2, own_bands[:, None], 0)),
-    ).astype(jnp.bfloat16)
-    payload = resampled.at[:, RB, 0, :].set(header)
+    table = jnp.stack([row_offset, col_offset, own_bands], axis=1).reshape(-1).astype(jnp.int32)
+    payload = conv_resample(swath_input, conv_weight, conv_bias, row_weights, col_weights, table)
     block_list, row_list, col_list, band_list = [payload], [row_offset], [col_offset], [own_bands]
     for step in (1, -1):
         got = shifted(payload, "lat", step)

time: 61.7 us -> 62.4 us (1.011)
  Pallas kernels: 8.19 us -> 8.96 us
    scatter x1 -> x0, local copies, waits for them, and re-layouts: 1.31 us -> none  [per_device(): payload = resampled.at[:, RB, 0, :].set(header)]
    pallas_call x1, Pallas kernels: 8.19 us -> 8.96 us  [conv_resample(): pl.pallas_call(_conv_body, grid_spec=pltpu.PrefetchScalarGridSpec(num_sca...]
    another operation x0 -> x1, other arithmetic: none -> 0.7 us  [per_device(): jnp.stack([row_offset, col_offset, own_bands], axis=1).reshape(-1)]
    reshape x0 -> x1, local copies, waits for them, and re-layouts: none -> 0.67 us  [per_device(): jnp.stack([row_offset, col_offset, own_bands], axis=1).reshape(-1)]
where the time goes in v16:
time: 62.4 us; the launch traced here: 62.1 us
  other arithmetic  15.9 us (25%)
  starting transfers between devices  14.5 us (23%)
  waiting for transfers between devices  14.5 us (23%)
  Pallas kernels  8.96 us (14%)
  matrix products  5.95 us (10%)
  local copies, waits for them, and re-layouts  1.87 us (3%)
    reduce_sum x4, other arithmetic, layer_apply(): centered = mixed - jnp.mean(mixed, axis=-1, keepdims=True)  11.8 us
    ppermute x2, waiting for transfers between devices, shifted(): lax.ppermute(value, axis, [(source, source + steps) for source in range(l...  9.74 us
    pallas_call x1, Pallas kernels, conv_resample(): pl.pallas_call(_conv_body, grid_spec=pltpu.PrefetchScalarGridSpec(num_sca...  8.96 us
    ppermute x2, starting transfers between devices, shifted(): lax.ppermute(value, axis, [(source, source + steps) for source in range(l...  5.41 us
    ppermute x1, starting transfers between devices, per_device(): north = lax.ppermute(lon_wide[length - reach:], 'lat', up)  3.36 us
    ppermute x1, waiting for transfers between devices, with_halo(): after = lax.ppermute(leading, axis, down)  3.14 us
    ppermute x1, starting transfers between devices, per_device(): south = lax.ppermute(lon_wide[:reach], 'lat', down)  3 us
    ppermute x1, starting transfers between devices, with_halo(): before = lax.ppermute(last, axis, up)  2.72 us
  transfers between devices with their start and end apart: 6, of which 4 were waited for; matrix products, arithmetic and copies ran while one was open for 14% of the time, Pallas kernels for 0%

profile of v16, /device:TPU:5, one launch (start us, length us, event | category | flops | bytes accessed | tf_op | source)
XLA Modules:
  0.0 62.1 jit_solution(8385249273817828719)
XLA Ops:
  0.0 0.7 %pad_add_fusion = s32[2,3]{0,1:T(4,128)S(1)} fusion(s32[2,1]{0,1:T(1,128)} %param.16, s32[2,1]{0,1:T(1,128)} %bitcast.385, s32[2,1]{0,1:T(1,128)} %bitcast.386), kind=kLoop, calls=%fused_computation.499 | loop fusion | flops 12 | bytes 48 | tf_op jit(solution)/shard_map/stack | solution.py:204
  0.7 0.1 copy.29
  0.8 0.7 %reshape.187.s_ref = s32[6]{0:T(128)} reshape(s32[2,3]{1,0:T(2,128)S(1)} %copy.29) | data formatting | bytes 48 | tf_op jit(solution)/shard_map/reshape | solution.py:204
  1.5 0.0 copy-start.5
  1.5 9.0 %shard_map.127 = bf16[2,272,256]{2,1,0:T(8,128)(2,1)} custom-call(s32[6]{0:T(128)} %reshape.187.s_ref, bf16[2,64,64,256]{3,2,1,0:T(8,128)(2,1)} %x_ref.1, bf16[3,3,256,256]{3,2,1,0:T(8,128)(2,1)} %w_ref.1, f32[1,256]{1,0:T(1,128)} %bitcast.387, bf16[2,16,32]{2,1,0:T(8,128)(2,1)} %r_ref.1, bf16[2,16,32]{2,1,0:T(8,128)(2,1)} %c_ref.1), custom_call_target="tpu_custom_call" | custom-call | tf_op jit(solution)/shard_map/pallas_call | solution.py:95
  10.4 3.2 %collective-permute-start.1 = (bf16[2,17,16,256]{3,2,1,0:T(8,128)(2,1)}, bf16[2,17,16,256]{3,2,1,0:T(8,128)(2,1)S(1)}, u32[]{:S(2)}, u32[]{:S(2)}) collective-permute-start(bf16[2,17,16,256]{3,2,1,0:T(8,128)(2,1)} %bitcast.174), channel_id=1, source_target_pairs={{8,0},{16,8},{24,16},{9,1},{17,9},{25,17},{10,2},{18,10},{26,18},{... | collective-permute-start | bytes 835592 | tf_op jit(solution)/shard_map/ppermute | solution.py:119
  13.6 2.2 %collective-permute-start = (bf16[2,17,16,256]{3,2,1,0:T(8,128)(2,1)}, bf16[2,17,16,256]{3,2,1,0:T(8,128)(2,1)S(1)}, u32[]{:S(2)}, u32[]{:S(2)}) collective-permute-start(bf16[2,17,16,256]{3,2,1,0:T(8,128)(2,1)} %bitcast.175), channel_id=1, source_target_pairs={{0,8},{8,16},{16,24},{1,9},{9,17},{17,25},{2,10},{10,18},{18,26},{... | collective-permute-start | bytes 835592 | tf_op jit(solution)/shard_map/ppermute | solution.py:119
  15.9 0.1 fusion.305
  16.2 4.0 %collective-permute-done.1 = bf16[2,17,16,256]{3,2,1,0:T(8,128)(2,1)S(1)} collective-permute-done((bf16[2,17,16,256]{3,2,1,0:T(8,128)(2,1)}, bf16[2,17,16,256]{3,2,1,0:T(8,128)(2,1)S(1)}, u32[]{:S(2)}, u32[]{:S(2)}) %collective-permute-start.1) | collective-permute-done | bytes 278560 | tf_op jit(solution)/shard_map/ppermute | solution.py:119
  20.2 0.2 slice_reduce_fusion
  20.4 5.7 %collective-permute-done = bf16[2,17,16,256]{3,2,1,0:T(8,128)(2,1)S(1)} collective-permute-done((bf16[2,17,16,256]{3,2,1,0:T(8,128)(2,1)}, bf16[2,17,16,256]{3,2,1,0:T(8,128)(2,1)S(1)}, u32[]{:S(2)}, u32[]{:S(2)}) %collective-permute-start) | collective-permute-done | bytes 278560 | tf_op jit(solution)/shard_map/ppermute | solution.py:119
  26.2 0.2 slice_reduce_fusion.1
  26.4 0.1 fusion.293
  26.5 0.1 iota_add_fusion.1
  26.6 0.1 iota_add_fusion
  26.6 1.0 %pad_maximum_fusion = bf16[6,17,16,256]{3,2,1,0:T(8,128)(2,1)S(1)} fusion(bf16[2,17,16,256]{3,2,1,0:T(8,128)(2,1)S(1)} %collective-permute-done.1, bf16[2,17,16,256]{3,2,1,0:T(8,128)(2,1)S(1)} %collective-permute-done, bf16[2,17,16,256]{3,2,1,0:T(8,128)(2,1)} %bitcast.176), kind=kLoop, calls=%fused_computation.28 | loop fusion | flops 835584 | bytes 1671168 | tf_op jit(solution)/shard_map/concatenate | solution.py:214
  27.7 0.6 convolution_convert_fusion
  28.3 0.4 fusion.17
  28.8 2.7 %collective-permute-start.2 = (bf16[24,6,256]{2,1,0:T(8,128)(2,1)S(1)}, bf16[24,6,256]{2,1,0:T(8,128)(2,1)S(1)}, u32[]{:S(2)}, u32[]{:S(2)}) collective-permute-start(bf16[24,6,256]{2,1,0:T(8,128)(2,1)S(1)} %get-tuple-element.23), channel_id=1, source_target_pairs={{0,1},{1,2},{2,3},{3,4},{4,5},{5,6},{6,7},{7,0},{8,9},{9,10},{10,1... | collective-permute-start | bytes 221192 | tf_op jit(solution)/shard_map/ppermute | solution.py:129
  31.5 1.6 %collective-permute-done.2 = bf16[24,6,256]{2,1,0:T(8,128)(2,1)S(1)} collective-permute-done((bf16[24,6,256]{2,1,0:T(8,128)(2,1)S(1)}, bf16[24,6,256]{2,1,0:T(8,128)(2,1)S(1)}, u32[]{:S(2)}, u32[]{:S(2)}) %collective-permute-start.2) | collective-permute-done | bytes 73760 | tf_op jit(solution)/shard_map/ppermute | solution.py:129
  33.1 3.1 %collective-permute-done.3 = bf16[24,6,256]{2,1,0:T(8,128)(2,1)S(1)} collective-permute-done((bf16[24,6,256]{2,1,0:T(8,128)(2,1)S(1)}, bf16[24,6,256]{2,1,0:T(8,128)(2,1)S(1)}, u32[]{:S(2)}, u32[]{:S(2)}) %collective-permute-start.3) | collective-permute-done | bytes 73760 | tf_op jit(solution)/shard_map/ppermute | solution.py:130
  36.3 0.2 fusion.294
  36.5 3.4 %collective-permute-start.4 = (bf16[6,36,256]{2,1,0:T(8,128)(2,1)S(1)}, bf16[6,36,256]{2,1,0:T(8,128)(2,1)S(1)}, u32[]{:S(2)}, u32[]{:S(2)}) collective-permute-start(bf16[6,36,256]{2,1,0:T(8,128)(2,1)S(1)} %get-tuple-element.21), channel_id=1, source_target_pairs={{0,8},{8,16},{16,24},{1,9},{9,17},{17,25},{2,10},{10,18},{18,26},{... | collective-permute-start | bytes 331784 | tf_op jit(solution)/shard_map/ppermute | solution.py:238
  39.8 3.0 %collective-permute-start.5 = (bf16[6,36,256]{2,1,0:T(8,128)(2,1)S(1)}, bf16[6,36,256]{2,1,0:T(8,128)(2,1)S(1)}, u32[]{:S(2)}, u32[]{:S(2)}) collective-permute-start(bf16[6,36,256]{2,1,0:T(8,128)(2,1)S(1)} %get-tuple-element.22), channel_id=1, source_target_pairs={{8,0},{16,8},{24,16},{9,1},{17,9},{25,17},{10,2},{18,10},{26,18},{... | collective-permute-start | bytes 331784 | tf_op jit(solution)/shard_map/ppermute | solution.py:239
  42.9 0.1 slice.1712
  42.9 0.0 copy-start.7
  42.9 4.4 %fusion.299 = (f32[18,32]{1,0:T(8,128)S(1)}, f32[18,32,256]{2,1,0:T(8,128)S(1)}) fusion(f32[256]{0:T(256)S(1)} %bitcast.276, f32[256]{0:T(256)S(1)} %bitcast.279, f32[256]{0:T(256)S(1)} %bitcast.282, f32[256]{0:T(256)S(1)} %bitcast.285, f32[256]{0:T(256)S(1)} %bitcast.288, f32[256]{0:T(256)S(1)} %bitcast.291, f32[256]{0:T(256)S(1)} %bitcast.294, ...), kind=kLoop, calls=%fused_computation.519 | loop fusion | flops 14450112 | bytes 22269184 | tf_op jit(solution)/shard_map/reduce_sum | solution.py:168
  47.4 0.3 multiply_reduce_fusion.1
  47.7 0.2 multiply_convert_fusion.1
  47.9 0.9 %fusion.7 = bf16[576,1024]{1,0:T(8,128)(2,1)S(1)} fusion(bf16[576,256]{1,0:T(8,128)(2,1)S(1)} %bitcast.180, bf16[2,256,1024]{2,1,0:T(8,128)(2,1)S(1)} %copy-done.7), kind=kOutput, calls=%fused_computation.9 | convolution fusion | flops 307298304 | bytes 1998848 | tf_op jit(solution)/shard_map/dot_general | solution.py:172
  48.9 0.3 copy-done
  49.1 0.5 fusion.144
  49.6 0.1 fusion.85
  49.8 1.4 %fusion.301 = (f32[6,32]{1,0:T(8,128)S(1)}, f32[6,32,256]{2,1,0:T(8,128)S(1)}) fusion(f32[256]{0:T(256)S(1)} %bitcast.277, f32[256]{0:T(256)S(1)} %bitcast.280, f32[256]{0:T(256)S(1)} %bitcast.283, f32[256]{0:T(256)S(1)} %bitcast.286, f32[256]{0:T(256)S(1)} %bitcast.289, f32[256]{0:T(256)S(1)} %bitcast.292, f32[256]{0:T(256)S(1)} %bitcast.295, ...), kind=kLoop, calls=%fused_computation.520 | loop fusion | flops 4816704 | bytes 7620352 | tf_op jit(solution)/shard_map/reduce_sum | solution.py:168
  51.3 1.4 %fusion.297 = (f32[6,32]{1,0:T(8,128)S(1)}, f32[6,32,256]{2,1,0:T(8,128)S(1)}) fusion(f32[256]{0:T(256)S(1)} %bitcast.278, f32[256]{0:T(256)S(1)} %bitcast.281, f32[256]{0:T(256)S(1)} %bitcast.284, f32[256]{0:T(256)S(1)} %bitcast.287, f32[256]{0:T(256)S(1)} %bitcast.290, f32[256]{0:T(256)S(1)} %bitcast.293, f32[256]{0:T(256)S(1)} %bitcast.296, ...), kind=kLoop, calls=%fused_computation.518 | loop fusion | flops 4816704 | bytes 7620352 | tf_op jit(solution)/shard_map/reduce_sum | solution.py:168
  52.8 0.2 multiply_reduce_fusion.2
  53.0 0.2 multiply_reduce_fusion.3
  53.2 0.2 multiply_convert_fusion.3
  53.4 0.4 fusion.36
  53.8 0.3 fusion.142
  54.1 0.4 fusion.28
  54.5 0.3 fusion.146
  54.8 0.1 fusion.159
  55.0 4.5 %fusion.295 = (f32[24,24]{1,0:T(8,128)S(1)}, f32[24,24,256]{2,1,0:T(8,128)S(1)}) fusion(f32[256]{0:T(256)S(1)} %bitcast.365, f32[30,30,256]{2,1,0:T(8,128)S(1)} %fusion.159, f32[256]{0:T(256)S(1)} %bitcast.366, f32[256]{0:T(256)S(1)} %bitcast.367, f32[256]{0:T(256)S(1)} %bitcast.368, f32[256]{0:T(256)S(1)} %bitcast.369, f32[256]{0:T(256)S(1)} %bitcast.370, ...), kind=kLoop, calls=%fused_computation.517 | loop fusion | flops 14450112 | bytes 29543680 | tf_op jit(solution)/shard_map/reduce_sum | solution.py:168
  59.5 0.3 multiply_reduce_fusion
  59.8 0.2 multiply_convert_fusion
  60.0 0.9 %fusion.15 = bf16[576,1024]{1,0:T(8,128)(2,1)S(1)} fusion(bf16[576,256]{1,0:T(8,128)(2,1)S(1)} %bitcast.179, bf16[2,256,1024]{2,1,0:T(8,128)(2,1)S(1)} %copy-done.7), kind=kOutput, calls=%fused_computation.17 | convolution fusion | flops 307298304 | bytes 1998848 | tf_op jit(solution)/shard_map/dot_general | solution.py:172
  60.9 1.2 %fusion.18 = bf16[24,24,256]{2,1,0:T(8,128)(2,1)} fusion(bf16[24,24,1024]{2,1,0:T(8,128)(2,1)S(1)} %bitcast.388, f32[30,30,256]{2,1,0:T(8,128)S(1)} %fusion.159, bf16[2,1024,256]{2,1,0:T(8,128)(2,1)S(1)} %copy-done), kind=kOutput, calls=%fused_computation.23 | convolution fusion | flops 302284800 | bytes 2588672 | tf_op jit(solution)/shard_map/dot_general | solution.py:175
  (46 shorter events, 0.5 us)
Async XLA Ops:
  1.5 14.4 %copy-start.2 = (f32[2,7,7,256]{3,0,2,1:T(2,128)S(1)}, f32[2,7,7,256]{3,0,2,1:T(2,128)}, u32[]{:S(2)}) copy-start(f32[2,7,7,256]{3,0,2,1:T(2,128)} %param.22) | copy-start | bytes 301060
  1.5 14.7 %copy-start.6 = (f32[2,256]{1,0:T(2,128)S(1)}, f32[2,256]{1,0:T(2,128)}, u32[]{:S(2)}) copy-start(f32[2,256]{1,0:T(2,128)} %param.23) | copy-start | bytes 6148
  1.5 24.9 %copy-start.3 = (s32[2,1]{0,1:T(1,128)S(1)}, s32[2,1]{0,1:T(1,128)}, u32[]{:S(2)}) copy-start(s32[2,1]{0,1:T(1,128)} %param.16) | copy-start | bytes 28
  1.5 24.9 %copy-start.4 = (s32[2]{0:T(128)S(1)}, s32[2]{0:T(128)}, u32[]{:S(2)}) copy-start(s32[2]{0:T(128)} %param.18) | copy-start | bytes 28
  1.5 24.9 %copy-start.5 = (s32[2]{0:T(128)S(1)}, s32[2]{0:T(128)}, u32[]{:S(2)}) copy-start(s32[2]{0:T(128)} %param.17) | copy-start | bytes 28
  10.4 17.9 %copy-start.1 = (bf16[24,24,256]{2,1,0:T(8,128)(2,1)S(1)}, bf16[24,24,256]{2,1,0:T(8,128)(2,1)}, u32[]{:S(2)}) copy-start(bf16[24,24,256]{2,1,0:T(8,128)(2,1)} %param.21) | copy-start | bytes 884740
  10.4 9.8 %collective-permute-start.1 = (bf16[2,17,16,256]{3,2,1,0:T(8,128)(2,1)}, bf16[2,17,16,256]{3,2,1,0:T(8,128)(2,1)S(1)}, u32[]{:S(2)}, u32[]{:S(2)}) collective-permute-start(bf16[2,17,16,256]{3,2,1,0:T(8,128)(2,1)} %bitcast.174), channel_id=1, source_target_pairs={{8,0},{16,8},{24,16},{9,1},{17,9},{25,17},{10,2},{18,10},{26,18},{... | collective-permute-start | bytes 835592 | tf_op jit(solution)/shard_map/ppermute | solution.py:119
  13.6 12.5 %collective-permute-start = (bf16[2,17,16,256]{3,2,1,0:T(8,128)(2,1)}, bf16[2,17,16,256]{3,2,1,0:T(8,128)(2,1)S(1)}, u32[]{:S(2)}, u32[]{:S(2)}) collective-permute-start(bf16[2,17,16,256]{3,2,1,0:T(8,128)(2,1)} %bitcast.175), channel_id=1, source_target_pairs={{0,8},{8,16},{16,24},{1,9},{9,17},{17,25},{2,10},{10,18},{18,26},{... | collective-permute-start | bytes 835592 | tf_op jit(solution)/shard_map/ppermute | solution.py:119
  28.8 4.4 %collective-permute-start.2 = (bf16[24,6,256]{2,1,0:T(8,128)(2,1)S(1)}, bf16[24,6,256]{2,1,0:T(8,128)(2,1)S(1)}, u32[]{:S(2)}, u32[]{:S(2)}) collective-permute-start(bf16[24,6,256]{2,1,0:T(8,128)(2,1)S(1)} %get-tuple-element.23), channel_id=1, source_target_pairs={{0,1},{1,2},{2,3},{3,4},{4,5},{5,6},{6,7},{7,0},{8,9},{9,10},{10,1... | collective-permute-start | bytes 221192 | tf_op jit(solution)/shard_map/ppermute | solution.py:129
  31.5 4.8 %collective-permute-start.3 = (bf16[24,6,256]{2,1,0:T(8,128)(2,1)S(1)}, bf16[24,6,256]{2,1,0:T(8,128)(2,1)S(1)}, u32[]{:S(2)}, u32[]{:S(2)}) collective-permute-start(bf16[24,6,256]{2,1,0:T(8,128)(2,1)S(1)} %get-tuple-element.24), channel_id=1, source_target_pairs={{1,0},{2,1},{3,2},{4,3},{5,4},{6,5},{7,6},{0,7},{9,8},{10,9},{11,1... | collective-permute-start | bytes 221192 | tf_op jit(solution)/shard_map/ppermute | solution.py:130
  36.5 14.8 %collective-permute-start.4 = (bf16[6,36,256]{2,1,0:T(8,128)(2,1)S(1)}, bf16[6,36,256]{2,1,0:T(8,128)(2,1)S(1)}, u32[]{:S(2)}, u32[]{:S(2)}) collective-permute-start(bf16[6,36,256]{2,1,0:T(8,128)(2,1)S(1)} %get-tuple-element.21), channel_id=1, source_target_pairs={{0,8},{8,16},{16,24},{1,9},{9,17},{17,25},{2,10},{10,18},{18,26},{... | collective-permute-start | bytes 331784 | tf_op jit(solution)/shard_map/ppermute | solution.py:238
  39.8 9.9 %collective-permute-start.5 = (bf16[6,36,256]{2,1,0:T(8,128)(2,1)S(1)}, bf16[6,36,256]{2,1,0:T(8,128)(2,1)S(1)}, u32[]{:S(2)}, u32[]{:S(2)}) collective-permute-start(bf16[6,36,256]{2,1,0:T(8,128)(2,1)S(1)} %get-tuple-element.22), channel_id=1, source_target_pairs={{8,0},{16,8},{24,16},{9,1},{17,9},{25,17},{10,2},{18,10},{26,18},{... | collective-permute-start | bytes 331784 | tf_op jit(solution)/shard_map/ppermute | solution.py:239
  42.9 5.0 %copy-start.7 = (bf16[2,256,1024]{2,1,0:T(8,128)(2,1)S(1)}, bf16[2,256,1024]{2,1,0:T(8,128)(2,1)}, u32[]{:S(2)}) copy-start(bf16[2,256,1024]{2,1,0:T(8,128)(2,1)} %param.24) | copy-start | bytes 3145732
  47.9 1.2 %copy-start = (bf16[2,1024,256]{2,1,0:T(8,128)(2,1)S(1)}, bf16[2,1024,256]{2,1,0:T(8,128)(2,1)}, u32[]{:S(2)}) copy-start(bf16[2,1024,256]{2,1,0:T(8,128)(2,1)} %param.25) | copy-start | bytes 3145732
